TPU v7x, 32 devices: a whole 2x2x4 slice. The times are simulated.
32 devices in a mesh: layer: 4 (over y, x), slab: 8 (over z, core).
Axes of the slice: x: 2, y: 2, z: 4, core: 2. Of those that a mesh axis runs over, the one named last changes fastest.
Arguments:
- labels: int32 [8192, 2048], P(('layer', 'slab')), parts along dimension 0, may hold values from 0 to 3
Outputs:
- q_panel: float32 [2, 2048, 20402], P(None, ('layer', 'slab')), parts along dimension 1
There are 4 independent parts, one for each index of `layer`. A program takes and returns all parts, laid end to end along the dimension named above; each array names one. Nothing has to cross between parts.
All inputs are finite; a program needn't handle non-finite values.
Results may differ from a plain program's by a relative error of at most 0.0003.
Values sent between devices are 32-bit elements; how exact they have to be, the bound alone decides.
No kernel may reach another device: no remote copies, remote signals or barrier semaphores. Data moves between devices by JAX's collectives and lax.ppermute only.
A program may use at most 192 MiB of HBM per device.

v0:
```python
import functools
import math

import jax
import jax.numpy as jnp
from jax import lax
from jax.experimental import pallas as pl
from jax.experimental.pallas import tpu as pltpu
from jax.sharding import PartitionSpec as P

HARM = 101
ROWS_DEV = 64
KEEP = 201
ORDERS = 10201
BLOCK_ROWS = 8
LANES = 128


PERMITS = (1.0, 2.1, 4.0, 12.1)


def extended_2(block, sides, width):
    for axis, dim in sides:
        count = lax.axis_size(axis)
        forward = [(i, i + 1) for i in range(count - 1)]
        forward.append((count - 1, 0))
        backward = [(target, source) for source, target in forward]
        low = lax.ppermute(
            lax.slice_in_dim(block, block.shape[dim] - width, None, axis=dim), axis, forward
        )
        high = lax.ppermute(lax.slice_in_dim(block, 0, width, axis=dim), axis, backward)
        block = jnp.concatenate([low, block, high], axis=dim)
    return block


def permittivity(labels):
    total = jnp.zeros(labels.shape, jnp.float32)
    for index_value in range(4):
        total = total + jnp.where(
            labels == index_value, jnp.float32(PERMITS[index_value]), jnp.float32(0.0)
        )
    return total


def smooth_once(extended):
    middle = extended[1:-1]
    return (
        4.0 * middle
        + extended[:-2]
        + extended[2:]
        + jnp.roll(middle, 1, 1)
        + jnp.roll(middle, -1, 1)
    ) / 8.0


def gradient(extended):
    middle = extended[1:-1]
    grad_x = (extended[2:] - extended[:-2]) / 2.0
    grad_y = (jnp.roll(middle, -1, 1) - jnp.roll(middle, 1, 1)) / 2.0
    return (grad_x, grad_y)


def rim_rows(field_in):
    return extended_2(field_in, (("slab", 0),), 1)


def row_transform(spectra_in, positions, frequency, map_width):
    phases = frequency[:, None] * positions[None, :] % map_width
    angles = phases.astype(jnp.float32) * (2.0 * math.pi / map_width)
    table = jnp.stack([jnp.cos(angles), jnp.sin(angles)])
    products = jnp.einsum("smx,kxcn->skmcn", table, spectra_in, precision=lax.Precision.HIGHEST)
    real_part = products[0, :, :, 0] + products[1, :, :, 1]
    imag_part = products[0, :, :, 1] - products[1, :, :, 0]
    return jnp.stack([real_part, imag_part])


def chunk_segments(total, half):
    chunks = []
    for start in range(0, total, LANES):
        width = min(LANES, total - start)
        runs = []
        for lane in range(width):
            flat = start + lane
            h, j = divmod(flat, half)
            u, v = divmod(j, HARM)
            if not runs or runs[-1][0] != h or runs[-1][1] != u:
                runs.append((h, u, lane, v))
        chunks.append((start, width, runs))
    return chunks


def assemble_kernel(a0_ref, b0_ref, first_ref, second_ref, dval_ref, fl_ref, o_ref, z_ref):
    s = pl.program_id(0)
    rb = pl.program_id(1)
    win = z_ref.shape[1] // BLOCK_ROWS
    span = win + BLOCK_ROWS
    row_iota = lax.broadcasted_iota(jnp.int32, (win, LANES), 0)
    lane_iota = lax.broadcasted_iota(jnp.int32, (win, LANES), 1)
    for rr in range(BLOCK_ROWS):
        row = rb * BLOCK_ROWS + rr
        a0 = a0_ref[row]
        b0 = b0_ref[row]
        first = first_ref[row]
        second = second_ref[row]
        shift = (LANES - b0) % LANES
        base = pl.multiple_of(a0 // BLOCK_ROWS * BLOCK_ROWS, BLOCK_ROWS)
        lift = (span - a0 % BLOCK_ROWS) % span
        spot = (row_iota == first) & (lane_iota == second)
        wrap = lane_iota + b0 < LANES
        for h in range(2):
            combo = 2 * (rr % 2) + h
            x_lo = fl_ref[0, combo, pl.ds(base, span), pl.ds(0, LANES)]
            x_hi = fl_ref[0, combo, pl.ds(base, span), pl.ds(LANES, LANES)]
            x_lo = pltpu.roll(x_lo, lift, 0)[:win]
            x_hi = pltpu.roll(x_hi, lift, 0)[:win]
            x = jnp.where(wrap, pltpu.roll(x_lo, shift, 1), pltpu.roll(x_hi, shift, 1))
            d = jnp.where(s == 0, dval_ref[h, row], jnp.float32(0.0))
            x = x + jnp.where(spot, d, jnp.float32(0.0))
            z_ref[h, pl.ds(rr, win, stride=BLOCK_ROWS), :] = x
    lane = lax.broadcasted_iota(jnp.int32, (BLOCK_ROWS, LANES), 1)
    for start, width, runs in chunk_segments(o_ref.shape[2], o_ref.shape[2] // 2):
        acc = None
        for h, u, l0, v0 in runs:
            src = z_ref[h, pl.ds(u * BLOCK_ROWS, BLOCK_ROWS), :]
            sh = (l0 - v0) % LANES
            if sh:
                src = pltpu.roll(src, sh, 1)
            acc = src if acc is None else jnp.where(lane >= l0, src, acc)
        if width < LANES:
            acc = acc[:, :width]
        o_ref[0, :, pl.ds(start, width)] = acc


def assemble(a0, b0, first, second, dvals, tables, rows):
    win = 104
    n_blocks = rows // BLOCK_ROWS
    total = 2 * ORDERS
    grid_spec = pltpu.PrefetchScalarGridSpec(
        num_scalar_prefetch=4,
        grid=(2, n_blocks),
        in_specs=[
            pl.BlockSpec(memory_space=pltpu.SMEM),
            pl.BlockSpec((1,) + tables.shape[1:], lambda s, rb, *_: (s, 0, 0, 0)),
        ],
        out_specs=pl.BlockSpec((1, BLOCK_ROWS, total), lambda s, rb, *_: (s, rb, 0)),
        scratch_shapes=[pltpu.VMEM((2, win * BLOCK_ROWS, LANES), jnp.float32)],
    )
    return pl.pallas_call(
        assemble_kernel,
        grid_spec=grid_spec,
        out_shape=jax.ShapeDtypeStruct((2, rows, total), jnp.float32),
        compiler_params=pltpu.CompilerParams(dimension_semantics=("arbitrary", "arbitrary")),
    )(a0, b0, first, second, dvals, tables)


def shards(labels):
    slab_rows = labels.shape[0]
    map_width = labels.shape[1]
    devices = lax.axis_size("slab")
    my_index = lax.axis_index("slab")
    permit = permittivity(labels)
    smooth = permit
    for sweep_index in range(3):
        smooth = smooth_once(rim_rows(smooth))
    grad_x, grad_y = gradient(rim_rows(smooth))
    scale = jnp.sqrt(grad_x * grad_x + grad_y * grad_y + 1.0)
    normal_x = grad_x / scale
    normal_y = grad_y / scale
    inverse = 1.0 / permit
    contrast = permit - inverse
    fields = jnp.stack(
        [
            permit,
            contrast * normal_x * normal_x,
            contrast * normal_x * normal_y,
            contrast * normal_y * normal_y,
        ]
    )
    padded_keep = -(-KEEP // devices) * devices
    frequency = (HARM - 1) - jnp.arange(padded_keep, dtype=jnp.int32)
    columns = jnp.arange(map_width, dtype=jnp.int32)
    phases = columns[:, None] * frequency[None, :] % map_width
    angles = phases.astype(jnp.float32) * (2.0 * math.pi / map_width)
    col_table = jnp.stack([jnp.cos(angles), -jnp.sin(angles)], axis=1)
    half_spectra = jnp.einsum("kxy,ycn->kxcn", fields, col_table, precision=lax.Precision.HIGHEST)
    my_positions = my_index * slab_rows + jnp.arange(slab_rows, dtype=jnp.int32)
    partial_value = row_transform(half_spectra, my_positions, frequency, map_width)
    summed = lax.psum(partial_value, "slab")
    coef = summed / float(map_width * map_width)
    tables = jnp.stack(
        [coef[:, 2], coef[:, 0] - coef[:, 3], coef[:, 1] - coef[:, 0], -coef[:, 2]], axis=1
    )
    tables = jnp.pad(tables, ((0, 0), (0, 0), (0, 0), (0, 2 * LANES - padded_keep)))
    rows = ROWS_DEV
    spacing = ORDERS // (rows * devices // 2)
    window_rows = my_index * rows + jnp.arange(rows, dtype=jnp.int32)
    order_index = window_rows // 2 * spacing
    first = order_index // HARM
    second = order_index % HARM
    centre = (HARM - 1) // 2
    kx = 0.3 + 0.02 * (first - centre).astype(jnp.float32)
    ky = 0.2 + 0.02 * (second - centre).astype(jnp.float32)
    lower = window_rows % 2 == 1
    left = jnp.where(lower, ky * ky, kx * ky)
    right = jnp.where(lower, -(kx * ky), -(kx * kx))
    dvals = jnp.stack([left, right])
    a0 = (HARM - 1) - first
    b0 = (HARM - 1) - second
    return assemble(a0, b0, first, second, dvals, tables, rows)


def solution(mesh):
    placed = (P(("layer", "slab"), None),)
    return jax.shard_map(
        shards,
        mesh=mesh,
        in_specs=placed,
        out_specs=P(None, ("layer", "slab"), None),
        check_vma=False,
    )
```

profile of v0, /device:TPU:0, one launch (start us, length us, event | category | flops | bytes accessed | tf_op | source)
XLA Modules:
  0.0 169.8 jit_solution(6230413417635000972)
XLA Ops:
  6.5 2.3 %select_add_fusion = f32[256,2048]{1,0:T(8,128)S(1)} fusion(s32[256,2048]{1,0:T(8,128)} %param.1), kind=kLoop, calls=%fused_computation.47 | loop fusion | flops 5767168 | bytes 4194304 | tf_op jit(solution)/shard_map/add | solution.py:39
  8.9 0.5 collective-permute-start
  9.4 4.1 %collective-permute-start.1 = (f32[1,2048]{1,0:T(1,128)S(1)}, f32[1,2048]{1,0:T(1,128)S(1)}, u32[]{:S(2)}, u32[]{:S(2)}) collective-permute-start(f32[1,2048]{1,0:T(1,128)S(1)} %get-tuple-element.35), channel_id=1, source_target_pairs={{1,0},{2,1},{3,2},{4,3},{5,4},{6,5},{7,6},{0,7},{9,8},{10,9},{11,1... | collective-permute-start | bytes 24584 | tf_op jit(solution)/shard_map/ppermute | solution.py:31
  13.5 2.8 %fusion.71 = (f32[256,2047]{1,0:T(8,128)}, f32[256,2047]{1,0:T(8,128)}) fusion(f32[256,2048]{1,0:T(8,128)S(1)} %select_add_fusion), kind=kLoop, calls=%fused_computation.130 | loop fusion | bytes 8384512 | tf_op jit(solution)/shard_map/jit(_roll_static)/slice | solution.py:51
  16.3 8.8 %fusion.38 = (f32[2048,1,208]{0,2,1:T(8,128)}, f32[2048,1,208]{0,2,1:T(8,128)}) fusion(s32[208]{0:T(256)S(1)} %iota_subtract_fusion), kind=kLoop, calls=%fused_computation.70 | loop fusion | flops 6389760 | bytes 3408704 | tf_op jit(solution)/shard_map/cos | solution.py:184
  25.1 0.9 fusion.45
  26.0 0.1 fusion.70
  26.1 0.0 collective-permute-done
  26.2 0.0 collective-permute-done.1
  26.2 3.1 %broadcast_multiply_fusion.1 = (f32[256,2048]{1,0:T(8,128)S(1)}, f32[256,2048]{1,0:T(8,128)S(1)}) fusion(f32[256,1]{1,0:T(8,128)S(1)} %get-tuple-element.37, f32[256,2047]{1,0:T(8,128)} %get-tuple-element.39, f32[256,2047]{1,0:T(8,128)} %get-tuple-element.38, f32[256,1]{1,0:T(8,128)S(1)} %get-tuple-element.36, f32[1,2048]{1,0:T(1,128)S(1)} %collective-permute-done.1, ...), kind=kLoop, calls=%fused_computation.64 | loop fusion | flops 5242880 | bytes 10502144 | tf_op jit(solution)/shard_map/div | solution.py:47
  29.3 0.8 fusion.68
  30.0 0.1 collective-permute-start.2
  30.1 3.5 %collective-permute-start.3 = (f32[1,2048]{1,0:T(1,128)S(1)}, f32[1,2048]{1,0:T(1,128)S(1)}, u32[]{:S(2)}, u32[]{:S(2)}) collective-permute-start(f32[1,2048]{1,0:T(1,128)S(1)} %get-tuple-element.29), channel_id=1, source_target_pairs={{1,0},{2,1},{3,2},{4,3},{5,4},{6,5},{7,6},{0,7},{9,8},{10,9},{11,1... | collective-permute-start | bytes 24584 | tf_op jit(solution)/shard_map/ppermute | solution.py:31
  33.6 0.1 fusion.67
  33.7 1.2 collective-permute-done.2
  35.0 0.0 collective-permute-done.3
  35.0 1.2 broadcast_multiply_fusion
  36.2 0.8 fusion.63
  37.0 0.1 collective-permute-start.4
  37.0 3.6 %collective-permute-start.5 = (f32[1,2048]{1,0:T(1,128)S(1)}, f32[1,2048]{1,0:T(1,128)S(1)}, u32[]{:S(2)}, u32[]{:S(2)}) collective-permute-start(f32[1,2048]{1,0:T(1,128)S(1)} %get-tuple-element.27), channel_id=1, source_target_pairs={{1,0},{2,1},{3,2},{4,3},{5,4},{6,5},{7,6},{0,7},{9,8},{10,9},{11,1... | collective-permute-start | bytes 24584 | tf_op jit(solution)/shard_map/ppermute | solution.py:31
  40.6 0.1 fusion.64
  40.7 1.2 collective-permute-done.4
  41.9 0.1 collective-permute-done.5
  42.0 0.9 fusion.15
  42.9 0.8 fusion.61
  43.6 3.6 %collective-permute-start.6 = (f32[1,2048]{1,0:T(1,128)S(1)}, f32[1,2048]{1,0:T(1,128)S(1)}, u32[]{:S(2)}, u32[]{:S(2)}) collective-permute-start(f32[1,2048]{1,0:T(1,128)S(1)} %get-tuple-element.16), channel_id=1, source_target_pairs={{1,0},{2,1},{3,2},{4,3},{5,4},{6,5},{7,6},{0,7},{9,8},{10,9},{11,1... | collective-permute-start | bytes 24584 | tf_op jit(solution)/shard_map/ppermute | solution.py:31
  47.2 0.0 collective-permute-start.7
  47.2 0.1 fusion.62
  47.3 1.3 collective-permute-done.6
  48.6 3.5 %collective-permute-done.7 = f32[1,2048]{1,0:T(1,128)S(1)} collective-permute-done((f32[1,2048]{1,0:T(1,128)S(1)}, f32[1,2048]{1,0:T(1,128)S(1)}, u32[]{:S(2)}, u32[]{:S(2)}) %collective-permute-start.7) | collective-permute-done | bytes 8224 | tf_op jit(solution)/shard_map/ppermute | solution.py:28
  52.1 3.6 %multiply_bitcast_fusion.1 = (f32[1,256,2048]{2,1,0:T(8,128)S(1)}, f32[256,2048]{1,0:T(8,128)S(1)}, f32[1,256,2048]{2,1,0:T(8,128)S(1)}) fusion(s32[256,2048]{1,0:T(8,128)S(1)} %copy-done, f32[256,2047]{1,0:T(8,128)S(1)} %get-tuple-element.19, f32[256,1]{1,0:T(8,128)S(1)} %get-tuple-element.21, f32[256,1]{1,0:T(8,128)S(1)} %get-tuple-element.20, ...), kind=kLoop, calls=%fused_computation.43 | loop fusion | flops 14680064 | bytes 14696448 | tf_op jit(solution)/shard_map/stack | solution.py:171
  55.7 3.6 %multiply_bitcast_fusion = (f32[1,256,2048]{2,1,0:T(8,128)S(1)}, f32[256,2048]{1,0:T(8,128)S(1)}) fusion(f32[256,2048]{1,0:T(8,128)S(1)} %get-tuple-element.6, s32[256,2048]{1,0:T(8,128)S(1)} %copy-done, f32[256,2048]{1,0:T(8,128)S(1)} %fusion.15, f32[1,2048]{1,0:T(1,128)S(1)} %collective-permute-done.7, f32[1,2048]{1,0:T(1,128)S(1)} %collective-permute-done.6, ...), kind=kLoop, calls=%fused_computation.42 | loop fusion | flops 14680064 | bytes 14696448 | tf_op jit(solution)/shard_map/stack | solution.py:171
  59.2 1.0 fusion.9
  60.3 0.4 copy-done.1
  60.7 0.5 copy-done.2
  61.2 11.4 %fusion.35 = f32[4,256,2,208,1]{1,3,2,0,4:T(8,128)S(1)} fusion(f32[2048,1,208]{0,2,1:T(8,128)S(1)} %copy-done.2, f32[2048,1,208]{0,2,1:T(8,128)S(1)} %copy-done.1, f32[1,256,2048]{2,1,0:T(8,128)S(1)} %fusion.9, f32[1,256,2048]{2,1,0:T(8,128)S(1)} %get-tuple-element.7, f32[1,256,2048]{2,1,0:T(8,128)S(1)} %get-tuple-element.5, ...), kind=kOutput, calls=%fused_computation.62 | convolution fusion | flops 10476126208 | bytes 13500416 | tf_op jit(solution)/shard_map/kxy,ycn->kxcn/dot_general | solution.py:185
  72.6 3.1 %convolution_bitcast_fusion = f32[2,4,208,2,208]{4,2,1,3,0:T(8,128)S(1)} fusion(f32[4,256,2,208,1]{1,3,2,0,4:T(8,128)S(1)} %fusion.35, f32[1,208,256]{2,1,0:T(8,128)S(1)} %get-tuple-element.45, f32[1,208,256]{2,1,0:T(8,128)S(1)} %get-tuple-element.44), kind=kOutput, calls=%fused_computation.48 | convolution fusion | flops 2126618624 | bytes 4898816 | tf_op jit(solution)/shard_map/smx,kxcn->skmcn/dot_general | solution.py:71
  75.6 0.2 fusion.37
  75.9 1.3 pad_maximum_fusion.8
  77.2 0.0 all-reduce.3.cloned.1.call-update
  77.3 0.6 and_select_fusion.4
  77.8 0.6 broadcast_subtract_fusion
  78.4 0.6 pad_maximum_fusion.9.dval_ref
  79.0 59.8 %all-reduce.3.cloned.1.call-done = f32[2,4,208,208]{3,2,1,0:T(8,128)} async-done(((f32[2,4,208,208]{3,2,1,0:T(8,128)}), f32[2,4,208,208]{3,2,1,0:T(8,128)}) %all-reduce.3.cloned.1.call-update) | async-done | bytes 1384464 | tf_op jit(solution)/shard_map/psum | solution.py:188
  138.9 1.6 broadcast_multiply_fusion.2
  140.4 0.2 fusion.72
  140.6 1.4 select_maximum_fusion.fl_ref
  142.0 20.9 %shard_map.17 = f32[2,64,20402]{2,1,0:T(8,128)} custom-call(s32[64]{0:T(128)} %get-tuple-element.53.a0_ref, s32[64]{0:T(128)} %get-tuple-element.52.b0_ref, s32[64]{0:T(128)} %get-tuple-element.49.first_ref, s32[64]{0:T(128)} %get-tuple-element.48.second_ref, f32[2,64]{1,0:T(2,128)} %pad_maximum_fusion.9.dval_ref, f32[2,4,208,256]{3,2,1,0:T(8,128)} %select_maximum_fusion.fl_ref), custom_call_target="tpu_custom_call" | custom-call | tf_op jit(solution)/shard_map/pallas_call | solution.py:148
  (12 shorter events, 0.1 us)
Async XLA Ops:
  6.5 132.3 %all-reduce.3.cloned.1.call-start = ((), (), s32[]{:S(2)}) async-start(), calls=%async_computation | async-start | bytes 3407872 | tf_op jit(solution)/shard_map/psum | solution.py:188
  8.9 17.2 %collective-permute-start = (f32[1,2048]{1,0:T(1,128)S(1)}, f32[1,2048]{1,0:T(1,128)S(1)}, u32[]{:S(2)}, u32[]{:S(2)}) collective-permute-start(f32[1,2048]{1,0:T(1,128)S(1)} %get-tuple-element.34), channel_id=1, source_target_pairs={{0,1},{1,2},{2,3},{3,4},{4,5},{5,6},{6,7},{7,0},{8,9},{9,10},{10,1... | collective-permute-start | bytes 24584 | tf_op jit(solution)/shard_map/ppermute | solution.py:28
  9.4 16.7 %collective-permute-start.1 = (f32[1,2048]{1,0:T(1,128)S(1)}, f32[1,2048]{1,0:T(1,128)S(1)}, u32[]{:S(2)}, u32[]{:S(2)}) collective-permute-start(f32[1,2048]{1,0:T(1,128)S(1)} %get-tuple-element.35), channel_id=1, source_target_pairs={{1,0},{2,1},{3,2},{4,3},{5,4},{6,5},{7,6},{0,7},{9,8},{10,9},{11,1... | collective-permute-start | bytes 24584 | tf_op jit(solution)/shard_map/ppermute | solution.py:31
  30.0 4.9 %collective-permute-start.2 = (f32[1,2048]{1,0:T(1,128)S(1)}, f32[1,2048]{1,0:T(1,128)S(1)}, u32[]{:S(2)}, u32[]{:S(2)}) collective-permute-start(f32[1,2048]{1,0:T(1,128)S(1)} %get-tuple-element.28), channel_id=1, source_target_pairs={{0,1},{1,2},{2,3},{3,4},{4,5},{5,6},{6,7},{7,0},{8,9},{9,10},{10,1... | collective-permute-start | bytes 24584 | tf_op jit(solution)/shard_map/ppermute | solution.py:28
  30.1 4.9 %collective-permute-start.3 = (f32[1,2048]{1,0:T(1,128)S(1)}, f32[1,2048]{1,0:T(1,128)S(1)}, u32[]{:S(2)}, u32[]{:S(2)}) collective-permute-start(f32[1,2048]{1,0:T(1,128)S(1)} %get-tuple-element.29), channel_id=1, source_target_pairs={{1,0},{2,1},{3,2},{4,3},{5,4},{6,5},{7,6},{0,7},{9,8},{10,9},{11,1... | collective-permute-start | bytes 24584 | tf_op jit(solution)/shard_map/ppermute | solution.py:31
  37.0 4.9 %collective-permute-start.4 = (f32[1,2048]{1,0:T(1,128)S(1)}, f32[1,2048]{1,0:T(1,128)S(1)}, u32[]{:S(2)}, u32[]{:S(2)}) collective-permute-start(f32[1,2048]{1,0:T(1,128)S(1)} %get-tuple-element.26), channel_id=1, source_target_pairs={{0,1},{1,2},{2,3},{3,4},{4,5},{5,6},{6,7},{7,0},{8,9},{9,10},{10,1... | collective-permute-start | bytes 24584 | tf_op jit(solution)/shard_map/ppermute | solution.py:28
  37.0 4.9 %collective-permute-start.5 = (f32[1,2048]{1,0:T(1,128)S(1)}, f32[1,2048]{1,0:T(1,128)S(1)}, u32[]{:S(2)}, u32[]{:S(2)}) collective-permute-start(f32[1,2048]{1,0:T(1,128)S(1)} %get-tuple-element.27), channel_id=1, source_target_pairs={{1,0},{2,1},{3,2},{4,3},{5,4},{6,5},{7,6},{0,7},{9,8},{10,9},{11,1... | collective-permute-start | bytes 24584 | tf_op jit(solution)/shard_map/ppermute | solution.py:31
  42.9 9.2 %copy-start = (s32[256,2048]{1,0:T(8,128)S(1)}, s32[256,2048]{1,0:T(8,128)}, u32[]{:S(2)}) copy-start(s32[256,2048]{1,0:T(8,128)} %param.1) | copy-start | bytes 6291460
  43.6 4.9 %collective-permute-start.6 = (f32[1,2048]{1,0:T(1,128)S(1)}, f32[1,2048]{1,0:T(1,128)S(1)}, u32[]{:S(2)}, u32[]{:S(2)}) collective-permute-start(f32[1,2048]{1,0:T(1,128)S(1)} %get-tuple-element.16), channel_id=1, source_target_pairs={{1,0},{2,1},{3,2},{4,3},{5,4},{6,5},{7,6},{0,7},{9,8},{10,9},{11,1... | collective-permute-start | bytes 24584 | tf_op jit(solution)/shard_map/ppermute | solution.py:31
  47.2 4.9 %collective-permute-start.7 = (f32[1,2048]{1,0:T(1,128)S(1)}, f32[1,2048]{1,0:T(1,128)S(1)}, u32[]{:S(2)}, u32[]{:S(2)}) collective-permute-start(f32[1,2048]{1,0:T(1,128)S(1)} %get-tuple-element.17), channel_id=1, source_target_pairs={{0,1},{1,2},{2,3},{3,4},{4,5},{5,6},{6,7},{7,0},{8,9},{9,10},{10,1... | collective-permute-start | bytes 24584 | tf_op jit(solution)/shard_map/ppermute | solution.py:28
  59.2 1.5 copy-start.1
  59.2 2.0 %copy-start.2 = (f32[2048,1,208]{0,2,1:T(8,128)S(1)}, f32[2048,1,208]{0,2,1:T(8,128)}, u32[]{:S(2)}) copy-start(f32[2048,1,208]{0,2,1:T(8,128)} %get-tuple-element.47) | copy-start | bytes 5111812
Sparse Core Ops, SparseCore 0:
  77.3 61.4 all-reduce.2
where the time goes:
time: 170 us
  waiting for transfers between devices  67.2 us (40%)
  other arithmetic  31.9 us (19%)
  Pallas kernels  20.9 us (12%)
  starting transfers between devices  15.4 us (9%)
  matrix products  14.4 us (8%)
  between operations  13.6 us (8%)
  local copies, waits for them, and re-layouts  6.36 us (4%)
    psum x1, waiting for transfers between devices, shards(): summed = lax.psum(partial_value, 'slab')  59.8 us
    pallas_call x1, Pallas kernels, assemble(): pl.pallas_call(assemble_kernel, grid_spec=grid_spec, out_shape=jax.ShapeD...  20.9 us
    ppermute x4, starting transfers between devices, extended_2(): lax.ppermute(lax.slice_in_dim(block, 0, width, axis=dim), axis, backward)  14.7 us
    dot_general x1, matrix products, shards(): jnp.einsum('kxy,ycn->kxcn', fields, col_table, precision=lax.Precision.HI...  11.4 us
    cos x1, other arithmetic, shards(): col_table = jnp.stack([jnp.cos(angles), -jnp.sin(angles)], axis=1)  8.83 us
    another operation x3, other arithmetic, shards(): jnp.stack([permit, contrast * normal_x * normal_x, contrast * normal_x *...  8.17 us
    ppermute x4, waiting for transfers between devices, extended_2(): lax.ppermute(lax.slice_in_dim(block, block.shape[dim] - width, None, axis...  5.95 us
    div x3, other arithmetic, smooth_once(): (4.0 * middle + extended[:-2] + extended[2:] + jnp.roll(middle, 1, 1) + j...  5.15 us
  transfers between devices with their start and end apart: 9, of which 6 were waited for; matrix products, arithmetic and copies ran while one was open for 9% of the time, Pallas kernels for 0%

commit v1 on v0

--- a/solution.py
+++ b/solution.py
@@ -159,10 +159,10 @@
     devices = lax.axis_size("slab")
     my_index = lax.axis_index("slab")
     permit = permittivity(labels)
-    smooth = permit
+    smooth = extended_2(permit, (("slab", 0),), 4)
     for sweep_index in range(3):
-        smooth = smooth_once(rim_rows(smooth))
-    grad_x, grad_y = gradient(rim_rows(smooth))
+        smooth = smooth_once(smooth)
+    grad_x, grad_y = gradient(smooth)
     scale = jnp.sqrt(grad_x * grad_x + grad_y * grad_y + 1.0)
     normal_x = grad_x / scale
     normal_y = grad_y / scale
@@ -177,9 +177,11 @@
         ]
     )
     padded_keep = -(-KEEP // devices) * devices
+    half_keep = -(-HARM // devices) * devices
     frequency = (HARM - 1) - jnp.arange(padded_keep, dtype=jnp.int32)
+    col_frequency = (HARM - 1) - jnp.arange(half_keep, dtype=jnp.int32)
     columns = jnp.arange(map_width, dtype=jnp.int32)
-    phases = columns[:, None] * frequency[None, :] % map_width
+    phases = columns[:, None] * col_frequency[None, :] % map_width
     angles = phases.astype(jnp.float32) * (2.0 * math.pi / map_width)
     col_table = jnp.stack([jnp.cos(angles), -jnp.sin(angles)], axis=1)
     half_spectra = jnp.einsum("kxy,ycn->kxcn", fields, col_table, precision=lax.Precision.HIGHEST)
@@ -187,10 +189,23 @@
     partial_value = row_transform(half_spectra, my_positions, frequency, map_width)
     summed = lax.psum(partial_value, "slab")
     coef = summed / float(map_width * map_width)
+    a_in = jnp.arange(padded_keep, dtype=jnp.int32)
+    c_in = jnp.arange(half_keep, dtype=jnp.int32)
+    b_out = jnp.arange(2 * LANES, dtype=jnp.int32)
+    flip_rows = (a_in[None, :] == (KEEP - 1) - a_in[:, None]).astype(jnp.float32)
+    keep_cols = ((c_in[:, None] == b_out[None, :]) & (b_out[None, :] < HARM)).astype(jnp.float32)
+    mirror_cols = (
+        (c_in[:, None] == (KEEP - 1) - b_out[None, :]) & (b_out[None, :] >= HARM)
+    ).astype(jnp.float32)
+    sign = jnp.array([1.0, -1.0], jnp.float32)[:, None, None, None]
+    direct = jnp.einsum("skac,cb->skab", coef, keep_cols, precision=lax.Precision.HIGHEST)
+    mirrored = jnp.einsum(
+        "ad,skdc,cb->skab", flip_rows, coef, mirror_cols, precision=lax.Precision.HIGHEST
+    )
+    full = direct + sign * mirrored
     tables = jnp.stack(
-        [coef[:, 2], coef[:, 0] - coef[:, 3], coef[:, 1] - coef[:, 0], -coef[:, 2]], axis=1
-    )
-    tables = jnp.pad(tables, ((0, 0), (0, 0), (0, 0), (0, 2 * LANES - padded_keep)))
+        [full[:, 2], full[:, 0] - full[:, 3], full[:, 1] - full[:, 0], -full[:, 2]], axis=1
+    )
     rows = ROWS_DEV
     spacing = ORDERS // (rows * devices // 2)
     window_rows = my_index * rows + jnp.arange(rows, dtype=jnp.int32)

time: 170 us -> 137 us (0.81)
  waiting for transfers between devices: 67.2 us -> 56.2 us
  starting transfers between devices: 15.4 us -> 4.64 us
  other arithmetic: 31.9 us -> 22.9 us
  local copies, waits for them, and re-layouts: 6.36 us -> 4.53 us
    ppermute x4 -> x1, starting transfers between devices: 14.7 us -> 4.09 us  [extended_2(): lax.ppermute(lax.slice_in_dim(block, 0, width, axis=dim), axis, backward)]
    ppermute x4 -> x1, waiting for transfers between devices: 5.95 us -> 0.01 us  [extended_2(): lax.ppermute(lax.slice_in_dim(block, block.shape[dim] - width, None, axis...]
    cos x1, other arithmetic: 8.83 us -> 4.3 us  [shards(): col_table = jnp.stack([jnp.cos(angles), -jnp.sin(angles)], axis=1)]
    slice x5 -> x0, local copies, waits for them, and re-layouts: 3.71 us -> none  [the longest x4 3.7 us: smooth_once(): jnp.roll(middle, 1, 1)]
    dot_general x0 -> x3, matrix products: none -> 3.68 us  [the longest x1 2.18 us: shards(): jnp.einsum('skac,cb->skab', coef, keep_cols, precision=lax.Precision.HIGH...]
    psum x1, waiting for transfers between devices: 59.8 us -> 56.2 us  [shards(): summed = lax.psum(partial_value, 'slab')]
    dot_general x1, matrix products: 11.4 us -> 8.7 us  [shards(): jnp.einsum('kxy,ycn->kxcn', fields, col_table, precision=lax.Precision.HI...]
    slice x2 -> x5, local copies, waits for them, and re-layouts: 0.84 us -> 2.81 us  [smooth_once(): jnp.roll(middle, -1, 1)]
  transfers between devices with their start and end apart: 9 -> 3, of which waited for: 6 -> 1; matrix products, arithmetic and copies ran while one was open for 9% -> 5% of each run, Pallas kernels for 0% -> 0%
where the time goes in v1:
time: 137 us
  waiting for transfers between devices  56.2 us (41%)
  other arithmetic  22.9 us (17%)
  Pallas kernels  20.9 us (15%)
  matrix products  13.9 us (10%)
  between operations  13.6 us (10%)
  starting transfers between devices  4.64 us (3%)
  local copies, waits for them, and re-layouts  4.53 us (3%)
    psum x1, waiting for transfers between devices, shards(): summed = lax.psum(partial_value, 'slab')  56.2 us
    pallas_call x1, Pallas kernels, assemble(): pl.pallas_call(assemble_kernel, grid_spec=grid_spec, out_shape=jax.ShapeD...  20.9 us
    dot_general x1, matrix products, shards(): jnp.einsum('kxy,ycn->kxcn', fields, col_table, precision=lax.Precision.HI...  8.7 us
    another operation x3, other arithmetic, shards(): jnp.stack([permit, contrast * normal_x * normal_x, contrast * normal_x *...  6.55 us
    cos x1, other arithmetic, shards(): col_table = jnp.stack([jnp.cos(angles), -jnp.sin(angles)], axis=1)  4.3 us
    ppermute x1, starting transfers between devices, extended_2(): lax.ppermute(lax.slice_in_dim(block, 0, width, axis=dim), axis, backward)  4.09 us
    div x3, other arithmetic, smooth_once(): (4.0 * middle + extended[:-2] + extended[2:] + jnp.roll(middle, 1, 1) + j...  4.07 us
    slice x5, local copies, waits for them, and re-layouts, smooth_once(): jnp.roll(middle, -1, 1)  2.81 us
  transfers between devices with their start and end apart: 3, of which 1 were waited for; matrix products, arithmetic and copies ran while one was open for 5% of the time, Pallas kernels for 0%

profile of v1, /device:TPU:0, one launch (start us, length us, event | category | flops | bytes accessed | tf_op | source)
XLA Modules:
  0.0 136.8 jit_solution(2479014607867713779)
XLA Ops:
  6.5 0.0 all-reduce.2.cloned.1.call-start
  6.5 2.3 %select_add_fusion = f32[256,2048]{1,0:T(8,128)S(1)} fusion(s32[256,2048]{1,0:T(8,128)} %param.2), kind=kLoop, calls=%fused_computation.45 | loop fusion | flops 5767168 | bytes 4194304 | tf_op jit(solution)/shard_map/add | solution.py:39
  8.9 0.5 collective-permute-start
  9.4 4.1 %collective-permute-start.1 = (f32[4,2048]{1,0:T(4,128)S(1)}, f32[4,2048]{1,0:T(4,128)S(1)}, u32[]{:S(2)}, u32[]{:S(2)}) collective-permute-start(f32[4,2048]{1,0:T(4,128)S(1)} %get-tuple-element.25), channel_id=1, source_target_pairs={{1,0},{2,1},{3,2},{4,3},{5,4},{6,5},{7,6},{0,7},{9,8},{10,9},{11,1... | collective-permute-start | bytes 98312 | tf_op jit(solution)/shard_map/ppermute | solution.py:31
  13.5 4.3 %fusion.43 = (f32[2048,1,104]{0,2,1:T(8,128)S(1)}, f32[2048,1,104]{0,2,1:T(8,128)}) fusion(s32[104]{0:T(128)S(1)} %iota_subtract_fusion.3), kind=kLoop, calls=%fused_computation.81 | loop fusion | flops 3194880 | bytes 1704352 | tf_op jit(solution)/shard_map/cos | solution.py:186
  17.9 0.9 fusion.51
  18.8 0.0 collective-permute-done
  18.8 0.0 collective-permute-done.1
  18.8 0.3 pad_maximum_fusion.4
  19.1 0.9 fusion.81
  20.0 2.3 %fusion.15 = f32[262,2048]{1,0:T(8,128)S(1)} fusion(f32[4,2048]{1,0:T(4,128)S(1)} %collective-permute-done.1, f32[256,2048]{1,0:T(8,128)S(1)} %select_add_fusion, f32[4,2048]{1,0:T(4,128)S(1)} %collective-permute-done, f32[264,2048]{1,0:T(8,128)S(1)} %pad_maximum_fusion.4, f32[262,2047]{1,0:T(8,128)S(1)} %get-tuple-element.22, ...), kind=kLoop, calls=%fused_computation.25 | loop fusion | flops 6438912 | bytes 15038416 | tf_op jit(solution)/shard_map/div | solution.py:47
  22.4 0.9 fusion.79
  23.2 0.1 fusion.80
  23.3 0.9 fusion.12
  24.2 0.9 fusion.77
  25.1 0.1 fusion.78
  25.2 0.9 fusion.9
  26.1 0.0 copy-start
  26.1 1.1 fusion.75
  27.2 0.1 fusion.76
  27.3 0.4 copy-done
  27.7 2.7 %multiply_bitcast_fusion.1 = (f32[1,256,2048]{2,1,0:T(8,128)S(1)}, f32[256,2048]{1,0:T(8,128)S(1)}, f32[1,256,2048]{2,1,0:T(8,128)S(1)}) fusion(s32[256,2048]{1,0:T(8,128)S(1)} %copy-done, f32[256,2047]{1,0:T(8,128)S(1)} %get-tuple-element.10, f32[256,1]{1,0:T(8,128)S(1)} %get-tuple-element.12, f32[256,1]{1,0:T(8,128)S(1)} %get-tuple-element.11, ...), kind=kLoop, calls=%fused_computation.41 | loop fusion | flops 13631488 | bytes 16777216 | tf_op jit(solution)/shard_map/stack | solution.py:171
  30.3 2.9 %multiply_bitcast_fusion = (f32[1,256,2048]{2,1,0:T(8,128)S(1)}, f32[256,2048]{1,0:T(8,128)S(1)}) fusion(f32[256,2048]{1,0:T(8,128)S(1)} %get-tuple-element.6, s32[256,2048]{1,0:T(8,128)S(1)} %copy-done, f32[258,2048]{1,0:T(8,128)S(1)} %fusion.9, f32[256,2047]{1,0:T(8,128)S(1)} %get-tuple-element.10, f32[256,1]{1,0:T(8,128)S(1)} %get-tuple-element.12, ...), kind=kLoop, calls=%fused_computation.40 | loop fusion | flops 13631488 | bytes 16777216 | tf_op jit(solution)/shard_map/stack | solution.py:171
  33.2 0.0 copy-start.2
  33.2 1.0 fusion.18
  34.3 0.1 copy-done.2
  34.4 8.7 %fusion.25 = f32[4,256,2,104,1]{1,3,4,2,0:T(8,128)S(1)} fusion(f32[2048,1,104]{0,2,1:T(8,128)S(1)} %copy-done.2, f32[2048,1,104]{0,2,1:T(8,128)S(1)} %get-tuple-element.32, f32[1,256,2048]{2,1,0:T(8,128)S(1)} %fusion.18, f32[1,256,2048]{2,1,0:T(8,128)S(1)} %get-tuple-element.7, f32[1,256,2048]{2,1,0:T(8,128)S(1)} %get-tuple-element.5, ...), kind=kOutput, calls=%fused_computation.52 | convolution fusion | flops 5241208832 | bytes 10944512 | tf_op jit(solution)/shard_map/kxy,ycn->kxcn/dot_general | solution.py:187
  43.1 1.5 %convolution_bitcast_fusion = f32[2,4,208,2,104]{2,4,0,3,1:T(8,128)S(1)} fusion(f32[4,256,2,104,1]{1,3,4,2,0:T(8,128)S(1)} %fusion.25, f32[1,208,256]{2,1,0:T(8,128)S(1)} %get-tuple-element.31, f32[1,208,256]{2,1,0:T(8,128)S(1)} %get-tuple-element.30), kind=kOutput, calls=%fused_computation.51 | convolution fusion | flops 1063362560 | bytes 2662400 | tf_op jit(solution)/shard_map/smx,kxcn->skmcn/dot_general | solution.py:71
  44.6 0.1 fusion.36
  44.7 0.1 fusion.38
  44.8 1.0 pad_maximum_fusion.6
  45.7 0.0 all-reduce.2.cloned.1.call-update
  45.8 0.5 and_select_fusion.4
  46.3 0.6 broadcast_subtract_fusion
  46.9 0.6 pad_maximum_fusion.7.dval_ref
  47.5 0.0 copy-start.3
  47.5 56.2 %all-reduce.2.cloned.1.call-done = f32[2,4,208,104]{2,3,1,0:T(8,128)} async-done(((f32[2,4,208,104]{2,3,1,0:T(8,128)}), f32[2,4,208,104]{2,3,1,0:T(8,128)}) %all-reduce.2.cloned.1.call-update) | async-done | bytes 692240 | tf_op jit(solution)/shard_map/psum | solution.py:190
  103.7 0.0 copy-start.1
  103.7 2.2 %fusion.34 = f32[2,4,208,256]{3,2,1,0:T(8,128)S(1)} fusion(f32[2,4,208,104]{2,3,1,0:T(8,128)} %all-reduce.2.cloned.1.call-done, pred[256]{0:T(512)(128)(4,1)S(1)} %iota_compare_fusion.4), kind=kOutput, calls=%fused_computation.66 | convolution fusion | flops 531854336 | bytes 2396416 | tf_op jit(solution)/shard_map/skac,cb->skab/dot_general | solution.py:201
  105.9 0.0 copy-done.1
  105.9 0.7 fusion.32
  106.6 0.0 copy-done.3
  106.6 0.8 multiply_add_fusion
  107.4 0.2 fusion.83
  107.6 1.4 %pad_maximum_fusion.5.fl_ref = f32[2,4,208,256]{3,2,1,0:T(8,128)} fusion(f32[2,1,208,256]{3,2,1,0:T(8,128)S(1)} %get-tuple-element.27, f32[2,1,208,256]{3,2,1,0:T(8,128)S(1)} %get-tuple-element.29, f32[2,1,208,256]{3,2,1,0:T(8,128)S(1)} %get-tuple-element.28, f32[2,1,208,256]{3,2,1,0:T(8,128)S(1)} %get-tuple-element.26), kind=kLoop, calls=%fused_computation.49 | loop fusion | flops 1277952 | bytes 3407872 | tf_op jit(solution)/shard_map/stack | solution.py:206
  109.0 20.9 %shard_map.28 = f32[2,64,20402]{2,1,0:T(8,128)} custom-call(s32[64]{0:T(128)} %get-tuple-element.39.a0_ref, s32[64]{0:T(128)} %get-tuple-element.38.b0_ref, s32[64]{0:T(128)} %get-tuple-element.35.first_ref, s32[64]{0:T(128)} %get-tuple-element.34.second_ref, f32[2,64]{1,0:T(2,128)} %pad_maximum_fusion.7.dval_ref, f32[2,4,208,256]{3,2,1,0:T(8,128)} %pad_maximum_fusion.5.fl_ref), custom_call_target="tpu_custom_call" | custom-call | tf_op jit(solution)/shard_map/pallas_call | solution.py:148
  (9 shorter events, 0.1 us)
Async XLA Ops:
  6.5 97.1 %all-reduce.2.cloned.1.call-start = ((), (), s32[]{:S(2)}) async-start(), calls=%async_computation | async-start | bytes 1703936 | tf_op jit(solution)/shard_map/psum | solution.py:190
  8.9 9.9 %collective-permute-start = (f32[4,2048]{1,0:T(4,128)S(1)}, f32[4,2048]{1,0:T(4,128)S(1)}, u32[]{:S(2)}, u32[]{:S(2)}) collective-permute-start(f32[4,2048]{1,0:T(4,128)S(1)} %get-tuple-element.24), channel_id=1, source_target_pairs={{0,1},{1,2},{2,3},{3,4},{4,5},{5,6},{6,7},{7,0},{8,9},{9,10},{10,1... | collective-permute-start | bytes 98312 | tf_op jit(solution)/shard_map/ppermute | solution.py:28
  9.4 9.4 %collective-permute-start.1 = (f32[4,2048]{1,0:T(4,128)S(1)}, f32[4,2048]{1,0:T(4,128)S(1)}, u32[]{:S(2)}, u32[]{:S(2)}) collective-permute-start(f32[4,2048]{1,0:T(4,128)S(1)} %get-tuple-element.25), channel_id=1, source_target_pairs={{1,0},{2,1},{3,2},{4,3},{5,4},{6,5},{7,6},{0,7},{9,8},{10,9},{11,1... | collective-permute-start | bytes 98312 | tf_op jit(solution)/shard_map/ppermute | solution.py:31
  26.1 1.6 %copy-start = (s32[256,2048]{1,0:T(8,128)S(1)}, s32[256,2048]{1,0:T(8,128)}, u32[]{:S(2)}) copy-start(s32[256,2048]{1,0:T(8,128)} %param.2) | copy-start | bytes 6291460
  33.2 1.2 copy-start.2
  47.5 59.1 %copy-start.3 = (f32[2]{0:T(128)S(1)}, f32[2]{0:T(128)}, u32[]{:S(2)}) copy-start(f32[2]{0:T(128)} %constant.127.clone) | copy-start | bytes 28
  103.7 2.2 %copy-start.1 = (f32[2,4,208,104]{2,3,1,0:T(8,128)S(1)}, f32[2,4,208,104]{2,3,1,0:T(8,128)}, u32[]{:S(2)}) copy-start(f32[2,4,208,104]{2,3,1,0:T(8,128)} %all-reduce.2.cloned.1.call-done) | copy-start | bytes 2076676
Sparse Core Ops, SparseCore 0:
  45.9 57.7 all-reduce.1

commit v2 on v1

--- a/solution.py
+++ b/solution.py
@@ -153,6 +153,26 @@
     )(a0, b0, first, second, dvals, tables)
 
 
+def line_sum(partial_value, my_index, devices):
+    core = my_index % 2
+    pairs = [(i, i ^ 1) for i in range(devices)]
+    keep = jnp.where(core == 0, partial_value[0], partial_value[1])
+    give = jnp.where(core == 0, partial_value[1], partial_value[0])
+    mine = keep + lax.ppermute(give, "slab", pairs)
+    right = [(i, i + 2) for i in range(devices - 2)]
+    left = [(i + 2, i) for i in range(devices - 2)]
+    from_left = jnp.zeros_like(mine)
+    from_right = jnp.zeros_like(mine)
+    for step in range(devices // 2 - 1):
+        from_left, from_right = (
+            lax.ppermute(mine + from_left, "slab", right),
+            lax.ppermute(mine + from_right, "slab", left),
+        )
+    total = mine + from_left + from_right
+    other = lax.ppermute(total, "slab", pairs)
+    return jnp.where(core == 0, jnp.stack([total, other]), jnp.stack([other, total]))
+
+
 def shards(labels):
     slab_rows = labels.shape[0]
     map_width = labels.shape[1]
@@ -187,7 +207,7 @@
     half_spectra = jnp.einsum("kxy,ycn->kxcn", fields, col_table, precision=lax.Precision.HIGHEST)
     my_positions = my_index * slab_rows + jnp.arange(slab_rows, dtype=jnp.int32)
     partial_value = row_transform(half_spectra, my_positions, frequency, map_width)
-    summed = lax.psum(partial_value, "slab")
+    summed = line_sum(partial_value, my_index, devices)
     coef = summed / float(map_width * map_width)
     a_in = jnp.arange(padded_keep, dtype=jnp.int32)
     c_in = jnp.arange(half_keep, dtype=jnp.int32)

time: 137 us -> 114 us (0.83)
  waiting for transfers between devices: 56.2 us -> 34.5 us
  starting transfers between devices: 4.64 us -> 18 us
  between operations: 13.6 us -> 0.34 us
    psum x1 -> x0, waiting for transfers between devices: 56.2 us -> none  [shards(): summed = lax.psum(partial_value, 'slab')]
    ppermute x0 -> x8, waiting for transfers between devices: none -> 34.5 us  [the longest x3 20.3 us: line_sum(): lax.ppermute(mine + from_left, 'slab', right)]
    ppermute x0 -> x8, starting transfers between devices: none -> 13.4 us  [the longest x3 9.12 us: line_sum(): lax.ppermute(mine + from_left, 'slab', right)]
  transfers between devices with their start and end apart: 3 -> 10, of which waited for: 1 -> 7; matrix products, arithmetic and copies ran while one was open for 5% -> 6% of each run, Pallas kernels for 0% -> 0%
where the time goes in v2:
time: 114 us; the launch traced here: 113 us
  waiting for transfers between devices  34.5 us (30%)
  other arithmetic  22.4 us (20%)
  Pallas kernels  20.9 us (18%)
  starting transfers between devices  18 us (16%)
  matrix products  12.7 us (11%)
  local copies, waits for them, and re-layouts  4.53 us (4%)
    pallas_call x1, Pallas kernels, assemble(): pl.pallas_call(assemble_kernel, grid_spec=grid_spec, out_shape=jax.ShapeD...  20.9 us
    ppermute x3, waiting for transfers between devices, line_sum(): lax.ppermute(mine + from_left, 'slab', right)  20.3 us
    ppermute x3, waiting for transfers between devices, line_sum(): lax.ppermute(mine + from_right, 'slab', left)  12.4 us
    ppermute x3, starting transfers between devices, line_sum(): lax.ppermute(mine + from_left, 'slab', right)  9.12 us
    dot_general x1, matrix products, shards(): jnp.einsum('kxy,ycn->kxcn', fields, col_table, precision=lax.Precision.HI...  8.7 us
    another operation x3, other arithmetic, shards(): jnp.stack([permit, contrast * normal_x * normal_x, contrast * normal_x *...  6.55 us
    cos x1, other arithmetic, shards(): col_table = jnp.stack([jnp.cos(angles), -jnp.sin(angles)], axis=1)  4.3 us
    ppermute x3, starting transfers between devices, line_sum(): lax.ppermute(mine + from_right, 'slab', left)  4.14 us
  transfers between devices with their start and end apart: 10, of which 7 were waited for; matrix products, arithmetic and copies ran while one was open for 6% of the time, Pallas kernels for 0%

profile of v2, /device:TPU:0, one launch (start us, length us, event | category | flops | bytes accessed | tf_op | source)
XLA Modules:
  0.0 113.4 jit_solution(15622055644025864712)
XLA Ops:
  0.0 2.3 %select_add_fusion = f32[256,2048]{1,0:T(8,128)S(1)} fusion(s32[256,2048]{1,0:T(8,128)} %param.2), kind=kLoop, calls=%fused_computation.45 | loop fusion | flops 5767168 | bytes 4194304 | tf_op jit(solution)/shard_map/add | solution.py:39
  2.4 0.5 collective-permute-start
  2.9 4.1 %collective-permute-start.1 = (f32[4,2048]{1,0:T(4,128)S(1)}, f32[4,2048]{1,0:T(4,128)S(1)}, u32[]{:S(2)}, u32[]{:S(2)}) collective-permute-start(f32[4,2048]{1,0:T(4,128)S(1)} %get-tuple-element.25), channel_id=1, source_target_pairs={{1,0},{2,1},{3,2},{4,3},{5,4},{6,5},{7,6},{0,7},{9,8},{10,9},{11,1... | collective-permute-start | bytes 98312 | tf_op jit(solution)/shard_map/ppermute | solution.py:31
  7.0 4.3 %fusion.43 = (f32[2048,1,104]{0,2,1:T(8,128)S(1)}, f32[2048,1,104]{0,2,1:T(8,128)}) fusion(s32[104]{0:T(128)S(1)} %iota_subtract_fusion.3), kind=kLoop, calls=%fused_computation.83 | loop fusion | flops 3194880 | bytes 1704352 | tf_op jit(solution)/shard_map/cos | solution.py:206
  11.3 0.9 fusion.53
  12.3 0.3 pad_maximum_fusion.4
  12.6 0.9 fusion.85
  13.4 2.3 %fusion.15 = f32[262,2048]{1,0:T(8,128)S(1)} fusion(f32[4,2048]{1,0:T(4,128)S(1)} %collective-permute-done.1, f32[256,2048]{1,0:T(8,128)S(1)} %select_add_fusion, f32[4,2048]{1,0:T(4,128)S(1)} %collective-permute-done, f32[264,2048]{1,0:T(8,128)S(1)} %pad_maximum_fusion.4, f32[262,2047]{1,0:T(8,128)S(1)} %get-tuple-element.22, ...), kind=kLoop, calls=%fused_computation.25 | loop fusion | flops 6438912 | bytes 15038416 | tf_op jit(solution)/shard_map/div | solution.py:47
  15.8 0.9 fusion.83
  16.7 0.1 fusion.84
  16.8 0.9 fusion.12
  17.6 0.9 fusion.81
  18.5 0.1 fusion.82
  18.6 0.9 fusion.9
  19.5 1.1 fusion.79
  20.6 0.1 fusion.80
  20.7 0.4 copy-done
  21.1 2.7 %multiply_bitcast_fusion.1 = (f32[1,256,2048]{2,1,0:T(8,128)S(1)}, f32[256,2048]{1,0:T(8,128)S(1)}, f32[1,256,2048]{2,1,0:T(8,128)S(1)}) fusion(s32[256,2048]{1,0:T(8,128)S(1)} %copy-done, f32[256,2047]{1,0:T(8,128)S(1)} %get-tuple-element.10, f32[256,1]{1,0:T(8,128)S(1)} %get-tuple-element.12, f32[256,1]{1,0:T(8,128)S(1)} %get-tuple-element.11, ...), kind=kLoop, calls=%fused_computation.41 | loop fusion | flops 13631488 | bytes 16777216 | tf_op jit(solution)/shard_map/stack | solution.py:191
  23.8 2.9 %multiply_bitcast_fusion = (f32[1,256,2048]{2,1,0:T(8,128)S(1)}, f32[256,2048]{1,0:T(8,128)S(1)}) fusion(f32[256,2048]{1,0:T(8,128)S(1)} %get-tuple-element.6, s32[256,2048]{1,0:T(8,128)S(1)} %copy-done, f32[258,2048]{1,0:T(8,128)S(1)} %fusion.9, f32[256,2047]{1,0:T(8,128)S(1)} %get-tuple-element.10, f32[256,1]{1,0:T(8,128)S(1)} %get-tuple-element.12, ...), kind=kLoop, calls=%fused_computation.40 | loop fusion | flops 13631488 | bytes 16777216 | tf_op jit(solution)/shard_map/stack | solution.py:191
  26.7 1.0 fusion.18
  27.7 0.1 copy-done.1
  27.8 8.7 %fusion.25 = f32[4,256,2,104,1]{1,3,4,2,0:T(8,128)S(1)} fusion(f32[2048,1,104]{0,2,1:T(8,128)S(1)} %copy-done.1, f32[2048,1,104]{0,2,1:T(8,128)S(1)} %get-tuple-element.36, f32[1,256,2048]{2,1,0:T(8,128)S(1)} %fusion.18, f32[1,256,2048]{2,1,0:T(8,128)S(1)} %get-tuple-element.7, f32[1,256,2048]{2,1,0:T(8,128)S(1)} %get-tuple-element.5, ...), kind=kOutput, calls=%fused_computation.52 | convolution fusion | flops 5241208832 | bytes 10944512 | tf_op jit(solution)/shard_map/kxy,ycn->kxcn/dot_general | solution.py:207
  36.5 1.5 %convolution_bitcast_fusion = f32[2,4,208,2,104]{2,4,0,3,1:T(8,128)S(1)} fusion(f32[4,256,2,104,1]{1,3,4,2,0:T(8,128)S(1)} %fusion.25, f32[1,208,256]{2,1,0:T(8,128)S(1)} %get-tuple-element.35, f32[1,208,256]{2,1,0:T(8,128)S(1)} %get-tuple-element.34), kind=kOutput, calls=%fused_computation.51 | convolution fusion | flops 1063362560 | bytes 2662400 | tf_op jit(solution)/shard_map/smx,kxcn->skmcn/dot_general | solution.py:71
  38.1 0.1 fusion.40
  38.2 1.8 %collective-permute-done.2 = f32[4,208,104]{1,2,0:T(8,128)S(1)} collective-permute-done((f32[4,208,104]{1,2,0:T(8,128)S(1)}, f32[4,208,104]{1,2,0:T(8,128)S(1)}, u32[]{:S(2)}, u32[]{:S(2)}) %collective-permute-start.2) | collective-permute-done | bytes 346144 | tf_op jit(solution)/shard_map/ppermute | solution.py:161
  40.0 0.1 bitcast_add_fusion
  40.1 2.1 %collective-permute-start.3 = (f32[4,208,104]{1,2,0:T(8,128)S(1)}, f32[4,208,104]{1,2,0:T(8,128)S(1)}, u32[]{:S(2)}, u32[]{:S(2)}) collective-permute-start(f32[4,208,104]{1,2,0:T(8,128)S(1)} %bitcast_add_fusion), channel_id=1, source_target_pairs={{0,2},{1,3},{2,4},{3,5},{4,6},{5,7},{8,10},{9,11},{10,12},{11,13},... | collective-permute-start | bytes 1038344 | tf_op jit(solution)/shard_map/ppermute | solution.py:168
  42.3 1.3 %collective-permute-start.6 = (f32[4,208,104]{1,2,0:T(8,128)S(1)}, f32[4,208,104]{1,2,0:T(8,128)S(1)}, u32[]{:S(2)}, u32[]{:S(2)}) collective-permute-start(f32[4,208,104]{1,2,0:T(8,128)S(1)} %bitcast_add_fusion), channel_id=1, source_target_pairs={{2,0},{3,1},{4,2},{5,3},{6,4},{7,5},{10,8},{11,9},{12,10},{13,11},... | collective-permute-start | bytes 1038344 | tf_op jit(solution)/shard_map/ppermute | solution.py:169
  43.6 8.0 %collective-permute-done.3 = f32[4,208,104]{1,2,0:T(8,128)S(1)} collective-permute-done((f32[4,208,104]{1,2,0:T(8,128)S(1)}, f32[4,208,104]{1,2,0:T(8,128)S(1)}, u32[]{:S(2)}, u32[]{:S(2)}) %collective-permute-start.3) | collective-permute-done | bytes 346144 | tf_op jit(solution)/shard_map/ppermute | solution.py:168
  51.6 4.1 %collective-permute-done.6 = f32[4,208,104]{1,2,0:T(8,128)S(1)} collective-permute-done((f32[4,208,104]{1,2,0:T(8,128)S(1)}, f32[4,208,104]{1,2,0:T(8,128)S(1)}, u32[]{:S(2)}, u32[]{:S(2)}) %collective-permute-start.6) | collective-permute-done | bytes 346144 | tf_op jit(solution)/shard_map/ppermute | solution.py:169
  55.8 3.5 %collective-permute-start.4 = (f32[4,208,104]{1,2,0:T(8,128)S(1)}, f32[4,208,104]{1,2,0:T(8,128)S(1)}, u32[]{:S(2)}, u32[]{:S(2)}) collective-permute-start(f32[4,208,104]{1,2,0:T(8,128)S(1)} %get-tuple-element.32), channel_id=1, source_target_pairs={{0,2},{1,3},{2,4},{3,5},{4,6},{5,7},{8,10},{9,11},{10,12},{11,13},... | collective-permute-start | bytes 1038344 | tf_op jit(solution)/shard_map/ppermute | solution.py:168
  59.3 1.3 %collective-permute-start.7 = (f32[4,208,104]{1,2,0:T(8,128)S(1)}, f32[4,208,104]{1,2,0:T(8,128)S(1)}, u32[]{:S(2)}, u32[]{:S(2)}) collective-permute-start(f32[4,208,104]{1,2,0:T(8,128)S(1)} %get-tuple-element.33), channel_id=1, source_target_pairs={{2,0},{3,1},{4,2},{5,3},{6,4},{7,5},{10,8},{11,9},{12,10},{13,11},... | collective-permute-start | bytes 1038344 | tf_op jit(solution)/shard_map/ppermute | solution.py:169
  60.6 6.9 %collective-permute-done.4 = f32[4,208,104]{1,2,0:T(8,128)S(1)} collective-permute-done((f32[4,208,104]{1,2,0:T(8,128)S(1)}, f32[4,208,104]{1,2,0:T(8,128)S(1)}, u32[]{:S(2)}, u32[]{:S(2)}) %collective-permute-start.4) | collective-permute-done | bytes 346144 | tf_op jit(solution)/shard_map/ppermute | solution.py:168
  67.5 4.1 %collective-permute-done.7 = f32[4,208,104]{1,2,0:T(8,128)S(1)} collective-permute-done((f32[4,208,104]{1,2,0:T(8,128)S(1)}, f32[4,208,104]{1,2,0:T(8,128)S(1)}, u32[]{:S(2)}, u32[]{:S(2)}) %collective-permute-start.7) | collective-permute-done | bytes 346144 | tf_op jit(solution)/shard_map/ppermute | solution.py:169
  71.7 0.1 fusion.88
  71.8 3.5 %collective-permute-start.5 = (f32[4,208,104]{1,2,0:T(8,128)S(1)}, f32[4,208,104]{1,2,0:T(8,128)S(1)}, u32[]{:S(2)}, u32[]{:S(2)}) collective-permute-start(f32[4,208,104]{1,2,0:T(8,128)S(1)} %get-tuple-element.30), channel_id=1, source_target_pairs={{0,2},{1,3},{2,4},{3,5},{4,6},{5,7},{8,10},{9,11},{10,12},{11,13},... | collective-permute-start | bytes 1038344 | tf_op jit(solution)/shard_map/ppermute | solution.py:168
  75.3 1.6 %collective-permute-start.8 = (f32[4,208,104]{1,2,0:T(8,128)S(1)}, f32[4,208,104]{1,2,0:T(8,128)S(1)}, u32[]{:S(2)}, u32[]{:S(2)}) collective-permute-start(f32[4,208,104]{1,2,0:T(8,128)S(1)} %get-tuple-element.31), channel_id=1, source_target_pairs={{2,0},{3,1},{4,2},{5,3},{6,4},{7,5},{10,8},{11,9},{12,10},{13,11},... | collective-permute-start | bytes 1038344 | tf_op jit(solution)/shard_map/ppermute | solution.py:169
  76.9 5.4 %collective-permute-done.5 = f32[4,208,104]{1,2,0:T(8,128)S(1)} collective-permute-done((f32[4,208,104]{1,2,0:T(8,128)S(1)}, f32[4,208,104]{1,2,0:T(8,128)S(1)}, u32[]{:S(2)}, u32[]{:S(2)}) %collective-permute-start.5) | collective-permute-done | bytes 346144 | tf_op jit(solution)/shard_map/ppermute | solution.py:168
  82.3 4.1 %collective-permute-done.8 = f32[4,208,104]{1,2,0:T(8,128)S(1)} collective-permute-done((f32[4,208,104]{1,2,0:T(8,128)S(1)}, f32[4,208,104]{1,2,0:T(8,128)S(1)}, u32[]{:S(2)}, u32[]{:S(2)}) %collective-permute-start.8) | collective-permute-done | bytes 346144 | tf_op jit(solution)/shard_map/ppermute | solution.py:169
  86.6 0.6 and_select_fusion.4
  87.2 0.6 broadcast_subtract_fusion
  87.8 0.6 pad_maximum_fusion.6.dval_ref
  88.4 0.7 fusion.33
  89.2 0.9 fusion.35
  90.1 0.8 multiply_add_fusion
  91.0 0.2 fusion.87
  91.1 1.4 %pad_maximum_fusion.5.fl_ref = f32[2,4,208,256]{3,2,1,0:T(8,128)} fusion(f32[2,1,208,256]{3,2,1,0:T(8,128)S(1)} %get-tuple-element.27, f32[2,1,208,256]{3,2,1,0:T(8,128)S(1)} %get-tuple-element.29, f32[2,1,208,256]{3,2,1,0:T(8,128)S(1)} %get-tuple-element.28, f32[2,1,208,256]{3,2,1,0:T(8,128)S(1)} %get-tuple-element.26), kind=kLoop, calls=%fused_computation.49 | loop fusion | flops 1277952 | bytes 3407872 | tf_op jit(solution)/shard_map/stack | solution.py:226
  92.5 20.9 %shard_map.28 = f32[2,64,20402]{2,1,0:T(8,128)} custom-call(s32[64]{0:T(128)} %get-tuple-element.43.a0_ref, s32[64]{0:T(128)} %get-tuple-element.42.b0_ref, s32[64]{0:T(128)} %get-tuple-element.39.first_ref, s32[64]{0:T(128)} %get-tuple-element.38.second_ref, f32[2,64]{1,0:T(2,128)} %pad_maximum_fusion.6.dval_ref, f32[2,4,208,256]{3,2,1,0:T(8,128)} %pad_maximum_fusion.5.fl_ref), custom_call_target="tpu_custom_call" | custom-call | tf_op jit(solution)/shard_map/pallas_call | solution.py:148
  (20 shorter events, 0.4 us)
Async XLA Ops:
  2.4 9.9 %collective-permute-start = (f32[4,2048]{1,0:T(4,128)S(1)}, f32[4,2048]{1,0:T(4,128)S(1)}, u32[]{:S(2)}, u32[]{:S(2)}) collective-permute-start(f32[4,2048]{1,0:T(4,128)S(1)} %get-tuple-element.24), channel_id=1, source_target_pairs={{0,1},{1,2},{2,3},{3,4},{4,5},{5,6},{6,7},{7,0},{8,9},{9,10},{10,1... | collective-permute-start | bytes 98312 | tf_op jit(solution)/shard_map/ppermute | solution.py:28
  2.9 9.3 %collective-permute-start.1 = (f32[4,2048]{1,0:T(4,128)S(1)}, f32[4,2048]{1,0:T(4,128)S(1)}, u32[]{:S(2)}, u32[]{:S(2)}) collective-permute-start(f32[4,2048]{1,0:T(4,128)S(1)} %get-tuple-element.25), channel_id=1, source_target_pairs={{1,0},{2,1},{3,2},{4,3},{5,4},{6,5},{7,6},{0,7},{9,8},{10,9},{11,1... | collective-permute-start | bytes 98312 | tf_op jit(solution)/shard_map/ppermute | solution.py:31
  19.5 1.6 %copy-start = (s32[256,2048]{1,0:T(8,128)S(1)}, s32[256,2048]{1,0:T(8,128)}, u32[]{:S(2)}) copy-start(s32[256,2048]{1,0:T(8,128)} %param.2) | copy-start | bytes 6291460
  26.6 1.2 %copy-start.1 = (f32[2048,1,104]{0,2,1:T(8,128)S(1)}, f32[2048,1,104]{0,2,1:T(8,128)}, u32[]{:S(2)}) copy-start(f32[2048,1,104]{0,2,1:T(8,128)} %get-tuple-element.37) | copy-start | bytes 2555908
  38.2 1.8 %collective-permute-start.2 = (f32[4,208,104]{1,2,0:T(8,128)S(1)}, f32[4,208,104]{1,2,0:T(8,128)S(1)}, u32[]{:S(2)}, u32[]{:S(2)}) collective-permute-start(f32[4,208,104]{1,2,0:T(8,128)S(1)} %fusion.40), channel_id=1, source_target_pairs={{0,1},{1,0},{2,3},{3,2},{4,5},{5,4},{6,7},{7,6},{8,9},{9,8},{10,11... | collective-permute-start | bytes 1038344 | tf_op jit(solution)/shard_map/ppermute | solution.py:161
  40.1 11.5 %collective-permute-start.3 = (f32[4,208,104]{1,2,0:T(8,128)S(1)}, f32[4,208,104]{1,2,0:T(8,128)S(1)}, u32[]{:S(2)}, u32[]{:S(2)}) collective-permute-start(f32[4,208,104]{1,2,0:T(8,128)S(1)} %bitcast_add_fusion), channel_id=1, source_target_pairs={{0,2},{1,3},{2,4},{3,5},{4,6},{5,7},{8,10},{9,11},{10,12},{11,13},... | collective-permute-start | bytes 1038344 | tf_op jit(solution)/shard_map/ppermute | solution.py:168
  42.3 13.5 %collective-permute-start.6 = (f32[4,208,104]{1,2,0:T(8,128)S(1)}, f32[4,208,104]{1,2,0:T(8,128)S(1)}, u32[]{:S(2)}, u32[]{:S(2)}) collective-permute-start(f32[4,208,104]{1,2,0:T(8,128)S(1)} %bitcast_add_fusion), channel_id=1, source_target_pairs={{2,0},{3,1},{4,2},{5,3},{6,4},{7,5},{10,8},{11,9},{12,10},{13,11},... | collective-permute-start | bytes 1038344 | tf_op jit(solution)/shard_map/ppermute | solution.py:169
  55.8 11.7 %collective-permute-start.4 = (f32[4,208,104]{1,2,0:T(8,128)S(1)}, f32[4,208,104]{1,2,0:T(8,128)S(1)}, u32[]{:S(2)}, u32[]{:S(2)}) collective-permute-start(f32[4,208,104]{1,2,0:T(8,128)S(1)} %get-tuple-element.32), channel_id=1, source_target_pairs={{0,2},{1,3},{2,4},{3,5},{4,6},{5,7},{8,10},{9,11},{10,12},{11,13},... | collective-permute-start | bytes 1038344 | tf_op jit(solution)/shard_map/ppermute | solution.py:168
  59.3 12.3 %collective-permute-start.7 = (f32[4,208,104]{1,2,0:T(8,128)S(1)}, f32[4,208,104]{1,2,0:T(8,128)S(1)}, u32[]{:S(2)}, u32[]{:S(2)}) collective-permute-start(f32[4,208,104]{1,2,0:T(8,128)S(1)} %get-tuple-element.33), channel_id=1, source_target_pairs={{2,0},{3,1},{4,2},{5,3},{6,4},{7,5},{10,8},{11,9},{12,10},{13,11},... | collective-permute-start | bytes 1038344 | tf_op jit(solution)/shard_map/ppermute | solution.py:169
  71.8 10.6 %collective-permute-start.5 = (f32[4,208,104]{1,2,0:T(8,128)S(1)}, f32[4,208,104]{1,2,0:T(8,128)S(1)}, u32[]{:S(2)}, u32[]{:S(2)}) collective-permute-start(f32[4,208,104]{1,2,0:T(8,128)S(1)} %get-tuple-element.30), channel_id=1, source_target_pairs={{0,2},{1,3},{2,4},{3,5},{4,6},{5,7},{8,10},{9,11},{10,12},{11,13},... | collective-permute-start | bytes 1038344 | tf_op jit(solution)/shard_map/ppermute | solution.py:168
  75.3 11.2 %collective-permute-start.8 = (f32[4,208,104]{1,2,0:T(8,128)S(1)}, f32[4,208,104]{1,2,0:T(8,128)S(1)}, u32[]{:S(2)}, u32[]{:S(2)}) collective-permute-start(f32[4,208,104]{1,2,0:T(8,128)S(1)} %get-tuple-element.31), channel_id=1, source_target_pairs={{2,0},{3,1},{4,2},{5,3},{6,4},{7,5},{10,8},{11,9},{12,10},{13,11},... | collective-permute-start | bytes 1038344 | tf_op jit(solution)/shard_map/ppermute | solution.py:169
  86.5 1.9 %collective-permute-start.9 = (f32[4,208,104]{1,2,0:T(8,128)S(1)}, f32[4,208,104]{1,2,0:T(8,128)S(1)}, u32[]{:S(2)}, u32[]{:S(2)}) collective-permute-start(f32[4,208,104]{1,2,0:T(8,128)S(1)} %add_add_fusion), channel_id=1, source_target_pairs={{0,1},{1,0},{2,3},{3,2},{4,5},{5,4},{6,7},{7,6},{8,9},{9,8},{10,11... | collective-permute-start | bytes 1038344 | tf_op jit(solution)/shard_map/ppermute | solution.py:172
  88.4 1.7 %copy-start.2 = (f32[2]{0:T(128)S(1)}, f32[2]{0:T(128)}, u32[]{:S(2)}) copy-start(f32[2]{0:T(128)} %constant.134.clone) | copy-start | bytes 28

commit v3 on v2

--- a/solution.py
+++ b/solution.py
@@ -68,7 +68,7 @@
     phases = frequency[:, None] * positions[None, :] % map_width
     angles = phases.astype(jnp.float32) * (2.0 * math.pi / map_width)
     table = jnp.stack([jnp.cos(angles), jnp.sin(angles)])
-    products = jnp.einsum("smx,kxcn->skmcn", table, spectra_in, precision=lax.Precision.HIGHEST)
+    products = jnp.einsum("smx,kxcn->skmcn", table, spectra_in, precision=lax.Precision.HIGH)
     real_part = products[0, :, :, 0] + products[1, :, :, 1]
     imag_part = products[0, :, :, 1] - products[1, :, :, 0]
     return jnp.stack([real_part, imag_part])
@@ -204,7 +204,7 @@
     phases = columns[:, None] * col_frequency[None, :] % map_width
     angles = phases.astype(jnp.float32) * (2.0 * math.pi / map_width)
     col_table = jnp.stack([jnp.cos(angles), -jnp.sin(angles)], axis=1)
-    half_spectra = jnp.einsum("kxy,ycn->kxcn", fields, col_table, precision=lax.Precision.HIGHEST)
+    half_spectra = jnp.einsum("kxy,ycn->kxcn", fields, col_table, precision=lax.Precision.HIGH)
     my_positions = my_index * slab_rows + jnp.arange(slab_rows, dtype=jnp.int32)
     partial_value = row_transform(half_spectra, my_positions, frequency, map_width)
     summed = line_sum(partial_value, my_index, devices)

time: 114 us -> 109 us (0.956)
  matrix products: 12.7 us -> 7.54 us
    dot_general x1, matrix products: 8.7 us -> 4.19 us  [shards(): jnp.einsum('kxy,ycn->kxcn', fields, col_table, precision=lax.Precision.HIGH)]
  transfers between devices with their start and end apart: 10 -> 10, of which waited for: 7 -> 7; matrix products, arithmetic and copies ran while one was open for 6% -> 7% of each run, Pallas kernels for 0% -> 0%
where the time goes in v3:
time: 109 us; the launch traced here: 108 us
  waiting for transfers between devices  34.8 us (32%)
  other arithmetic  22.4 us (21%)
  Pallas kernels  20.9 us (19%)
  starting transfers between devices  17.8 us (16%)
  matrix products  7.54 us (7%)
  local copies, waits for them, and re-layouts  4.53 us (4%)
    pallas_call x1, Pallas kernels, assemble(): pl.pallas_call(assemble_kernel, grid_spec=grid_spec, out_shape=jax.ShapeD...  20.9 us
    ppermute x3, waiting for transfers between devices, line_sum(): lax.ppermute(mine + from_left, 'slab', right)  20.6 us
    ppermute x3, waiting for transfers between devices, line_sum(): lax.ppermute(mine + from_right, 'slab', left)  12.4 us
    ppermute x3, starting transfers between devices, line_sum(): lax.ppermute(mine + from_left, 'slab', right)  9.12 us
    another operation x3, other arithmetic, shards(): jnp.stack([permit, contrast * normal_x * normal_x, contrast * normal_x *...  6.55 us
    cos x1, other arithmetic, shards(): col_table = jnp.stack([jnp.cos(angles), -jnp.sin(angles)], axis=1)  4.3 us
    dot_general x1, matrix products, shards(): jnp.einsum('kxy,ycn->kxcn', fields, col_table, precision=lax.Precision.HIGH)  4.19 us
    ppermute x1, starting transfers between devices, extended_2(): lax.ppermute(lax.slice_in_dim(block, 0, width, axis=dim), axis, backward)  4.09 us
  transfers between devices with their start and end apart: 10, of which 7 were waited for; matrix products, arithmetic and copies ran while one was open for 7% of the time, Pallas kernels for 0%

profile of v3, /device:TPU:0, one launch (start us, length us, event | category | flops | bytes accessed | tf_op | source)
XLA Modules:
  0.0 108.3 jit_solution(7890829159601713822)
XLA Ops:
  0.0 2.3 %select_add_fusion = f32[256,2048]{1,0:T(8,128)S(1)} fusion(s32[256,2048]{1,0:T(8,128)} %param.2), kind=kLoop, calls=%fused_computation.45 | loop fusion | flops 5767168 | bytes 4194304 | tf_op jit(solution)/shard_map/add | solution.py:39
  2.4 0.5 collective-permute-start
  2.9 4.1 %collective-permute-start.1 = (f32[4,2048]{1,0:T(4,128)S(1)}, f32[4,2048]{1,0:T(4,128)S(1)}, u32[]{:S(2)}, u32[]{:S(2)}) collective-permute-start(f32[4,2048]{1,0:T(4,128)S(1)} %get-tuple-element.25), channel_id=1, source_target_pairs={{1,0},{2,1},{3,2},{4,3},{5,4},{6,5},{7,6},{0,7},{9,8},{10,9},{11,1... | collective-permute-start | bytes 98312 | tf_op jit(solution)/shard_map/ppermute | solution.py:31
  7.0 4.3 %fusion.43 = (f32[2048,1,104]{0,2,1:T(8,128)S(1)}, f32[2048,1,104]{0,2,1:T(8,128)}) fusion(s32[104]{0:T(128)S(1)} %iota_subtract_fusion.3), kind=kLoop, calls=%fused_computation.83 | loop fusion | flops 3194880 | bytes 1704352 | tf_op jit(solution)/shard_map/cos | solution.py:206
  11.3 0.9 fusion.53
  12.3 0.3 pad_maximum_fusion.4
  12.6 0.9 fusion.85
  13.4 2.3 %fusion.15 = f32[262,2048]{1,0:T(8,128)S(1)} fusion(f32[4,2048]{1,0:T(4,128)S(1)} %collective-permute-done.1, f32[256,2048]{1,0:T(8,128)S(1)} %select_add_fusion, f32[4,2048]{1,0:T(4,128)S(1)} %collective-permute-done, f32[264,2048]{1,0:T(8,128)S(1)} %pad_maximum_fusion.4, f32[262,2047]{1,0:T(8,128)S(1)} %get-tuple-element.22, ...), kind=kLoop, calls=%fused_computation.25 | loop fusion | flops 6438912 | bytes 15038416 | tf_op jit(solution)/shard_map/div | solution.py:47
  15.8 0.9 fusion.83
  16.7 0.1 fusion.84
  16.8 0.9 fusion.12
  17.6 0.9 fusion.81
  18.5 0.1 fusion.82
  18.6 0.9 fusion.9
  19.5 1.1 fusion.79
  20.6 0.1 fusion.80
  20.7 0.4 copy-done
  21.1 2.7 %multiply_bitcast_fusion.1 = (f32[1,256,2048]{2,1,0:T(8,128)S(1)}, f32[256,2048]{1,0:T(8,128)S(1)}, f32[1,256,2048]{2,1,0:T(8,128)S(1)}) fusion(s32[256,2048]{1,0:T(8,128)S(1)} %copy-done, f32[256,2047]{1,0:T(8,128)S(1)} %get-tuple-element.10, f32[256,1]{1,0:T(8,128)S(1)} %get-tuple-element.12, f32[256,1]{1,0:T(8,128)S(1)} %get-tuple-element.11, ...), kind=kLoop, calls=%fused_computation.41 | loop fusion | flops 13631488 | bytes 16777216 | tf_op jit(solution)/shard_map/stack | solution.py:191
  23.8 2.9 %multiply_bitcast_fusion = (f32[1,256,2048]{2,1,0:T(8,128)S(1)}, f32[256,2048]{1,0:T(8,128)S(1)}) fusion(f32[256,2048]{1,0:T(8,128)S(1)} %get-tuple-element.6, s32[256,2048]{1,0:T(8,128)S(1)} %copy-done, f32[258,2048]{1,0:T(8,128)S(1)} %fusion.9, f32[256,2047]{1,0:T(8,128)S(1)} %get-tuple-element.10, f32[256,1]{1,0:T(8,128)S(1)} %get-tuple-element.12, ...), kind=kLoop, calls=%fused_computation.40 | loop fusion | flops 13631488 | bytes 16777216 | tf_op jit(solution)/shard_map/stack | solution.py:191
  26.7 1.0 fusion.18
  27.7 0.1 copy-done.1
  27.8 4.2 %fusion.25 = f32[4,256,2,104,1]{1,3,4,2,0:T(8,128)S(1)} fusion(f32[2048,1,104]{0,2,1:T(8,128)S(1)} %copy-done.1, f32[2048,1,104]{0,2,1:T(8,128)S(1)} %get-tuple-element.36, f32[1,256,2048]{2,1,0:T(8,128)S(1)} %fusion.18, f32[1,256,2048]{2,1,0:T(8,128)S(1)} %get-tuple-element.7, f32[1,256,2048]{2,1,0:T(8,128)S(1)} %get-tuple-element.5, ...), kind=kOutput, calls=%fused_computation.52 | convolution fusion | flops 2623963136 | bytes 10944512 | tf_op jit(solution)/shard_map/kxy,ycn->kxcn/dot_general | solution.py:207
  32.0 0.9 convolution_bitcast_fusion
  32.9 0.1 fusion.40
  33.1 1.8 %collective-permute-done.2 = f32[4,208,104]{1,2,0:T(8,128)S(1)} collective-permute-done((f32[4,208,104]{1,2,0:T(8,128)S(1)}, f32[4,208,104]{1,2,0:T(8,128)S(1)}, u32[]{:S(2)}, u32[]{:S(2)}) %collective-permute-start.2) | collective-permute-done | bytes 346144 | tf_op jit(solution)/shard_map/ppermute | solution.py:161
  34.8 0.1 bitcast_add_fusion
  35.0 2.1 %collective-permute-start.3 = (f32[4,208,104]{1,2,0:T(8,128)S(1)}, f32[4,208,104]{1,2,0:T(8,128)S(1)}, u32[]{:S(2)}, u32[]{:S(2)}) collective-permute-start(f32[4,208,104]{1,2,0:T(8,128)S(1)} %bitcast_add_fusion), channel_id=1, source_target_pairs={{0,2},{1,3},{2,4},{3,5},{4,6},{5,7},{8,10},{9,11},{10,12},{11,13},... | collective-permute-start | bytes 1038344 | tf_op jit(solution)/shard_map/ppermute | solution.py:168
  37.1 1.3 %collective-permute-start.6 = (f32[4,208,104]{1,2,0:T(8,128)S(1)}, f32[4,208,104]{1,2,0:T(8,128)S(1)}, u32[]{:S(2)}, u32[]{:S(2)}) collective-permute-start(f32[4,208,104]{1,2,0:T(8,128)S(1)} %bitcast_add_fusion), channel_id=1, source_target_pairs={{2,0},{3,1},{4,2},{5,3},{6,4},{7,5},{10,8},{11,9},{12,10},{13,11},... | collective-permute-start | bytes 1038344 | tf_op jit(solution)/shard_map/ppermute | solution.py:169
  38.4 8.0 %collective-permute-done.3 = f32[4,208,104]{1,2,0:T(8,128)S(1)} collective-permute-done((f32[4,208,104]{1,2,0:T(8,128)S(1)}, f32[4,208,104]{1,2,0:T(8,128)S(1)}, u32[]{:S(2)}, u32[]{:S(2)}) %collective-permute-start.3) | collective-permute-done | bytes 346144 | tf_op jit(solution)/shard_map/ppermute | solution.py:168
  46.4 4.1 %collective-permute-done.6 = f32[4,208,104]{1,2,0:T(8,128)S(1)} collective-permute-done((f32[4,208,104]{1,2,0:T(8,128)S(1)}, f32[4,208,104]{1,2,0:T(8,128)S(1)}, u32[]{:S(2)}, u32[]{:S(2)}) %collective-permute-start.6) | collective-permute-done | bytes 346144 | tf_op jit(solution)/shard_map/ppermute | solution.py:169
  50.7 3.5 %collective-permute-start.4 = (f32[4,208,104]{1,2,0:T(8,128)S(1)}, f32[4,208,104]{1,2,0:T(8,128)S(1)}, u32[]{:S(2)}, u32[]{:S(2)}) collective-permute-start(f32[4,208,104]{1,2,0:T(8,128)S(1)} %get-tuple-element.32), channel_id=1, source_target_pairs={{0,2},{1,3},{2,4},{3,5},{4,6},{5,7},{8,10},{9,11},{10,12},{11,13},... | collective-permute-start | bytes 1038344 | tf_op jit(solution)/shard_map/ppermute | solution.py:168
  54.2 1.3 %collective-permute-start.7 = (f32[4,208,104]{1,2,0:T(8,128)S(1)}, f32[4,208,104]{1,2,0:T(8,128)S(1)}, u32[]{:S(2)}, u32[]{:S(2)}) collective-permute-start(f32[4,208,104]{1,2,0:T(8,128)S(1)} %get-tuple-element.33), channel_id=1, source_target_pairs={{2,0},{3,1},{4,2},{5,3},{6,4},{7,5},{10,8},{11,9},{12,10},{13,11},... | collective-permute-start | bytes 1038344 | tf_op jit(solution)/shard_map/ppermute | solution.py:169
  55.5 6.9 %collective-permute-done.4 = f32[4,208,104]{1,2,0:T(8,128)S(1)} collective-permute-done((f32[4,208,104]{1,2,0:T(8,128)S(1)}, f32[4,208,104]{1,2,0:T(8,128)S(1)}, u32[]{:S(2)}, u32[]{:S(2)}) %collective-permute-start.4) | collective-permute-done | bytes 346144 | tf_op jit(solution)/shard_map/ppermute | solution.py:168
  62.4 4.1 %collective-permute-done.7 = f32[4,208,104]{1,2,0:T(8,128)S(1)} collective-permute-done((f32[4,208,104]{1,2,0:T(8,128)S(1)}, f32[4,208,104]{1,2,0:T(8,128)S(1)}, u32[]{:S(2)}, u32[]{:S(2)}) %collective-permute-start.7) | collective-permute-done | bytes 346144 | tf_op jit(solution)/shard_map/ppermute | solution.py:169
  66.5 0.1 fusion.88
  66.6 3.5 %collective-permute-start.5 = (f32[4,208,104]{1,2,0:T(8,128)S(1)}, f32[4,208,104]{1,2,0:T(8,128)S(1)}, u32[]{:S(2)}, u32[]{:S(2)}) collective-permute-start(f32[4,208,104]{1,2,0:T(8,128)S(1)} %get-tuple-element.30), channel_id=1, source_target_pairs={{0,2},{1,3},{2,4},{3,5},{4,6},{5,7},{8,10},{9,11},{10,12},{11,13},... | collective-permute-start | bytes 1038344 | tf_op jit(solution)/shard_map/ppermute | solution.py:168
  70.1 1.3 %collective-permute-start.8 = (f32[4,208,104]{1,2,0:T(8,128)S(1)}, f32[4,208,104]{1,2,0:T(8,128)S(1)}, u32[]{:S(2)}, u32[]{:S(2)}) collective-permute-start(f32[4,208,104]{1,2,0:T(8,128)S(1)} %get-tuple-element.31), channel_id=1, source_target_pairs={{2,0},{3,1},{4,2},{5,3},{6,4},{7,5},{10,8},{11,9},{12,10},{13,11},... | collective-permute-start | bytes 1038344 | tf_op jit(solution)/shard_map/ppermute | solution.py:169
  71.4 5.7 %collective-permute-done.5 = f32[4,208,104]{1,2,0:T(8,128)S(1)} collective-permute-done((f32[4,208,104]{1,2,0:T(8,128)S(1)}, f32[4,208,104]{1,2,0:T(8,128)S(1)}, u32[]{:S(2)}, u32[]{:S(2)}) %collective-permute-start.5) | collective-permute-done | bytes 346144 | tf_op jit(solution)/shard_map/ppermute | solution.py:168
  77.1 4.1 %collective-permute-done.8 = f32[4,208,104]{1,2,0:T(8,128)S(1)} collective-permute-done((f32[4,208,104]{1,2,0:T(8,128)S(1)}, f32[4,208,104]{1,2,0:T(8,128)S(1)}, u32[]{:S(2)}, u32[]{:S(2)}) %collective-permute-start.8) | collective-permute-done | bytes 346144 | tf_op jit(solution)/shard_map/ppermute | solution.py:169
  81.4 0.6 and_select_fusion.4
  82.1 0.6 broadcast_subtract_fusion
  82.7 0.6 pad_maximum_fusion.6.dval_ref
  83.2 0.7 fusion.33
  84.0 0.9 fusion.35
  84.9 0.8 multiply_add_fusion
  85.8 0.2 fusion.87
  85.9 1.4 %pad_maximum_fusion.5.fl_ref = f32[2,4,208,256]{3,2,1,0:T(8,128)} fusion(f32[2,1,208,256]{3,2,1,0:T(8,128)S(1)} %get-tuple-element.27, f32[2,1,208,256]{3,2,1,0:T(8,128)S(1)} %get-tuple-element.29, f32[2,1,208,256]{3,2,1,0:T(8,128)S(1)} %get-tuple-element.28, f32[2,1,208,256]{3,2,1,0:T(8,128)S(1)} %get-tuple-element.26), kind=kLoop, calls=%fused_computation.49 | loop fusion | flops 1277952 | bytes 3407872 | tf_op jit(solution)/shard_map/stack | solution.py:226
  87.3 20.9 %shard_map.28 = f32[2,64,20402]{2,1,0:T(8,128)} custom-call(s32[64]{0:T(128)} %get-tuple-element.43.a0_ref, s32[64]{0:T(128)} %get-tuple-element.42.b0_ref, s32[64]{0:T(128)} %get-tuple-element.39.first_ref, s32[64]{0:T(128)} %get-tuple-element.38.second_ref, f32[2,64]{1,0:T(2,128)} %pad_maximum_fusion.6.dval_ref, f32[2,4,208,256]{3,2,1,0:T(8,128)} %pad_maximum_fusion.5.fl_ref), custom_call_target="tpu_custom_call" | custom-call | tf_op jit(solution)/shard_map/pallas_call | solution.py:148
  (20 shorter events, 0.4 us)
Async XLA Ops:
  2.4 9.9 %collective-permute-start = (f32[4,2048]{1,0:T(4,128)S(1)}, f32[4,2048]{1,0:T(4,128)S(1)}, u32[]{:S(2)}, u32[]{:S(2)}) collective-permute-start(f32[4,2048]{1,0:T(4,128)S(1)} %get-tuple-element.24), channel_id=1, source_target_pairs={{0,1},{1,2},{2,3},{3,4},{4,5},{5,6},{6,7},{7,0},{8,9},{9,10},{10,1... | collective-permute-start | bytes 98312 | tf_op jit(solution)/shard_map/ppermute | solution.py:28
  2.9 9.3 %collective-permute-start.1 = (f32[4,2048]{1,0:T(4,128)S(1)}, f32[4,2048]{1,0:T(4,128)S(1)}, u32[]{:S(2)}, u32[]{:S(2)}) collective-permute-start(f32[4,2048]{1,0:T(4,128)S(1)} %get-tuple-element.25), channel_id=1, source_target_pairs={{1,0},{2,1},{3,2},{4,3},{5,4},{6,5},{7,6},{0,7},{9,8},{10,9},{11,1... | collective-permute-start | bytes 98312 | tf_op jit(solution)/shard_map/ppermute | solution.py:31
  19.5 1.6 %copy-start = (s32[256,2048]{1,0:T(8,128)S(1)}, s32[256,2048]{1,0:T(8,128)}, u32[]{:S(2)}) copy-start(s32[256,2048]{1,0:T(8,128)} %param.2) | copy-start | bytes 6291460
  26.6 1.2 %copy-start.1 = (f32[2048,1,104]{0,2,1:T(8,128)S(1)}, f32[2048,1,104]{0,2,1:T(8,128)}, u32[]{:S(2)}) copy-start(f32[2048,1,104]{0,2,1:T(8,128)} %get-tuple-element.37) | copy-start | bytes 2555908
  33.0 1.8 %collective-permute-start.2 = (f32[4,208,104]{1,2,0:T(8,128)S(1)}, f32[4,208,104]{1,2,0:T(8,128)S(1)}, u32[]{:S(2)}, u32[]{:S(2)}) collective-permute-start(f32[4,208,104]{1,2,0:T(8,128)S(1)} %fusion.40), channel_id=1, source_target_pairs={{0,1},{1,0},{2,3},{3,2},{4,5},{5,4},{6,7},{7,6},{8,9},{9,8},{10,11... | collective-permute-start | bytes 1038344 | tf_op jit(solution)/shard_map/ppermute | solution.py:161
  35.0 11.5 %collective-permute-start.3 = (f32[4,208,104]{1,2,0:T(8,128)S(1)}, f32[4,208,104]{1,2,0:T(8,128)S(1)}, u32[]{:S(2)}, u32[]{:S(2)}) collective-permute-start(f32[4,208,104]{1,2,0:T(8,128)S(1)} %bitcast_add_fusion), channel_id=1, source_target_pairs={{0,2},{1,3},{2,4},{3,5},{4,6},{5,7},{8,10},{9,11},{10,12},{11,13},... | collective-permute-start | bytes 1038344 | tf_op jit(solution)/shard_map/ppermute | solution.py:168
  37.1 13.5 %collective-permute-start.6 = (f32[4,208,104]{1,2,0:T(8,128)S(1)}, f32[4,208,104]{1,2,0:T(8,128)S(1)}, u32[]{:S(2)}, u32[]{:S(2)}) collective-permute-start(f32[4,208,104]{1,2,0:T(8,128)S(1)} %bitcast_add_fusion), channel_id=1, source_target_pairs={{2,0},{3,1},{4,2},{5,3},{6,4},{7,5},{10,8},{11,9},{12,10},{13,11},... | collective-permute-start | bytes 1038344 | tf_op jit(solution)/shard_map/ppermute | solution.py:169
  50.7 11.7 %collective-permute-start.4 = (f32[4,208,104]{1,2,0:T(8,128)S(1)}, f32[4,208,104]{1,2,0:T(8,128)S(1)}, u32[]{:S(2)}, u32[]{:S(2)}) collective-permute-start(f32[4,208,104]{1,2,0:T(8,128)S(1)} %get-tuple-element.32), channel_id=1, source_target_pairs={{0,2},{1,3},{2,4},{3,5},{4,6},{5,7},{8,10},{9,11},{10,12},{11,13},... | collective-permute-start | bytes 1038344 | tf_op jit(solution)/shard_map/ppermute | solution.py:168
  54.2 12.3 %collective-permute-start.7 = (f32[4,208,104]{1,2,0:T(8,128)S(1)}, f32[4,208,104]{1,2,0:T(8,128)S(1)}, u32[]{:S(2)}, u32[]{:S(2)}) collective-permute-start(f32[4,208,104]{1,2,0:T(8,128)S(1)} %get-tuple-element.33), channel_id=1, source_target_pairs={{2,0},{3,1},{4,2},{5,3},{6,4},{7,5},{10,8},{11,9},{12,10},{13,11},... | collective-permute-start | bytes 1038344 | tf_op jit(solution)/shard_map/ppermute | solution.py:169
  66.6 10.6 %collective-permute-start.5 = (f32[4,208,104]{1,2,0:T(8,128)S(1)}, f32[4,208,104]{1,2,0:T(8,128)S(1)}, u32[]{:S(2)}, u32[]{:S(2)}) collective-permute-start(f32[4,208,104]{1,2,0:T(8,128)S(1)} %get-tuple-element.30), channel_id=1, source_target_pairs={{0,2},{1,3},{2,4},{3,5},{4,6},{5,7},{8,10},{9,11},{10,12},{11,13},... | collective-permute-start | bytes 1038344 | tf_op jit(solution)/shard_map/ppermute | solution.py:168
  70.1 11.2 %collective-permute-start.8 = (f32[4,208,104]{1,2,0:T(8,128)S(1)}, f32[4,208,104]{1,2,0:T(8,128)S(1)}, u32[]{:S(2)}, u32[]{:S(2)}) collective-permute-start(f32[4,208,104]{1,2,0:T(8,128)S(1)} %get-tuple-element.31), channel_id=1, source_target_pairs={{2,0},{3,1},{4,2},{5,3},{6,4},{7,5},{10,8},{11,9},{12,10},{13,11},... | collective-permute-start | bytes 1038344 | tf_op jit(solution)/shard_map/ppermute | solution.py:169
  81.4 1.9 %collective-permute-start.9 = (f32[4,208,104]{1,2,0:T(8,128)S(1)}, f32[4,208,104]{1,2,0:T(8,128)S(1)}, u32[]{:S(2)}, u32[]{:S(2)}) collective-permute-start(f32[4,208,104]{1,2,0:T(8,128)S(1)} %add_add_fusion), channel_id=1, source_target_pairs={{0,1},{1,0},{2,3},{3,2},{4,5},{5,4},{6,7},{7,6},{8,9},{9,8},{10,11... | collective-permute-start | bytes 1038344 | tf_op jit(solution)/shard_map/ppermute | solution.py:172
  83.2 1.7 %copy-start.2 = (f32[2]{0:T(128)S(1)}, f32[2]{0:T(128)}, u32[]{:S(2)}) copy-start(f32[2]{0:T(128)} %constant.134.clone) | copy-start | bytes 28

commit v4 on v3

--- a/solution.py
+++ b/solution.py
@@ -92,10 +92,10 @@
 def assemble_kernel(a0_ref, b0_ref, first_ref, second_ref, dval_ref, fl_ref, o_ref, z_ref):
     s = pl.program_id(0)
     rb = pl.program_id(1)
-    win = z_ref.shape[1] // BLOCK_ROWS
-    span = win + BLOCK_ROWS
-    row_iota = lax.broadcasted_iota(jnp.int32, (win, LANES), 0)
-    lane_iota = lax.broadcasted_iota(jnp.int32, (win, LANES), 1)
+    span = z_ref.shape[1] // BLOCK_ROWS - BLOCK_ROWS
+    lane_iota = lax.broadcasted_iota(jnp.int32, (span, LANES), 1)
+    sub = lax.broadcasted_iota(jnp.int32, (BLOCK_ROWS, LANES), 0)
+    lane = lax.broadcasted_iota(jnp.int32, (BLOCK_ROWS, LANES), 1)
     for rr in range(BLOCK_ROWS):
         row = rb * BLOCK_ROWS + rr
         a0 = a0_ref[row]
@@ -104,24 +104,24 @@
         second = second_ref[row]
         shift = (LANES - b0) % LANES
         base = pl.multiple_of(a0 // BLOCK_ROWS * BLOCK_ROWS, BLOCK_ROWS)
-        lift = (span - a0 % BLOCK_ROWS) % span
-        spot = (row_iota == first) & (lane_iota == second)
+        off = a0 % BLOCK_ROWS
+        dest = pl.multiple_of((BLOCK_ROWS - off) * BLOCK_ROWS, BLOCK_ROWS) + rr
+        spot_tile = pl.multiple_of((first + BLOCK_ROWS) * BLOCK_ROWS, BLOCK_ROWS)
         wrap = lane_iota + b0 < LANES
+        spot = (sub == rr) & (lane == second)
         for h in range(2):
             combo = 2 * (rr % 2) + h
             x_lo = fl_ref[0, combo, pl.ds(base, span), pl.ds(0, LANES)]
             x_hi = fl_ref[0, combo, pl.ds(base, span), pl.ds(LANES, LANES)]
-            x_lo = pltpu.roll(x_lo, lift, 0)[:win]
-            x_hi = pltpu.roll(x_hi, lift, 0)[:win]
             x = jnp.where(wrap, pltpu.roll(x_lo, shift, 1), pltpu.roll(x_hi, shift, 1))
+            z_ref[h, pl.ds(dest, span, stride=BLOCK_ROWS), :] = x
             d = jnp.where(s == 0, dval_ref[h, row], jnp.float32(0.0))
-            x = x + jnp.where(spot, d, jnp.float32(0.0))
-            z_ref[h, pl.ds(rr, win, stride=BLOCK_ROWS), :] = x
-    lane = lax.broadcasted_iota(jnp.int32, (BLOCK_ROWS, LANES), 1)
+            tile = z_ref[h, pl.ds(spot_tile, BLOCK_ROWS), :]
+            z_ref[h, pl.ds(spot_tile, BLOCK_ROWS), :] = tile + jnp.where(spot, d, jnp.float32(0.0))
     for start, width, runs in chunk_segments(o_ref.shape[2], o_ref.shape[2] // 2):
         acc = None
         for h, u, l0, v0 in runs:
-            src = z_ref[h, pl.ds(u * BLOCK_ROWS, BLOCK_ROWS), :]
+            src = z_ref[h, pl.ds((u + BLOCK_ROWS) * BLOCK_ROWS, BLOCK_ROWS), :]
             sh = (l0 - v0) % LANES
             if sh:
                 src = pltpu.roll(src, sh, 1)
@@ -132,7 +132,7 @@
 
 
 def assemble(a0, b0, first, second, dvals, tables, rows):
-    win = 104
+    span = 112
     n_blocks = rows // BLOCK_ROWS
     total = 2 * ORDERS
     grid_spec = pltpu.PrefetchScalarGridSpec(
@@ -143,7 +143,7 @@
             pl.BlockSpec((1,) + tables.shape[1:], lambda s, rb, *_: (s, 0, 0, 0)),
         ],
         out_specs=pl.BlockSpec((1, BLOCK_ROWS, total), lambda s, rb, *_: (s, rb, 0)),
-        scratch_shapes=[pltpu.VMEM((2, win * BLOCK_ROWS, LANES), jnp.float32)],
+        scratch_shapes=[pltpu.VMEM((2, (span + BLOCK_ROWS) * BLOCK_ROWS, LANES), jnp.float32)],
     )
     return pl.pallas_call(
         assemble_kernel,

time: 109 us -> 108 us (level)
  no operation moved by 1% of the time
where the time goes in v4:
time: 108 us; the launch traced here: 107 us
  waiting for transfers between devices  34.8 us (32%)
  other arithmetic  22.4 us (21%)
  Pallas kernels  20.1 us (19%)
  starting transfers between devices  17.8 us (16%)
  matrix products  7.54 us (7%)
  local copies, waits for them, and re-layouts  4.53 us (4%)
    ppermute x3, waiting for transfers between devices, line_sum(): lax.ppermute(mine + from_left, 'slab', right)  20.6 us
    pallas_call x1, Pallas kernels, assemble(): pl.pallas_call(assemble_kernel, grid_spec=grid_spec, out_shape=jax.ShapeD...  20.1 us
    ppermute x3, waiting for transfers between devices, line_sum(): lax.ppermute(mine + from_right, 'slab', left)  12.4 us
    ppermute x3, starting transfers between devices, line_sum(): lax.ppermute(mine + from_left, 'slab', right)  9.12 us
    another operation x3, other arithmetic, shards(): jnp.stack([permit, contrast * normal_x * normal_x, contrast * normal_x *...  6.55 us
    cos x1, other arithmetic, shards(): col_table = jnp.stack([jnp.cos(angles), -jnp.sin(angles)], axis=1)  4.3 us
    dot_general x1, matrix products, shards(): jnp.einsum('kxy,ycn->kxcn', fields, col_table, precision=lax.Precision.HIGH)  4.19 us
    ppermute x1, starting transfers between devices, extended_2(): lax.ppermute(lax.slice_in_dim(block, 0, width, axis=dim), axis, backward)  4.09 us
  transfers between devices with their start and end apart: 10, of which 7 were waited for; matrix products, arithmetic and copies ran while one was open for 7% of the time, Pallas kernels for 0%

profile of v4, /device:TPU:0, one launch (start us, length us, event | category | flops | bytes accessed | tf_op | source)
XLA Modules:
  0.0 107.4 jit_solution(1538186713618367840)
XLA Ops:
  0.0 2.3 %select_add_fusion = f32[256,2048]{1,0:T(8,128)S(1)} fusion(s32[256,2048]{1,0:T(8,128)} %param.2), kind=kLoop, calls=%fused_computation.45 | loop fusion | flops 5767168 | bytes 4194304 | tf_op jit(solution)/shard_map/add | solution.py:39
  2.4 0.5 collective-permute-start
  2.9 4.1 %collective-permute-start.1 = (f32[4,2048]{1,0:T(4,128)S(1)}, f32[4,2048]{1,0:T(4,128)S(1)}, u32[]{:S(2)}, u32[]{:S(2)}) collective-permute-start(f32[4,2048]{1,0:T(4,128)S(1)} %get-tuple-element.25), channel_id=1, source_target_pairs={{1,0},{2,1},{3,2},{4,3},{5,4},{6,5},{7,6},{0,7},{9,8},{10,9},{11,1... | collective-permute-start | bytes 98312 | tf_op jit(solution)/shard_map/ppermute | solution.py:31
  7.0 4.3 %fusion.43 = (f32[2048,1,104]{0,2,1:T(8,128)S(1)}, f32[2048,1,104]{0,2,1:T(8,128)}) fusion(s32[104]{0:T(128)S(1)} %iota_subtract_fusion.3), kind=kLoop, calls=%fused_computation.83 | loop fusion | flops 3194880 | bytes 1704352 | tf_op jit(solution)/shard_map/cos | solution.py:206
  11.3 0.9 fusion.53
  12.3 0.3 pad_maximum_fusion.4
  12.6 0.9 fusion.85
  13.4 2.3 %fusion.15 = f32[262,2048]{1,0:T(8,128)S(1)} fusion(f32[4,2048]{1,0:T(4,128)S(1)} %collective-permute-done.1, f32[256,2048]{1,0:T(8,128)S(1)} %select_add_fusion, f32[4,2048]{1,0:T(4,128)S(1)} %collective-permute-done, f32[264,2048]{1,0:T(8,128)S(1)} %pad_maximum_fusion.4, f32[262,2047]{1,0:T(8,128)S(1)} %get-tuple-element.22, ...), kind=kLoop, calls=%fused_computation.25 | loop fusion | flops 6438912 | bytes 15038416 | tf_op jit(solution)/shard_map/div | solution.py:47
  15.8 0.9 fusion.83
  16.7 0.1 fusion.84
  16.8 0.9 fusion.12
  17.6 0.9 fusion.81
  18.5 0.1 fusion.82
  18.6 0.9 fusion.9
  19.5 1.1 fusion.79
  20.6 0.1 fusion.80
  20.7 0.4 copy-done
  21.1 2.7 %multiply_bitcast_fusion.1 = (f32[1,256,2048]{2,1,0:T(8,128)S(1)}, f32[256,2048]{1,0:T(8,128)S(1)}, f32[1,256,2048]{2,1,0:T(8,128)S(1)}) fusion(s32[256,2048]{1,0:T(8,128)S(1)} %copy-done, f32[256,2047]{1,0:T(8,128)S(1)} %get-tuple-element.10, f32[256,1]{1,0:T(8,128)S(1)} %get-tuple-element.12, f32[256,1]{1,0:T(8,128)S(1)} %get-tuple-element.11, ...), kind=kLoop, calls=%fused_computation.41 | loop fusion | flops 13631488 | bytes 16777216 | tf_op jit(solution)/shard_map/stack | solution.py:191
  23.8 2.9 %multiply_bitcast_fusion = (f32[1,256,2048]{2,1,0:T(8,128)S(1)}, f32[256,2048]{1,0:T(8,128)S(1)}) fusion(f32[256,2048]{1,0:T(8,128)S(1)} %get-tuple-element.6, s32[256,2048]{1,0:T(8,128)S(1)} %copy-done, f32[258,2048]{1,0:T(8,128)S(1)} %fusion.9, f32[256,2047]{1,0:T(8,128)S(1)} %get-tuple-element.10, f32[256,1]{1,0:T(8,128)S(1)} %get-tuple-element.12, ...), kind=kLoop, calls=%fused_computation.40 | loop fusion | flops 13631488 | bytes 16777216 | tf_op jit(solution)/shard_map/stack | solution.py:191
  26.7 1.0 fusion.18
  27.7 0.1 copy-done.1
  27.8 4.2 %fusion.25 = f32[4,256,2,104,1]{1,3,4,2,0:T(8,128)S(1)} fusion(f32[2048,1,104]{0,2,1:T(8,128)S(1)} %copy-done.1, f32[2048,1,104]{0,2,1:T(8,128)S(1)} %get-tuple-element.36, f32[1,256,2048]{2,1,0:T(8,128)S(1)} %fusion.18, f32[1,256,2048]{2,1,0:T(8,128)S(1)} %get-tuple-element.7, f32[1,256,2048]{2,1,0:T(8,128)S(1)} %get-tuple-element.5, ...), kind=kOutput, calls=%fused_computation.52 | convolution fusion | flops 2623963136 | bytes 10944512 | tf_op jit(solution)/shard_map/kxy,ycn->kxcn/dot_general | solution.py:207
  32.0 0.9 convolution_bitcast_fusion
  32.9 0.1 fusion.40
  33.1 1.8 %collective-permute-done.2 = f32[4,208,104]{1,2,0:T(8,128)S(1)} collective-permute-done((f32[4,208,104]{1,2,0:T(8,128)S(1)}, f32[4,208,104]{1,2,0:T(8,128)S(1)}, u32[]{:S(2)}, u32[]{:S(2)}) %collective-permute-start.2) | collective-permute-done | bytes 346144 | tf_op jit(solution)/shard_map/ppermute | solution.py:161
  34.8 0.1 bitcast_add_fusion
  35.0 2.1 %collective-permute-start.3 = (f32[4,208,104]{1,2,0:T(8,128)S(1)}, f32[4,208,104]{1,2,0:T(8,128)S(1)}, u32[]{:S(2)}, u32[]{:S(2)}) collective-permute-start(f32[4,208,104]{1,2,0:T(8,128)S(1)} %bitcast_add_fusion), channel_id=1, source_target_pairs={{0,2},{1,3},{2,4},{3,5},{4,6},{5,7},{8,10},{9,11},{10,12},{11,13},... | collective-permute-start | bytes 1038344 | tf_op jit(solution)/shard_map/ppermute | solution.py:168
  37.1 1.3 %collective-permute-start.6 = (f32[4,208,104]{1,2,0:T(8,128)S(1)}, f32[4,208,104]{1,2,0:T(8,128)S(1)}, u32[]{:S(2)}, u32[]{:S(2)}) collective-permute-start(f32[4,208,104]{1,2,0:T(8,128)S(1)} %bitcast_add_fusion), channel_id=1, source_target_pairs={{2,0},{3,1},{4,2},{5,3},{6,4},{7,5},{10,8},{11,9},{12,10},{13,11},... | collective-permute-start | bytes 1038344 | tf_op jit(solution)/shard_map/ppermute | solution.py:169
  38.4 8.0 %collective-permute-done.3 = f32[4,208,104]{1,2,0:T(8,128)S(1)} collective-permute-done((f32[4,208,104]{1,2,0:T(8,128)S(1)}, f32[4,208,104]{1,2,0:T(8,128)S(1)}, u32[]{:S(2)}, u32[]{:S(2)}) %collective-permute-start.3) | collective-permute-done | bytes 346144 | tf_op jit(solution)/shard_map/ppermute | solution.py:168
  46.4 4.1 %collective-permute-done.6 = f32[4,208,104]{1,2,0:T(8,128)S(1)} collective-permute-done((f32[4,208,104]{1,2,0:T(8,128)S(1)}, f32[4,208,104]{1,2,0:T(8,128)S(1)}, u32[]{:S(2)}, u32[]{:S(2)}) %collective-permute-start.6) | collective-permute-done | bytes 346144 | tf_op jit(solution)/shard_map/ppermute | solution.py:169
  50.7 3.5 %collective-permute-start.4 = (f32[4,208,104]{1,2,0:T(8,128)S(1)}, f32[4,208,104]{1,2,0:T(8,128)S(1)}, u32[]{:S(2)}, u32[]{:S(2)}) collective-permute-start(f32[4,208,104]{1,2,0:T(8,128)S(1)} %get-tuple-element.32), channel_id=1, source_target_pairs={{0,2},{1,3},{2,4},{3,5},{4,6},{5,7},{8,10},{9,11},{10,12},{11,13},... | collective-permute-start | bytes 1038344 | tf_op jit(solution)/shard_map/ppermute | solution.py:168
  54.2 1.3 %collective-permute-start.7 = (f32[4,208,104]{1,2,0:T(8,128)S(1)}, f32[4,208,104]{1,2,0:T(8,128)S(1)}, u32[]{:S(2)}, u32[]{:S(2)}) collective-permute-start(f32[4,208,104]{1,2,0:T(8,128)S(1)} %get-tuple-element.33), channel_id=1, source_target_pairs={{2,0},{3,1},{4,2},{5,3},{6,4},{7,5},{10,8},{11,9},{12,10},{13,11},... | collective-permute-start | bytes 1038344 | tf_op jit(solution)/shard_map/ppermute | solution.py:169
  55.5 6.9 %collective-permute-done.4 = f32[4,208,104]{1,2,0:T(8,128)S(1)} collective-permute-done((f32[4,208,104]{1,2,0:T(8,128)S(1)}, f32[4,208,104]{1,2,0:T(8,128)S(1)}, u32[]{:S(2)}, u32[]{:S(2)}) %collective-permute-start.4) | collective-permute-done | bytes 346144 | tf_op jit(solution)/shard_map/ppermute | solution.py:168
  62.4 4.1 %collective-permute-done.7 = f32[4,208,104]{1,2,0:T(8,128)S(1)} collective-permute-done((f32[4,208,104]{1,2,0:T(8,128)S(1)}, f32[4,208,104]{1,2,0:T(8,128)S(1)}, u32[]{:S(2)}, u32[]{:S(2)}) %collective-permute-start.7) | collective-permute-done | bytes 346144 | tf_op jit(solution)/shard_map/ppermute | solution.py:169
  66.5 0.1 fusion.88
  66.6 3.5 %collective-permute-start.5 = (f32[4,208,104]{1,2,0:T(8,128)S(1)}, f32[4,208,104]{1,2,0:T(8,128)S(1)}, u32[]{:S(2)}, u32[]{:S(2)}) collective-permute-start(f32[4,208,104]{1,2,0:T(8,128)S(1)} %get-tuple-element.30), channel_id=1, source_target_pairs={{0,2},{1,3},{2,4},{3,5},{4,6},{5,7},{8,10},{9,11},{10,12},{11,13},... | collective-permute-start | bytes 1038344 | tf_op jit(solution)/shard_map/ppermute | solution.py:168
  70.1 1.3 %collective-permute-start.8 = (f32[4,208,104]{1,2,0:T(8,128)S(1)}, f32[4,208,104]{1,2,0:T(8,128)S(1)}, u32[]{:S(2)}, u32[]{:S(2)}) collective-permute-start(f32[4,208,104]{1,2,0:T(8,128)S(1)} %get-tuple-element.31), channel_id=1, source_target_pairs={{2,0},{3,1},{4,2},{5,3},{6,4},{7,5},{10,8},{11,9},{12,10},{13,11},... | collective-permute-start | bytes 1038344 | tf_op jit(solution)/shard_map/ppermute | solution.py:169
  71.4 5.7 %collective-permute-done.5 = f32[4,208,104]{1,2,0:T(8,128)S(1)} collective-permute-done((f32[4,208,104]{1,2,0:T(8,128)S(1)}, f32[4,208,104]{1,2,0:T(8,128)S(1)}, u32[]{:S(2)}, u32[]{:S(2)}) %collective-permute-start.5) | collective-permute-done | bytes 346144 | tf_op jit(solution)/shard_map/ppermute | solution.py:168
  77.1 4.1 %collective-permute-done.8 = f32[4,208,104]{1,2,0:T(8,128)S(1)} collective-permute-done((f32[4,208,104]{1,2,0:T(8,128)S(1)}, f32[4,208,104]{1,2,0:T(8,128)S(1)}, u32[]{:S(2)}, u32[]{:S(2)}) %collective-permute-start.8) | collective-permute-done | bytes 346144 | tf_op jit(solution)/shard_map/ppermute | solution.py:169
  81.4 0.6 and_select_fusion.4
  82.1 0.6 broadcast_subtract_fusion
  82.7 0.6 pad_maximum_fusion.6.dval_ref
  83.2 0.7 fusion.33
  84.0 0.9 fusion.35
  84.9 0.8 multiply_add_fusion
  85.8 0.2 fusion.87
  85.9 1.4 %pad_maximum_fusion.5.fl_ref = f32[2,4,208,256]{3,2,1,0:T(8,128)} fusion(f32[2,1,208,256]{3,2,1,0:T(8,128)S(1)} %get-tuple-element.27, f32[2,1,208,256]{3,2,1,0:T(8,128)S(1)} %get-tuple-element.29, f32[2,1,208,256]{3,2,1,0:T(8,128)S(1)} %get-tuple-element.28, f32[2,1,208,256]{3,2,1,0:T(8,128)S(1)} %get-tuple-element.26), kind=kLoop, calls=%fused_computation.49 | loop fusion | flops 1277952 | bytes 3407872 | tf_op jit(solution)/shard_map/stack | solution.py:226
  87.3 20.1 %shard_map.28 = f32[2,64,20402]{2,1,0:T(8,128)} custom-call(s32[64]{0:T(128)} %get-tuple-element.43.a0_ref, s32[64]{0:T(128)} %get-tuple-element.42.b0_ref, s32[64]{0:T(128)} %get-tuple-element.39.first_ref, s32[64]{0:T(128)} %get-tuple-element.38.second_ref, f32[2,64]{1,0:T(2,128)} %pad_maximum_fusion.6.dval_ref, f32[2,4,208,256]{3,2,1,0:T(8,128)} %pad_maximum_fusion.5.fl_ref), custom_call_target="tpu_custom_call" | custom-call | tf_op jit(solution)/shard_map/pallas_call | solution.py:148
  (20 shorter events, 0.4 us)
Async XLA Ops:
  2.4 9.9 %collective-permute-start = (f32[4,2048]{1,0:T(4,128)S(1)}, f32[4,2048]{1,0:T(4,128)S(1)}, u32[]{:S(2)}, u32[]{:S(2)}) collective-permute-start(f32[4,2048]{1,0:T(4,128)S(1)} %get-tuple-element.24), channel_id=1, source_target_pairs={{0,1},{1,2},{2,3},{3,4},{4,5},{5,6},{6,7},{7,0},{8,9},{9,10},{10,1... | collective-permute-start | bytes 98312 | tf_op jit(solution)/shard_map/ppermute | solution.py:28
  2.9 9.3 %collective-permute-start.1 = (f32[4,2048]{1,0:T(4,128)S(1)}, f32[4,2048]{1,0:T(4,128)S(1)}, u32[]{:S(2)}, u32[]{:S(2)}) collective-permute-start(f32[4,2048]{1,0:T(4,128)S(1)} %get-tuple-element.25), channel_id=1, source_target_pairs={{1,0},{2,1},{3,2},{4,3},{5,4},{6,5},{7,6},{0,7},{9,8},{10,9},{11,1... | collective-permute-start | bytes 98312 | tf_op jit(solution)/shard_map/ppermute | solution.py:31
  19.5 1.6 %copy-start = (s32[256,2048]{1,0:T(8,128)S(1)}, s32[256,2048]{1,0:T(8,128)}, u32[]{:S(2)}) copy-start(s32[256,2048]{1,0:T(8,128)} %param.2) | copy-start | bytes 6291460
  26.6 1.2 %copy-start.1 = (f32[2048,1,104]{0,2,1:T(8,128)S(1)}, f32[2048,1,104]{0,2,1:T(8,128)}, u32[]{:S(2)}) copy-start(f32[2048,1,104]{0,2,1:T(8,128)} %get-tuple-element.37) | copy-start | bytes 2555908
  33.0 1.8 %collective-permute-start.2 = (f32[4,208,104]{1,2,0:T(8,128)S(1)}, f32[4,208,104]{1,2,0:T(8,128)S(1)}, u32[]{:S(2)}, u32[]{:S(2)}) collective-permute-start(f32[4,208,104]{1,2,0:T(8,128)S(1)} %fusion.40), channel_id=1, source_target_pairs={{0,1},{1,0},{2,3},{3,2},{4,5},{5,4},{6,7},{7,6},{8,9},{9,8},{10,11... | collective-permute-start | bytes 1038344 | tf_op jit(solution)/shard_map/ppermute | solution.py:161
  35.0 11.5 %collective-permute-start.3 = (f32[4,208,104]{1,2,0:T(8,128)S(1)}, f32[4,208,104]{1,2,0:T(8,128)S(1)}, u32[]{:S(2)}, u32[]{:S(2)}) collective-permute-start(f32[4,208,104]{1,2,0:T(8,128)S(1)} %bitcast_add_fusion), channel_id=1, source_target_pairs={{0,2},{1,3},{2,4},{3,5},{4,6},{5,7},{8,10},{9,11},{10,12},{11,13},... | collective-permute-start | bytes 1038344 | tf_op jit(solution)/shard_map/ppermute | solution.py:168
  37.1 13.5 %collective-permute-start.6 = (f32[4,208,104]{1,2,0:T(8,128)S(1)}, f32[4,208,104]{1,2,0:T(8,128)S(1)}, u32[]{:S(2)}, u32[]{:S(2)}) collective-permute-start(f32[4,208,104]{1,2,0:T(8,128)S(1)} %bitcast_add_fusion), channel_id=1, source_target_pairs={{2,0},{3,1},{4,2},{5,3},{6,4},{7,5},{10,8},{11,9},{12,10},{13,11},... | collective-permute-start | bytes 1038344 | tf_op jit(solution)/shard_map/ppermute | solution.py:169
  50.7 11.7 %collective-permute-start.4 = (f32[4,208,104]{1,2,0:T(8,128)S(1)}, f32[4,208,104]{1,2,0:T(8,128)S(1)}, u32[]{:S(2)}, u32[]{:S(2)}) collective-permute-start(f32[4,208,104]{1,2,0:T(8,128)S(1)} %get-tuple-element.32), channel_id=1, source_target_pairs={{0,2},{1,3},{2,4},{3,5},{4,6},{5,7},{8,10},{9,11},{10,12},{11,13},... | collective-permute-start | bytes 1038344 | tf_op jit(solution)/shard_map/ppermute | solution.py:168
  54.2 12.3 %collective-permute-start.7 = (f32[4,208,104]{1,2,0:T(8,128)S(1)}, f32[4,208,104]{1,2,0:T(8,128)S(1)}, u32[]{:S(2)}, u32[]{:S(2)}) collective-permute-start(f32[4,208,104]{1,2,0:T(8,128)S(1)} %get-tuple-element.33), channel_id=1, source_target_pairs={{2,0},{3,1},{4,2},{5,3},{6,4},{7,5},{10,8},{11,9},{12,10},{13,11},... | collective-permute-start | bytes 1038344 | tf_op jit(solution)/shard_map/ppermute | solution.py:169
  66.6 10.6 %collective-permute-start.5 = (f32[4,208,104]{1,2,0:T(8,128)S(1)}, f32[4,208,104]{1,2,0:T(8,128)S(1)}, u32[]{:S(2)}, u32[]{:S(2)}) collective-permute-start(f32[4,208,104]{1,2,0:T(8,128)S(1)} %get-tuple-element.30), channel_id=1, source_target_pairs={{0,2},{1,3},{2,4},{3,5},{4,6},{5,7},{8,10},{9,11},{10,12},{11,13},... | collective-permute-start | bytes 1038344 | tf_op jit(solution)/shard_map/ppermute | solution.py:168
  70.1 11.2 %collective-permute-start.8 = (f32[4,208,104]{1,2,0:T(8,128)S(1)}, f32[4,208,104]{1,2,0:T(8,128)S(1)}, u32[]{:S(2)}, u32[]{:S(2)}) collective-permute-start(f32[4,208,104]{1,2,0:T(8,128)S(1)} %get-tuple-element.31), channel_id=1, source_target_pairs={{2,0},{3,1},{4,2},{5,3},{6,4},{7,5},{10,8},{11,9},{12,10},{13,11},... | collective-permute-start | bytes 1038344 | tf_op jit(solution)/shard_map/ppermute | solution.py:169
  81.4 1.9 %collective-permute-start.9 = (f32[4,208,104]{1,2,0:T(8,128)S(1)}, f32[4,208,104]{1,2,0:T(8,128)S(1)}, u32[]{:S(2)}, u32[]{:S(2)}) collective-permute-start(f32[4,208,104]{1,2,0:T(8,128)S(1)} %add_add_fusion), channel_id=1, source_target_pairs={{0,1},{1,0},{2,3},{3,2},{4,5},{5,4},{6,7},{7,6},{8,9},{9,8},{10,11... | collective-permute-start | bytes 1038344 | tf_op jit(solution)/shard_map/ppermute | solution.py:172
  83.2 1.7 %copy-start.2 = (f32[2]{0:T(128)S(1)}, f32[2]{0:T(128)}, u32[]{:S(2)}) copy-start(f32[2]{0:T(128)} %constant.134.clone) | copy-start | bytes 28

commit v5 on v4

--- a/solution.py
+++ b/solution.py
@@ -118,13 +118,15 @@
             d = jnp.where(s == 0, dval_ref[h, row], jnp.float32(0.0))
             tile = z_ref[h, pl.ds(spot_tile, BLOCK_ROWS), :]
             z_ref[h, pl.ds(spot_tile, BLOCK_ROWS), :] = tile + jnp.where(spot, d, jnp.float32(0.0))
+    placed = {}
     for start, width, runs in chunk_segments(o_ref.shape[2], o_ref.shape[2] // 2):
         acc = None
         for h, u, l0, v0 in runs:
-            src = z_ref[h, pl.ds((u + BLOCK_ROWS) * BLOCK_ROWS, BLOCK_ROWS), :]
-            sh = (l0 - v0) % LANES
-            if sh:
-                src = pltpu.roll(src, sh, 1)
+            if (h, u) not in placed:
+                src = z_ref[h, pl.ds((u + BLOCK_ROWS) * BLOCK_ROWS, BLOCK_ROWS), :]
+                sh = (l0 - v0) % LANES
+                placed[(h, u)] = pltpu.roll(src, sh, 1) if sh else src
+            src = placed[(h, u)]
             acc = src if acc is None else jnp.where(lane >= l0, src, acc)
         if width < LANES:
             acc = acc[:, :width]

time: 108 us -> 105 us (0.972)
  Pallas kernels: 20.1 us -> 17.6 us
    pallas_call x1, Pallas kernels: 20.1 us -> 17.6 us  [assemble(): pl.pallas_call(assemble_kernel, grid_spec=grid_spec, out_shape=jax.ShapeD...]
where the time goes in v5:
time: 105 us
  waiting for transfers between devices  34.8 us (33%)
  other arithmetic  22.4 us (21%)
  starting transfers between devices  17.8 us (17%)
  Pallas kernels  17.6 us (17%)
  matrix products  7.54 us (7%)
  local copies, waits for them, and re-layouts  4.53 us (4%)
    ppermute x3, waiting for transfers between devices, line_sum(): lax.ppermute(mine + from_left, 'slab', right)  20.6 us
    pallas_call x1, Pallas kernels, assemble(): pl.pallas_call(assemble_kernel, grid_spec=grid_spec, out_shape=jax.ShapeD...  17.6 us
    ppermute x3, waiting for transfers between devices, line_sum(): lax.ppermute(mine + from_right, 'slab', left)  12.4 us
    ppermute x3, starting transfers between devices, line_sum(): lax.ppermute(mine + from_left, 'slab', right)  9.12 us
    another operation x3, other arithmetic, shards(): jnp.stack([permit, contrast * normal_x * normal_x, contrast * normal_x *...  6.55 us
    cos x1, other arithmetic, shards(): col_table = jnp.stack([jnp.cos(angles), -jnp.sin(angles)], axis=1)  4.3 us
    dot_general x1, matrix products, shards(): jnp.einsum('kxy,ycn->kxcn', fields, col_table, precision=lax.Precision.HIGH)  4.19 us
    ppermute x1, starting transfers between devices, extended_2(): lax.ppermute(lax.slice_in_dim(block, 0, width, axis=dim), axis, backward)  4.09 us
  transfers between devices with their start and end apart: 10, of which 7 were waited for; matrix products, arithmetic and copies ran while one was open for 7% of the time, Pallas kernels for 0%

profile of v5, /device:TPU:0, one launch (start us, length us, event | category | flops | bytes accessed | tf_op | source)
XLA Modules:
  0.0 105.0 jit_solution(16457434200901929529)
XLA Ops:
  0.0 2.3 %select_add_fusion = f32[256,2048]{1,0:T(8,128)S(1)} fusion(s32[256,2048]{1,0:T(8,128)} %param.2), kind=kLoop, calls=%fused_computation.45 | loop fusion | flops 5767168 | bytes 4194304 | tf_op jit(solution)/shard_map/add | solution.py:39
  2.4 0.5 collective-permute-start
  2.9 4.1 %collective-permute-start.1 = (f32[4,2048]{1,0:T(4,128)S(1)}, f32[4,2048]{1,0:T(4,128)S(1)}, u32[]{:S(2)}, u32[]{:S(2)}) collective-permute-start(f32[4,2048]{1,0:T(4,128)S(1)} %get-tuple-element.25), channel_id=1, source_target_pairs={{1,0},{2,1},{3,2},{4,3},{5,4},{6,5},{7,6},{0,7},{9,8},{10,9},{11,1... | collective-permute-start | bytes 98312 | tf_op jit(solution)/shard_map/ppermute | solution.py:31
  7.0 4.3 %fusion.43 = (f32[2048,1,104]{0,2,1:T(8,128)S(1)}, f32[2048,1,104]{0,2,1:T(8,128)}) fusion(s32[104]{0:T(128)S(1)} %iota_subtract_fusion.3), kind=kLoop, calls=%fused_computation.83 | loop fusion | flops 3194880 | bytes 1704352 | tf_op jit(solution)/shard_map/cos | solution.py:208
  11.3 0.9 fusion.53
  12.3 0.3 pad_maximum_fusion.4
  12.6 0.9 fusion.85
  13.4 2.3 %fusion.15 = f32[262,2048]{1,0:T(8,128)S(1)} fusion(f32[4,2048]{1,0:T(4,128)S(1)} %collective-permute-done.1, f32[256,2048]{1,0:T(8,128)S(1)} %select_add_fusion, f32[4,2048]{1,0:T(4,128)S(1)} %collective-permute-done, f32[264,2048]{1,0:T(8,128)S(1)} %pad_maximum_fusion.4, f32[262,2047]{1,0:T(8,128)S(1)} %get-tuple-element.22, ...), kind=kLoop, calls=%fused_computation.25 | loop fusion | flops 6438912 | bytes 15038416 | tf_op jit(solution)/shard_map/div | solution.py:47
  15.8 0.9 fusion.83
  16.7 0.1 fusion.84
  16.8 0.9 fusion.12
  17.6 0.9 fusion.81
  18.5 0.1 fusion.82
  18.6 0.9 fusion.9
  19.5 1.1 %fusion.79 = (f32[256,2047]{1,0:T(8,128)S(1)}, f32[256,2047]{1,0:T(8,128)S(1)}) fusion(f32[258,2048]{1,0:T(8,128)S(1)} %fusion.9), kind=kLoop, calls=%fused_computation.150 | loop fusion | bytes 8384512 | tf_op jit(solution)/shard_map/jit(_roll_static)/slice | solution.py:59
  20.6 0.1 fusion.80
  20.7 0.4 copy-done
  21.1 2.7 %multiply_bitcast_fusion.1 = (f32[1,256,2048]{2,1,0:T(8,128)S(1)}, f32[256,2048]{1,0:T(8,128)S(1)}, f32[1,256,2048]{2,1,0:T(8,128)S(1)}) fusion(s32[256,2048]{1,0:T(8,128)S(1)} %copy-done, f32[256,2047]{1,0:T(8,128)S(1)} %get-tuple-element.10, f32[256,1]{1,0:T(8,128)S(1)} %get-tuple-element.12, f32[256,1]{1,0:T(8,128)S(1)} %get-tuple-element.11, ...), kind=kLoop, calls=%fused_computation.41 | loop fusion | flops 13631488 | bytes 16777216 | tf_op jit(solution)/shard_map/stack | solution.py:193
  23.8 2.9 %multiply_bitcast_fusion = (f32[1,256,2048]{2,1,0:T(8,128)S(1)}, f32[256,2048]{1,0:T(8,128)S(1)}) fusion(f32[256,2048]{1,0:T(8,128)S(1)} %get-tuple-element.6, s32[256,2048]{1,0:T(8,128)S(1)} %copy-done, f32[258,2048]{1,0:T(8,128)S(1)} %fusion.9, f32[256,2047]{1,0:T(8,128)S(1)} %get-tuple-element.10, f32[256,1]{1,0:T(8,128)S(1)} %get-tuple-element.12, ...), kind=kLoop, calls=%fused_computation.40 | loop fusion | flops 13631488 | bytes 16777216 | tf_op jit(solution)/shard_map/stack | solution.py:193
  26.7 1.0 fusion.18
  27.7 0.1 copy-done.1
  27.8 4.2 %fusion.25 = f32[4,256,2,104,1]{1,3,4,2,0:T(8,128)S(1)} fusion(f32[2048,1,104]{0,2,1:T(8,128)S(1)} %copy-done.1, f32[2048,1,104]{0,2,1:T(8,128)S(1)} %get-tuple-element.36, f32[1,256,2048]{2,1,0:T(8,128)S(1)} %fusion.18, f32[1,256,2048]{2,1,0:T(8,128)S(1)} %get-tuple-element.7, f32[1,256,2048]{2,1,0:T(8,128)S(1)} %get-tuple-element.5, ...), kind=kOutput, calls=%fused_computation.52 | convolution fusion | flops 2623963136 | bytes 10944512 | tf_op jit(solution)/shard_map/kxy,ycn->kxcn/dot_general | solution.py:209
  32.0 0.9 convolution_bitcast_fusion
  32.9 0.1 fusion.40
  33.1 1.8 %collective-permute-done.2 = f32[4,208,104]{1,2,0:T(8,128)S(1)} collective-permute-done((f32[4,208,104]{1,2,0:T(8,128)S(1)}, f32[4,208,104]{1,2,0:T(8,128)S(1)}, u32[]{:S(2)}, u32[]{:S(2)}) %collective-permute-start.2) | collective-permute-done | bytes 346144 | tf_op jit(solution)/shard_map/ppermute | solution.py:163
  34.8 0.1 bitcast_add_fusion
  35.0 2.1 %collective-permute-start.3 = (f32[4,208,104]{1,2,0:T(8,128)S(1)}, f32[4,208,104]{1,2,0:T(8,128)S(1)}, u32[]{:S(2)}, u32[]{:S(2)}) collective-permute-start(f32[4,208,104]{1,2,0:T(8,128)S(1)} %bitcast_add_fusion), channel_id=1, source_target_pairs={{0,2},{1,3},{2,4},{3,5},{4,6},{5,7},{8,10},{9,11},{10,12},{11,13},... | collective-permute-start | bytes 1038344 | tf_op jit(solution)/shard_map/ppermute | solution.py:170
  37.1 1.3 %collective-permute-start.6 = (f32[4,208,104]{1,2,0:T(8,128)S(1)}, f32[4,208,104]{1,2,0:T(8,128)S(1)}, u32[]{:S(2)}, u32[]{:S(2)}) collective-permute-start(f32[4,208,104]{1,2,0:T(8,128)S(1)} %bitcast_add_fusion), channel_id=1, source_target_pairs={{2,0},{3,1},{4,2},{5,3},{6,4},{7,5},{10,8},{11,9},{12,10},{13,11},... | collective-permute-start | bytes 1038344 | tf_op jit(solution)/shard_map/ppermute | solution.py:171
  38.4 8.0 %collective-permute-done.3 = f32[4,208,104]{1,2,0:T(8,128)S(1)} collective-permute-done((f32[4,208,104]{1,2,0:T(8,128)S(1)}, f32[4,208,104]{1,2,0:T(8,128)S(1)}, u32[]{:S(2)}, u32[]{:S(2)}) %collective-permute-start.3) | collective-permute-done | bytes 346144 | tf_op jit(solution)/shard_map/ppermute | solution.py:170
  46.4 4.1 %collective-permute-done.6 = f32[4,208,104]{1,2,0:T(8,128)S(1)} collective-permute-done((f32[4,208,104]{1,2,0:T(8,128)S(1)}, f32[4,208,104]{1,2,0:T(8,128)S(1)}, u32[]{:S(2)}, u32[]{:S(2)}) %collective-permute-start.6) | collective-permute-done | bytes 346144 | tf_op jit(solution)/shard_map/ppermute | solution.py:171
  50.7 3.5 %collective-permute-start.4 = (f32[4,208,104]{1,2,0:T(8,128)S(1)}, f32[4,208,104]{1,2,0:T(8,128)S(1)}, u32[]{:S(2)}, u32[]{:S(2)}) collective-permute-start(f32[4,208,104]{1,2,0:T(8,128)S(1)} %get-tuple-element.32), channel_id=1, source_target_pairs={{0,2},{1,3},{2,4},{3,5},{4,6},{5,7},{8,10},{9,11},{10,12},{11,13},... | collective-permute-start | bytes 1038344 | tf_op jit(solution)/shard_map/ppermute | solution.py:170
  54.2 1.3 %collective-permute-start.7 = (f32[4,208,104]{1,2,0:T(8,128)S(1)}, f32[4,208,104]{1,2,0:T(8,128)S(1)}, u32[]{:S(2)}, u32[]{:S(2)}) collective-permute-start(f32[4,208,104]{1,2,0:T(8,128)S(1)} %get-tuple-element.33), channel_id=1, source_target_pairs={{2,0},{3,1},{4,2},{5,3},{6,4},{7,5},{10,8},{11,9},{12,10},{13,11},... | collective-permute-start | bytes 1038344 | tf_op jit(solution)/shard_map/ppermute | solution.py:171
  55.5 6.9 %collective-permute-done.4 = f32[4,208,104]{1,2,0:T(8,128)S(1)} collective-permute-done((f32[4,208,104]{1,2,0:T(8,128)S(1)}, f32[4,208,104]{1,2,0:T(8,128)S(1)}, u32[]{:S(2)}, u32[]{:S(2)}) %collective-permute-start.4) | collective-permute-done | bytes 346144 | tf_op jit(solution)/shard_map/ppermute | solution.py:170
  62.4 4.1 %collective-permute-done.7 = f32[4,208,104]{1,2,0:T(8,128)S(1)} collective-permute-done((f32[4,208,104]{1,2,0:T(8,128)S(1)}, f32[4,208,104]{1,2,0:T(8,128)S(1)}, u32[]{:S(2)}, u32[]{:S(2)}) %collective-permute-start.7) | collective-permute-done | bytes 346144 | tf_op jit(solution)/shard_map/ppermute | solution.py:171
  66.5 0.1 fusion.88
  66.6 3.5 %collective-permute-start.5 = (f32[4,208,104]{1,2,0:T(8,128)S(1)}, f32[4,208,104]{1,2,0:T(8,128)S(1)}, u32[]{:S(2)}, u32[]{:S(2)}) collective-permute-start(f32[4,208,104]{1,2,0:T(8,128)S(1)} %get-tuple-element.30), channel_id=1, source_target_pairs={{0,2},{1,3},{2,4},{3,5},{4,6},{5,7},{8,10},{9,11},{10,12},{11,13},... | collective-permute-start | bytes 1038344 | tf_op jit(solution)/shard_map/ppermute | solution.py:170
  70.1 1.3 %collective-permute-start.8 = (f32[4,208,104]{1,2,0:T(8,128)S(1)}, f32[4,208,104]{1,2,0:T(8,128)S(1)}, u32[]{:S(2)}, u32[]{:S(2)}) collective-permute-start(f32[4,208,104]{1,2,0:T(8,128)S(1)} %get-tuple-element.31), channel_id=1, source_target_pairs={{2,0},{3,1},{4,2},{5,3},{6,4},{7,5},{10,8},{11,9},{12,10},{13,11},... | collective-permute-start | bytes 1038344 | tf_op jit(solution)/shard_map/ppermute | solution.py:171
  71.4 5.7 %collective-permute-done.5 = f32[4,208,104]{1,2,0:T(8,128)S(1)} collective-permute-done((f32[4,208,104]{1,2,0:T(8,128)S(1)}, f32[4,208,104]{1,2,0:T(8,128)S(1)}, u32[]{:S(2)}, u32[]{:S(2)}) %collective-permute-start.5) | collective-permute-done | bytes 346144 | tf_op jit(solution)/shard_map/ppermute | solution.py:170
  77.1 4.1 %collective-permute-done.8 = f32[4,208,104]{1,2,0:T(8,128)S(1)} collective-permute-done((f32[4,208,104]{1,2,0:T(8,128)S(1)}, f32[4,208,104]{1,2,0:T(8,128)S(1)}, u32[]{:S(2)}, u32[]{:S(2)}) %collective-permute-start.8) | collective-permute-done | bytes 346144 | tf_op jit(solution)/shard_map/ppermute | solution.py:171
  81.4 0.6 and_select_fusion.4
  82.1 0.6 broadcast_subtract_fusion
  82.7 0.6 pad_maximum_fusion.6.dval_ref
  83.2 0.7 fusion.33
  84.0 0.9 fusion.35
  84.9 0.8 multiply_add_fusion
  85.8 0.2 fusion.87
  85.9 1.4 %pad_maximum_fusion.5.fl_ref = f32[2,4,208,256]{3,2,1,0:T(8,128)} fusion(f32[2,1,208,256]{3,2,1,0:T(8,128)S(1)} %get-tuple-element.27, f32[2,1,208,256]{3,2,1,0:T(8,128)S(1)} %get-tuple-element.29, f32[2,1,208,256]{3,2,1,0:T(8,128)S(1)} %get-tuple-element.28, f32[2,1,208,256]{3,2,1,0:T(8,128)S(1)} %get-tuple-element.26), kind=kLoop, calls=%fused_computation.49 | loop fusion | flops 1277952 | bytes 3407872 | tf_op jit(solution)/shard_map/stack | solution.py:228
  87.3 17.6 %shard_map.28 = f32[2,64,20402]{2,1,0:T(8,128)} custom-call(s32[64]{0:T(128)} %get-tuple-element.43.a0_ref, s32[64]{0:T(128)} %get-tuple-element.42.b0_ref, s32[64]{0:T(128)} %get-tuple-element.39.first_ref, s32[64]{0:T(128)} %get-tuple-element.38.second_ref, f32[2,64]{1,0:T(2,128)} %pad_maximum_fusion.6.dval_ref, f32[2,4,208,256]{3,2,1,0:T(8,128)} %pad_maximum_fusion.5.fl_ref), custom_call_target="tpu_custom_call" | custom-call | tf_op jit(solution)/shard_map/pallas_call | solution.py:150
  (20 shorter events, 0.4 us)
Async XLA Ops:
  2.4 9.9 %collective-permute-start = (f32[4,2048]{1,0:T(4,128)S(1)}, f32[4,2048]{1,0:T(4,128)S(1)}, u32[]{:S(2)}, u32[]{:S(2)}) collective-permute-start(f32[4,2048]{1,0:T(4,128)S(1)} %get-tuple-element.24), channel_id=1, source_target_pairs={{0,1},{1,2},{2,3},{3,4},{4,5},{5,6},{6,7},{7,0},{8,9},{9,10},{10,1... | collective-permute-start | bytes 98312 | tf_op jit(solution)/shard_map/ppermute | solution.py:28
  2.9 9.3 %collective-permute-start.1 = (f32[4,2048]{1,0:T(4,128)S(1)}, f32[4,2048]{1,0:T(4,128)S(1)}, u32[]{:S(2)}, u32[]{:S(2)}) collective-permute-start(f32[4,2048]{1,0:T(4,128)S(1)} %get-tuple-element.25), channel_id=1, source_target_pairs={{1,0},{2,1},{3,2},{4,3},{5,4},{6,5},{7,6},{0,7},{9,8},{10,9},{11,1... | collective-permute-start | bytes 98312 | tf_op jit(solution)/shard_map/ppermute | solution.py:31
  19.5 1.6 %copy-start = (s32[256,2048]{1,0:T(8,128)S(1)}, s32[256,2048]{1,0:T(8,128)}, u32[]{:S(2)}) copy-start(s32[256,2048]{1,0:T(8,128)} %param.2) | copy-start | bytes 6291460
  26.6 1.2 %copy-start.1 = (f32[2048,1,104]{0,2,1:T(8,128)S(1)}, f32[2048,1,104]{0,2,1:T(8,128)}, u32[]{:S(2)}) copy-start(f32[2048,1,104]{0,2,1:T(8,128)} %get-tuple-element.37) | copy-start | bytes 2555908
  33.0 1.8 %collective-permute-start.2 = (f32[4,208,104]{1,2,0:T(8,128)S(1)}, f32[4,208,104]{1,2,0:T(8,128)S(1)}, u32[]{:S(2)}, u32[]{:S(2)}) collective-permute-start(f32[4,208,104]{1,2,0:T(8,128)S(1)} %fusion.40), channel_id=1, source_target_pairs={{0,1},{1,0},{2,3},{3,2},{4,5},{5,4},{6,7},{7,6},{8,9},{9,8},{10,11... | collective-permute-start | bytes 1038344 | tf_op jit(solution)/shard_map/ppermute | solution.py:163
  35.0 11.5 %collective-permute-start.3 = (f32[4,208,104]{1,2,0:T(8,128)S(1)}, f32[4,208,104]{1,2,0:T(8,128)S(1)}, u32[]{:S(2)}, u32[]{:S(2)}) collective-permute-start(f32[4,208,104]{1,2,0:T(8,128)S(1)} %bitcast_add_fusion), channel_id=1, source_target_pairs={{0,2},{1,3},{2,4},{3,5},{4,6},{5,7},{8,10},{9,11},{10,12},{11,13},... | collective-permute-start | bytes 1038344 | tf_op jit(solution)/shard_map/ppermute | solution.py:170
  37.1 13.5 %collective-permute-start.6 = (f32[4,208,104]{1,2,0:T(8,128)S(1)}, f32[4,208,104]{1,2,0:T(8,128)S(1)}, u32[]{:S(2)}, u32[]{:S(2)}) collective-permute-start(f32[4,208,104]{1,2,0:T(8,128)S(1)} %bitcast_add_fusion), channel_id=1, source_target_pairs={{2,0},{3,1},{4,2},{5,3},{6,4},{7,5},{10,8},{11,9},{12,10},{13,11},... | collective-permute-start | bytes 1038344 | tf_op jit(solution)/shard_map/ppermute | solution.py:171
  50.7 11.7 %collective-permute-start.4 = (f32[4,208,104]{1,2,0:T(8,128)S(1)}, f32[4,208,104]{1,2,0:T(8,128)S(1)}, u32[]{:S(2)}, u32[]{:S(2)}) collective-permute-start(f32[4,208,104]{1,2,0:T(8,128)S(1)} %get-tuple-element.32), channel_id=1, source_target_pairs={{0,2},{1,3},{2,4},{3,5},{4,6},{5,7},{8,10},{9,11},{10,12},{11,13},... | collective-permute-start | bytes 1038344 | tf_op jit(solution)/shard_map/ppermute | solution.py:170
  54.2 12.3 %collective-permute-start.7 = (f32[4,208,104]{1,2,0:T(8,128)S(1)}, f32[4,208,104]{1,2,0:T(8,128)S(1)}, u32[]{:S(2)}, u32[]{:S(2)}) collective-permute-start(f32[4,208,104]{1,2,0:T(8,128)S(1)} %get-tuple-element.33), channel_id=1, source_target_pairs={{2,0},{3,1},{4,2},{5,3},{6,4},{7,5},{10,8},{11,9},{12,10},{13,11},... | collective-permute-start | bytes 1038344 | tf_op jit(solution)/shard_map/ppermute | solution.py:171
  66.6 10.6 %collective-permute-start.5 = (f32[4,208,104]{1,2,0:T(8,128)S(1)}, f32[4,208,104]{1,2,0:T(8,128)S(1)}, u32[]{:S(2)}, u32[]{:S(2)}) collective-permute-start(f32[4,208,104]{1,2,0:T(8,128)S(1)} %get-tuple-element.30), channel_id=1, source_target_pairs={{0,2},{1,3},{2,4},{3,5},{4,6},{5,7},{8,10},{9,11},{10,12},{11,13},... | collective-permute-start | bytes 1038344 | tf_op jit(solution)/shard_map/ppermute | solution.py:170
  70.1 11.2 %collective-permute-start.8 = (f32[4,208,104]{1,2,0:T(8,128)S(1)}, f32[4,208,104]{1,2,0:T(8,128)S(1)}, u32[]{:S(2)}, u32[]{:S(2)}) collective-permute-start(f32[4,208,104]{1,2,0:T(8,128)S(1)} %get-tuple-element.31), channel_id=1, source_target_pairs={{2,0},{3,1},{4,2},{5,3},{6,4},{7,5},{10,8},{11,9},{12,10},{13,11},... | collective-permute-start | bytes 1038344 | tf_op jit(solution)/shard_map/ppermute | solution.py:171
  81.4 1.9 %collective-permute-start.9 = (f32[4,208,104]{1,2,0:T(8,128)S(1)}, f32[4,208,104]{1,2,0:T(8,128)S(1)}, u32[]{:S(2)}, u32[]{:S(2)}) collective-permute-start(f32[4,208,104]{1,2,0:T(8,128)S(1)} %add_add_fusion), channel_id=1, source_target_pairs={{0,1},{1,0},{2,3},{3,2},{4,5},{5,4},{6,7},{7,6},{8,9},{9,8},{10,11... | collective-permute-start | bytes 1038344 | tf_op jit(solution)/shard_map/ppermute | solution.py:174
  83.2 1.7 %copy-start.2 = (f32[2]{0:T(128)S(1)}, f32[2]{0:T(128)}, u32[]{:S(2)}) copy-start(f32[2]{0:T(128)} %constant.134.clone) | copy-start | bytes 28

commit v6 on v5

--- a/solution.py
+++ b/solution.py
@@ -158,8 +158,10 @@
 def line_sum(partial_value, my_index, devices):
     core = my_index % 2
     pairs = [(i, i ^ 1) for i in range(devices)]
-    keep = jnp.where(core == 0, partial_value[0], partial_value[1])
-    give = jnp.where(core == 0, partial_value[1], partial_value[0])
+    half_shape = partial_value.shape[1:]
+    dense = (-1, LANES) if math.prod(half_shape) % LANES == 0 else half_shape
+    keep = jnp.where(core == 0, partial_value[0], partial_value[1]).reshape(dense)
+    give = jnp.where(core == 0, partial_value[1], partial_value[0]).reshape(dense)
     mine = keep + lax.ppermute(give, "slab", pairs)
     right = [(i, i + 2) for i in range(devices - 2)]
     left = [(i + 2, i) for i in range(devices - 2)]
@@ -171,7 +173,8 @@
             lax.ppermute(mine + from_right, "slab", left),
         )
     total = mine + from_left + from_right
-    other = lax.ppermute(total, "slab", pairs)
+    other = lax.ppermute(total, "slab", pairs).reshape(half_shape)
+    total = total.reshape(half_shape)
     return jnp.where(core == 0, jnp.stack([total, other]), jnp.stack([other, total]))
 
 

time: 105 us -> 102 us (0.971)
  waiting for transfers between devices: 34.8 us -> 29.1 us
  local copies, waits for them, and re-layouts: 4.53 us -> 6.82 us
    ppermute x3, waiting for transfers between devices: 20.6 us -> 15.6 us  [line_sum(): lax.ppermute(mine + from_left, 'slab', right)]
    another operation x0 -> x4, local copies, waits for them, and re-layouts: none -> 1.21 us  [line_sum(): jnp.stack([total, other])]
    select_n x0 -> x4, local copies, waits for them, and re-layouts: none -> 1.08 us  [the longest x2 0.54 us: line_sum(): jnp.where(core == 0, partial_value[1], partial_value[0]).reshape(dense)]
  transfers between devices with their start and end apart: 10 -> 10, of which waited for: 7 -> 7; matrix products, arithmetic and copies ran while one was open for 7% -> 8% of each run, Pallas kernels for 0% -> 0%
where the time goes in v6:
time: 102 us
  waiting for transfers between devices  29.1 us (29%)
  other arithmetic  22.3 us (22%)
  starting transfers between devices  17.8 us (17%)
  Pallas kernels  17.6 us (17%)
  matrix products  7.53 us (7%)
  local copies, waits for them, and re-layouts  6.82 us (7%)
    pallas_call x1, Pallas kernels, assemble(): pl.pallas_call(assemble_kernel, grid_spec=grid_spec, out_shape=jax.ShapeD...  17.6 us
    ppermute x3, waiting for transfers between devices, line_sum(): lax.ppermute(mine + from_left, 'slab', right)  15.6 us
    ppermute x3, waiting for transfers between devices, line_sum(): lax.ppermute(mine + from_right, 'slab', left)  12.4 us
    ppermute x3, starting transfers between devices, line_sum(): lax.ppermute(mine + from_left, 'slab', right)  9.11 us
    another operation x3, other arithmetic, shards(): jnp.stack([permit, contrast * normal_x * normal_x, contrast * normal_x *...  6.55 us
    cos x1, other arithmetic, shards(): col_table = jnp.stack([jnp.cos(angles), -jnp.sin(angles)], axis=1)  4.3 us
    dot_general x1, matrix products, shards(): jnp.einsum('kxy,ycn->kxcn', fields, col_table, precision=lax.Precision.HIGH)  4.19 us
    ppermute x1, starting transfers between devices, extended_2(): lax.ppermute(lax.slice_in_dim(block, 0, width, axis=dim), axis, backward)  4.09 us
  transfers between devices with their start and end apart: 10, of which 7 were waited for; matrix products, arithmetic and copies ran while one was open for 8% of the time, Pallas kernels for 0%

profile of v6, /device:TPU:0, one launch (start us, length us, event | category | flops | bytes accessed | tf_op | source)
XLA Modules:
  0.0 101.5 jit_solution(3304697481252159983)
XLA Ops:
  0.0 2.3 %select_add_fusion = f32[256,2048]{1,0:T(8,128)S(1)} fusion(s32[256,2048]{1,0:T(8,128)} %param.2), kind=kLoop, calls=%fused_computation.45 | loop fusion | flops 5767168 | bytes 4194304 | tf_op jit(solution)/shard_map/add | solution.py:39
  2.4 0.5 collective-permute-start
  2.9 4.1 %collective-permute-start.1 = (f32[4,2048]{1,0:T(4,128)S(1)}, f32[4,2048]{1,0:T(4,128)S(1)}, u32[]{:S(2)}, u32[]{:S(2)}) collective-permute-start(f32[4,2048]{1,0:T(4,128)S(1)} %get-tuple-element.25), channel_id=1, source_target_pairs={{1,0},{2,1},{3,2},{4,3},{5,4},{6,5},{7,6},{0,7},{9,8},{10,9},{11,1... | collective-permute-start | bytes 98312 | tf_op jit(solution)/shard_map/ppermute | solution.py:31
  7.0 4.3 %fusion.41 = (f32[2048,1,104]{0,2,1:T(8,128)S(1)}, f32[2048,1,104]{0,2,1:T(8,128)}) fusion(s32[104]{0:T(128)S(1)} %iota_subtract_fusion.3), kind=kLoop, calls=%fused_computation.76 | loop fusion | flops 3194880 | bytes 1704352 | tf_op jit(solution)/shard_map/cos | solution.py:211
  11.3 0.9 fusion.51
  12.3 0.3 pad_maximum_fusion.4
  12.6 0.9 fusion.83
  13.4 2.3 %fusion.15 = f32[262,2048]{1,0:T(8,128)S(1)} fusion(f32[4,2048]{1,0:T(4,128)S(1)} %collective-permute-done.1, f32[256,2048]{1,0:T(8,128)S(1)} %select_add_fusion, f32[4,2048]{1,0:T(4,128)S(1)} %collective-permute-done, f32[264,2048]{1,0:T(8,128)S(1)} %pad_maximum_fusion.4, f32[262,2047]{1,0:T(8,128)S(1)} %get-tuple-element.22, ...), kind=kLoop, calls=%fused_computation.25 | loop fusion | flops 6438912 | bytes 15038416 | tf_op jit(solution)/shard_map/div | solution.py:47
  15.8 0.9 fusion.81
  16.8 0.9 fusion.12
  17.6 0.9 fusion.79
  18.6 0.9 fusion.9
  19.5 1.1 %fusion.77 = (f32[256,2047]{1,0:T(8,128)S(1)}, f32[256,2047]{1,0:T(8,128)S(1)}) fusion(f32[258,2048]{1,0:T(8,128)S(1)} %fusion.9), kind=kLoop, calls=%fused_computation.146 | loop fusion | bytes 8384512 | tf_op jit(solution)/shard_map/jit(_roll_static)/slice | solution.py:59
  20.7 0.4 copy-done
  21.1 2.7 %multiply_bitcast_fusion.1 = (f32[1,256,2048]{2,1,0:T(8,128)S(1)}, f32[256,2048]{1,0:T(8,128)S(1)}, f32[1,256,2048]{2,1,0:T(8,128)S(1)}) fusion(s32[256,2048]{1,0:T(8,128)S(1)} %copy-done, f32[256,2047]{1,0:T(8,128)S(1)} %get-tuple-element.10, f32[256,1]{1,0:T(8,128)S(1)} %get-tuple-element.12, f32[256,1]{1,0:T(8,128)S(1)} %get-tuple-element.11, ...), kind=kLoop, calls=%fused_computation.41 | loop fusion | flops 13631488 | bytes 16777216 | tf_op jit(solution)/shard_map/stack | solution.py:196
  23.8 2.9 %multiply_bitcast_fusion = (f32[1,256,2048]{2,1,0:T(8,128)S(1)}, f32[256,2048]{1,0:T(8,128)S(1)}) fusion(f32[256,2048]{1,0:T(8,128)S(1)} %get-tuple-element.6, s32[256,2048]{1,0:T(8,128)S(1)} %copy-done, f32[258,2048]{1,0:T(8,128)S(1)} %fusion.9, f32[256,2047]{1,0:T(8,128)S(1)} %get-tuple-element.10, f32[256,1]{1,0:T(8,128)S(1)} %get-tuple-element.12, ...), kind=kLoop, calls=%fused_computation.40 | loop fusion | flops 13631488 | bytes 16777216 | tf_op jit(solution)/shard_map/stack | solution.py:196
  26.7 1.0 %fusion.18 = f32[1,256,2048]{2,1,0:T(8,128)S(1)} fusion(f32[256,2048]{1,0:T(8,128)S(1)} %get-tuple-element.8, s32[256,2048]{1,0:T(8,128)S(1)} %copy-done), kind=kLoop, calls=%fused_computation.35 | loop fusion | flops 7864320 | bytes 6291456 | tf_op jit(solution)/shard_map/stack | solution.py:196
  27.8 4.2 %fusion.25 = f32[4,256,2,104,1]{1,3,4,2,0:T(8,128)S(1)} fusion(f32[2048,1,104]{0,2,1:T(8,128)S(1)} %copy-done.1, f32[2048,1,104]{0,2,1:T(8,128)S(1)} %get-tuple-element.38, f32[1,256,2048]{2,1,0:T(8,128)S(1)} %fusion.18, f32[1,256,2048]{2,1,0:T(8,128)S(1)} %get-tuple-element.7, f32[1,256,2048]{2,1,0:T(8,128)S(1)} %get-tuple-element.5, ...), kind=kOutput, calls=%fused_computation.52 | convolution fusion | flops 2623963136 | bytes 10944512 | tf_op jit(solution)/shard_map/kxy,ycn->kxcn/dot_general | solution.py:212
  32.0 0.9 convolution_bitcast_fusion
  33.0 0.2 copy.6
  33.2 0.4 select_n.172
  33.6 0.2 copy.5
  33.8 0.4 select_n.170
  34.2 1.1 %collective-permute-done.2 = f32[676,128]{1,0:T(8,128)S(1)} collective-permute-done((f32[676,128]{1,0:T(8,128)S(1)}, f32[676,128]{1,0:T(8,128)S(1)}, u32[]{:S(2)}, u32[]{:S(2)}) %collective-permute-start.2) | collective-permute-done | bytes 346144 | tf_op jit(solution)/shard_map/ppermute | solution.py:165
  35.3 2.1 %collective-permute-start.3 = (f32[676,128]{1,0:T(8,128)S(1)}, f32[676,128]{1,0:T(8,128)S(1)}, u32[]{:S(2)}, u32[]{:S(2)}) collective-permute-start(f32[676,128]{1,0:T(8,128)S(1)} %add.302), channel_id=1, source_target_pairs={{0,2},{1,3},{2,4},{3,5},{4,6},{5,7},{8,10},{9,11},{10,12},{11,13},... | collective-permute-start | bytes 1038344 | tf_op jit(solution)/shard_map/ppermute | solution.py:172
  37.5 1.3 %collective-permute-start.6 = (f32[676,128]{1,0:T(8,128)S(1)}, f32[676,128]{1,0:T(8,128)S(1)}, u32[]{:S(2)}, u32[]{:S(2)}) collective-permute-start(f32[676,128]{1,0:T(8,128)S(1)} %add.302), channel_id=1, source_target_pairs={{2,0},{3,1},{4,2},{5,3},{6,4},{7,5},{10,8},{11,9},{12,10},{13,11},... | collective-permute-start | bytes 1038344 | tf_op jit(solution)/shard_map/ppermute | solution.py:173
  38.8 6.4 %collective-permute-done.3 = f32[676,128]{1,0:T(8,128)S(1)} collective-permute-done((f32[676,128]{1,0:T(8,128)S(1)}, f32[676,128]{1,0:T(8,128)S(1)}, u32[]{:S(2)}, u32[]{:S(2)}) %collective-permute-start.3) | collective-permute-done | bytes 346144 | tf_op jit(solution)/shard_map/ppermute | solution.py:172
  45.1 4.1 %collective-permute-done.6 = f32[676,128]{1,0:T(8,128)S(1)} collective-permute-done((f32[676,128]{1,0:T(8,128)S(1)}, f32[676,128]{1,0:T(8,128)S(1)}, u32[]{:S(2)}, u32[]{:S(2)}) %collective-permute-start.6) | collective-permute-done | bytes 346144 | tf_op jit(solution)/shard_map/ppermute | solution.py:173
  49.3 3.5 %collective-permute-start.4 = (f32[676,128]{1,0:T(8,128)S(1)}, f32[676,128]{1,0:T(8,128)S(1)}, u32[]{:S(2)}, u32[]{:S(2)}) collective-permute-start(f32[676,128]{1,0:T(8,128)S(1)} %get-tuple-element.34), channel_id=1, source_target_pairs={{0,2},{1,3},{2,4},{3,5},{4,6},{5,7},{8,10},{9,11},{10,12},{11,13},... | collective-permute-start | bytes 1038344 | tf_op jit(solution)/shard_map/ppermute | solution.py:172
  52.8 1.3 %collective-permute-start.7 = (f32[676,128]{1,0:T(8,128)S(1)}, f32[676,128]{1,0:T(8,128)S(1)}, u32[]{:S(2)}, u32[]{:S(2)}) collective-permute-start(f32[676,128]{1,0:T(8,128)S(1)} %get-tuple-element.35), channel_id=1, source_target_pairs={{2,0},{3,1},{4,2},{5,3},{6,4},{7,5},{10,8},{11,9},{12,10},{13,11},... | collective-permute-start | bytes 1038344 | tf_op jit(solution)/shard_map/ppermute | solution.py:173
  54.1 5.2 %collective-permute-done.4 = f32[676,128]{1,0:T(8,128)S(1)} collective-permute-done((f32[676,128]{1,0:T(8,128)S(1)}, f32[676,128]{1,0:T(8,128)S(1)}, u32[]{:S(2)}, u32[]{:S(2)}) %collective-permute-start.4) | collective-permute-done | bytes 346144 | tf_op jit(solution)/shard_map/ppermute | solution.py:172
  59.4 4.1 %collective-permute-done.7 = f32[676,128]{1,0:T(8,128)S(1)} collective-permute-done((f32[676,128]{1,0:T(8,128)S(1)}, f32[676,128]{1,0:T(8,128)S(1)}, u32[]{:S(2)}, u32[]{:S(2)}) %collective-permute-start.7) | collective-permute-done | bytes 346144 | tf_op jit(solution)/shard_map/ppermute | solution.py:173
  63.5 3.5 %collective-permute-start.5 = (f32[676,128]{1,0:T(8,128)S(1)}, f32[676,128]{1,0:T(8,128)S(1)}, u32[]{:S(2)}, u32[]{:S(2)}) collective-permute-start(f32[676,128]{1,0:T(8,128)S(1)} %get-tuple-element.32), channel_id=1, source_target_pairs={{0,2},{1,3},{2,4},{3,5},{4,6},{5,7},{8,10},{9,11},{10,12},{11,13},... | collective-permute-start | bytes 1038344 | tf_op jit(solution)/shard_map/ppermute | solution.py:172
  67.0 1.3 %collective-permute-start.8 = (f32[676,128]{1,0:T(8,128)S(1)}, f32[676,128]{1,0:T(8,128)S(1)}, u32[]{:S(2)}, u32[]{:S(2)}) collective-permute-start(f32[676,128]{1,0:T(8,128)S(1)} %get-tuple-element.33), channel_id=1, source_target_pairs={{2,0},{3,1},{4,2},{5,3},{6,4},{7,5},{10,8},{11,9},{12,10},{13,11},... | collective-permute-start | bytes 1038344 | tf_op jit(solution)/shard_map/ppermute | solution.py:173
  68.4 4.0 %collective-permute-done.5 = f32[676,128]{1,0:T(8,128)S(1)} collective-permute-done((f32[676,128]{1,0:T(8,128)S(1)}, f32[676,128]{1,0:T(8,128)S(1)}, u32[]{:S(2)}, u32[]{:S(2)}) %collective-permute-start.5) | collective-permute-done | bytes 346144 | tf_op jit(solution)/shard_map/ppermute | solution.py:172
  72.4 4.1 %collective-permute-done.8 = f32[676,128]{1,0:T(8,128)S(1)} collective-permute-done((f32[676,128]{1,0:T(8,128)S(1)}, f32[676,128]{1,0:T(8,128)S(1)}, u32[]{:S(2)}, u32[]{:S(2)}) %collective-permute-start.8) | collective-permute-done | bytes 346144 | tf_op jit(solution)/shard_map/ppermute | solution.py:173
  76.7 0.6 and_select_fusion.4
  77.3 0.6 broadcast_subtract_fusion
  77.9 0.6 pad_maximum_fusion.6.dval_ref
  78.5 0.4 stack_reshape.8
  79.0 0.2 copy.7
  79.2 0.4 stack_reshape.9
  79.6 0.2 copy.8
  79.8 0.7 fusion.33
  80.6 0.9 fusion.35
  81.5 0.8 multiply_add_fusion
  82.5 1.4 %pad_maximum_fusion.5.fl_ref = f32[2,4,208,256]{3,2,1,0:T(8,128)} fusion(f32[2,1,208,256]{3,2,1,0:T(8,128)S(1)} %get-tuple-element.27, f32[2,1,208,256]{3,2,1,0:T(8,128)S(1)} %get-tuple-element.29, f32[2,1,208,256]{3,2,1,0:T(8,128)S(1)} %get-tuple-element.28, f32[2,1,208,256]{3,2,1,0:T(8,128)S(1)} %get-tuple-element.26), kind=kLoop, calls=%fused_computation.49 | loop fusion | flops 1277952 | bytes 3407872 | tf_op jit(solution)/shard_map/stack | solution.py:231
  83.9 17.6 %shard_map.28 = f32[2,64,20402]{2,1,0:T(8,128)} custom-call(s32[64]{0:T(128)} %get-tuple-element.45.a0_ref, s32[64]{0:T(128)} %get-tuple-element.44.b0_ref, s32[64]{0:T(128)} %get-tuple-element.41.first_ref, s32[64]{0:T(128)} %get-tuple-element.40.second_ref, f32[2,64]{1,0:T(2,128)} %pad_maximum_fusion.6.dval_ref, f32[2,4,208,256]{3,2,1,0:T(8,128)} %pad_maximum_fusion.5.fl_ref), custom_call_target="tpu_custom_call" | custom-call | tf_op jit(solution)/shard_map/pallas_call | solution.py:150
  (28 shorter events, 1.2 us)
Async XLA Ops:
  2.4 9.9 %collective-permute-start = (f32[4,2048]{1,0:T(4,128)S(1)}, f32[4,2048]{1,0:T(4,128)S(1)}, u32[]{:S(2)}, u32[]{:S(2)}) collective-permute-start(f32[4,2048]{1,0:T(4,128)S(1)} %get-tuple-element.24), channel_id=1, source_target_pairs={{0,1},{1,2},{2,3},{3,4},{4,5},{5,6},{6,7},{7,0},{8,9},{9,10},{10,1... | collective-permute-start | bytes 98312 | tf_op jit(solution)/shard_map/ppermute | solution.py:28
  2.9 9.3 %collective-permute-start.1 = (f32[4,2048]{1,0:T(4,128)S(1)}, f32[4,2048]{1,0:T(4,128)S(1)}, u32[]{:S(2)}, u32[]{:S(2)}) collective-permute-start(f32[4,2048]{1,0:T(4,128)S(1)} %get-tuple-element.25), channel_id=1, source_target_pairs={{1,0},{2,1},{3,2},{4,3},{5,4},{6,5},{7,6},{0,7},{9,8},{10,9},{11,1... | collective-permute-start | bytes 98312 | tf_op jit(solution)/shard_map/ppermute | solution.py:31
  19.5 1.6 %copy-start = (s32[256,2048]{1,0:T(8,128)S(1)}, s32[256,2048]{1,0:T(8,128)}, u32[]{:S(2)}) copy-start(s32[256,2048]{1,0:T(8,128)} %param.2) | copy-start | bytes 6291460
  26.6 1.2 %copy-start.1 = (f32[2048,1,104]{0,2,1:T(8,128)S(1)}, f32[2048,1,104]{0,2,1:T(8,128)}, u32[]{:S(2)}) copy-start(f32[2048,1,104]{0,2,1:T(8,128)} %get-tuple-element.39) | copy-start | bytes 2555908
  33.5 1.7 %collective-permute-start.2 = (f32[676,128]{1,0:T(8,128)S(1)}, f32[676,128]{1,0:T(8,128)S(1)}, u32[]{:S(2)}, u32[]{:S(2)}) collective-permute-start(f32[676,128]{1,0:T(8,128)S(1)} %select_n.172), channel_id=1, source_target_pairs={{0,1},{1,0},{2,3},{3,2},{4,5},{5,4},{6,7},{7,6},{8,9},{9,8},{10,11... | collective-permute-start | bytes 1038344 | tf_op jit(solution)/shard_map/ppermute | solution.py:165
  35.3 9.8 %collective-permute-start.3 = (f32[676,128]{1,0:T(8,128)S(1)}, f32[676,128]{1,0:T(8,128)S(1)}, u32[]{:S(2)}, u32[]{:S(2)}) collective-permute-start(f32[676,128]{1,0:T(8,128)S(1)} %add.302), channel_id=1, source_target_pairs={{0,2},{1,3},{2,4},{3,5},{4,6},{5,7},{8,10},{9,11},{10,12},{11,13},... | collective-permute-start | bytes 1038344 | tf_op jit(solution)/shard_map/ppermute | solution.py:172
  37.5 11.8 %collective-permute-start.6 = (f32[676,128]{1,0:T(8,128)S(1)}, f32[676,128]{1,0:T(8,128)S(1)}, u32[]{:S(2)}, u32[]{:S(2)}) collective-permute-start(f32[676,128]{1,0:T(8,128)S(1)} %add.302), channel_id=1, source_target_pairs={{2,0},{3,1},{4,2},{5,3},{6,4},{7,5},{10,8},{11,9},{12,10},{13,11},... | collective-permute-start | bytes 1038344 | tf_op jit(solution)/shard_map/ppermute | solution.py:173
  49.3 10.0 %collective-permute-start.4 = (f32[676,128]{1,0:T(8,128)S(1)}, f32[676,128]{1,0:T(8,128)S(1)}, u32[]{:S(2)}, u32[]{:S(2)}) collective-permute-start(f32[676,128]{1,0:T(8,128)S(1)} %get-tuple-element.34), channel_id=1, source_target_pairs={{0,2},{1,3},{2,4},{3,5},{4,6},{5,7},{8,10},{9,11},{10,12},{11,13},... | collective-permute-start | bytes 1038344 | tf_op jit(solution)/shard_map/ppermute | solution.py:172
  52.8 10.7 %collective-permute-start.7 = (f32[676,128]{1,0:T(8,128)S(1)}, f32[676,128]{1,0:T(8,128)S(1)}, u32[]{:S(2)}, u32[]{:S(2)}) collective-permute-start(f32[676,128]{1,0:T(8,128)S(1)} %get-tuple-element.35), channel_id=1, source_target_pairs={{2,0},{3,1},{4,2},{5,3},{6,4},{7,5},{10,8},{11,9},{12,10},{13,11},... | collective-permute-start | bytes 1038344 | tf_op jit(solution)/shard_map/ppermute | solution.py:173
  63.5 8.9 %collective-permute-start.5 = (f32[676,128]{1,0:T(8,128)S(1)}, f32[676,128]{1,0:T(8,128)S(1)}, u32[]{:S(2)}, u32[]{:S(2)}) collective-permute-start(f32[676,128]{1,0:T(8,128)S(1)} %get-tuple-element.32), channel_id=1, source_target_pairs={{0,2},{1,3},{2,4},{3,5},{4,6},{5,7},{8,10},{9,11},{10,12},{11,13},... | collective-permute-start | bytes 1038344 | tf_op jit(solution)/shard_map/ppermute | solution.py:172
  67.0 9.5 %collective-permute-start.8 = (f32[676,128]{1,0:T(8,128)S(1)}, f32[676,128]{1,0:T(8,128)S(1)}, u32[]{:S(2)}, u32[]{:S(2)}) collective-permute-start(f32[676,128]{1,0:T(8,128)S(1)} %get-tuple-element.33), channel_id=1, source_target_pairs={{2,0},{3,1},{4,2},{5,3},{6,4},{7,5},{10,8},{11,9},{12,10},{13,11},... | collective-permute-start | bytes 1038344 | tf_op jit(solution)/shard_map/ppermute | solution.py:173
  76.6 2.5 %collective-permute-start.9 = (f32[676,128]{1,0:T(8,128)S(1)}, f32[676,128]{1,0:T(8,128)S(1)}, u32[]{:S(2)}, u32[]{:S(2)}) collective-permute-start(f32[676,128]{1,0:T(8,128)S(1)} %add_add_fusion), channel_id=1, source_target_pairs={{0,1},{1,0},{2,3},{3,2},{4,5},{5,4},{6,7},{7,6},{8,9},{9,8},{10,11... | collective-permute-start | bytes 1038344 | tf_op jit(solution)/shard_map/ppermute | solution.py:176
  79.8 1.7 %copy-start.2 = (f32[2]{0:T(128)S(1)}, f32[2]{0:T(128)}, u32[]{:S(2)}) copy-start(f32[2]{0:T(128)} %constant.134.clone) | copy-start | bytes 28

commit v7 on v6

--- a/solution.py
+++ b/solution.py
@@ -163,16 +163,24 @@
     keep = jnp.where(core == 0, partial_value[0], partial_value[1]).reshape(dense)
     give = jnp.where(core == 0, partial_value[1], partial_value[0]).reshape(dense)
     mine = keep + lax.ppermute(give, "slab", pairs)
-    right = [(i, i + 2) for i in range(devices - 2)]
-    left = [(i + 2, i) for i in range(devices - 2)]
-    from_left = jnp.zeros_like(mine)
-    from_right = jnp.zeros_like(mine)
-    for step in range(devices // 2 - 1):
-        from_left, from_right = (
-            lax.ppermute(mine + from_left, "slab", right),
-            lax.ppermute(mine + from_right, "slab", left),
-        )
-    total = mine + from_left + from_right
+    chips = devices // 2
+    if chips & (chips - 1) == 0:
+        total = mine
+        bit = 2
+        while bit < devices:
+            total = total + lax.ppermute(total, "slab", [(i, i ^ bit) for i in range(devices)])
+            bit *= 2
+    else:
+        right = [(i, i + 2) for i in range(devices - 2)]
+        left = [(i + 2, i) for i in range(devices - 2)]
+        from_left = jnp.zeros_like(mine)
+        from_right = jnp.zeros_like(mine)
+        for step in range(chips - 1):
+            from_left, from_right = (
+                lax.ppermute(mine + from_left, "slab", right),
+                lax.ppermute(mine + from_right, "slab", left),
+            )
+        total = mine + from_left + from_right
     other = lax.ppermute(total, "slab", pairs).reshape(half_shape)
     total = total.reshape(half_shape)
     return jnp.where(core == 0, jnp.stack([total, other]), jnp.stack([other, total]))

time: 102 us -> 88.3 us (0.87)
  starting transfers between devices: 17.8 us -> 6.36 us
  waiting for transfers between devices: 29.1 us -> 27.3 us
    ppermute x6 -> x2, starting transfers between devices: 13 us -> 1.57 us  [line_sum(): lax.ppermute(total, 'slab', [(i, i ^ bit) for i in range(devices)])]
    ppermute x6 -> x2, waiting for transfers between devices: 28 us -> 26.2 us  [line_sum(): lax.ppermute(total, 'slab', [(i, i ^ bit) for i in range(devices)])]
  transfers between devices with their start and end apart: 10 -> 6, of which waited for: 7 -> 3; matrix products, arithmetic and copies ran while one was open for 8% -> 9% of each run, Pallas kernels for 0% -> 0%
where the time goes in v7:
time: 88.3 us; the launch traced here: 88 us
  waiting for transfers between devices  27.3 us (31%)
  other arithmetic  22.1 us (25%)
  Pallas kernels  17.6 us (20%)
  matrix products  7.54 us (9%)
  local copies, waits for them, and re-layouts  6.82 us (8%)
  starting transfers between devices  6.36 us (7%)
    ppermute x2, waiting for transfers between devices, line_sum(): lax.ppermute(total, 'slab', [(i, i ^ bit) for i in range(devices)])  26.2 us
    pallas_call x1, Pallas kernels, assemble(): pl.pallas_call(assemble_kernel, grid_spec=grid_spec, out_shape=jax.ShapeD...  17.6 us
    another operation x3, other arithmetic, shards(): jnp.stack([permit, contrast * normal_x * normal_x, contrast * normal_x *...  6.55 us
    cos x1, other arithmetic, shards(): col_table = jnp.stack([jnp.cos(angles), -jnp.sin(angles)], axis=1)  4.3 us
    dot_general x1, matrix products, shards(): jnp.einsum('kxy,ycn->kxcn', fields, col_table, precision=lax.Precision.HIGH)  4.19 us
    ppermute x1, starting transfers between devices, extended_2(): lax.ppermute(lax.slice_in_dim(block, 0, width, axis=dim), axis, backward)  4.09 us
    div x3, other arithmetic, smooth_once(): (4.0 * middle + extended[:-2] + extended[2:] + jnp.roll(middle, 1, 1) + j...  4.07 us
    slice x5, local copies, waits for them, and re-layouts, smooth_once(): jnp.roll(middle, -1, 1)  2.81 us
  transfers between devices with their start and end apart: 6, of which 3 were waited for; matrix products, arithmetic and copies ran while one was open for 9% of the time, Pallas kernels for 0%

profile of v7, /device:TPU:0, one launch (start us, length us, event | category | flops | bytes accessed | tf_op | source)
XLA Modules:
  0.0 88.0 jit_solution(15105918701081118700)
XLA Ops:
  0.0 2.3 %select_add_fusion = f32[256,2048]{1,0:T(8,128)S(1)} fusion(s32[256,2048]{1,0:T(8,128)} %param.2), kind=kLoop, calls=%fused_computation.45 | loop fusion | flops 5767168 | bytes 4194304 | tf_op jit(solution)/shard_map/add | solution.py:39
  2.4 0.5 collective-permute-start
  2.9 4.1 %collective-permute-start.1 = (f32[4,2048]{1,0:T(4,128)S(1)}, f32[4,2048]{1,0:T(4,128)S(1)}, u32[]{:S(2)}, u32[]{:S(2)}) collective-permute-start(f32[4,2048]{1,0:T(4,128)S(1)} %get-tuple-element.25), channel_id=1, source_target_pairs={{1,0},{2,1},{3,2},{4,3},{5,4},{6,5},{7,6},{0,7},{9,8},{10,9},{11,1... | collective-permute-start | bytes 98312 | tf_op jit(solution)/shard_map/ppermute | solution.py:31
  7.0 4.3 %fusion.41 = (f32[2048,1,104]{0,2,1:T(8,128)S(1)}, f32[2048,1,104]{0,2,1:T(8,128)}) fusion(s32[104]{0:T(128)S(1)} %iota_subtract_fusion.3), kind=kLoop, calls=%fused_computation.76 | loop fusion | flops 3194880 | bytes 1704352 | tf_op jit(solution)/shard_map/cos | solution.py:219
  11.3 0.9 %fusion.51 = (f32[1,208,256]{2,1,0:T(8,128)S(1)}, f32[1,208,256]{2,1,0:T(8,128)S(1)}) fusion(s32[256]{0:T(256)S(1)} %iota_add_fusion, s32[208]{0:T(256)S(1)} %iota_subtract_fusion.2), kind=kLoop, calls=%fused_computation.95 | loop fusion | flops 745472 | bytes 427840 | tf_op jit(solution)/shard_map/cos | solution.py:70
  12.3 0.3 pad_maximum_fusion.4
  12.6 0.9 fusion.83
  13.4 2.3 %fusion.15 = f32[262,2048]{1,0:T(8,128)S(1)} fusion(f32[4,2048]{1,0:T(4,128)S(1)} %collective-permute-done.1, f32[256,2048]{1,0:T(8,128)S(1)} %select_add_fusion, f32[4,2048]{1,0:T(4,128)S(1)} %collective-permute-done, f32[264,2048]{1,0:T(8,128)S(1)} %pad_maximum_fusion.4, f32[262,2047]{1,0:T(8,128)S(1)} %get-tuple-element.22, ...), kind=kLoop, calls=%fused_computation.25 | loop fusion | flops 6438912 | bytes 15038416 | tf_op jit(solution)/shard_map/div | solution.py:47
  15.8 0.9 fusion.81
  16.7 0.1 fusion.82
  16.8 0.9 fusion.12
  17.6 0.9 fusion.79
  18.5 0.1 fusion.80
  18.6 0.9 fusion.9
  19.5 1.1 %fusion.77 = (f32[256,2047]{1,0:T(8,128)S(1)}, f32[256,2047]{1,0:T(8,128)S(1)}) fusion(f32[258,2048]{1,0:T(8,128)S(1)} %fusion.9), kind=kLoop, calls=%fused_computation.145 | loop fusion | bytes 8384512 | tf_op jit(solution)/shard_map/jit(_roll_static)/slice | solution.py:59
  20.6 0.1 fusion.78
  20.7 0.4 copy-done
  21.1 2.7 %multiply_bitcast_fusion.1 = (f32[1,256,2048]{2,1,0:T(8,128)S(1)}, f32[256,2048]{1,0:T(8,128)S(1)}, f32[1,256,2048]{2,1,0:T(8,128)S(1)}) fusion(s32[256,2048]{1,0:T(8,128)S(1)} %copy-done, f32[256,2047]{1,0:T(8,128)S(1)} %get-tuple-element.10, f32[256,1]{1,0:T(8,128)S(1)} %get-tuple-element.12, f32[256,1]{1,0:T(8,128)S(1)} %get-tuple-element.11, ...), kind=kLoop, calls=%fused_computation.41 | loop fusion | flops 13631488 | bytes 16777216 | tf_op jit(solution)/shard_map/stack | solution.py:204
  23.8 2.9 %multiply_bitcast_fusion = (f32[1,256,2048]{2,1,0:T(8,128)S(1)}, f32[256,2048]{1,0:T(8,128)S(1)}) fusion(f32[256,2048]{1,0:T(8,128)S(1)} %get-tuple-element.6, s32[256,2048]{1,0:T(8,128)S(1)} %copy-done, f32[258,2048]{1,0:T(8,128)S(1)} %fusion.9, f32[256,2047]{1,0:T(8,128)S(1)} %get-tuple-element.10, f32[256,1]{1,0:T(8,128)S(1)} %get-tuple-element.12, ...), kind=kLoop, calls=%fused_computation.40 | loop fusion | flops 13631488 | bytes 16777216 | tf_op jit(solution)/shard_map/stack | solution.py:204
  26.7 1.0 %fusion.18 = f32[1,256,2048]{2,1,0:T(8,128)S(1)} fusion(f32[256,2048]{1,0:T(8,128)S(1)} %get-tuple-element.8, s32[256,2048]{1,0:T(8,128)S(1)} %copy-done), kind=kLoop, calls=%fused_computation.35 | loop fusion | flops 7864320 | bytes 6291456 | tf_op jit(solution)/shard_map/stack | solution.py:204
  27.7 0.1 copy-done.1
  27.8 4.2 %fusion.25 = f32[4,256,2,104,1]{1,3,4,2,0:T(8,128)S(1)} fusion(f32[2048,1,104]{0,2,1:T(8,128)S(1)} %copy-done.1, f32[2048,1,104]{0,2,1:T(8,128)S(1)} %get-tuple-element.34, f32[1,256,2048]{2,1,0:T(8,128)S(1)} %fusion.18, f32[1,256,2048]{2,1,0:T(8,128)S(1)} %get-tuple-element.7, f32[1,256,2048]{2,1,0:T(8,128)S(1)} %get-tuple-element.5, ...), kind=kOutput, calls=%fused_computation.52 | convolution fusion | flops 2623963136 | bytes 10944512 | tf_op jit(solution)/shard_map/kxy,ycn->kxcn/dot_general | solution.py:220
  32.0 0.9 convolution_bitcast_fusion
  32.9 0.1 broadcast_select_fusion
  33.0 0.2 copy.6
  33.2 0.4 select_n.172
  33.5 0.1 collective-permute-start.2
  33.6 0.2 copy.5
  33.8 0.4 select_n.170
  34.2 1.1 %collective-permute-done.2 = f32[676,128]{1,0:T(8,128)S(1)} collective-permute-done((f32[676,128]{1,0:T(8,128)S(1)}, f32[676,128]{1,0:T(8,128)S(1)}, u32[]{:S(2)}, u32[]{:S(2)}) %collective-permute-start.2) | collective-permute-done | bytes 346144 | tf_op jit(solution)/shard_map/ppermute | solution.py:165
  35.3 0.3 collective-permute-start.3
  35.6 10.0 %collective-permute-done.3 = f32[676,128]{1,0:T(8,128)S(1)} collective-permute-done((f32[676,128]{1,0:T(8,128)S(1)}, f32[676,128]{1,0:T(8,128)S(1)}, u32[]{:S(2)}, u32[]{:S(2)}) %collective-permute-start.3) | collective-permute-done | bytes 346144 | tf_op jit(solution)/shard_map/ppermute | solution.py:171
  45.6 1.3 %collective-permute-start.4 = (f32[676,128]{1,0:T(8,128)S(1)}, f32[676,128]{1,0:T(8,128)S(1)}, u32[]{:S(2)}, u32[]{:S(2)}) collective-permute-start(f32[676,128]{1,0:T(8,128)S(1)} %add.291), channel_id=1, source_target_pairs={{0,4},{1,5},{2,6},{3,7},{4,0},{5,1},{6,2},{7,3},{8,12},{9,13},{10,... | collective-permute-start | bytes 1038344 | tf_op jit(solution)/shard_map/ppermute | solution.py:171
  47.0 16.2 %collective-permute-done.4 = f32[676,128]{1,0:T(8,128)S(1)} collective-permute-done((f32[676,128]{1,0:T(8,128)S(1)}, f32[676,128]{1,0:T(8,128)S(1)}, u32[]{:S(2)}, u32[]{:S(2)}) %collective-permute-start.4) | collective-permute-done | bytes 346144 | tf_op jit(solution)/shard_map/ppermute | solution.py:171
  63.2 0.1 collective-permute-start.5
  63.3 0.5 and_select_fusion.4
  63.9 0.6 broadcast_subtract_fusion
  64.5 0.6 pad_maximum_fusion.6.dval_ref
  65.1 0.4 stack_reshape.8
  65.5 0.2 copy.7
  65.7 0.4 stack_reshape.9
  66.1 0.2 copy.8
  66.3 0.7 fusion.33
  67.1 0.9 %fusion.35 = f32[2,4,208,256]{3,2,1,0:T(8,128)S(1)} fusion(f32[1,4,208,104]{2,3,1,0:T(8,128)S(1)} %copy.8, f32[1,4,208,104]{2,3,1,0:T(8,128)S(1)} %copy.7, pred[]{:T(512)S(6)} %eq.93, pred[256]{0:T(512)(128)(4,1)S(1)} %iota_compare_fusion.4), kind=kOutput, calls=%fused_computation.66 | convolution fusion | flops 532373504 | bytes 2396417 | tf_op jit(solution)/shard_map/skac,cb->skab/dot_general | solution.py:234
  68.0 0.8 multiply_add_fusion
  68.8 0.2 fusion.85
  69.0 1.4 %pad_maximum_fusion.5.fl_ref = f32[2,4,208,256]{3,2,1,0:T(8,128)} fusion(f32[2,1,208,256]{3,2,1,0:T(8,128)S(1)} %get-tuple-element.27, f32[2,1,208,256]{3,2,1,0:T(8,128)S(1)} %get-tuple-element.29, f32[2,1,208,256]{3,2,1,0:T(8,128)S(1)} %get-tuple-element.28, f32[2,1,208,256]{3,2,1,0:T(8,128)S(1)} %get-tuple-element.26), kind=kLoop, calls=%fused_computation.49 | loop fusion | flops 1277952 | bytes 3407872 | tf_op jit(solution)/shard_map/stack | solution.py:239
  70.4 17.6 %shard_map.28 = f32[2,64,20402]{2,1,0:T(8,128)} custom-call(s32[64]{0:T(128)} %get-tuple-element.41.a0_ref, s32[64]{0:T(128)} %get-tuple-element.40.b0_ref, s32[64]{0:T(128)} %get-tuple-element.37.first_ref, s32[64]{0:T(128)} %get-tuple-element.36.second_ref, f32[2,64]{1,0:T(2,128)} %pad_maximum_fusion.6.dval_ref, f32[2,4,208,256]{3,2,1,0:T(8,128)} %pad_maximum_fusion.5.fl_ref), custom_call_target="tpu_custom_call" | custom-call | tf_op jit(solution)/shard_map/pallas_call | solution.py:150
  (19 shorter events, 0.3 us)
Async XLA Ops:
  2.4 9.9 %collective-permute-start = (f32[4,2048]{1,0:T(4,128)S(1)}, f32[4,2048]{1,0:T(4,128)S(1)}, u32[]{:S(2)}, u32[]{:S(2)}) collective-permute-start(f32[4,2048]{1,0:T(4,128)S(1)} %get-tuple-element.24), channel_id=1, source_target_pairs={{0,1},{1,2},{2,3},{3,4},{4,5},{5,6},{6,7},{7,0},{8,9},{9,10},{10,1... | collective-permute-start | bytes 98312 | tf_op jit(solution)/shard_map/ppermute | solution.py:28
  2.9 9.3 %collective-permute-start.1 = (f32[4,2048]{1,0:T(4,128)S(1)}, f32[4,2048]{1,0:T(4,128)S(1)}, u32[]{:S(2)}, u32[]{:S(2)}) collective-permute-start(f32[4,2048]{1,0:T(4,128)S(1)} %get-tuple-element.25), channel_id=1, source_target_pairs={{1,0},{2,1},{3,2},{4,3},{5,4},{6,5},{7,6},{0,7},{9,8},{10,9},{11,1... | collective-permute-start | bytes 98312 | tf_op jit(solution)/shard_map/ppermute | solution.py:31
  19.5 1.6 %copy-start = (s32[256,2048]{1,0:T(8,128)S(1)}, s32[256,2048]{1,0:T(8,128)}, u32[]{:S(2)}) copy-start(s32[256,2048]{1,0:T(8,128)} %param.2) | copy-start | bytes 6291460
  26.6 1.2 %copy-start.1 = (f32[2048,1,104]{0,2,1:T(8,128)S(1)}, f32[2048,1,104]{0,2,1:T(8,128)}, u32[]{:S(2)}) copy-start(f32[2048,1,104]{0,2,1:T(8,128)} %get-tuple-element.35) | copy-start | bytes 2555908
  33.5 1.7 %collective-permute-start.2 = (f32[676,128]{1,0:T(8,128)S(1)}, f32[676,128]{1,0:T(8,128)S(1)}, u32[]{:S(2)}, u32[]{:S(2)}) collective-permute-start(f32[676,128]{1,0:T(8,128)S(1)} %select_n.172), channel_id=1, source_target_pairs={{0,1},{1,0},{2,3},{3,2},{4,5},{5,4},{6,7},{7,6},{8,9},{9,8},{10,11... | collective-permute-start | bytes 1038344 | tf_op jit(solution)/shard_map/ppermute | solution.py:165
  35.3 10.3 %collective-permute-start.3 = (f32[676,128]{1,0:T(8,128)S(1)}, f32[676,128]{1,0:T(8,128)S(1)}, u32[]{:S(2)}, u32[]{:S(2)}) collective-permute-start(f32[676,128]{1,0:T(8,128)S(1)} %add.290), channel_id=1, source_target_pairs={{0,2},{1,3},{2,0},{3,1},{4,6},{5,7},{6,4},{7,5},{8,10},{9,11},{10,... | collective-permute-start | bytes 1038344 | tf_op jit(solution)/shard_map/ppermute | solution.py:171
  45.6 17.6 %collective-permute-start.4 = (f32[676,128]{1,0:T(8,128)S(1)}, f32[676,128]{1,0:T(8,128)S(1)}, u32[]{:S(2)}, u32[]{:S(2)}) collective-permute-start(f32[676,128]{1,0:T(8,128)S(1)} %add.291), channel_id=1, source_target_pairs={{0,4},{1,5},{2,6},{3,7},{4,0},{5,1},{6,2},{7,3},{8,12},{9,13},{10,... | collective-permute-start | bytes 1038344 | tf_op jit(solution)/shard_map/ppermute | solution.py:171
  63.2 2.5 %collective-permute-start.5 = (f32[676,128]{1,0:T(8,128)S(1)}, f32[676,128]{1,0:T(8,128)S(1)}, u32[]{:S(2)}, u32[]{:S(2)}) collective-permute-start(f32[676,128]{1,0:T(8,128)S(1)} %add.292), channel_id=1, source_target_pairs={{0,1},{1,0},{2,3},{3,2},{4,5},{5,4},{6,7},{7,6},{8,9},{9,8},{10,11... | collective-permute-start | bytes 1038344 | tf_op jit(solution)/shard_map/ppermute | solution.py:184
  66.3 1.7 %copy-start.2 = (f32[2]{0:T(128)S(1)}, f32[2]{0:T(128)}, u32[]{:S(2)}) copy-start(f32[2]{0:T(128)} %constant.134.clone) | copy-start | bytes 28

commit v8 on v7

--- a/solution.py
+++ b/solution.py
@@ -72,6 +72,56 @@
     real_part = products[0, :, :, 0] + products[1, :, :, 1]
     imag_part = products[0, :, :, 1] - products[1, :, :, 0]
     return jnp.stack([real_part, imag_part])
+
+
+FIELD_ROWS = 32
+RIM = 4
+
+
+def field_kernel(ext_ref, o_ref, work_ref):
+    i = pl.program_id(0)
+    start = pl.multiple_of(i * FIELD_ROWS, 8)
+    count = FIELD_ROWS + 2 * RIM
+    work_ref[pl.ds(0, count), :] = ext_ref[pl.ds(start, count), :]
+    width = work_ref.shape[1]
+    permit = work_ref[pl.ds(RIM, FIELD_ROWS), :]
+    for sweep_index in range(3):
+        count -= 2
+        middle = work_ref[pl.ds(1, count), :]
+        smooth = (
+            4.0 * middle
+            + work_ref[pl.ds(0, count), :]
+            + work_ref[pl.ds(2, count), :]
+            + pltpu.roll(middle, 1, 1)
+            + pltpu.roll(middle, width - 1, 1)
+        ) / 8.0
+        work_ref[pl.ds(0, count), :] = smooth
+    count -= 2
+    middle = work_ref[pl.ds(1, count), :]
+    grad_x = (work_ref[pl.ds(2, count), :] - work_ref[pl.ds(0, count), :]) / 2.0
+    grad_y = (pltpu.roll(middle, width - 1, 1) - pltpu.roll(middle, 1, 1)) / 2.0
+    scale = jnp.sqrt(grad_x * grad_x + grad_y * grad_y + 1.0)
+    normal_x = grad_x / scale
+    normal_y = grad_y / scale
+    inverse = 1.0 / permit
+    contrast = permit - inverse
+    o_ref[0] = permit
+    o_ref[1] = contrast * normal_x * normal_x
+    o_ref[2] = contrast * normal_x * normal_y
+    o_ref[3] = contrast * normal_y * normal_y
+
+
+def field_stack(extended):
+    rows = extended.shape[0] - 2 * RIM
+    width = extended.shape[1]
+    return pl.pallas_call(
+        field_kernel,
+        grid=(rows // FIELD_ROWS,),
+        in_specs=[pl.BlockSpec(extended.shape, lambda i: (0, 0))],
+        out_specs=pl.BlockSpec((4, FIELD_ROWS, width), lambda i: (0, i, 0)),
+        out_shape=jax.ShapeDtypeStruct((4, rows, width), jnp.float32),
+        scratch_shapes=[pltpu.VMEM((FIELD_ROWS + 2 * RIM, width), jnp.float32)],
+    )(extended)
 
 
 def chunk_segments(total, half):
@@ -192,23 +242,7 @@
     devices = lax.axis_size("slab")
     my_index = lax.axis_index("slab")
     permit = permittivity(labels)
-    smooth = extended_2(permit, (("slab", 0),), 4)
-    for sweep_index in range(3):
-        smooth = smooth_once(smooth)
-    grad_x, grad_y = gradient(smooth)
-    scale = jnp.sqrt(grad_x * grad_x + grad_y * grad_y + 1.0)
-    normal_x = grad_x / scale
-    normal_y = grad_y / scale
-    inverse = 1.0 / permit
-    contrast = permit - inverse
-    fields = jnp.stack(
-        [
-            permit,
-            contrast * normal_x * normal_x,
-            contrast * normal_x * normal_y,
-            contrast * normal_y * normal_y,
-        ]
-    )
+    fields = field_stack(extended_2(permit, (("slab", 0),), RIM))
     padded_keep = -(-KEEP // devices) * devices
     half_keep = -(-HARM // devices) * devices
     frequency = (HARM - 1) - jnp.arange(padded_keep, dtype=jnp.int32)

time: 88.3 us -> 89.5 us (1.014)
  Pallas kernels: 17.6 us -> 30.4 us
  other arithmetic: 22.1 us -> 12.8 us
  local copies, waits for them, and re-layouts: 6.82 us -> 2.32 us
  matrix products: 7.54 us -> 9.95 us
    pallas_call x0 -> x1, Pallas kernels: none -> 12.8 us  [field_stack(): pl.pallas_call(field_kernel, grid=(rows // FIELD_ROWS,), in_specs=[pl.Blo...]
    another operation x3 -> x0, other arithmetic: 6.55 us -> none  [shards(): jnp.stack([permit, contrast * normal_x * normal_x, contrast * normal_x *...]
    div x3 -> x0, other arithmetic: 4.07 us -> none  [smooth_once(): (4.0 * middle + extended[:-2] + extended[2:] + jnp.roll(middle, 1, 1) + j...]
    slice x7 -> x0, local copies, waits for them, and re-layouts: 3.98 us -> none  [the longest x5 2.81 us: smooth_once(): jnp.roll(middle, -1, 1)]
    dot_general x1, matrix products: 4.19 us -> 6.62 us  [shards(): jnp.einsum('kxy,ycn->kxcn', fields, col_table, precision=lax.Precision.HIGH)]
    concatenate x1, other arithmetic: 0.3 us -> 1.58 us  [extended_2(): block = jnp.concatenate([low, block, high], axis=dim)]
where the time goes in v8:
time: 89.5 us; the launch traced here: 89.3 us
  Pallas kernels  30.4 us (34%)
  waiting for transfers between devices  27.3 us (31%)
  other arithmetic  12.8 us (14%)
  matrix products  9.95 us (11%)
  starting transfers between devices  6.37 us (7%)
  local copies, waits for them, and re-layouts  2.32 us (3%)
    ppermute x2, waiting for transfers between devices, line_sum(): lax.ppermute(total, 'slab', [(i, i ^ bit) for i in range(devices)])  26.2 us
    pallas_call x1, Pallas kernels, assemble(): pl.pallas_call(assemble_kernel, grid_spec=grid_spec, out_shape=jax.ShapeD...  17.6 us
    pallas_call x1, Pallas kernels, field_stack(): pl.pallas_call(field_kernel, grid=(rows // FIELD_ROWS,), in_specs=[pl.Blo...  12.8 us
    dot_general x1, matrix products, shards(): jnp.einsum('kxy,ycn->kxcn', fields, col_table, precision=lax.Precision.HIGH)  6.62 us
    cos x1, other arithmetic, shards(): col_table = jnp.stack([jnp.cos(angles), -jnp.sin(angles)], axis=1)  4.31 us
    ppermute x1, starting transfers between devices, extended_2(): lax.ppermute(lax.slice_in_dim(block, 0, width, axis=dim), axis, backward)  4.09 us
    add x1, other arithmetic, permittivity(): total + jnp.where(labels == index_value, jnp.float32(PERMITS[index_value]...  2.33 us
  transfers between devices with their start and end apart: 6, of which 3 were waited for; matrix products, arithmetic and copies ran while one was open for 9% of the time, Pallas kernels for 0%

profile of v8, /device:TPU:0, one launch (start us, length us, event | category | flops | bytes accessed | tf_op | source)
XLA Modules:
  0.0 89.3 jit_solution(13988128228573022194)
XLA Ops:
  0.0 2.3 %select_add_fusion = f32[256,2048]{1,0:T(8,128)S(1)} fusion(s32[256,2048]{1,0:T(8,128)} %param.2), kind=kLoop, calls=%fused_computation.3 | loop fusion | flops 5767168 | bytes 4194304 | tf_op jit(solution)/shard_map/add | solution.py:39
  2.4 0.5 collective-permute-start
  2.9 4.1 %collective-permute-start.1 = (f32[4,2048]{1,0:T(4,128)S(1)}, f32[4,2048]{1,0:T(4,128)S(1)}, u32[]{:S(2)}, u32[]{:S(2)}) collective-permute-start(f32[4,2048]{1,0:T(4,128)S(1)} %get-tuple-element.6), channel_id=1, source_target_pairs={{1,0},{2,1},{3,2},{4,3},{5,4},{6,5},{7,6},{0,7},{9,8},{10,9},{11,1... | collective-permute-start | bytes 98312 | tf_op jit(solution)/shard_map/ppermute | solution.py:31
  7.0 4.3 %fusion.22 = (f32[2048,1,104]{0,2,1:T(8,128)S(1)}, f32[2048,1,104]{0,2,1:T(8,128)}) fusion(s32[104]{0:T(128)S(1)} %iota_subtract_fusion.3), kind=kLoop, calls=%fused_computation.34 | loop fusion | flops 3194880 | bytes 1704352 | tf_op jit(solution)/shard_map/cos | solution.py:253
  11.3 0.9 %fusion.32 = (f32[1,208,256]{2,1,0:T(8,128)S(1)}, f32[1,208,256]{2,1,0:T(8,128)S(1)}) fusion(s32[256]{0:T(256)S(1)} %iota_add_fusion, s32[208]{0:T(256)S(1)} %iota_subtract_fusion.2), kind=kLoop, calls=%fused_computation.53 | loop fusion | flops 745472 | bytes 427840 | tf_op jit(solution)/shard_map/cos | solution.py:70
  12.2 0.0 collective-permute-done
  12.3 0.0 collective-permute-done.1
  12.3 1.6 %pad_maximum_fusion.ext_ref = f32[264,2048]{1,0:T(8,128)} fusion(f32[4,2048]{1,0:T(4,128)S(1)} %collective-permute-done.1, f32[256,2048]{1,0:T(8,128)S(1)} %select_add_fusion, f32[4,2048]{1,0:T(4,128)S(1)} %collective-permute-done), kind=kLoop, calls=%fused_computation.2 | loop fusion | flops 1081344 | bytes 4325376 | tf_op jit(solution)/shard_map/concatenate | solution.py:32
  13.8 0.0 copy-start
  13.8 12.8 %shard_map.28 = f32[4,256,2048]{2,1,0:T(8,128)} custom-call(f32[264,2048]{1,0:T(8,128)} %pad_maximum_fusion.ext_ref), custom_call_target="tpu_custom_call" | custom-call | tf_op jit(solution)/shard_map/pallas_call | solution.py:117
  26.6 0.0 copy-done
  26.6 6.6 %fusion.4 = f32[4,256,2,104,1]{1,3,4,2,0:T(8,128)S(1)} fusion(f32[2048,1,104]{0,2,1:T(8,128)S(1)} %copy-done, f32[2048,1,104]{0,2,1:T(8,128)S(1)} %get-tuple-element.15, f32[4,256,2048]{2,1,0:T(8,128)} %shard_map.28), kind=kOutput, calls=%fused_computation.10 | convolution fusion | flops 2617671680 | bytes 10944512 | tf_op jit(solution)/shard_map/kxy,ycn->kxcn/dot_general | solution.py:254
  33.2 0.9 convolution_bitcast_fusion
  34.1 0.1 broadcast_select_fusion
  34.2 0.2 copy.6
  34.4 0.4 select_n.172
  34.8 0.1 collective-permute-start.2
  34.8 0.2 copy.5
  35.0 0.4 select_n.170
  35.4 1.1 %collective-permute-done.2 = f32[676,128]{1,0:T(8,128)S(1)} collective-permute-done((f32[676,128]{1,0:T(8,128)S(1)}, f32[676,128]{1,0:T(8,128)S(1)}, u32[]{:S(2)}, u32[]{:S(2)}) %collective-permute-start.2) | collective-permute-done | bytes 346144 | tf_op jit(solution)/shard_map/ppermute | solution.py:215
  36.5 0.1 add.234
  36.5 0.3 collective-permute-start.3
  36.8 10.0 %collective-permute-done.3 = f32[676,128]{1,0:T(8,128)S(1)} collective-permute-done((f32[676,128]{1,0:T(8,128)S(1)}, f32[676,128]{1,0:T(8,128)S(1)}, u32[]{:S(2)}, u32[]{:S(2)}) %collective-permute-start.3) | collective-permute-done | bytes 346144 | tf_op jit(solution)/shard_map/ppermute | solution.py:221
  46.8 0.1 add.235
  46.9 1.3 %collective-permute-start.4 = (f32[676,128]{1,0:T(8,128)S(1)}, f32[676,128]{1,0:T(8,128)S(1)}, u32[]{:S(2)}, u32[]{:S(2)}) collective-permute-start(f32[676,128]{1,0:T(8,128)S(1)} %add.235), channel_id=1, source_target_pairs={{0,4},{1,5},{2,6},{3,7},{4,0},{5,1},{6,2},{7,3},{8,12},{9,13},{10,... | collective-permute-start | bytes 1038344 | tf_op jit(solution)/shard_map/ppermute | solution.py:221
  48.2 16.2 %collective-permute-done.4 = f32[676,128]{1,0:T(8,128)S(1)} collective-permute-done((f32[676,128]{1,0:T(8,128)S(1)}, f32[676,128]{1,0:T(8,128)S(1)}, u32[]{:S(2)}, u32[]{:S(2)}) %collective-permute-start.4) | collective-permute-done | bytes 346144 | tf_op jit(solution)/shard_map/ppermute | solution.py:221
  64.4 0.1 add.236
  64.5 0.1 collective-permute-start.5
  64.5 0.6 and_select_fusion.4
  65.1 0.6 broadcast_subtract_fusion
  65.7 0.6 pad_maximum_fusion.2.dval_ref
  66.3 0.4 stack_reshape.8
  66.8 0.2 copy.7
  67.0 0.0 collective-permute-done.5
  67.0 0.4 stack_reshape.9
  67.4 0.2 copy.8
  67.6 0.0 copy-start.1
  67.6 0.7 fusion.14
  68.3 0.9 %fusion.16 = f32[2,4,208,256]{3,2,1,0:T(8,128)S(1)} fusion(f32[1,4,208,104]{2,3,1,0:T(8,128)S(1)} %copy.8, f32[1,4,208,104]{2,3,1,0:T(8,128)S(1)} %copy.7, pred[]{:T(512)S(6)} %eq.93, pred[256]{0:T(512)(128)(4,1)S(1)} %iota_compare_fusion.4), kind=kOutput, calls=%fused_computation.24 | convolution fusion | flops 532373504 | bytes 2396417 | tf_op jit(solution)/shard_map/skac,cb->skab/dot_general | solution.py:268
  69.3 0.0 copy-done.1
  69.3 0.8 multiply_add_fusion
  70.1 0.2 fusion.56
  70.3 1.4 %pad_maximum_fusion.1.fl_ref = f32[2,4,208,256]{3,2,1,0:T(8,128)} fusion(f32[2,1,208,256]{3,2,1,0:T(8,128)S(1)} %get-tuple-element.8, f32[2,1,208,256]{3,2,1,0:T(8,128)S(1)} %get-tuple-element.10, f32[2,1,208,256]{3,2,1,0:T(8,128)S(1)} %get-tuple-element.9, f32[2,1,208,256]{3,2,1,0:T(8,128)S(1)} %get-tuple-element.7), kind=kLoop, calls=%fused_computation.7 | loop fusion | flops 1277952 | bytes 3407872 | tf_op jit(solution)/shard_map/stack | solution.py:273
  71.7 17.6 %shard_map.29 = f32[2,64,20402]{2,1,0:T(8,128)} custom-call(s32[64]{0:T(128)} %get-tuple-element.22.a0_ref, s32[64]{0:T(128)} %get-tuple-element.21.b0_ref, s32[64]{0:T(128)} %get-tuple-element.18.first_ref, s32[64]{0:T(128)} %get-tuple-element.17.second_ref, f32[2,64]{1,0:T(2,128)} %pad_maximum_fusion.2.dval_ref, f32[2,4,208,256]{3,2,1,0:T(8,128)} %pad_maximum_fusion.1.fl_ref), custom_call_target="tpu_custom_call" | custom-call | tf_op jit(solution)/shard_map/pallas_call | solution.py:200
  (9 shorter events, 0.1 us)
Async XLA Ops:
  2.4 9.9 %collective-permute-start = (f32[4,2048]{1,0:T(4,128)S(1)}, f32[4,2048]{1,0:T(4,128)S(1)}, u32[]{:S(2)}, u32[]{:S(2)}) collective-permute-start(f32[4,2048]{1,0:T(4,128)S(1)} %get-tuple-element.5), channel_id=1, source_target_pairs={{0,1},{1,2},{2,3},{3,4},{4,5},{5,6},{6,7},{7,0},{8,9},{9,10},{10,1... | collective-permute-start | bytes 98312 | tf_op jit(solution)/shard_map/ppermute | solution.py:28
  2.9 9.4 %collective-permute-start.1 = (f32[4,2048]{1,0:T(4,128)S(1)}, f32[4,2048]{1,0:T(4,128)S(1)}, u32[]{:S(2)}, u32[]{:S(2)}) collective-permute-start(f32[4,2048]{1,0:T(4,128)S(1)} %get-tuple-element.6), channel_id=1, source_target_pairs={{1,0},{2,1},{3,2},{4,3},{5,4},{6,5},{7,6},{0,7},{9,8},{10,9},{11,1... | collective-permute-start | bytes 98312 | tf_op jit(solution)/shard_map/ppermute | solution.py:31
  13.8 12.8 %copy-start = (f32[2048,1,104]{0,2,1:T(8,128)S(1)}, f32[2048,1,104]{0,2,1:T(8,128)}, u32[]{:S(2)}) copy-start(f32[2048,1,104]{0,2,1:T(8,128)} %get-tuple-element.16) | copy-start | bytes 2555908
  34.8 1.7 %collective-permute-start.2 = (f32[676,128]{1,0:T(8,128)S(1)}, f32[676,128]{1,0:T(8,128)S(1)}, u32[]{:S(2)}, u32[]{:S(2)}) collective-permute-start(f32[676,128]{1,0:T(8,128)S(1)} %select_n.172), channel_id=1, source_target_pairs={{0,1},{1,0},{2,3},{3,2},{4,5},{5,4},{6,7},{7,6},{8,9},{9,8},{10,11... | collective-permute-start | bytes 1038344 | tf_op jit(solution)/shard_map/ppermute | solution.py:215
  36.5 10.3 %collective-permute-start.3 = (f32[676,128]{1,0:T(8,128)S(1)}, f32[676,128]{1,0:T(8,128)S(1)}, u32[]{:S(2)}, u32[]{:S(2)}) collective-permute-start(f32[676,128]{1,0:T(8,128)S(1)} %add.234), channel_id=1, source_target_pairs={{0,2},{1,3},{2,0},{3,1},{4,6},{5,7},{6,4},{7,5},{8,10},{9,11},{10,... | collective-permute-start | bytes 1038344 | tf_op jit(solution)/shard_map/ppermute | solution.py:221
  46.9 17.5 %collective-permute-start.4 = (f32[676,128]{1,0:T(8,128)S(1)}, f32[676,128]{1,0:T(8,128)S(1)}, u32[]{:S(2)}, u32[]{:S(2)}) collective-permute-start(f32[676,128]{1,0:T(8,128)S(1)} %add.235), channel_id=1, source_target_pairs={{0,4},{1,5},{2,6},{3,7},{4,0},{5,1},{6,2},{7,3},{8,12},{9,13},{10,... | collective-permute-start | bytes 1038344 | tf_op jit(solution)/shard_map/ppermute | solution.py:221
  64.5 2.5 %collective-permute-start.5 = (f32[676,128]{1,0:T(8,128)S(1)}, f32[676,128]{1,0:T(8,128)S(1)}, u32[]{:S(2)}, u32[]{:S(2)}) collective-permute-start(f32[676,128]{1,0:T(8,128)S(1)} %add.236), channel_id=1, source_target_pairs={{0,1},{1,0},{2,3},{3,2},{4,5},{5,4},{6,7},{7,6},{8,9},{9,8},{10,11... | collective-permute-start | bytes 1038344 | tf_op jit(solution)/shard_map/ppermute | solution.py:234
  67.6 1.7 %copy-start.1 = (f32[2]{0:T(128)S(1)}, f32[2]{0:T(128)}, u32[]{:S(2)}) copy-start(f32[2]{0:T(128)} %constant.119.clone) | copy-start | bytes 28

commit v9 on v7

--- a/solution.py
+++ b/solution.py
@@ -164,12 +164,24 @@
     give = jnp.where(core == 0, partial_value[1], partial_value[0]).reshape(dense)
     mine = keep + lax.ppermute(give, "slab", pairs)
     chips = devices // 2
-    if chips & (chips - 1) == 0:
-        total = mine
-        bit = 2
+    if chips & (chips - 1) == 0 and chips > 1 and len(dense) == 2:
+        rows = mine.shape[0]
+        padded = -(-rows // 16) * 16
+        grown = jnp.pad(mine, ((0, padded - rows), (0, 0)))
+        upper = (my_index // 2) % 2
+        halves = (grown[: padded // 2], grown[padded // 2 :])
+        pair = [(i, i ^ 2) for i in range(devices)]
+        kept = jnp.where(upper == 0, halves[0], halves[1])
+        sent = jnp.where(upper == 0, halves[1], halves[0])
+        kept = kept + lax.ppermute(sent, "slab", pair)
+        bit = 4
         while bit < devices:
-            total = total + lax.ppermute(total, "slab", [(i, i ^ bit) for i in range(devices)])
+            kept = kept + lax.ppermute(kept, "slab", [(i, i ^ bit) for i in range(devices)])
             bit *= 2
+        back = lax.ppermute(kept, "slab", pair)
+        total = jnp.where(
+            upper == 0, jnp.concatenate([kept, back]), jnp.concatenate([back, kept])
+        )[:rows]
     else:
         right = [(i, i + 2) for i in range(devices - 2)]
         left = [(i + 2, i) for i in range(devices - 2)]

time: 88.3 us -> 83.7 us (0.948)
  waiting for transfers between devices: 27.3 us -> 22.6 us
    ppermute x2 -> x3, waiting for transfers between devices: 26.2 us -> 21.5 us  [the longest x1 8.88 us: line_sum(): lax.ppermute(kept, 'slab', [(i, i ^ bit) for i in range(devices)])]
  transfers between devices with their start and end apart: 6 -> 7, of which waited for: 3 -> 4; matrix products, arithmetic and copies ran while one was open for 9% -> 10% of each run, Pallas kernels for 0% -> 0%
where the time goes in v9:
time: 83.7 us; the launch traced here: 83.4 us
  waiting for transfers between devices  22.6 us (27%)
  other arithmetic  22.1 us (26%)
  Pallas kernels  17.6 us (21%)
  matrix products  7.53 us (9%)
  local copies, waits for them, and re-layouts  6.82 us (8%)
  starting transfers between devices  6.42 us (8%)
    pallas_call x1, Pallas kernels, assemble(): pl.pallas_call(assemble_kernel, grid_spec=grid_spec, out_shape=jax.ShapeD...  17.6 us
    ppermute x1, waiting for transfers between devices, line_sum(): lax.ppermute(kept, 'slab', [(i, i ^ bit) for i in range(devices)])  8.88 us
    another operation x3, other arithmetic, shards(): jnp.stack([permit, contrast * normal_x * normal_x, contrast * normal_x *...  6.55 us
    ppermute x1, waiting for transfers between devices, line_sum(): back = lax.ppermute(kept, 'slab', pair)  6.32 us
    ppermute x1, waiting for transfers between devices, line_sum(): kept = kept + lax.ppermute(sent, 'slab', pair)  6.29 us
    cos x1, other arithmetic, shards(): col_table = jnp.stack([jnp.cos(angles), -jnp.sin(angles)], axis=1)  4.3 us
    dot_general x1, matrix products, shards(): jnp.einsum('kxy,ycn->kxcn', fields, col_table, precision=lax.Precision.HIGH)  4.19 us
    ppermute x1, starting transfers between devices, extended_2(): lax.ppermute(lax.slice_in_dim(block, 0, width, axis=dim), axis, backward)  4.09 us
  transfers between devices with their start and end apart: 7, of which 4 were waited for; matrix products, arithmetic and copies ran while one was open for 10% of the time, Pallas kernels for 0%

profile of v9, /device:TPU:0, one launch (start us, length us, event | category | flops | bytes accessed | tf_op | source)
XLA Modules:
  0.0 83.4 jit_solution(14559621767253988858)
XLA Ops:
  0.0 2.3 %select_add_fusion = f32[256,2048]{1,0:T(8,128)S(1)} fusion(s32[256,2048]{1,0:T(8,128)} %param.2), kind=kLoop, calls=%fused_computation.45 | loop fusion | flops 5767168 | bytes 4194304 | tf_op jit(solution)/shard_map/add | solution.py:39
  2.4 0.5 collective-permute-start
  2.9 4.1 %collective-permute-start.1 = (f32[4,2048]{1,0:T(4,128)S(1)}, f32[4,2048]{1,0:T(4,128)S(1)}, u32[]{:S(2)}, u32[]{:S(2)}) collective-permute-start(f32[4,2048]{1,0:T(4,128)S(1)} %get-tuple-element.25), channel_id=1, source_target_pairs={{1,0},{2,1},{3,2},{4,3},{5,4},{6,5},{7,6},{0,7},{9,8},{10,9},{11,1... | collective-permute-start | bytes 98312 | tf_op jit(solution)/shard_map/ppermute | solution.py:31
  7.0 4.3 %fusion.41 = (f32[2048,1,104]{0,2,1:T(8,128)S(1)}, f32[2048,1,104]{0,2,1:T(8,128)}) fusion(s32[104]{0:T(128)S(1)} %iota_subtract_fusion.3), kind=kLoop, calls=%fused_computation.76 | loop fusion | flops 3194880 | bytes 1704352 | tf_op jit(solution)/shard_map/cos | solution.py:231
  11.3 0.9 %fusion.52 = (f32[1,208,256]{2,1,0:T(8,128)S(1)}, f32[1,208,256]{2,1,0:T(8,128)S(1)}) fusion(s32[256]{0:T(256)S(1)} %iota_add_fusion, s32[208]{0:T(256)S(1)} %iota_subtract_fusion.2), kind=kLoop, calls=%fused_computation.101 | loop fusion | flops 745472 | bytes 427840 | tf_op jit(solution)/shard_map/cos | solution.py:70
  12.3 0.3 pad_maximum_fusion.4
  12.6 0.9 %fusion.84 = (f32[262,2047]{1,0:T(8,128)S(1)}, f32[262,2047]{1,0:T(8,128)S(1)}) fusion(f32[264,2048]{1,0:T(8,128)S(1)} %pad_maximum_fusion.4), kind=kLoop, calls=%fused_computation.157 | loop fusion | bytes 8581024 | tf_op jit(solution)/shard_map/jit(_roll_static)/slice | solution.py:52
  13.4 2.3 %fusion.15 = f32[262,2048]{1,0:T(8,128)S(1)} fusion(f32[4,2048]{1,0:T(4,128)S(1)} %collective-permute-done.1, f32[256,2048]{1,0:T(8,128)S(1)} %select_add_fusion, f32[4,2048]{1,0:T(4,128)S(1)} %collective-permute-done, f32[264,2048]{1,0:T(8,128)S(1)} %pad_maximum_fusion.4, f32[262,2047]{1,0:T(8,128)S(1)} %get-tuple-element.22, ...), kind=kLoop, calls=%fused_computation.25 | loop fusion | flops 6438912 | bytes 15038416 | tf_op jit(solution)/shard_map/div | solution.py:47
  15.8 0.9 %fusion.82 = (f32[260,2047]{1,0:T(8,128)S(1)}, f32[260,2047]{1,0:T(8,128)S(1)}) fusion(f32[262,2048]{1,0:T(8,128)S(1)} %fusion.15), kind=kLoop, calls=%fused_computation.155 | loop fusion | bytes 8515520 | tf_op jit(solution)/shard_map/jit(_roll_static)/slice | solution.py:52
  16.7 0.1 fusion.83
  16.8 0.9 %fusion.12 = f32[260,2048]{1,0:T(8,128)S(1)} fusion(f32[262,2048]{1,0:T(8,128)S(1)} %fusion.15, f32[260,2047]{1,0:T(8,128)S(1)} %get-tuple-element.18, f32[260,1]{1,0:T(8,128)S(1)} %get-tuple-element.20, f32[260,1]{1,0:T(8,128)S(1)} %get-tuple-element.19, f32[260,2047]{1,0:T(8,128)S(1)} %get-tuple-element.17), kind=kLoop, calls=%fused_computation.19 | loop fusion | flops 4259840 | bytes 12779520 | tf_op jit(solution)/shard_map/div | solution.py:47
  17.6 0.9 %fusion.80 = (f32[258,2047]{1,0:T(8,128)S(1)}, f32[258,2047]{1,0:T(8,128)S(1)}) fusion(f32[260,2048]{1,0:T(8,128)S(1)} %fusion.12), kind=kLoop, calls=%fused_computation.153 | loop fusion | bytes 8450016 | tf_op jit(solution)/shard_map/jit(_roll_static)/slice | solution.py:52
  18.5 0.1 fusion.81
  18.6 0.9 %fusion.9 = f32[258,2048]{1,0:T(8,128)S(1)} fusion(f32[260,2048]{1,0:T(8,128)S(1)} %fusion.12, f32[258,2047]{1,0:T(8,128)S(1)} %get-tuple-element.14, f32[258,1]{1,0:T(8,128)S(1)} %get-tuple-element.16, f32[258,1]{1,0:T(8,128)S(1)} %get-tuple-element.15, f32[258,2047]{1,0:T(8,128)S(1)} %get-tuple-element.13), kind=kLoop, calls=%fused_computation.13 | loop fusion | flops 4227072 | bytes 12681216 | tf_op jit(solution)/shard_map/div | solution.py:47
  19.5 1.1 %fusion.78 = (f32[256,2047]{1,0:T(8,128)S(1)}, f32[256,2047]{1,0:T(8,128)S(1)}) fusion(f32[258,2048]{1,0:T(8,128)S(1)} %fusion.9), kind=kLoop, calls=%fused_computation.151 | loop fusion | bytes 8384512 | tf_op jit(solution)/shard_map/jit(_roll_static)/slice | solution.py:59
  20.6 0.1 fusion.79
  20.7 0.4 copy-done
  21.1 2.7 %multiply_bitcast_fusion.1 = (f32[1,256,2048]{2,1,0:T(8,128)S(1)}, f32[256,2048]{1,0:T(8,128)S(1)}, f32[1,256,2048]{2,1,0:T(8,128)S(1)}) fusion(s32[256,2048]{1,0:T(8,128)S(1)} %copy-done, f32[256,2047]{1,0:T(8,128)S(1)} %get-tuple-element.10, f32[256,1]{1,0:T(8,128)S(1)} %get-tuple-element.12, f32[256,1]{1,0:T(8,128)S(1)} %get-tuple-element.11, ...), kind=kLoop, calls=%fused_computation.41 | loop fusion | flops 13631488 | bytes 16777216 | tf_op jit(solution)/shard_map/stack | solution.py:216
  23.8 2.9 %multiply_bitcast_fusion = (f32[1,256,2048]{2,1,0:T(8,128)S(1)}, f32[256,2048]{1,0:T(8,128)S(1)}) fusion(f32[256,2048]{1,0:T(8,128)S(1)} %get-tuple-element.6, s32[256,2048]{1,0:T(8,128)S(1)} %copy-done, f32[258,2048]{1,0:T(8,128)S(1)} %fusion.9, f32[256,2047]{1,0:T(8,128)S(1)} %get-tuple-element.10, f32[256,1]{1,0:T(8,128)S(1)} %get-tuple-element.12, ...), kind=kLoop, calls=%fused_computation.40 | loop fusion | flops 13631488 | bytes 16777216 | tf_op jit(solution)/shard_map/stack | solution.py:216
  26.7 1.0 %fusion.18 = f32[1,256,2048]{2,1,0:T(8,128)S(1)} fusion(f32[256,2048]{1,0:T(8,128)S(1)} %get-tuple-element.8, s32[256,2048]{1,0:T(8,128)S(1)} %copy-done), kind=kLoop, calls=%fused_computation.35 | loop fusion | flops 7864320 | bytes 6291456 | tf_op jit(solution)/shard_map/stack | solution.py:216
  27.7 0.1 copy-done.1
  27.8 4.2 %fusion.25 = f32[4,256,2,104,1]{1,3,4,2,0:T(8,128)S(1)} fusion(f32[2048,1,104]{0,2,1:T(8,128)S(1)} %copy-done.1, f32[2048,1,104]{0,2,1:T(8,128)S(1)} %get-tuple-element.34, f32[1,256,2048]{2,1,0:T(8,128)S(1)} %fusion.18, f32[1,256,2048]{2,1,0:T(8,128)S(1)} %get-tuple-element.7, f32[1,256,2048]{2,1,0:T(8,128)S(1)} %get-tuple-element.5, ...), kind=kOutput, calls=%fused_computation.52 | convolution fusion | flops 2623963136 | bytes 10944512 | tf_op jit(solution)/shard_map/kxy,ycn->kxcn/dot_general | solution.py:232
  32.0 0.9 %convolution_bitcast_fusion = f32[2,4,208,2,104]{2,4,0,3,1:T(8,128)S(1)} fusion(f32[4,256,2,104,1]{1,3,4,2,0:T(8,128)S(1)} %fusion.25, f32[1,208,256]{2,1,0:T(8,128)S(1)} %get-tuple-element.33, f32[1,208,256]{2,1,0:T(8,128)S(1)} %get-tuple-element.32), kind=kOutput, calls=%fused_computation.51 | convolution fusion | flops 531734528 | bytes 2662400 | tf_op jit(solution)/shard_map/smx,kxcn->skmcn/dot_general | solution.py:71
  32.9 0.1 broadcast_select_fusion
  33.0 0.2 copy.6
  33.2 0.4 select_n.204
  33.5 0.1 collective-permute-start.2
  33.6 0.2 copy.5
  33.8 0.4 select_n.202
  34.2 1.1 %collective-permute-done.2 = f32[676,128]{1,0:T(8,128)S(1)} collective-permute-done((f32[676,128]{1,0:T(8,128)S(1)}, f32[676,128]{1,0:T(8,128)S(1)}, u32[]{:S(2)}, u32[]{:S(2)}) %collective-permute-start.2) | collective-permute-done | bytes 346144 | tf_op jit(solution)/shard_map/ppermute | solution.py:165
  35.3 0.3 collective-permute-start.3
  35.6 6.3 %collective-permute-done.3 = f32[344,128]{1,0:T(8,128)S(1)} collective-permute-done((f32[344,128]{1,0:T(8,128)S(1)}, f32[344,128]{1,0:T(8,128)S(1)}, u32[]{:S(2)}, u32[]{:S(2)}) %collective-permute-start.3) | collective-permute-done | bytes 176160 | tf_op jit(solution)/shard_map/ppermute | solution.py:176
  41.9 1.3 %collective-permute-start.4 = (f32[344,128]{1,0:T(8,128)S(1)}, f32[344,128]{1,0:T(8,128)S(1)}, u32[]{:S(2)}, u32[]{:S(2)}) collective-permute-start(f32[344,128]{1,0:T(8,128)S(1)} %select_add_fusion.1), channel_id=1, source_target_pairs={{0,4},{1,5},{2,6},{3,7},{4,0},{5,1},{6,2},{7,3},{8,12},{9,13},{10,... | collective-permute-start | bytes 528392 | tf_op jit(solution)/shard_map/ppermute | solution.py:179
  43.2 8.9 %collective-permute-done.4 = f32[344,128]{1,0:T(8,128)S(1)} collective-permute-done((f32[344,128]{1,0:T(8,128)S(1)}, f32[344,128]{1,0:T(8,128)S(1)}, u32[]{:S(2)}, u32[]{:S(2)}) %collective-permute-start.4) | collective-permute-done | bytes 176160 | tf_op jit(solution)/shard_map/ppermute | solution.py:179
  52.3 6.3 %collective-permute-done.5 = f32[344,128]{1,0:T(8,128)S(1)} collective-permute-done((f32[344,128]{1,0:T(8,128)S(1)}, f32[344,128]{1,0:T(8,128)S(1)}, u32[]{:S(2)}, u32[]{:S(2)}) %collective-permute-start.5) | collective-permute-done | bytes 176160 | tf_op jit(solution)/shard_map/ppermute | solution.py:181
  58.7 0.6 and_select_fusion.4
  59.3 0.6 broadcast_subtract_fusion
  59.9 0.5 pad_maximum_fusion.8.dval_ref
  60.4 0.4 stack_reshape.8
  60.9 0.2 copy.7
  61.1 0.4 stack_reshape.9
  61.5 0.2 copy.8
  61.7 0.7 fusion.33
  62.5 0.9 %fusion.35 = f32[2,4,208,256]{3,2,1,0:T(8,128)S(1)} fusion(f32[1,4,208,104]{2,3,1,0:T(8,128)S(1)} %copy.8, f32[1,4,208,104]{2,3,1,0:T(8,128)S(1)} %copy.7, pred[]{:T(512)S(6)} %eq.99, pred[256]{0:T(512)(128)(4,1)S(1)} %iota_compare_fusion.4), kind=kOutput, calls=%fused_computation.66 | convolution fusion | flops 532373504 | bytes 2396417 | tf_op jit(solution)/shard_map/skac,cb->skab/dot_general | solution.py:246
  63.4 0.8 multiply_add_fusion
  64.2 0.2 fusion.86
  64.4 1.4 %pad_maximum_fusion.5.fl_ref = f32[2,4,208,256]{3,2,1,0:T(8,128)} fusion(f32[2,1,208,256]{3,2,1,0:T(8,128)S(1)} %get-tuple-element.27, f32[2,1,208,256]{3,2,1,0:T(8,128)S(1)} %get-tuple-element.29, f32[2,1,208,256]{3,2,1,0:T(8,128)S(1)} %get-tuple-element.28, f32[2,1,208,256]{3,2,1,0:T(8,128)S(1)} %get-tuple-element.26), kind=kLoop, calls=%fused_computation.49 | loop fusion | flops 1277952 | bytes 3407872 | tf_op jit(solution)/shard_map/stack | solution.py:251
  65.8 17.6 %shard_map.28 = f32[2,64,20402]{2,1,0:T(8,128)} custom-call(s32[64]{0:T(128)} %get-tuple-element.41.a0_ref, s32[64]{0:T(128)} %get-tuple-element.40.b0_ref, s32[64]{0:T(128)} %get-tuple-element.37.first_ref, s32[64]{0:T(128)} %get-tuple-element.36.second_ref, f32[2,64]{1,0:T(2,128)} %pad_maximum_fusion.8.dval_ref, f32[2,4,208,256]{3,2,1,0:T(8,128)} %pad_maximum_fusion.5.fl_ref), custom_call_target="tpu_custom_call" | custom-call | tf_op jit(solution)/shard_map/pallas_call | solution.py:150
  (23 shorter events, 0.4 us)
Async XLA Ops:
  2.4 9.9 %collective-permute-start = (f32[4,2048]{1,0:T(4,128)S(1)}, f32[4,2048]{1,0:T(4,128)S(1)}, u32[]{:S(2)}, u32[]{:S(2)}) collective-permute-start(f32[4,2048]{1,0:T(4,128)S(1)} %get-tuple-element.24), channel_id=1, source_target_pairs={{0,1},{1,2},{2,3},{3,4},{4,5},{5,6},{6,7},{7,0},{8,9},{9,10},{10,1... | collective-permute-start | bytes 98312 | tf_op jit(solution)/shard_map/ppermute | solution.py:28
  2.9 9.3 %collective-permute-start.1 = (f32[4,2048]{1,0:T(4,128)S(1)}, f32[4,2048]{1,0:T(4,128)S(1)}, u32[]{:S(2)}, u32[]{:S(2)}) collective-permute-start(f32[4,2048]{1,0:T(4,128)S(1)} %get-tuple-element.25), channel_id=1, source_target_pairs={{1,0},{2,1},{3,2},{4,3},{5,4},{6,5},{7,6},{0,7},{9,8},{10,9},{11,1... | collective-permute-start | bytes 98312 | tf_op jit(solution)/shard_map/ppermute | solution.py:31
  19.5 1.6 %copy-start = (s32[256,2048]{1,0:T(8,128)S(1)}, s32[256,2048]{1,0:T(8,128)}, u32[]{:S(2)}) copy-start(s32[256,2048]{1,0:T(8,128)} %param.2) | copy-start | bytes 6291460
  26.6 1.2 %copy-start.1 = (f32[2048,1,104]{0,2,1:T(8,128)S(1)}, f32[2048,1,104]{0,2,1:T(8,128)}, u32[]{:S(2)}) copy-start(f32[2048,1,104]{0,2,1:T(8,128)} %get-tuple-element.35) | copy-start | bytes 2555908
  33.5 1.7 %collective-permute-start.2 = (f32[676,128]{1,0:T(8,128)S(1)}, f32[676,128]{1,0:T(8,128)S(1)}, u32[]{:S(2)}, u32[]{:S(2)}) collective-permute-start(f32[676,128]{1,0:T(8,128)S(1)} %select_n.204), channel_id=1, source_target_pairs={{0,1},{1,0},{2,3},{3,2},{4,5},{5,4},{6,7},{7,6},{8,9},{9,8},{10,11... | collective-permute-start | bytes 1038344 | tf_op jit(solution)/shard_map/ppermute | solution.py:165
  35.3 6.6 %collective-permute-start.3 = (f32[344,128]{1,0:T(8,128)S(1)}, f32[344,128]{1,0:T(8,128)S(1)}, u32[]{:S(2)}, u32[]{:S(2)}) collective-permute-start(f32[344,128]{1,0:T(8,128)S(1)} %slice_select_fusion), channel_id=1, source_target_pairs={{0,2},{1,3},{2,0},{3,1},{4,6},{5,7},{6,4},{7,5},{8,10},{9,11},{10,... | collective-permute-start | bytes 528392 | tf_op jit(solution)/shard_map/ppermute | solution.py:176
  41.9 10.2 %collective-permute-start.4 = (f32[344,128]{1,0:T(8,128)S(1)}, f32[344,128]{1,0:T(8,128)S(1)}, u32[]{:S(2)}, u32[]{:S(2)}) collective-permute-start(f32[344,128]{1,0:T(8,128)S(1)} %select_add_fusion.1), channel_id=1, source_target_pairs={{0,4},{1,5},{2,6},{3,7},{4,0},{5,1},{6,2},{7,3},{8,12},{9,13},{10,... | collective-permute-start | bytes 528392 | tf_op jit(solution)/shard_map/ppermute | solution.py:179
  52.1 6.5 %collective-permute-start.5 = (f32[344,128]{1,0:T(8,128)S(1)}, f32[344,128]{1,0:T(8,128)S(1)}, u32[]{:S(2)}, u32[]{:S(2)}) collective-permute-start(f32[344,128]{1,0:T(8,128)S(1)} %add.299), channel_id=1, source_target_pairs={{0,2},{1,3},{2,0},{3,1},{4,6},{5,7},{6,4},{7,5},{8,10},{9,11},{10,... | collective-permute-start | bytes 528392 | tf_op jit(solution)/shard_map/ppermute | solution.py:181
  58.6 2.4 %collective-permute-start.6 = (f32[676,128]{1,0:T(8,128)S(1)}, f32[676,128]{1,0:T(8,128)S(1)}, u32[]{:S(2)}, u32[]{:S(2)}) collective-permute-start(f32[676,128]{1,0:T(8,128)S(1)} %fusion.44), channel_id=1, source_target_pairs={{0,1},{1,0},{2,3},{3,2},{4,5},{5,4},{6,7},{7,6},{8,9},{9,8},{10,11... | collective-permute-start | bytes 1038344 | tf_op jit(solution)/shard_map/ppermute | solution.py:196
  61.7 1.7 %copy-start.2 = (f32[2]{0:T(128)S(1)}, f32[2]{0:T(128)}, u32[]{:S(2)}) copy-start(f32[2]{0:T(128)} %constant.148.clone) | copy-start | bytes 28

commit v10 on v9

--- a/solution.py
+++ b/solution.py
@@ -204,6 +204,15 @@
     devices = lax.axis_size("slab")
     my_index = lax.axis_index("slab")
     permit = permittivity(labels)
+    padded_keep = -(-KEEP // devices) * devices
+    half_keep = -(-HARM // devices) * devices
+    frequency = (HARM - 1) - jnp.arange(padded_keep, dtype=jnp.int32)
+    col_frequency = (HARM - 1) - jnp.arange(half_keep, dtype=jnp.int32)
+    columns = jnp.arange(map_width, dtype=jnp.int32)
+    phases = columns[:, None] * col_frequency[None, :] % map_width
+    angles = phases.astype(jnp.float32) * (2.0 * math.pi / map_width)
+    col_table = jnp.stack([jnp.cos(angles), -jnp.sin(angles)], axis=1)
+    col_table, permit = lax.optimization_barrier((col_table, permit))
     smooth = extended_2(permit, (("slab", 0),), 4)
     for sweep_index in range(3):
         smooth = smooth_once(smooth)
@@ -221,14 +230,6 @@
             contrast * normal_y * normal_y,
         ]
     )
-    padded_keep = -(-KEEP // devices) * devices
-    half_keep = -(-HARM // devices) * devices
-    frequency = (HARM - 1) - jnp.arange(padded_keep, dtype=jnp.int32)
-    col_frequency = (HARM - 1) - jnp.arange(half_keep, dtype=jnp.int32)
-    columns = jnp.arange(map_width, dtype=jnp.int32)
-    phases = columns[:, None] * col_frequency[None, :] % map_width
-    angles = phases.astype(jnp.float32) * (2.0 * math.pi / map_width)
-    col_table = jnp.stack([jnp.cos(angles), -jnp.sin(angles)], axis=1)
     half_spectra = jnp.einsum("kxy,ycn->kxcn", fields, col_table, precision=lax.Precision.HIGH)
     my_positions = my_index * slab_rows + jnp.arange(slab_rows, dtype=jnp.int32)
     partial_value = row_transform(half_spectra, my_positions, frequency, map_width)

time: 83.7 us -> 83.9 us (level)
  starting transfers between devices: 6.42 us -> 9.98 us
  waiting for transfers between devices: 22.6 us -> 19.4 us
  other arithmetic: 22.1 us -> 20.7 us
    ppermute x1, waiting for transfers between devices: 6.32 us -> 4.69 us  [line_sum(): back = lax.ppermute(kept, 'slab', pair)]
    another operation x3, other arithmetic: 6.55 us -> 4.98 us  [shards(): jnp.stack([permit, contrast * normal_x * normal_x, contrast * normal_x *...]
    ppermute x1, starting transfers between devices: 1.29 us -> 2.68 us  [line_sum(): lax.ppermute(kept, 'slab', [(i, i ^ bit) for i in range(devices)])]
    another operation x0 -> x1, other arithmetic: none -> 1.3 us  [shards(): col_table = jnp.stack([jnp.cos(angles), -jnp.sin(angles)], axis=1)]
    ppermute x1, starting transfers between devices: 0.28 us -> 1.42 us  [line_sum(): kept = kept + lax.ppermute(sent, 'slab', pair)]
    ppermute x1, waiting for transfers between devices: 6.29 us -> 5.16 us  [line_sum(): kept = kept + lax.ppermute(sent, 'slab', pair)]
    ppermute x1, waiting for transfers between devices: 8.88 us -> 7.93 us  [line_sum(): lax.ppermute(kept, 'slab', [(i, i ^ bit) for i in range(devices)])]
    cos x1, other arithmetic: 4.3 us -> 3.4 us  [shards(): col_table = jnp.stack([jnp.cos(angles), -jnp.sin(angles)], axis=1)]
  transfers between devices with their start and end apart: 7 -> 7, of which waited for: 4 -> 6; matrix products, arithmetic and copies ran while one was open for 10% -> 5% of each run, Pallas kernels for 0% -> 0%
where the time goes in v10:
time: 83.9 us; the launch traced here: 82.8 us
  other arithmetic  20.7 us (25%)
  waiting for transfers between devices  19.4 us (23%)
  Pallas kernels  17.6 us (21%)
  starting transfers between devices  9.98 us (12%)
  matrix products  7.58 us (9%)
  local copies, waits for them, and re-layouts  7.21 us (9%)
    pallas_call x1, Pallas kernels, assemble(): pl.pallas_call(assemble_kernel, grid_spec=grid_spec, out_shape=jax.ShapeD...  17.6 us
    ppermute x1, waiting for transfers between devices, line_sum(): lax.ppermute(kept, 'slab', [(i, i ^ bit) for i in range(devices)])  7.93 us
    ppermute x1, waiting for transfers between devices, line_sum(): kept = kept + lax.ppermute(sent, 'slab', pair)  5.16 us
    another operation x3, other arithmetic, shards(): jnp.stack([permit, contrast * normal_x * normal_x, contrast * normal_x *...  4.98 us
    ppermute x1, waiting for transfers between devices, line_sum(): back = lax.ppermute(kept, 'slab', pair)  4.69 us
    ppermute x1, starting transfers between devices, extended_2(): lax.ppermute(lax.slice_in_dim(block, 0, width, axis=dim), axis, backward)  4.27 us
    dot_general x1, matrix products, shards(): jnp.einsum('kxy,ycn->kxcn', fields, col_table, precision=lax.Precision.HIGH)  4.23 us
    div x3, other arithmetic, smooth_once(): (4.0 * middle + extended[:-2] + extended[2:] + jnp.roll(middle, 1, 1) + j...  3.89 us
  transfers between devices with their start and end apart: 7, of which 6 were waited for; matrix products, arithmetic and copies ran while one was open for 5% of the time, Pallas kernels for 0%

profile of v10, /device:TPU:0, one launch (start us, length us, event | category | flops | bytes accessed | tf_op | source)
XLA Modules:
  0.0 82.8 jit_solution(3175960681314106144)
XLA Ops:
  0.0 3.4 %fusion.42 = (f32[2048,1,104]{0,2,1:T(8,128)S(1)}, f32[2048,1,104]{0,2,1:T(8,128)S(1)}) fusion(s32[104]{0:T(128)S(1)} %iota_subtract_fusion.3), kind=kLoop, calls=%fused_computation.75 | loop fusion | flops 3194880 | bytes 1704352 | tf_op jit(solution)/shard_map/cos | solution.py:214
  3.4 2.3 %select_add_fusion = f32[256,2048]{1,0:T(8,128)S(1)} fusion(s32[256,2048]{1,0:T(8,128)} %param.2), kind=kLoop, calls=%fused_computation.45 | loop fusion | flops 5767168 | bytes 4194304 | tf_op jit(solution)/shard_map/add | solution.py:39
  5.8 1.3 %pad_maximum_fusion.5 = f32[2048,2,104]{0,2,1:T(8,128)} fusion(f32[2048,1,104]{0,2,1:T(8,128)S(1)} %get-tuple-element.38, f32[2048,1,104]{0,2,1:T(8,128)S(1)} %get-tuple-element.37), kind=kLoop, calls=%fused_computation.46 | loop fusion | flops 425984 | bytes 3407872 | tf_op jit(solution)/shard_map/stack | solution.py:214
  7.1 0.5 collective-permute-start
  7.6 4.3 %collective-permute-start.1 = (f32[4,2048]{1,0:T(4,128)S(1)}, f32[4,2048]{1,0:T(4,128)S(1)}, u32[]{:S(2)}, u32[]{:S(2)}) collective-permute-start(f32[4,2048]{1,0:T(4,128)S(1)} %get-tuple-element.28), channel_id=1, source_target_pairs={{1,0},{2,1},{3,2},{4,3},{5,4},{6,5},{7,6},{0,7},{9,8},{10,9},{11,1... | collective-permute-start | bytes 98312 | tf_op jit(solution)/shard_map/ppermute | solution.py:31
  11.9 0.9 %fusion.53 = (f32[1,208,256]{2,1,0:T(8,128)S(1)}, f32[1,208,256]{2,1,0:T(8,128)S(1)}) fusion(s32[256]{0:T(256)S(1)} %iota_add_fusion, s32[208]{0:T(256)S(1)} %iota_subtract_fusion.2), kind=kLoop, calls=%fused_computation.100 | loop fusion | flops 745472 | bytes 427840 | tf_op jit(solution)/shard_map/cos | solution.py:70
  12.8 0.4 collective-permute-done
  13.2 0.2 collective-permute-done.1
  13.5 0.3 pad_maximum_fusion.4
  13.8 0.9 %fusion.84 = (f32[262,2047]{1,0:T(8,128)S(1)}, f32[262,2047]{1,0:T(8,128)S(1)}) fusion(f32[264,2048]{1,0:T(8,128)S(1)} %pad_maximum_fusion.4), kind=kLoop, calls=%fused_computation.155 | loop fusion | bytes 8581024 | tf_op jit(solution)/shard_map/jit(_roll_static)/slice | solution.py:52
  14.7 2.1 %fusion.15 = f32[262,2048]{1,0:T(8,128)S(1)} fusion(f32[4,2048]{1,0:T(4,128)S(1)} %collective-permute-done.1, f32[256,2048]{1,0:T(8,128)S(1)} %select_add_fusion, f32[4,2048]{1,0:T(4,128)S(1)} %collective-permute-done, f32[264,2048]{1,0:T(8,128)S(1)} %pad_maximum_fusion.4, f32[262,2047]{1,0:T(8,128)S(1)} %get-tuple-element.26, ...), kind=kLoop, calls=%fused_computation.25 | loop fusion | flops 6438912 | bytes 15038416 | tf_op jit(solution)/shard_map/div | solution.py:47
  16.8 0.9 %fusion.82 = (f32[260,2047]{1,0:T(8,128)S(1)}, f32[260,2047]{1,0:T(8,128)S(1)}) fusion(f32[262,2048]{1,0:T(8,128)S(1)} %fusion.15), kind=kLoop, calls=%fused_computation.153 | loop fusion | bytes 8515520 | tf_op jit(solution)/shard_map/jit(_roll_static)/slice | solution.py:52
  17.8 0.9 %fusion.12 = f32[260,2048]{1,0:T(8,128)S(1)} fusion(f32[262,2048]{1,0:T(8,128)S(1)} %fusion.15, f32[260,2047]{1,0:T(8,128)S(1)} %get-tuple-element.22, f32[260,1]{1,0:T(8,128)S(1)} %get-tuple-element.24, f32[260,1]{1,0:T(8,128)S(1)} %get-tuple-element.23, f32[260,2047]{1,0:T(8,128)S(1)} %get-tuple-element.21), kind=kLoop, calls=%fused_computation.19 | loop fusion | flops 4259840 | bytes 12779520 | tf_op jit(solution)/shard_map/div | solution.py:47
  18.7 0.9 %fusion.80 = (f32[258,2047]{1,0:T(8,128)S(1)}, f32[258,2047]{1,0:T(8,128)S(1)}) fusion(f32[260,2048]{1,0:T(8,128)S(1)} %fusion.12), kind=kLoop, calls=%fused_computation.151 | loop fusion | bytes 8450016 | tf_op jit(solution)/shard_map/jit(_roll_static)/slice | solution.py:52
  19.7 0.9 %fusion.9 = f32[258,2048]{1,0:T(8,128)S(1)} fusion(f32[260,2048]{1,0:T(8,128)S(1)} %fusion.12, f32[258,2047]{1,0:T(8,128)S(1)} %get-tuple-element.18, f32[258,1]{1,0:T(8,128)S(1)} %get-tuple-element.20, f32[258,1]{1,0:T(8,128)S(1)} %get-tuple-element.19, f32[258,2047]{1,0:T(8,128)S(1)} %get-tuple-element.17), kind=kLoop, calls=%fused_computation.13 | loop fusion | flops 4227072 | bytes 12681216 | tf_op jit(solution)/shard_map/div | solution.py:47
  20.5 1.1 %fusion.78 = (f32[256,2047]{1,0:T(8,128)S(1)}, f32[256,2047]{1,0:T(8,128)S(1)}) fusion(f32[258,2048]{1,0:T(8,128)S(1)} %fusion.9), kind=kLoop, calls=%fused_computation.149 | loop fusion | bytes 8384512 | tf_op jit(solution)/shard_map/jit(_roll_static)/slice | solution.py:59
  21.7 2.1 %multiply_bitcast_fusion.1 = (f32[1,256,2048]{2,1,0:T(8,128)S(1)}, f32[256,2048]{1,0:T(8,128)S(1)}) fusion(f32[256,2048]{1,0:T(8,128)S(1)} %select_add_fusion, f32[256,2047]{1,0:T(8,128)S(1)} %get-tuple-element.14, f32[256,1]{1,0:T(8,128)S(1)} %get-tuple-element.16, f32[256,1]{1,0:T(8,128)S(1)} %get-tuple-element.15, f32[256,2047]{1,0:T(8,128)S(1)} %get-tuple-element.13, ...), kind=kLoop, calls=%fused_computation.41 | loop fusion | flops 7864320 | bytes 14680064 | tf_op jit(solution)/shard_map/stack | solution.py:225
  23.9 2.3 %multiply_bitcast_fusion = (f32[1,256,2048]{2,1,0:T(8,128)S(1)}, f32[256,2048]{1,0:T(8,128)S(1)}) fusion(f32[256,2048]{1,0:T(8,128)S(1)} %get-tuple-element.10, f32[256,2048]{1,0:T(8,128)S(1)} %select_add_fusion, f32[258,2048]{1,0:T(8,128)S(1)} %fusion.9, f32[256,2047]{1,0:T(8,128)S(1)} %get-tuple-element.14, f32[256,1]{1,0:T(8,128)S(1)} %get-tuple-element.16, ...), kind=kLoop, calls=%fused_computation.40 | loop fusion | flops 7864320 | bytes 16777216 | tf_op jit(solution)/shard_map/stack | solution.py:225
  26.2 0.5 fusion.18
  26.7 0.9 %copy-done = f32[2048,2,104]{0,2,1:T(8,128)S(1)} copy-done((f32[2048,2,104]{0,2,1:T(8,128)S(1)}, f32[2048,2,104]{0,2,1:T(8,128)}, u32[]{:S(2)}) %copy-start) | copy-done | bytes 1703960
  27.7 4.2 %fusion.24 = f32[4,256,2,104,1]{1,3,4,2,0:T(8,128)S(1)} fusion(f32[2048,2,104]{0,2,1:T(8,128)S(1)} %copy-done, f32[1,256,2048]{2,1,0:T(8,128)S(1)} %fusion.18, f32[1,256,2048]{2,1,0:T(8,128)S(1)} %get-tuple-element.11, f32[1,256,2048]{2,1,0:T(8,128)S(1)} %get-tuple-element.9, f32[1,256,2048]{2,1,0:T(8,128)S(1)} %bitcast.55), kind=kOutput, calls=%fused_computation.51 | convolution fusion | flops 2623537152 | bytes 10944512 | tf_op jit(solution)/shard_map/kxy,ycn->kxcn/dot_general | solution.py:233
  31.9 0.9 %convolution_bitcast_fusion = f32[2,4,208,2,104]{2,4,0,3,1:T(8,128)S(1)} fusion(f32[4,256,2,104,1]{1,3,4,2,0:T(8,128)S(1)} %fusion.24, f32[1,208,256]{2,1,0:T(8,128)S(1)} %get-tuple-element.36, f32[1,208,256]{2,1,0:T(8,128)S(1)} %get-tuple-element.35), kind=kOutput, calls=%fused_computation.50 | convolution fusion | flops 531734528 | bytes 2662400 | tf_op jit(solution)/shard_map/smx,kxcn->skmcn/dot_general | solution.py:71
  32.8 0.1 broadcast_select_fusion
  32.9 0.2 copy.6
  33.1 0.4 select_n.204
  33.4 0.2 collective-permute-start.2
  33.6 0.2 copy.5
  33.8 0.4 select_n.202
  34.2 1.0 %collective-permute-done.2 = f32[676,128]{1,0:T(8,128)S(1)} collective-permute-done((f32[676,128]{1,0:T(8,128)S(1)}, f32[676,128]{1,0:T(8,128)S(1)}, u32[]{:S(2)}, u32[]{:S(2)}) %collective-permute-start.2) | collective-permute-done | bytes 346144 | tf_op jit(solution)/shard_map/ppermute | solution.py:165
  35.2 1.4 %collective-permute-start.3 = (f32[344,128]{1,0:T(8,128)S(1)}, f32[344,128]{1,0:T(8,128)S(1)}, u32[]{:S(2)}, u32[]{:S(2)}) collective-permute-start(f32[344,128]{1,0:T(8,128)S(1)} %slice_select_fusion), channel_id=1, source_target_pairs={{0,2},{1,3},{2,0},{3,1},{4,6},{5,7},{6,4},{7,5},{8,10},{9,11},{10,... | collective-permute-start | bytes 528392 | tf_op jit(solution)/shard_map/ppermute | solution.py:176
  36.7 5.2 %collective-permute-done.3 = f32[344,128]{1,0:T(8,128)S(1)} collective-permute-done((f32[344,128]{1,0:T(8,128)S(1)}, f32[344,128]{1,0:T(8,128)S(1)}, u32[]{:S(2)}, u32[]{:S(2)}) %collective-permute-start.3) | collective-permute-done | bytes 176160 | tf_op jit(solution)/shard_map/ppermute | solution.py:176
  41.8 2.7 %collective-permute-start.4 = (f32[344,128]{1,0:T(8,128)S(1)}, f32[344,128]{1,0:T(8,128)S(1)}, u32[]{:S(2)}, u32[]{:S(2)}) collective-permute-start(f32[344,128]{1,0:T(8,128)S(1)} %select_add_fusion.1), channel_id=1, source_target_pairs={{0,4},{1,5},{2,6},{3,7},{4,0},{5,1},{6,2},{7,3},{8,12},{9,13},{10,... | collective-permute-start | bytes 528392 | tf_op jit(solution)/shard_map/ppermute | solution.py:179
  44.5 7.9 %collective-permute-done.4 = f32[344,128]{1,0:T(8,128)S(1)} collective-permute-done((f32[344,128]{1,0:T(8,128)S(1)}, f32[344,128]{1,0:T(8,128)S(1)}, u32[]{:S(2)}, u32[]{:S(2)}) %collective-permute-start.4) | collective-permute-done | bytes 176160 | tf_op jit(solution)/shard_map/ppermute | solution.py:179
  52.5 0.8 collective-permute-start.5
  53.3 4.7 %collective-permute-done.5 = f32[344,128]{1,0:T(8,128)S(1)} collective-permute-done((f32[344,128]{1,0:T(8,128)S(1)}, f32[344,128]{1,0:T(8,128)S(1)}, u32[]{:S(2)}, u32[]{:S(2)}) %collective-permute-start.5) | collective-permute-done | bytes 176160 | tf_op jit(solution)/shard_map/ppermute | solution.py:181
  58.1 0.5 and_select_fusion.4
  58.7 0.6 broadcast_subtract_fusion
  59.3 0.6 pad_maximum_fusion.9.dval_ref
  59.9 0.4 stack_reshape.8
  60.3 0.2 copy.7
  60.5 0.4 stack_reshape.9
  60.9 0.2 copy.8
  61.1 0.7 fusion.34
  61.9 0.9 %fusion.36 = f32[2,4,208,256]{3,2,1,0:T(8,128)S(1)} fusion(f32[1,4,208,104]{2,3,1,0:T(8,128)S(1)} %copy.8, f32[1,4,208,104]{2,3,1,0:T(8,128)S(1)} %copy.7, pred[]{:T(512)S(6)} %eq.99, pred[256]{0:T(512)(128)(4,1)S(1)} %iota_compare_fusion.4), kind=kOutput, calls=%fused_computation.65 | convolution fusion | flops 532373504 | bytes 2396417 | tf_op jit(solution)/shard_map/skac,cb->skab/dot_general | solution.py:247
  62.8 0.8 multiply_add_fusion
  63.7 0.2 fusion.86
  63.8 1.4 %pad_maximum_fusion.6.fl_ref = f32[2,4,208,256]{3,2,1,0:T(8,128)} fusion(f32[2,1,208,256]{3,2,1,0:T(8,128)S(1)} %get-tuple-element.30, f32[2,1,208,256]{3,2,1,0:T(8,128)S(1)} %get-tuple-element.32, f32[2,1,208,256]{3,2,1,0:T(8,128)S(1)} %get-tuple-element.31, f32[2,1,208,256]{3,2,1,0:T(8,128)S(1)} %get-tuple-element.29), kind=kLoop, calls=%fused_computation.47 | loop fusion | flops 1277952 | bytes 3407872 | tf_op jit(solution)/shard_map/stack | solution.py:252
  65.2 17.6 %shard_map.28 = f32[2,64,20402]{2,1,0:T(8,128)} custom-call(s32[64]{0:T(128)} %get-tuple-element.44.a0_ref, s32[64]{0:T(128)} %get-tuple-element.43.b0_ref, s32[64]{0:T(128)} %get-tuple-element.40.first_ref, s32[64]{0:T(128)} %get-tuple-element.39.second_ref, f32[2,64]{1,0:T(2,128)} %pad_maximum_fusion.9.dval_ref, f32[2,4,208,256]{3,2,1,0:T(8,128)} %pad_maximum_fusion.6.fl_ref), custom_call_target="tpu_custom_call" | custom-call | tf_op jit(solution)/shard_map/pallas_call | solution.py:150
  (22 shorter events, 0.6 us)
Async XLA Ops:
  7.1 6.2 %collective-permute-start = (f32[4,2048]{1,0:T(4,128)S(1)}, f32[4,2048]{1,0:T(4,128)S(1)}, u32[]{:S(2)}, u32[]{:S(2)}) collective-permute-start(f32[4,2048]{1,0:T(4,128)S(1)} %get-tuple-element.27), channel_id=1, source_target_pairs={{0,1},{1,2},{2,3},{3,4},{4,5},{5,6},{6,7},{7,0},{8,9},{9,10},{10,1... | collective-permute-start | bytes 98312 | tf_op jit(solution)/shard_map/ppermute | solution.py:28
  7.6 5.9 %collective-permute-start.1 = (f32[4,2048]{1,0:T(4,128)S(1)}, f32[4,2048]{1,0:T(4,128)S(1)}, u32[]{:S(2)}, u32[]{:S(2)}) collective-permute-start(f32[4,2048]{1,0:T(4,128)S(1)} %get-tuple-element.28), channel_id=1, source_target_pairs={{1,0},{2,1},{3,2},{4,3},{5,4},{6,5},{7,6},{0,7},{9,8},{10,9},{11,1... | collective-permute-start | bytes 98312 | tf_op jit(solution)/shard_map/ppermute | solution.py:31
  26.2 1.5 %copy-start = (f32[2048,2,104]{0,2,1:T(8,128)S(1)}, f32[2048,2,104]{0,2,1:T(8,128)}, u32[]{:S(2)}) copy-start(f32[2048,2,104]{0,2,1:T(8,128)} %pad_maximum_fusion.5) | copy-start | bytes 5111812
  33.4 1.7 %collective-permute-start.2 = (f32[676,128]{1,0:T(8,128)S(1)}, f32[676,128]{1,0:T(8,128)S(1)}, u32[]{:S(2)}, u32[]{:S(2)}) collective-permute-start(f32[676,128]{1,0:T(8,128)S(1)} %select_n.204), channel_id=1, source_target_pairs={{0,1},{1,0},{2,3},{3,2},{4,5},{5,4},{6,7},{7,6},{8,9},{9,8},{10,11... | collective-permute-start | bytes 1038344 | tf_op jit(solution)/shard_map/ppermute | solution.py:165
  35.2 6.6 %collective-permute-start.3 = (f32[344,128]{1,0:T(8,128)S(1)}, f32[344,128]{1,0:T(8,128)S(1)}, u32[]{:S(2)}, u32[]{:S(2)}) collective-permute-start(f32[344,128]{1,0:T(8,128)S(1)} %slice_select_fusion), channel_id=1, source_target_pairs={{0,2},{1,3},{2,0},{3,1},{4,6},{5,7},{6,4},{7,5},{8,10},{9,11},{10,... | collective-permute-start | bytes 528392 | tf_op jit(solution)/shard_map/ppermute | solution.py:176
  41.8 10.6 %collective-permute-start.4 = (f32[344,128]{1,0:T(8,128)S(1)}, f32[344,128]{1,0:T(8,128)S(1)}, u32[]{:S(2)}, u32[]{:S(2)}) collective-permute-start(f32[344,128]{1,0:T(8,128)S(1)} %select_add_fusion.1), channel_id=1, source_target_pairs={{0,4},{1,5},{2,6},{3,7},{4,0},{5,1},{6,2},{7,3},{8,12},{9,13},{10,... | collective-permute-start | bytes 528392 | tf_op jit(solution)/shard_map/ppermute | solution.py:179
  52.5 5.5 %collective-permute-start.5 = (f32[344,128]{1,0:T(8,128)S(1)}, f32[344,128]{1,0:T(8,128)S(1)}, u32[]{:S(2)}, u32[]{:S(2)}) collective-permute-start(f32[344,128]{1,0:T(8,128)S(1)} %add.299), channel_id=1, source_target_pairs={{0,2},{1,3},{2,0},{3,1},{4,6},{5,7},{6,4},{7,5},{8,10},{9,11},{10,... | collective-permute-start | bytes 528392 | tf_op jit(solution)/shard_map/ppermute | solution.py:181
  58.0 2.5 %collective-permute-start.6 = (f32[676,128]{1,0:T(8,128)S(1)}, f32[676,128]{1,0:T(8,128)S(1)}, u32[]{:S(2)}, u32[]{:S(2)}) collective-permute-start(f32[676,128]{1,0:T(8,128)S(1)} %fusion.45), channel_id=1, source_target_pairs={{0,1},{1,0},{2,3},{3,2},{4,5},{5,4},{6,7},{7,6},{8,9},{9,8},{10,11... | collective-permute-start | bytes 1038344 | tf_op jit(solution)/shard_map/ppermute | solution.py:196
  61.1 1.7 %copy-start.1 = (f32[2]{0:T(128)S(1)}, f32[2]{0:T(128)}, u32[]{:S(2)}) copy-start(f32[2]{0:T(128)} %constant.148.clone) | copy-start | bytes 28

commit v11 on v10

--- a/solution.py
+++ b/solution.py
@@ -13,6 +13,8 @@
 KEEP = 201
 ORDERS = 10201
 BLOCK_ROWS = 8
+COPIES = 4
+COPY_STEP = 28
 LANES = 128
 
 
@@ -102,18 +104,17 @@
         b0 = b0_ref[row]
         first = first_ref[row]
         second = second_ref[row]
-        shift = (LANES - b0) % LANES
+        copy = jnp.minimum(b0 // COPY_STEP, COPIES - 1)
+        shift = (LANES - (b0 - COPY_STEP * copy)) % LANES
         base = pl.multiple_of(a0 // BLOCK_ROWS * BLOCK_ROWS, BLOCK_ROWS)
         off = a0 % BLOCK_ROWS
         dest = pl.multiple_of((BLOCK_ROWS - off) * BLOCK_ROWS, BLOCK_ROWS) + rr
         spot_tile = pl.multiple_of((first + BLOCK_ROWS) * BLOCK_ROWS, BLOCK_ROWS)
-        wrap = lane_iota + b0 < LANES
         spot = (sub == rr) & (lane == second)
         for h in range(2):
             combo = 2 * (rr % 2) + h
-            x_lo = fl_ref[0, combo, pl.ds(base, span), pl.ds(0, LANES)]
-            x_hi = fl_ref[0, combo, pl.ds(base, span), pl.ds(LANES, LANES)]
-            x = jnp.where(wrap, pltpu.roll(x_lo, shift, 1), pltpu.roll(x_hi, shift, 1))
+            x = fl_ref[0, copy, combo, pl.ds(base, span), :]
+            x = pltpu.roll(x, shift, 1)
             z_ref[h, pl.ds(dest, span, stride=BLOCK_ROWS), :] = x
             d = jnp.where(s == 0, dval_ref[h, row], jnp.float32(0.0))
             tile = z_ref[h, pl.ds(spot_tile, BLOCK_ROWS), :]
@@ -142,7 +143,7 @@
         grid=(2, n_blocks),
         in_specs=[
             pl.BlockSpec(memory_space=pltpu.SMEM),
-            pl.BlockSpec((1,) + tables.shape[1:], lambda s, rb, *_: (s, 0, 0, 0)),
+            pl.BlockSpec((1,) + tables.shape[1:], lambda s, rb, *_: (s, 0, 0, 0, 0)),
         ],
         out_specs=pl.BlockSpec((1, BLOCK_ROWS, total), lambda s, rb, *_: (s, rb, 0)),
         scratch_shapes=[pltpu.VMEM((2, (span + BLOCK_ROWS) * BLOCK_ROWS, LANES), jnp.float32)],
@@ -252,6 +253,9 @@
     tables = jnp.stack(
         [full[:, 2], full[:, 0] - full[:, 3], full[:, 1] - full[:, 0], -full[:, 2]], axis=1
     )
+    tables = jnp.stack(
+        [tables[..., COPY_STEP * c : COPY_STEP * c + LANES] for c in range(COPIES)], axis=1
+    )
     rows = ROWS_DEV
     spacing = ORDERS // (rows * devices // 2)
     window_rows = my_index * rows + jnp.arange(rows, dtype=jnp.int32)

time: 83.9 us -> 84.1 us (level)
  Pallas kernels: 17.6 us -> 16.3 us
    another operation x0 -> x1, other arithmetic: none -> 1.96 us  [shards(): jnp.stack([tables[..., COPY_STEP * c:COPY_STEP * c + LANES] for c in rang...]
    pallas_call x1, Pallas kernels: 17.6 us -> 16.3 us  [assemble(): pl.pallas_call(assemble_kernel, grid_spec=grid_spec, out_shape=jax.ShapeD...]
    another operation x1, other arithmetic: 1.39 us -> 0.15 us  [shards(): jnp.stack([full[:, 2], full[:, 0] - full[:, 3], full[:, 1] - full[:, 0],...]
where the time goes in v11:
time: 84.1 us; the launch traced here: 83 us
  other arithmetic  21.5 us (26%)
  waiting for transfers between devices  19.4 us (23%)
  Pallas kernels  16.3 us (19%)
  starting transfers between devices  9.98 us (12%)
  local copies, waits for them, and re-layouts  7.94 us (9%)
  matrix products  7.58 us (9%)
    pallas_call x1, Pallas kernels, assemble(): pl.pallas_call(assemble_kernel, grid_spec=grid_spec, out_shape=jax.ShapeD...  16.3 us
    ppermute x1, waiting for transfers between devices, line_sum(): lax.ppermute(kept, 'slab', [(i, i ^ bit) for i in range(devices)])  7.93 us
    ppermute x1, waiting for transfers between devices, line_sum(): kept = kept + lax.ppermute(sent, 'slab', pair)  5.16 us
    another operation x3, other arithmetic, shards(): jnp.stack([permit, contrast * normal_x * normal_x, contrast * normal_x *...  4.98 us
    ppermute x1, waiting for transfers between devices, line_sum(): back = lax.ppermute(kept, 'slab', pair)  4.69 us
    ppermute x1, starting transfers between devices, extended_2(): lax.ppermute(lax.slice_in_dim(block, 0, width, axis=dim), axis, backward)  4.27 us
    dot_general x1, matrix products, shards(): jnp.einsum('kxy,ycn->kxcn', fields, col_table, precision=lax.Precision.HIGH)  4.23 us
    div x3, other arithmetic, smooth_once(): (4.0 * middle + extended[:-2] + extended[2:] + jnp.roll(middle, 1, 1) + j...  3.89 us
  transfers between devices with their start and end apart: 7, of which 6 were waited for; matrix products, arithmetic and copies ran while one was open for 5% of the time, Pallas kernels for 0%

profile of v11, /device:TPU:0, one launch (start us, length us, event | category | flops | bytes accessed | tf_op | source)
XLA Modules:
  0.0 83.0 jit_solution(9359255752242138049)
XLA Ops:
  0.0 3.4 %fusion.42 = (f32[2048,1,104]{0,2,1:T(8,128)S(1)}, f32[2048,1,104]{0,2,1:T(8,128)S(1)}) fusion(s32[104]{0:T(128)S(1)} %iota_subtract_fusion.3), kind=kLoop, calls=%fused_computation.80 | loop fusion | flops 3194880 | bytes 1704352 | tf_op jit(solution)/shard_map/cos | solution.py:215
  3.4 2.3 %select_add_fusion = f32[256,2048]{1,0:T(8,128)S(1)} fusion(s32[256,2048]{1,0:T(8,128)} %param.2), kind=kLoop, calls=%fused_computation.46 | loop fusion | flops 5767168 | bytes 4194304 | tf_op jit(solution)/shard_map/add | solution.py:41
  5.8 1.3 %pad_maximum_fusion.6 = f32[2048,2,104]{0,2,1:T(8,128)} fusion(f32[2048,1,104]{0,2,1:T(8,128)S(1)} %get-tuple-element.42, f32[2048,1,104]{0,2,1:T(8,128)S(1)} %get-tuple-element.41), kind=kLoop, calls=%fused_computation.47 | loop fusion | flops 425984 | bytes 3407872 | tf_op jit(solution)/shard_map/stack | solution.py:215
  7.1 0.5 collective-permute-start
  7.6 4.3 %collective-permute-start.1 = (f32[4,2048]{1,0:T(4,128)S(1)}, f32[4,2048]{1,0:T(4,128)S(1)}, u32[]{:S(2)}, u32[]{:S(2)}) collective-permute-start(f32[4,2048]{1,0:T(4,128)S(1)} %get-tuple-element.28), channel_id=1, source_target_pairs={{1,0},{2,1},{3,2},{4,3},{5,4},{6,5},{7,6},{0,7},{9,8},{10,9},{11,1... | collective-permute-start | bytes 98312 | tf_op jit(solution)/shard_map/ppermute | solution.py:33
  11.9 0.9 %fusion.53 = (f32[1,208,256]{2,1,0:T(8,128)S(1)}, f32[1,208,256]{2,1,0:T(8,128)S(1)}) fusion(s32[256]{0:T(256)S(1)} %iota_add_fusion, s32[208]{0:T(256)S(1)} %iota_subtract_fusion.2), kind=kLoop, calls=%fused_computation.105 | loop fusion | flops 745472 | bytes 427840 | tf_op jit(solution)/shard_map/cos | solution.py:72
  12.8 0.4 collective-permute-done
  13.2 0.2 collective-permute-done.1
  13.5 0.3 pad_maximum_fusion.5
  13.8 0.9 %fusion.84 = (f32[262,2047]{1,0:T(8,128)S(1)}, f32[262,2047]{1,0:T(8,128)S(1)}) fusion(f32[264,2048]{1,0:T(8,128)S(1)} %pad_maximum_fusion.5), kind=kLoop, calls=%fused_computation.160 | loop fusion | bytes 8581024 | tf_op jit(solution)/shard_map/jit(_roll_static)/slice | solution.py:54
  14.7 2.1 %fusion.15 = f32[262,2048]{1,0:T(8,128)S(1)} fusion(f32[4,2048]{1,0:T(4,128)S(1)} %collective-permute-done.1, f32[256,2048]{1,0:T(8,128)S(1)} %select_add_fusion, f32[4,2048]{1,0:T(4,128)S(1)} %collective-permute-done, f32[264,2048]{1,0:T(8,128)S(1)} %pad_maximum_fusion.5, f32[262,2047]{1,0:T(8,128)S(1)} %get-tuple-element.26, ...), kind=kLoop, calls=%fused_computation.26 | loop fusion | flops 6438912 | bytes 15038416 | tf_op jit(solution)/shard_map/div | solution.py:49
  16.8 0.9 %fusion.82 = (f32[260,2047]{1,0:T(8,128)S(1)}, f32[260,2047]{1,0:T(8,128)S(1)}) fusion(f32[262,2048]{1,0:T(8,128)S(1)} %fusion.15), kind=kLoop, calls=%fused_computation.158 | loop fusion | bytes 8515520 | tf_op jit(solution)/shard_map/jit(_roll_static)/slice | solution.py:54
  17.8 0.9 %fusion.12 = f32[260,2048]{1,0:T(8,128)S(1)} fusion(f32[262,2048]{1,0:T(8,128)S(1)} %fusion.15, f32[260,2047]{1,0:T(8,128)S(1)} %get-tuple-element.22, f32[260,1]{1,0:T(8,128)S(1)} %get-tuple-element.24, f32[260,1]{1,0:T(8,128)S(1)} %get-tuple-element.23, f32[260,2047]{1,0:T(8,128)S(1)} %get-tuple-element.21), kind=kLoop, calls=%fused_computation.20 | loop fusion | flops 4259840 | bytes 12779520 | tf_op jit(solution)/shard_map/div | solution.py:49
  18.7 0.9 %fusion.80 = (f32[258,2047]{1,0:T(8,128)S(1)}, f32[258,2047]{1,0:T(8,128)S(1)}) fusion(f32[260,2048]{1,0:T(8,128)S(1)} %fusion.12), kind=kLoop, calls=%fused_computation.156 | loop fusion | bytes 8450016 | tf_op jit(solution)/shard_map/jit(_roll_static)/slice | solution.py:54
  19.7 0.9 %fusion.9 = f32[258,2048]{1,0:T(8,128)S(1)} fusion(f32[260,2048]{1,0:T(8,128)S(1)} %fusion.12, f32[258,2047]{1,0:T(8,128)S(1)} %get-tuple-element.18, f32[258,1]{1,0:T(8,128)S(1)} %get-tuple-element.20, f32[258,1]{1,0:T(8,128)S(1)} %get-tuple-element.19, f32[258,2047]{1,0:T(8,128)S(1)} %get-tuple-element.17), kind=kLoop, calls=%fused_computation.14 | loop fusion | flops 4227072 | bytes 12681216 | tf_op jit(solution)/shard_map/div | solution.py:49
  20.5 1.1 %fusion.78 = (f32[256,2047]{1,0:T(8,128)S(1)}, f32[256,2047]{1,0:T(8,128)S(1)}) fusion(f32[258,2048]{1,0:T(8,128)S(1)} %fusion.9), kind=kLoop, calls=%fused_computation.154 | loop fusion | bytes 8384512 | tf_op jit(solution)/shard_map/jit(_roll_static)/slice | solution.py:61
  21.7 2.1 %multiply_bitcast_fusion.1 = (f32[1,256,2048]{2,1,0:T(8,128)S(1)}, f32[256,2048]{1,0:T(8,128)S(1)}) fusion(f32[256,2048]{1,0:T(8,128)S(1)} %select_add_fusion, f32[256,2047]{1,0:T(8,128)S(1)} %get-tuple-element.14, f32[256,1]{1,0:T(8,128)S(1)} %get-tuple-element.16, f32[256,1]{1,0:T(8,128)S(1)} %get-tuple-element.15, f32[256,2047]{1,0:T(8,128)S(1)} %get-tuple-element.13, ...), kind=kLoop, calls=%fused_computation.42 | loop fusion | flops 7864320 | bytes 14680064 | tf_op jit(solution)/shard_map/stack | solution.py:226
  23.9 2.3 %multiply_bitcast_fusion = (f32[1,256,2048]{2,1,0:T(8,128)S(1)}, f32[256,2048]{1,0:T(8,128)S(1)}) fusion(f32[256,2048]{1,0:T(8,128)S(1)} %get-tuple-element.10, f32[256,2048]{1,0:T(8,128)S(1)} %select_add_fusion, f32[258,2048]{1,0:T(8,128)S(1)} %fusion.9, f32[256,2047]{1,0:T(8,128)S(1)} %get-tuple-element.14, f32[256,1]{1,0:T(8,128)S(1)} %get-tuple-element.16, ...), kind=kLoop, calls=%fused_computation.41 | loop fusion | flops 7864320 | bytes 16777216 | tf_op jit(solution)/shard_map/stack | solution.py:226
  26.2 0.5 fusion.18
  26.7 0.9 %copy-done = f32[2048,2,104]{0,2,1:T(8,128)S(1)} copy-done((f32[2048,2,104]{0,2,1:T(8,128)S(1)}, f32[2048,2,104]{0,2,1:T(8,128)}, u32[]{:S(2)}) %copy-start) | copy-done | bytes 1703960
  27.7 4.2 %fusion.24 = f32[4,256,2,104,1]{1,3,4,2,0:T(8,128)S(1)} fusion(f32[2048,2,104]{0,2,1:T(8,128)S(1)} %copy-done, f32[1,256,2048]{2,1,0:T(8,128)S(1)} %fusion.18, f32[1,256,2048]{2,1,0:T(8,128)S(1)} %get-tuple-element.11, f32[1,256,2048]{2,1,0:T(8,128)S(1)} %get-tuple-element.9, f32[1,256,2048]{2,1,0:T(8,128)S(1)} %bitcast.69), kind=kOutput, calls=%fused_computation.52 | convolution fusion | flops 2623537152 | bytes 10944512 | tf_op jit(solution)/shard_map/kxy,ycn->kxcn/dot_general | solution.py:234
  31.9 0.9 %convolution_bitcast_fusion = f32[2,4,208,2,104]{2,4,0,3,1:T(8,128)S(1)} fusion(f32[4,256,2,104,1]{1,3,4,2,0:T(8,128)S(1)} %fusion.24, f32[1,208,256]{2,1,0:T(8,128)S(1)} %get-tuple-element.40, f32[1,208,256]{2,1,0:T(8,128)S(1)} %get-tuple-element.39), kind=kOutput, calls=%fused_computation.51 | convolution fusion | flops 531734528 | bytes 2662400 | tf_op jit(solution)/shard_map/smx,kxcn->skmcn/dot_general | solution.py:73
  32.9 0.2 copy.12
  33.1 0.4 select_n.204
  33.4 0.2 collective-permute-start.2
  33.6 0.2 copy.11
  33.8 0.4 select_n.202
  34.2 1.0 %collective-permute-done.2 = f32[676,128]{1,0:T(8,128)S(1)} collective-permute-done((f32[676,128]{1,0:T(8,128)S(1)}, f32[676,128]{1,0:T(8,128)S(1)}, u32[]{:S(2)}, u32[]{:S(2)}) %collective-permute-start.2) | collective-permute-done | bytes 346144 | tf_op jit(solution)/shard_map/ppermute | solution.py:166
  35.2 1.4 %collective-permute-start.3 = (f32[344,128]{1,0:T(8,128)S(1)}, f32[344,128]{1,0:T(8,128)S(1)}, u32[]{:S(2)}, u32[]{:S(2)}) collective-permute-start(f32[344,128]{1,0:T(8,128)S(1)} %slice_select_fusion), channel_id=1, source_target_pairs={{0,2},{1,3},{2,0},{3,1},{4,6},{5,7},{6,4},{7,5},{8,10},{9,11},{10,... | collective-permute-start | bytes 528392 | tf_op jit(solution)/shard_map/ppermute | solution.py:177
  36.7 5.2 %collective-permute-done.3 = f32[344,128]{1,0:T(8,128)S(1)} collective-permute-done((f32[344,128]{1,0:T(8,128)S(1)}, f32[344,128]{1,0:T(8,128)S(1)}, u32[]{:S(2)}, u32[]{:S(2)}) %collective-permute-start.3) | collective-permute-done | bytes 176160 | tf_op jit(solution)/shard_map/ppermute | solution.py:177
  41.8 2.7 %collective-permute-start.4 = (f32[344,128]{1,0:T(8,128)S(1)}, f32[344,128]{1,0:T(8,128)S(1)}, u32[]{:S(2)}, u32[]{:S(2)}) collective-permute-start(f32[344,128]{1,0:T(8,128)S(1)} %select_add_fusion.1), channel_id=1, source_target_pairs={{0,4},{1,5},{2,6},{3,7},{4,0},{5,1},{6,2},{7,3},{8,12},{9,13},{10,... | collective-permute-start | bytes 528392 | tf_op jit(solution)/shard_map/ppermute | solution.py:180
  44.5 7.9 %collective-permute-done.4 = f32[344,128]{1,0:T(8,128)S(1)} collective-permute-done((f32[344,128]{1,0:T(8,128)S(1)}, f32[344,128]{1,0:T(8,128)S(1)}, u32[]{:S(2)}, u32[]{:S(2)}) %collective-permute-start.4) | collective-permute-done | bytes 176160 | tf_op jit(solution)/shard_map/ppermute | solution.py:180
  52.5 0.8 collective-permute-start.5
  53.3 4.7 %collective-permute-done.5 = f32[344,128]{1,0:T(8,128)S(1)} collective-permute-done((f32[344,128]{1,0:T(8,128)S(1)}, f32[344,128]{1,0:T(8,128)S(1)}, u32[]{:S(2)}, u32[]{:S(2)}) %collective-permute-start.5) | collective-permute-done | bytes 176160 | tf_op jit(solution)/shard_map/ppermute | solution.py:182
  58.1 0.6 and_select_fusion.4
  58.7 0.6 broadcast_subtract_fusion
  59.3 0.6 pad_maximum_fusion.10.dval_ref
  59.9 0.4 stack_reshape.8
  60.3 0.2 copy.13
  60.5 0.4 stack_reshape.9
  60.9 0.2 copy.14
  61.2 0.7 fusion.34
  61.9 0.9 %fusion.36 = f32[2,4,208,256]{3,2,1,0:T(8,128)S(1)} fusion(f32[1,4,208,104]{2,3,1,0:T(8,128)S(1)} %copy.14, f32[1,4,208,104]{2,3,1,0:T(8,128)S(1)} %copy.13, pred[]{:T(512)S(6)} %eq.99, pred[256]{0:T(512)(128)(4,1)S(1)} %iota_compare_fusion.4), kind=kOutput, calls=%fused_computation.70 | convolution fusion | flops 532373504 | bytes 2396417 | tf_op jit(solution)/shard_map/skac,cb->skab/dot_general | solution.py:248
  62.8 0.8 multiply_add_fusion
  63.7 0.2 fusion.86
  64.0 0.7 slice_bitcast_fusion.3
  64.7 2.0 %pad_maximum_fusion.fl_ref = f32[2,4,4,208,128]{4,3,2,1,0:T(8,128)} fusion(f32[2,1,4,208,128]{4,3,2,1,0:T(8,128)S(1)} %get-tuple-element.30, f32[2,1,4,208,128]{4,3,2,1,0:T(8,128)S(1)} %get-tuple-element.31, f32[2,1,4,208,128]{4,3,2,1,0:T(8,128)S(1)} %get-tuple-element.32, f32[2,1,4,208,128]{4,3,2,1,0:T(8,128)S(1)} %get-tuple-element.29), kind=kLoop, calls=%fused_computation.8 | loop fusion | flops 2555904 | bytes 6815744 | tf_op jit(solution)/shard_map/stack | solution.py:256
  66.7 16.3 %shard_map.28 = f32[2,64,20402]{2,1,0:T(8,128)} custom-call(s32[64]{0:T(128)} %get-tuple-element.48.a0_ref, s32[64]{0:T(128)} %get-tuple-element.47.b0_ref, s32[64]{0:T(128)} %get-tuple-element.44.first_ref, s32[64]{0:T(128)} %get-tuple-element.43.second_ref, f32[2,64]{1,0:T(2,128)} %pad_maximum_fusion.10.dval_ref, f32[2,4,4,208,128]{4,3,2,1,0:T(8,128)} %pad_maximum_fusion.fl_ref), custom_call_target="tpu_custom_call" | custom-call | tf_op jit(solution)/shard_map/pallas_call | solution.py:151
  (24 shorter events, 0.9 us)
Async XLA Ops:
  7.1 6.2 %collective-permute-start = (f32[4,2048]{1,0:T(4,128)S(1)}, f32[4,2048]{1,0:T(4,128)S(1)}, u32[]{:S(2)}, u32[]{:S(2)}) collective-permute-start(f32[4,2048]{1,0:T(4,128)S(1)} %get-tuple-element.27), channel_id=1, source_target_pairs={{0,1},{1,2},{2,3},{3,4},{4,5},{5,6},{6,7},{7,0},{8,9},{9,10},{10,1... | collective-permute-start | bytes 98312 | tf_op jit(solution)/shard_map/ppermute | solution.py:30
  7.6 5.9 %collective-permute-start.1 = (f32[4,2048]{1,0:T(4,128)S(1)}, f32[4,2048]{1,0:T(4,128)S(1)}, u32[]{:S(2)}, u32[]{:S(2)}) collective-permute-start(f32[4,2048]{1,0:T(4,128)S(1)} %get-tuple-element.28), channel_id=1, source_target_pairs={{1,0},{2,1},{3,2},{4,3},{5,4},{6,5},{7,6},{0,7},{9,8},{10,9},{11,1... | collective-permute-start | bytes 98312 | tf_op jit(solution)/shard_map/ppermute | solution.py:33
  26.2 1.5 %copy-start = (f32[2048,2,104]{0,2,1:T(8,128)S(1)}, f32[2048,2,104]{0,2,1:T(8,128)}, u32[]{:S(2)}) copy-start(f32[2048,2,104]{0,2,1:T(8,128)} %pad_maximum_fusion.6) | copy-start | bytes 5111812
  33.4 1.7 %collective-permute-start.2 = (f32[676,128]{1,0:T(8,128)S(1)}, f32[676,128]{1,0:T(8,128)S(1)}, u32[]{:S(2)}, u32[]{:S(2)}) collective-permute-start(f32[676,128]{1,0:T(8,128)S(1)} %select_n.204), channel_id=1, source_target_pairs={{0,1},{1,0},{2,3},{3,2},{4,5},{5,4},{6,7},{7,6},{8,9},{9,8},{10,11... | collective-permute-start | bytes 1038344 | tf_op jit(solution)/shard_map/ppermute | solution.py:166
  35.2 6.6 %collective-permute-start.3 = (f32[344,128]{1,0:T(8,128)S(1)}, f32[344,128]{1,0:T(8,128)S(1)}, u32[]{:S(2)}, u32[]{:S(2)}) collective-permute-start(f32[344,128]{1,0:T(8,128)S(1)} %slice_select_fusion), channel_id=1, source_target_pairs={{0,2},{1,3},{2,0},{3,1},{4,6},{5,7},{6,4},{7,5},{8,10},{9,11},{10,... | collective-permute-start | bytes 528392 | tf_op jit(solution)/shard_map/ppermute | solution.py:177
  41.8 10.6 %collective-permute-start.4 = (f32[344,128]{1,0:T(8,128)S(1)}, f32[344,128]{1,0:T(8,128)S(1)}, u32[]{:S(2)}, u32[]{:S(2)}) collective-permute-start(f32[344,128]{1,0:T(8,128)S(1)} %select_add_fusion.1), channel_id=1, source_target_pairs={{0,4},{1,5},{2,6},{3,7},{4,0},{5,1},{6,2},{7,3},{8,12},{9,13},{10,... | collective-permute-start | bytes 528392 | tf_op jit(solution)/shard_map/ppermute | solution.py:180
  52.5 5.5 %collective-permute-start.5 = (f32[344,128]{1,0:T(8,128)S(1)}, f32[344,128]{1,0:T(8,128)S(1)}, u32[]{:S(2)}, u32[]{:S(2)}) collective-permute-start(f32[344,128]{1,0:T(8,128)S(1)} %add.299), channel_id=1, source_target_pairs={{0,2},{1,3},{2,0},{3,1},{4,6},{5,7},{6,4},{7,5},{8,10},{9,11},{10,... | collective-permute-start | bytes 528392 | tf_op jit(solution)/shard_map/ppermute | solution.py:182
  58.0 2.5 %collective-permute-start.6 = (f32[676,128]{1,0:T(8,128)S(1)}, f32[676,128]{1,0:T(8,128)S(1)}, u32[]{:S(2)}, u32[]{:S(2)}) collective-permute-start(f32[676,128]{1,0:T(8,128)S(1)} %fusion.45), channel_id=1, source_target_pairs={{0,1},{1,0},{2,3},{3,2},{4,5},{5,4},{6,7},{7,6},{8,9},{9,8},{10,11... | collective-permute-start | bytes 1038344 | tf_op jit(solution)/shard_map/ppermute | solution.py:197
  61.1 1.7 %copy-start.1 = (f32[2]{0:T(128)S(1)}, f32[2]{0:T(128)}, u32[]{:S(2)}) copy-start(f32[2]{0:T(128)} %constant.148.clone) | copy-start | bytes 28

commit v12 on v11

--- a/solution.py
+++ b/solution.py
@@ -91,13 +91,14 @@
     return chunks
 
 
-def assemble_kernel(a0_ref, b0_ref, first_ref, second_ref, dval_ref, fl_ref, o_ref, z_ref):
+def assemble_kernel(a0_ref, b0_ref, first_ref, second_ref, dval_ref, fl_ref, o_ref, z_ref, zt_ref, sems):
     s = pl.program_id(0)
     rb = pl.program_id(1)
-    span = z_ref.shape[1] // BLOCK_ROWS - BLOCK_ROWS
-    lane_iota = lax.broadcasted_iota(jnp.int32, (span, LANES), 1)
+    span = zt_ref.shape[1]
     sub = lax.broadcasted_iota(jnp.int32, (BLOCK_ROWS, LANES), 0)
     lane = lax.broadcasted_iota(jnp.int32, (BLOCK_ROWS, LANES), 1)
+    copies = []
+    spots = []
     for rr in range(BLOCK_ROWS):
         row = rb * BLOCK_ROWS + rr
         a0 = a0_ref[row]
@@ -108,23 +109,29 @@
         shift = (LANES - (b0 - COPY_STEP * copy)) % LANES
         base = pl.multiple_of(a0 // BLOCK_ROWS * BLOCK_ROWS, BLOCK_ROWS)
         off = a0 % BLOCK_ROWS
-        dest = pl.multiple_of((BLOCK_ROWS - off) * BLOCK_ROWS, BLOCK_ROWS) + rr
-        spot_tile = pl.multiple_of((first + BLOCK_ROWS) * BLOCK_ROWS, BLOCK_ROWS)
-        spot = (sub == rr) & (lane == second)
         for h in range(2):
             combo = 2 * (rr % 2) + h
+            slot = 2 * rr + h
             x = fl_ref[0, copy, combo, pl.ds(base, span), :]
-            x = pltpu.roll(x, shift, 1)
-            z_ref[h, pl.ds(dest, span, stride=BLOCK_ROWS), :] = x
+            zt_ref[slot] = pltpu.roll(x, shift, 1)
+            move = pltpu.make_async_copy(
+                zt_ref.at[slot], z_ref.at[h, pl.ds(BLOCK_ROWS - off, span), rr], sems.at[slot]
+            )
+            move.start()
+            copies.append(move)
             d = jnp.where(s == 0, dval_ref[h, row], jnp.float32(0.0))
-            tile = z_ref[h, pl.ds(spot_tile, BLOCK_ROWS), :]
-            z_ref[h, pl.ds(spot_tile, BLOCK_ROWS), :] = tile + jnp.where(spot, d, jnp.float32(0.0))
+            spots.append((h, rr, first + BLOCK_ROWS, second, d))
+    for move in copies:
+        move.wait()
+    for h, rr, tile_index, second, d in spots:
+        spot = (sub == rr) & (lane == second)
+        z_ref[h, tile_index] = z_ref[h, tile_index] + jnp.where(spot, d, jnp.float32(0.0))
     placed = {}
     for start, width, runs in chunk_segments(o_ref.shape[2], o_ref.shape[2] // 2):
         acc = None
         for h, u, l0, v0 in runs:
             if (h, u) not in placed:
-                src = z_ref[h, pl.ds((u + BLOCK_ROWS) * BLOCK_ROWS, BLOCK_ROWS), :]
+                src = z_ref[h, u + BLOCK_ROWS]
                 sh = (l0 - v0) % LANES
                 placed[(h, u)] = pltpu.roll(src, sh, 1) if sh else src
             src = placed[(h, u)]
@@ -146,7 +153,11 @@
             pl.BlockSpec((1,) + tables.shape[1:], lambda s, rb, *_: (s, 0, 0, 0, 0)),
         ],
         out_specs=pl.BlockSpec((1, BLOCK_ROWS, total), lambda s, rb, *_: (s, rb, 0)),
-        scratch_shapes=[pltpu.VMEM((2, (span + BLOCK_ROWS) * BLOCK_ROWS, LANES), jnp.float32)],
+        scratch_shapes=[
+            pltpu.VMEM((2, span + BLOCK_ROWS, BLOCK_ROWS, LANES), jnp.float32),
+            pltpu.VMEM((2 * BLOCK_ROWS, span, LANES), jnp.float32),
+            pltpu.SemaphoreType.DMA((2 * BLOCK_ROWS,)),
+        ],
     )
     return pl.pallas_call(
         assemble_kernel,

time: 84.1 us -> 108 us (1.28)
  Pallas kernels: 16.3 us -> 40.8 us
    pallas_call x1, Pallas kernels: 16.3 us -> 40.8 us  [assemble(): pl.pallas_call(assemble_kernel, grid_spec=grid_spec, out_shape=jax.ShapeD...]
  transfers between devices with their start and end apart: 7 -> 7, of which waited for: 6 -> 6; matrix products, arithmetic and copies ran while one was open for 5% -> 4% of each run, Pallas kernels for 0% -> 0%
where the time goes in v12:
time: 108 us
  Pallas kernels  40.8 us (38%)
  other arithmetic  21.5 us (20%)
  waiting for transfers between devices  19.4 us (18%)
  starting transfers between devices  9.98 us (9%)
  local copies, waits for them, and re-layouts  7.94 us (7%)
  matrix products  7.58 us (7%)
    pallas_call x1, Pallas kernels, assemble(): pl.pallas_call(assemble_kernel, grid_spec=grid_spec, out_shape=jax.ShapeD...  40.8 us
    ppermute x1, waiting for transfers between devices, line_sum(): lax.ppermute(kept, 'slab', [(i, i ^ bit) for i in range(devices)])  7.93 us
    ppermute x1, waiting for transfers between devices, line_sum(): kept = kept + lax.ppermute(sent, 'slab', pair)  5.16 us
    another operation x3, other arithmetic, shards(): jnp.stack([permit, contrast * normal_x * normal_x, contrast * normal_x *...  4.98 us
    ppermute x1, waiting for transfers between devices, line_sum(): back = lax.ppermute(kept, 'slab', pair)  4.69 us
    ppermute x1, starting transfers between devices, extended_2(): lax.ppermute(lax.slice_in_dim(block, 0, width, axis=dim), axis, backward)  4.27 us
    dot_general x1, matrix products, shards(): jnp.einsum('kxy,ycn->kxcn', fields, col_table, precision=lax.Precision.HIGH)  4.23 us
    div x3, other arithmetic, smooth_once(): (4.0 * middle + extended[:-2] + extended[2:] + jnp.roll(middle, 1, 1) + j...  3.89 us
  transfers between devices with their start and end apart: 7, of which 6 were waited for; matrix products, arithmetic and copies ran while one was open for 4% of the time, Pallas kernels for 0%

profile of v12, /device:TPU:0, one launch (start us, length us, event | category | flops | bytes accessed | tf_op | source)
XLA Modules:
  0.0 107.7 jit_solution(17749008303522615051)
XLA Ops:
  0.0 3.4 %fusion.42 = (f32[2048,1,104]{0,2,1:T(8,128)S(1)}, f32[2048,1,104]{0,2,1:T(8,128)S(1)}) fusion(s32[104]{0:T(128)S(1)} %iota_subtract_fusion.3), kind=kLoop, calls=%fused_computation.80 | loop fusion | flops 3194880 | bytes 1704352 | tf_op jit(solution)/shard_map/cos | solution.py:226
  3.4 2.3 %select_add_fusion = f32[256,2048]{1,0:T(8,128)S(1)} fusion(s32[256,2048]{1,0:T(8,128)} %param.2), kind=kLoop, calls=%fused_computation.46 | loop fusion | flops 5767168 | bytes 4194304 | tf_op jit(solution)/shard_map/add | solution.py:41
  5.8 1.3 %pad_maximum_fusion.6 = f32[2048,2,104]{0,2,1:T(8,128)} fusion(f32[2048,1,104]{0,2,1:T(8,128)S(1)} %get-tuple-element.42, f32[2048,1,104]{0,2,1:T(8,128)S(1)} %get-tuple-element.41), kind=kLoop, calls=%fused_computation.47 | loop fusion | flops 425984 | bytes 3407872 | tf_op jit(solution)/shard_map/stack | solution.py:226
  7.1 0.5 collective-permute-start
  7.6 4.3 %collective-permute-start.1 = (f32[4,2048]{1,0:T(4,128)S(1)}, f32[4,2048]{1,0:T(4,128)S(1)}, u32[]{:S(2)}, u32[]{:S(2)}) collective-permute-start(f32[4,2048]{1,0:T(4,128)S(1)} %get-tuple-element.28), channel_id=1, source_target_pairs={{1,0},{2,1},{3,2},{4,3},{5,4},{6,5},{7,6},{0,7},{9,8},{10,9},{11,1... | collective-permute-start | bytes 98312 | tf_op jit(solution)/shard_map/ppermute | solution.py:33
  11.9 0.9 fusion.53
  12.8 0.4 collective-permute-done
  13.2 0.2 collective-permute-done.1
  13.5 0.3 pad_maximum_fusion.5
  13.8 0.9 fusion.84
  14.7 2.1 %fusion.15 = f32[262,2048]{1,0:T(8,128)S(1)} fusion(f32[4,2048]{1,0:T(4,128)S(1)} %collective-permute-done.1, f32[256,2048]{1,0:T(8,128)S(1)} %select_add_fusion, f32[4,2048]{1,0:T(4,128)S(1)} %collective-permute-done, f32[264,2048]{1,0:T(8,128)S(1)} %pad_maximum_fusion.5, f32[262,2047]{1,0:T(8,128)S(1)} %get-tuple-element.26, ...), kind=kLoop, calls=%fused_computation.26 | loop fusion | flops 6438912 | bytes 15038416 | tf_op jit(solution)/shard_map/div | solution.py:49
  16.8 0.9 fusion.82
  17.8 0.9 fusion.12
  18.7 0.9 fusion.80
  19.7 0.9 fusion.9
  20.5 1.1 fusion.78
  21.7 2.1 %multiply_bitcast_fusion.1 = (f32[1,256,2048]{2,1,0:T(8,128)S(1)}, f32[256,2048]{1,0:T(8,128)S(1)}) fusion(f32[256,2048]{1,0:T(8,128)S(1)} %select_add_fusion, f32[256,2047]{1,0:T(8,128)S(1)} %get-tuple-element.14, f32[256,1]{1,0:T(8,128)S(1)} %get-tuple-element.16, f32[256,1]{1,0:T(8,128)S(1)} %get-tuple-element.15, f32[256,2047]{1,0:T(8,128)S(1)} %get-tuple-element.13, ...), kind=kLoop, calls=%fused_computation.42 | loop fusion | flops 7864320 | bytes 14680064 | tf_op jit(solution)/shard_map/stack | solution.py:237
  23.9 2.3 %multiply_bitcast_fusion = (f32[1,256,2048]{2,1,0:T(8,128)S(1)}, f32[256,2048]{1,0:T(8,128)S(1)}) fusion(f32[256,2048]{1,0:T(8,128)S(1)} %get-tuple-element.10, f32[256,2048]{1,0:T(8,128)S(1)} %select_add_fusion, f32[258,2048]{1,0:T(8,128)S(1)} %fusion.9, f32[256,2047]{1,0:T(8,128)S(1)} %get-tuple-element.14, f32[256,1]{1,0:T(8,128)S(1)} %get-tuple-element.16, ...), kind=kLoop, calls=%fused_computation.41 | loop fusion | flops 7864320 | bytes 16777216 | tf_op jit(solution)/shard_map/stack | solution.py:237
  26.2 0.5 fusion.18
  26.7 0.9 copy-done
  27.7 4.2 %fusion.24 = f32[4,256,2,104,1]{1,3,4,2,0:T(8,128)S(1)} fusion(f32[2048,2,104]{0,2,1:T(8,128)S(1)} %copy-done, f32[1,256,2048]{2,1,0:T(8,128)S(1)} %fusion.18, f32[1,256,2048]{2,1,0:T(8,128)S(1)} %get-tuple-element.11, f32[1,256,2048]{2,1,0:T(8,128)S(1)} %get-tuple-element.9, f32[1,256,2048]{2,1,0:T(8,128)S(1)} %bitcast.69), kind=kOutput, calls=%fused_computation.52 | convolution fusion | flops 2623537152 | bytes 10944512 | tf_op jit(solution)/shard_map/kxy,ycn->kxcn/dot_general | solution.py:245
  31.9 0.9 convolution_bitcast_fusion
  32.9 0.2 copy.12
  33.1 0.4 select_n.204
  33.4 0.2 collective-permute-start.2
  33.6 0.2 copy.11
  33.8 0.4 select_n.202
  34.2 1.0 collective-permute-done.2
  35.2 1.4 %collective-permute-start.3 = (f32[344,128]{1,0:T(8,128)S(1)}, f32[344,128]{1,0:T(8,128)S(1)}, u32[]{:S(2)}, u32[]{:S(2)}) collective-permute-start(f32[344,128]{1,0:T(8,128)S(1)} %slice_select_fusion), channel_id=1, source_target_pairs={{0,2},{1,3},{2,0},{3,1},{4,6},{5,7},{6,4},{7,5},{8,10},{9,11},{10,... | collective-permute-start | bytes 528392 | tf_op jit(solution)/shard_map/ppermute | solution.py:188
  36.7 5.2 %collective-permute-done.3 = f32[344,128]{1,0:T(8,128)S(1)} collective-permute-done((f32[344,128]{1,0:T(8,128)S(1)}, f32[344,128]{1,0:T(8,128)S(1)}, u32[]{:S(2)}, u32[]{:S(2)}) %collective-permute-start.3) | collective-permute-done | bytes 176160 | tf_op jit(solution)/shard_map/ppermute | solution.py:188
  41.8 2.7 %collective-permute-start.4 = (f32[344,128]{1,0:T(8,128)S(1)}, f32[344,128]{1,0:T(8,128)S(1)}, u32[]{:S(2)}, u32[]{:S(2)}) collective-permute-start(f32[344,128]{1,0:T(8,128)S(1)} %select_add_fusion.1), channel_id=1, source_target_pairs={{0,4},{1,5},{2,6},{3,7},{4,0},{5,1},{6,2},{7,3},{8,12},{9,13},{10,... | collective-permute-start | bytes 528392 | tf_op jit(solution)/shard_map/ppermute | solution.py:191
  44.5 7.9 %collective-permute-done.4 = f32[344,128]{1,0:T(8,128)S(1)} collective-permute-done((f32[344,128]{1,0:T(8,128)S(1)}, f32[344,128]{1,0:T(8,128)S(1)}, u32[]{:S(2)}, u32[]{:S(2)}) %collective-permute-start.4) | collective-permute-done | bytes 176160 | tf_op jit(solution)/shard_map/ppermute | solution.py:191
  52.5 0.8 collective-permute-start.5
  53.3 4.7 %collective-permute-done.5 = f32[344,128]{1,0:T(8,128)S(1)} collective-permute-done((f32[344,128]{1,0:T(8,128)S(1)}, f32[344,128]{1,0:T(8,128)S(1)}, u32[]{:S(2)}, u32[]{:S(2)}) %collective-permute-start.5) | collective-permute-done | bytes 176160 | tf_op jit(solution)/shard_map/ppermute | solution.py:193
  58.1 0.6 and_select_fusion.4
  58.7 0.6 broadcast_subtract_fusion
  59.3 0.6 pad_maximum_fusion.10.dval_ref
  59.9 0.4 stack_reshape.8
  60.3 0.2 copy.13
  60.5 0.4 stack_reshape.9
  60.9 0.2 copy.14
  61.2 0.7 fusion.34
  61.9 0.9 fusion.36
  62.8 0.8 multiply_add_fusion
  63.7 0.2 fusion.86
  64.0 0.7 slice_bitcast_fusion.3
  64.7 2.0 %pad_maximum_fusion.fl_ref = f32[2,4,4,208,128]{4,3,2,1,0:T(8,128)} fusion(f32[2,1,4,208,128]{4,3,2,1,0:T(8,128)S(1)} %get-tuple-element.30, f32[2,1,4,208,128]{4,3,2,1,0:T(8,128)S(1)} %get-tuple-element.31, f32[2,1,4,208,128]{4,3,2,1,0:T(8,128)S(1)} %get-tuple-element.32, f32[2,1,4,208,128]{4,3,2,1,0:T(8,128)S(1)} %get-tuple-element.29), kind=kLoop, calls=%fused_computation.8 | loop fusion | flops 2555904 | bytes 6815744 | tf_op jit(solution)/shard_map/stack | solution.py:267
  66.7 40.8 %shard_map.28 = f32[2,64,20402]{2,1,0:T(8,128)} custom-call(s32[64]{0:T(128)} %get-tuple-element.48.a0_ref, s32[64]{0:T(128)} %get-tuple-element.47.b0_ref, s32[64]{0:T(128)} %get-tuple-element.44.first_ref, s32[64]{0:T(128)} %get-tuple-element.43.second_ref, f32[2,64]{1,0:T(2,128)} %pad_maximum_fusion.10.dval_ref, f32[2,4,4,208,128]{4,3,2,1,0:T(8,128)} %pad_maximum_fusion.fl_ref), custom_call_target="tpu_custom_call" | custom-call | tf_op jit(solution)/shard_map/pallas_call | solution.py:162
  (24 shorter events, 0.9 us)
Async XLA Ops:
  7.1 6.2 %collective-permute-start = (f32[4,2048]{1,0:T(4,128)S(1)}, f32[4,2048]{1,0:T(4,128)S(1)}, u32[]{:S(2)}, u32[]{:S(2)}) collective-permute-start(f32[4,2048]{1,0:T(4,128)S(1)} %get-tuple-element.27), channel_id=1, source_target_pairs={{0,1},{1,2},{2,3},{3,4},{4,5},{5,6},{6,7},{7,0},{8,9},{9,10},{10,1... | collective-permute-start | bytes 98312 | tf_op jit(solution)/shard_map/ppermute | solution.py:30
  7.6 5.9 %collective-permute-start.1 = (f32[4,2048]{1,0:T(4,128)S(1)}, f32[4,2048]{1,0:T(4,128)S(1)}, u32[]{:S(2)}, u32[]{:S(2)}) collective-permute-start(f32[4,2048]{1,0:T(4,128)S(1)} %get-tuple-element.28), channel_id=1, source_target_pairs={{1,0},{2,1},{3,2},{4,3},{5,4},{6,5},{7,6},{0,7},{9,8},{10,9},{11,1... | collective-permute-start | bytes 98312 | tf_op jit(solution)/shard_map/ppermute | solution.py:33
  26.2 1.5 %copy-start = (f32[2048,2,104]{0,2,1:T(8,128)S(1)}, f32[2048,2,104]{0,2,1:T(8,128)}, u32[]{:S(2)}) copy-start(f32[2048,2,104]{0,2,1:T(8,128)} %pad_maximum_fusion.6) | copy-start | bytes 5111812
  33.4 1.7 %collective-permute-start.2 = (f32[676,128]{1,0:T(8,128)S(1)}, f32[676,128]{1,0:T(8,128)S(1)}, u32[]{:S(2)}, u32[]{:S(2)}) collective-permute-start(f32[676,128]{1,0:T(8,128)S(1)} %select_n.204), channel_id=1, source_target_pairs={{0,1},{1,0},{2,3},{3,2},{4,5},{5,4},{6,7},{7,6},{8,9},{9,8},{10,11... | collective-permute-start | bytes 1038344 | tf_op jit(solution)/shard_map/ppermute | solution.py:177
  35.2 6.6 %collective-permute-start.3 = (f32[344,128]{1,0:T(8,128)S(1)}, f32[344,128]{1,0:T(8,128)S(1)}, u32[]{:S(2)}, u32[]{:S(2)}) collective-permute-start(f32[344,128]{1,0:T(8,128)S(1)} %slice_select_fusion), channel_id=1, source_target_pairs={{0,2},{1,3},{2,0},{3,1},{4,6},{5,7},{6,4},{7,5},{8,10},{9,11},{10,... | collective-permute-start | bytes 528392 | tf_op jit(solution)/shard_map/ppermute | solution.py:188
  41.8 10.6 %collective-permute-start.4 = (f32[344,128]{1,0:T(8,128)S(1)}, f32[344,128]{1,0:T(8,128)S(1)}, u32[]{:S(2)}, u32[]{:S(2)}) collective-permute-start(f32[344,128]{1,0:T(8,128)S(1)} %select_add_fusion.1), channel_id=1, source_target_pairs={{0,4},{1,5},{2,6},{3,7},{4,0},{5,1},{6,2},{7,3},{8,12},{9,13},{10,... | collective-permute-start | bytes 528392 | tf_op jit(solution)/shard_map/ppermute | solution.py:191
  52.5 5.5 %collective-permute-start.5 = (f32[344,128]{1,0:T(8,128)S(1)}, f32[344,128]{1,0:T(8,128)S(1)}, u32[]{:S(2)}, u32[]{:S(2)}) collective-permute-start(f32[344,128]{1,0:T(8,128)S(1)} %add.299), channel_id=1, source_target_pairs={{0,2},{1,3},{2,0},{3,1},{4,6},{5,7},{6,4},{7,5},{8,10},{9,11},{10,... | collective-permute-start | bytes 528392 | tf_op jit(solution)/shard_map/ppermute | solution.py:193
  58.0 2.5 %collective-permute-start.6 = (f32[676,128]{1,0:T(8,128)S(1)}, f32[676,128]{1,0:T(8,128)S(1)}, u32[]{:S(2)}, u32[]{:S(2)}) collective-permute-start(f32[676,128]{1,0:T(8,128)S(1)} %fusion.45), channel_id=1, source_target_pairs={{0,1},{1,0},{2,3},{3,2},{4,5},{5,4},{6,7},{7,6},{8,9},{9,8},{10,11... | collective-permute-start | bytes 1038344 | tf_op jit(solution)/shard_map/ppermute | solution.py:208
  61.1 1.7 %copy-start.1 = (f32[2]{0:T(128)S(1)}, f32[2]{0:T(128)}, u32[]{:S(2)}) copy-start(f32[2]{0:T(128)} %constant.148.clone) | copy-start | bytes 28

commit v13 on v11

--- a/solution.py
+++ b/solution.py
@@ -91,19 +91,29 @@
     return chunks
 
 
-def assemble_kernel(a0_ref, b0_ref, first_ref, second_ref, dval_ref, fl_ref, o_ref, z_ref):
+def assemble_kernel(index_ref, fl_ref, o_ref, z_ref):
     s = pl.program_id(0)
     rb = pl.program_id(1)
+    rows = o_ref.shape[1] * pl.num_programs(1)
+    spacing = ORDERS // (rows * index_ref[1] // 2)
+    centre = (HARM - 1) // 2
     span = z_ref.shape[1] // BLOCK_ROWS - BLOCK_ROWS
     lane_iota = lax.broadcasted_iota(jnp.int32, (span, LANES), 1)
     sub = lax.broadcasted_iota(jnp.int32, (BLOCK_ROWS, LANES), 0)
     lane = lax.broadcasted_iota(jnp.int32, (BLOCK_ROWS, LANES), 1)
     for rr in range(BLOCK_ROWS):
         row = rb * BLOCK_ROWS + rr
-        a0 = a0_ref[row]
-        b0 = b0_ref[row]
-        first = first_ref[row]
-        second = second_ref[row]
+        order_index = (index_ref[0] * rows + row) // 2 * spacing
+        first = order_index // HARM
+        second = order_index % HARM
+        a0 = (HARM - 1) - first
+        b0 = (HARM - 1) - second
+        kx = 0.3 + 0.02 * (first - centre).astype(jnp.float32)
+        ky = 0.2 + 0.02 * (second - centre).astype(jnp.float32)
+        if rr % 2:
+            diagonal = (ky * ky, -(kx * ky))
+        else:
+            diagonal = (kx * ky, -(kx * kx))
         copy = jnp.minimum(b0 // COPY_STEP, COPIES - 1)
         shift = (LANES - (b0 - COPY_STEP * copy)) % LANES
         base = pl.multiple_of(a0 // BLOCK_ROWS * BLOCK_ROWS, BLOCK_ROWS)
@@ -116,7 +126,7 @@
             x = fl_ref[0, copy, combo, pl.ds(base, span), :]
             x = pltpu.roll(x, shift, 1)
             z_ref[h, pl.ds(dest, span, stride=BLOCK_ROWS), :] = x
-            d = jnp.where(s == 0, dval_ref[h, row], jnp.float32(0.0))
+            d = jnp.where(s == 0, diagonal[h], jnp.float32(0.0))
             tile = z_ref[h, pl.ds(spot_tile, BLOCK_ROWS), :]
             z_ref[h, pl.ds(spot_tile, BLOCK_ROWS), :] = tile + jnp.where(spot, d, jnp.float32(0.0))
     placed = {}
@@ -134,15 +144,14 @@
         o_ref[0, :, pl.ds(start, width)] = acc
 
 
-def assemble(a0, b0, first, second, dvals, tables, rows):
+def assemble(index, tables, rows):
     span = 112
     n_blocks = rows // BLOCK_ROWS
     total = 2 * ORDERS
     grid_spec = pltpu.PrefetchScalarGridSpec(
-        num_scalar_prefetch=4,
+        num_scalar_prefetch=1,
         grid=(2, n_blocks),
         in_specs=[
-            pl.BlockSpec(memory_space=pltpu.SMEM),
             pl.BlockSpec((1,) + tables.shape[1:], lambda s, rb, *_: (s, 0, 0, 0, 0)),
         ],
         out_specs=pl.BlockSpec((1, BLOCK_ROWS, total), lambda s, rb, *_: (s, rb, 0)),
@@ -153,7 +162,7 @@
         grid_spec=grid_spec,
         out_shape=jax.ShapeDtypeStruct((2, rows, total), jnp.float32),
         compiler_params=pltpu.CompilerParams(dimension_semantics=("arbitrary", "arbitrary")),
-    )(a0, b0, first, second, dvals, tables)
+    )(index, tables)
 
 
 def line_sum(partial_value, my_index, devices):
@@ -256,22 +265,8 @@
     tables = jnp.stack(
         [tables[..., COPY_STEP * c : COPY_STEP * c + LANES] for c in range(COPIES)], axis=1
     )
-    rows = ROWS_DEV
-    spacing = ORDERS // (rows * devices // 2)
-    window_rows = my_index * rows + jnp.arange(rows, dtype=jnp.int32)
-    order_index = window_rows // 2 * spacing
-    first = order_index // HARM
-    second = order_index % HARM
-    centre = (HARM - 1) // 2
-    kx = 0.3 + 0.02 * (first - centre).astype(jnp.float32)
-    ky = 0.2 + 0.02 * (second - centre).astype(jnp.float32)
-    lower = window_rows % 2 == 1
-    left = jnp.where(lower, ky * ky, kx * ky)
-    right = jnp.where(lower, -(kx * ky), -(kx * kx))
-    dvals = jnp.stack([left, right])
-    a0 = (HARM - 1) - first
-    b0 = (HARM - 1) - second
-    return assemble(a0, b0, first, second, dvals, tables, rows)
+    index = jnp.stack([my_index, devices]).astype(jnp.int32)
+    return assemble(index, tables, ROWS_DEV)
 
 
 def solution(mesh):

time: 84.1 us -> 82.4 us (0.980)
  other arithmetic: 21.5 us -> 20.3 us
  transfers between devices with their start and end apart: 7 -> 7, of which waited for: 6 -> 7; matrix products, arithmetic and copies ran while one was open for 5% -> 3% of each run, Pallas kernels for 0% -> 0%
where the time goes in v13:
time: 82.4 us; the launch traced here: 81.7 us
  other arithmetic  20.3 us (25%)
  waiting for transfers between devices  19.8 us (24%)
  Pallas kernels  15.8 us (19%)
  starting transfers between devices  9.98 us (12%)
  local copies, waits for them, and re-layouts  7.94 us (10%)
  matrix products  7.58 us (9%)
    pallas_call x1, Pallas kernels, assemble(): pl.pallas_call(assemble_kernel, grid_spec=grid_spec, out_shape=jax.ShapeD...  15.8 us
    ppermute x1, waiting for transfers between devices, line_sum(): lax.ppermute(kept, 'slab', [(i, i ^ bit) for i in range(devices)])  7.94 us
    ppermute x1, waiting for transfers between devices, line_sum(): kept = kept + lax.ppermute(sent, 'slab', pair)  5.16 us
    another operation x3, other arithmetic, shards(): jnp.stack([permit, contrast * normal_x * normal_x, contrast * normal_x *...  4.98 us
    ppermute x1, waiting for transfers between devices, line_sum(): back = lax.ppermute(kept, 'slab', pair)  4.72 us
    ppermute x1, starting transfers between devices, extended_2(): lax.ppermute(lax.slice_in_dim(block, 0, width, axis=dim), axis, backward)  4.27 us
    dot_general x1, matrix products, shards(): jnp.einsum('kxy,ycn->kxcn', fields, col_table, precision=lax.Precision.HIGH)  4.23 us
    div x3, other arithmetic, smooth_once(): (4.0 * middle + extended[:-2] + extended[2:] + jnp.roll(middle, 1, 1) + j...  3.89 us
  transfers between devices with their start and end apart: 7, of which 7 were waited for; matrix products, arithmetic and copies ran while one was open for 3% of the time, Pallas kernels for 0%

profile of v13, /device:TPU:0, one launch (start us, length us, event | category | flops | bytes accessed | tf_op | source)
XLA Modules:
  0.0 81.7 jit_solution(13028917925261635462)
XLA Ops:
  0.0 3.4 %fusion.42 = (f32[2048,1,104]{0,2,1:T(8,128)S(1)}, f32[2048,1,104]{0,2,1:T(8,128)S(1)}) fusion(s32[104]{0:T(128)S(1)} %iota_subtract_fusion.3), kind=kLoop, calls=%fused_computation.80 | loop fusion | flops 3194880 | bytes 1704352 | tf_op jit(solution)/shard_map/cos | solution.py:224
  3.4 2.3 %select_add_fusion = f32[256,2048]{1,0:T(8,128)S(1)} fusion(s32[256,2048]{1,0:T(8,128)} %param.2), kind=kLoop, calls=%fused_computation.46 | loop fusion | flops 5767168 | bytes 4194304 | tf_op jit(solution)/shard_map/add | solution.py:41
  5.8 1.3 %pad_maximum_fusion.6 = f32[2048,2,104]{0,2,1:T(8,128)} fusion(f32[2048,1,104]{0,2,1:T(8,128)S(1)} %get-tuple-element.42, f32[2048,1,104]{0,2,1:T(8,128)S(1)} %get-tuple-element.41), kind=kLoop, calls=%fused_computation.47 | loop fusion | flops 425984 | bytes 3407872 | tf_op jit(solution)/shard_map/stack | solution.py:224
  7.1 0.5 collective-permute-start
  7.6 4.3 %collective-permute-start.1 = (f32[4,2048]{1,0:T(4,128)S(1)}, f32[4,2048]{1,0:T(4,128)S(1)}, u32[]{:S(2)}, u32[]{:S(2)}) collective-permute-start(f32[4,2048]{1,0:T(4,128)S(1)} %get-tuple-element.28), channel_id=1, source_target_pairs={{1,0},{2,1},{3,2},{4,3},{5,4},{6,5},{7,6},{0,7},{9,8},{10,9},{11,1... | collective-permute-start | bytes 98312 | tf_op jit(solution)/shard_map/ppermute | solution.py:33
  11.9 0.9 %fusion.53 = (f32[1,208,256]{2,1,0:T(8,128)S(1)}, f32[1,208,256]{2,1,0:T(8,128)S(1)}) fusion(s32[256]{0:T(256)S(1)} %iota_add_fusion, s32[208]{0:T(256)S(1)} %iota_subtract_fusion.2), kind=kLoop, calls=%fused_computation.105 | loop fusion | flops 745472 | bytes 427840 | tf_op jit(solution)/shard_map/cos | solution.py:72
  12.8 0.4 collective-permute-done
  13.2 0.2 collective-permute-done.1
  13.5 0.3 pad_maximum_fusion.5
  13.8 0.9 %fusion.77 = (f32[262,2047]{1,0:T(8,128)S(1)}, f32[262,2047]{1,0:T(8,128)S(1)}) fusion(f32[264,2048]{1,0:T(8,128)S(1)} %pad_maximum_fusion.5), kind=kLoop, calls=%fused_computation.134 | loop fusion | bytes 8581024 | tf_op jit(solution)/shard_map/jit(_roll_static)/slice | solution.py:54
  14.7 2.1 %fusion.15 = f32[262,2048]{1,0:T(8,128)S(1)} fusion(f32[4,2048]{1,0:T(4,128)S(1)} %collective-permute-done.1, f32[256,2048]{1,0:T(8,128)S(1)} %select_add_fusion, f32[4,2048]{1,0:T(4,128)S(1)} %collective-permute-done, f32[264,2048]{1,0:T(8,128)S(1)} %pad_maximum_fusion.5, f32[262,2047]{1,0:T(8,128)S(1)} %get-tuple-element.26, ...), kind=kLoop, calls=%fused_computation.26 | loop fusion | flops 6438912 | bytes 15038416 | tf_op jit(solution)/shard_map/div | solution.py:49
  16.8 0.9 %fusion.75 = (f32[260,2047]{1,0:T(8,128)S(1)}, f32[260,2047]{1,0:T(8,128)S(1)}) fusion(f32[262,2048]{1,0:T(8,128)S(1)} %fusion.15), kind=kLoop, calls=%fused_computation.132 | loop fusion | bytes 8515520 | tf_op jit(solution)/shard_map/jit(_roll_static)/slice | solution.py:54
  17.8 0.9 %fusion.12 = f32[260,2048]{1,0:T(8,128)S(1)} fusion(f32[262,2048]{1,0:T(8,128)S(1)} %fusion.15, f32[260,2047]{1,0:T(8,128)S(1)} %get-tuple-element.22, f32[260,1]{1,0:T(8,128)S(1)} %get-tuple-element.24, f32[260,1]{1,0:T(8,128)S(1)} %get-tuple-element.23, f32[260,2047]{1,0:T(8,128)S(1)} %get-tuple-element.21), kind=kLoop, calls=%fused_computation.20 | loop fusion | flops 4259840 | bytes 12779520 | tf_op jit(solution)/shard_map/div | solution.py:49
  18.7 0.9 %fusion.73 = (f32[258,2047]{1,0:T(8,128)S(1)}, f32[258,2047]{1,0:T(8,128)S(1)}) fusion(f32[260,2048]{1,0:T(8,128)S(1)} %fusion.12), kind=kLoop, calls=%fused_computation.130 | loop fusion | bytes 8450016 | tf_op jit(solution)/shard_map/jit(_roll_static)/slice | solution.py:54
  19.7 0.9 %fusion.9 = f32[258,2048]{1,0:T(8,128)S(1)} fusion(f32[260,2048]{1,0:T(8,128)S(1)} %fusion.12, f32[258,2047]{1,0:T(8,128)S(1)} %get-tuple-element.18, f32[258,1]{1,0:T(8,128)S(1)} %get-tuple-element.20, f32[258,1]{1,0:T(8,128)S(1)} %get-tuple-element.19, f32[258,2047]{1,0:T(8,128)S(1)} %get-tuple-element.17), kind=kLoop, calls=%fused_computation.14 | loop fusion | flops 4227072 | bytes 12681216 | tf_op jit(solution)/shard_map/div | solution.py:49
  20.5 1.1 %fusion.71 = (f32[256,2047]{1,0:T(8,128)S(1)}, f32[256,2047]{1,0:T(8,128)S(1)}) fusion(f32[258,2048]{1,0:T(8,128)S(1)} %fusion.9), kind=kLoop, calls=%fused_computation.128 | loop fusion | bytes 8384512 | tf_op jit(solution)/shard_map/jit(_roll_static)/slice | solution.py:61
  21.7 2.1 %multiply_bitcast_fusion.1 = (f32[1,256,2048]{2,1,0:T(8,128)S(1)}, f32[256,2048]{1,0:T(8,128)S(1)}) fusion(f32[256,2048]{1,0:T(8,128)S(1)} %select_add_fusion, f32[256,2047]{1,0:T(8,128)S(1)} %get-tuple-element.14, f32[256,1]{1,0:T(8,128)S(1)} %get-tuple-element.16, f32[256,1]{1,0:T(8,128)S(1)} %get-tuple-element.15, f32[256,2047]{1,0:T(8,128)S(1)} %get-tuple-element.13, ...), kind=kLoop, calls=%fused_computation.42 | loop fusion | flops 7864320 | bytes 14680064 | tf_op jit(solution)/shard_map/stack | solution.py:235
  23.9 2.3 %multiply_bitcast_fusion = (f32[1,256,2048]{2,1,0:T(8,128)S(1)}, f32[256,2048]{1,0:T(8,128)S(1)}) fusion(f32[256,2048]{1,0:T(8,128)S(1)} %get-tuple-element.10, f32[256,2048]{1,0:T(8,128)S(1)} %select_add_fusion, f32[258,2048]{1,0:T(8,128)S(1)} %fusion.9, f32[256,2047]{1,0:T(8,128)S(1)} %get-tuple-element.14, f32[256,1]{1,0:T(8,128)S(1)} %get-tuple-element.16, ...), kind=kLoop, calls=%fused_computation.41 | loop fusion | flops 7864320 | bytes 16777216 | tf_op jit(solution)/shard_map/stack | solution.py:235
  26.2 0.5 fusion.18
  26.7 0.9 %copy-done = f32[2048,2,104]{0,2,1:T(8,128)S(1)} copy-done((f32[2048,2,104]{0,2,1:T(8,128)S(1)}, f32[2048,2,104]{0,2,1:T(8,128)}, u32[]{:S(2)}) %copy-start) | copy-done | bytes 1703960
  27.7 4.2 %fusion.24 = f32[4,256,2,104,1]{1,3,4,2,0:T(8,128)S(1)} fusion(f32[2048,2,104]{0,2,1:T(8,128)S(1)} %copy-done, f32[1,256,2048]{2,1,0:T(8,128)S(1)} %fusion.18, f32[1,256,2048]{2,1,0:T(8,128)S(1)} %get-tuple-element.11, f32[1,256,2048]{2,1,0:T(8,128)S(1)} %get-tuple-element.9, f32[1,256,2048]{2,1,0:T(8,128)S(1)} %bitcast.70), kind=kOutput, calls=%fused_computation.52 | convolution fusion | flops 2623537152 | bytes 10944512 | tf_op jit(solution)/shard_map/kxy,ycn->kxcn/dot_general | solution.py:243
  31.9 0.9 %convolution_bitcast_fusion = f32[2,4,208,2,104]{2,4,0,3,1:T(8,128)S(1)} fusion(f32[4,256,2,104,1]{1,3,4,2,0:T(8,128)S(1)} %fusion.24, f32[1,208,256]{2,1,0:T(8,128)S(1)} %get-tuple-element.40, f32[1,208,256]{2,1,0:T(8,128)S(1)} %get-tuple-element.39), kind=kOutput, calls=%fused_computation.51 | convolution fusion | flops 531734528 | bytes 2662400 | tf_op jit(solution)/shard_map/smx,kxcn->skmcn/dot_general | solution.py:73
  32.9 0.2 copy.12
  33.1 0.4 select_n.128
  33.4 0.2 collective-permute-start.2
  33.6 0.2 copy.11
  33.8 0.4 select_n.126
  34.2 1.0 %collective-permute-done.2 = f32[676,128]{1,0:T(8,128)S(1)} collective-permute-done((f32[676,128]{1,0:T(8,128)S(1)}, f32[676,128]{1,0:T(8,128)S(1)}, u32[]{:S(2)}, u32[]{:S(2)}) %collective-permute-start.2) | collective-permute-done | bytes 346144 | tf_op jit(solution)/shard_map/ppermute | solution.py:175
  35.2 1.4 %collective-permute-start.3 = (f32[344,128]{1,0:T(8,128)S(1)}, f32[344,128]{1,0:T(8,128)S(1)}, u32[]{:S(2)}, u32[]{:S(2)}) collective-permute-start(f32[344,128]{1,0:T(8,128)S(1)} %slice_select_fusion), channel_id=1, source_target_pairs={{0,2},{1,3},{2,0},{3,1},{4,6},{5,7},{6,4},{7,5},{8,10},{9,11},{10,... | collective-permute-start | bytes 528392 | tf_op jit(solution)/shard_map/ppermute | solution.py:186
  36.7 5.2 %collective-permute-done.3 = f32[344,128]{1,0:T(8,128)S(1)} collective-permute-done((f32[344,128]{1,0:T(8,128)S(1)}, f32[344,128]{1,0:T(8,128)S(1)}, u32[]{:S(2)}, u32[]{:S(2)}) %collective-permute-start.3) | collective-permute-done | bytes 176160 | tf_op jit(solution)/shard_map/ppermute | solution.py:186
  41.9 2.7 %collective-permute-start.4 = (f32[344,128]{1,0:T(8,128)S(1)}, f32[344,128]{1,0:T(8,128)S(1)}, u32[]{:S(2)}, u32[]{:S(2)}) collective-permute-start(f32[344,128]{1,0:T(8,128)S(1)} %select_add_fusion.1), channel_id=1, source_target_pairs={{0,4},{1,5},{2,6},{3,7},{4,0},{5,1},{6,2},{7,3},{8,12},{9,13},{10,... | collective-permute-start | bytes 528392 | tf_op jit(solution)/shard_map/ppermute | solution.py:189
  44.5 7.9 %collective-permute-done.4 = f32[344,128]{1,0:T(8,128)S(1)} collective-permute-done((f32[344,128]{1,0:T(8,128)S(1)}, f32[344,128]{1,0:T(8,128)S(1)}, u32[]{:S(2)}, u32[]{:S(2)}) %collective-permute-start.4) | collective-permute-done | bytes 176160 | tf_op jit(solution)/shard_map/ppermute | solution.py:189
  52.5 0.8 collective-permute-start.5
  53.3 4.7 %collective-permute-done.5 = f32[344,128]{1,0:T(8,128)S(1)} collective-permute-done((f32[344,128]{1,0:T(8,128)S(1)}, f32[344,128]{1,0:T(8,128)S(1)}, u32[]{:S(2)}, u32[]{:S(2)}) %collective-permute-start.5) | collective-permute-done | bytes 176160 | tf_op jit(solution)/shard_map/ppermute | solution.py:191
  58.1 0.6 pad_add_fusion.index_ref
  58.8 0.4 stack_reshape.8
  59.2 0.2 copy.13
  59.4 0.4 collective-permute-done.6
  59.8 0.4 stack_reshape.9
  60.2 0.2 copy.14
  60.4 0.7 fusion.34
  61.2 0.9 %fusion.36 = f32[2,4,208,256]{3,2,1,0:T(8,128)S(1)} fusion(f32[1,4,208,104]{2,3,1,0:T(8,128)S(1)} %copy.14, f32[1,4,208,104]{2,3,1,0:T(8,128)S(1)} %copy.13, pred[]{:T(512)S(6)} %eq.80, pred[256]{0:T(512)(128)(4,1)S(1)} %iota_compare_fusion.4), kind=kOutput, calls=%fused_computation.70 | convolution fusion | flops 532373504 | bytes 2396417 | tf_op jit(solution)/shard_map/skac,cb->skab/dot_general | solution.py:257
  62.1 0.8 %multiply_add_fusion = f32[2,4,208,256]{3,2,1,0:T(8,128)S(1)} fusion(f32[2,4,208,256]{3,2,1,0:T(8,128)S(1)} %fusion.36, f32[2,4,104,208]{2,3,1,0:T(8,128)S(1)} %fusion.34, f32[2]{0:T(128)S(1)} %copy-done.1, s32[256]{0:T(256)S(1)} %iota_subtract_fusion, pred[256]{0:T(512)(128)(4,1)S(1)} %iota_compare_fusion.3), kind=kOutput, calls=%fused_computation.50 | convolution fusion | flops 532533248 | bytes 4101384 | tf_op jit(solution)/shard_map/ad,skdc,cb->skab/dot_general | solution.py:258
  62.9 0.2 fusion.79
  63.1 0.2 pad_maximum_fusion.7
  63.3 0.7 slice_bitcast_fusion.3
  64.0 1.9 %pad_maximum_fusion.fl_ref = f32[2,4,4,208,128]{4,3,2,1,0:T(8,128)} fusion(f32[2,1,4,208,128]{4,3,2,1,0:T(8,128)S(1)} %get-tuple-element.30, f32[2,1,4,208,128]{4,3,2,1,0:T(8,128)S(1)} %get-tuple-element.31, f32[2,1,4,208,128]{4,3,2,1,0:T(8,128)S(1)} %get-tuple-element.32, f32[2,1,4,208,128]{4,3,2,1,0:T(8,128)S(1)} %get-tuple-element.29), kind=kLoop, calls=%fused_computation.8 | loop fusion | flops 2555904 | bytes 6815744 | tf_op jit(solution)/shard_map/stack | solution.py:265
  65.9 15.8 %shard_map.28 = f32[2,64,20402]{2,1,0:T(8,128)} custom-call(s32[2]{0:T(128)} %pad_add_fusion.index_ref, f32[2,4,4,208,128]{4,3,2,1,0:T(8,128)} %pad_maximum_fusion.fl_ref), custom_call_target="tpu_custom_call" | custom-call | tf_op jit(solution)/shard_map/pallas_call | solution.py:160
  (21 shorter events, 0.7 us)
Async XLA Ops:
  7.1 6.2 %collective-permute-start = (f32[4,2048]{1,0:T(4,128)S(1)}, f32[4,2048]{1,0:T(4,128)S(1)}, u32[]{:S(2)}, u32[]{:S(2)}) collective-permute-start(f32[4,2048]{1,0:T(4,128)S(1)} %get-tuple-element.27), channel_id=1, source_target_pairs={{0,1},{1,2},{2,3},{3,4},{4,5},{5,6},{6,7},{7,0},{8,9},{9,10},{10,1... | collective-permute-start | bytes 98312 | tf_op jit(solution)/shard_map/ppermute | solution.py:30
  7.6 5.9 %collective-permute-start.1 = (f32[4,2048]{1,0:T(4,128)S(1)}, f32[4,2048]{1,0:T(4,128)S(1)}, u32[]{:S(2)}, u32[]{:S(2)}) collective-permute-start(f32[4,2048]{1,0:T(4,128)S(1)} %get-tuple-element.28), channel_id=1, source_target_pairs={{1,0},{2,1},{3,2},{4,3},{5,4},{6,5},{7,6},{0,7},{9,8},{10,9},{11,1... | collective-permute-start | bytes 98312 | tf_op jit(solution)/shard_map/ppermute | solution.py:33
  26.2 1.5 %copy-start = (f32[2048,2,104]{0,2,1:T(8,128)S(1)}, f32[2048,2,104]{0,2,1:T(8,128)}, u32[]{:S(2)}) copy-start(f32[2048,2,104]{0,2,1:T(8,128)} %pad_maximum_fusion.6) | copy-start | bytes 5111812
  33.4 1.7 %collective-permute-start.2 = (f32[676,128]{1,0:T(8,128)S(1)}, f32[676,128]{1,0:T(8,128)S(1)}, u32[]{:S(2)}, u32[]{:S(2)}) collective-permute-start(f32[676,128]{1,0:T(8,128)S(1)} %select_n.128), channel_id=1, source_target_pairs={{0,1},{1,0},{2,3},{3,2},{4,5},{5,4},{6,7},{7,6},{8,9},{9,8},{10,11... | collective-permute-start | bytes 1038344 | tf_op jit(solution)/shard_map/ppermute | solution.py:175
  35.2 6.6 %collective-permute-start.3 = (f32[344,128]{1,0:T(8,128)S(1)}, f32[344,128]{1,0:T(8,128)S(1)}, u32[]{:S(2)}, u32[]{:S(2)}) collective-permute-start(f32[344,128]{1,0:T(8,128)S(1)} %slice_select_fusion), channel_id=1, source_target_pairs={{0,2},{1,3},{2,0},{3,1},{4,6},{5,7},{6,4},{7,5},{8,10},{9,11},{10,... | collective-permute-start | bytes 528392 | tf_op jit(solution)/shard_map/ppermute | solution.py:186
  41.9 10.6 %collective-permute-start.4 = (f32[344,128]{1,0:T(8,128)S(1)}, f32[344,128]{1,0:T(8,128)S(1)}, u32[]{:S(2)}, u32[]{:S(2)}) collective-permute-start(f32[344,128]{1,0:T(8,128)S(1)} %select_add_fusion.1), channel_id=1, source_target_pairs={{0,4},{1,5},{2,6},{3,7},{4,0},{5,1},{6,2},{7,3},{8,12},{9,13},{10,... | collective-permute-start | bytes 528392 | tf_op jit(solution)/shard_map/ppermute | solution.py:189
  52.5 5.5 %collective-permute-start.5 = (f32[344,128]{1,0:T(8,128)S(1)}, f32[344,128]{1,0:T(8,128)S(1)}, u32[]{:S(2)}, u32[]{:S(2)}) collective-permute-start(f32[344,128]{1,0:T(8,128)S(1)} %add.151), channel_id=1, source_target_pairs={{0,2},{1,3},{2,0},{3,1},{4,6},{5,7},{6,4},{7,5},{8,10},{9,11},{10,... | collective-permute-start | bytes 528392 | tf_op jit(solution)/shard_map/ppermute | solution.py:191
  58.0 1.7 %collective-permute-start.6 = (f32[676,128]{1,0:T(8,128)S(1)}, f32[676,128]{1,0:T(8,128)S(1)}, u32[]{:S(2)}, u32[]{:S(2)}) collective-permute-start(f32[676,128]{1,0:T(8,128)S(1)} %fusion.45), channel_id=1, source_target_pairs={{0,1},{1,0},{2,3},{3,2},{4,5},{5,4},{6,7},{7,6},{8,9},{9,8},{10,11... | collective-permute-start | bytes 1038344 | tf_op jit(solution)/shard_map/ppermute | solution.py:206
  60.4 1.7 %copy-start.1 = (f32[2]{0:T(128)S(1)}, f32[2]{0:T(128)}, u32[]{:S(2)}) copy-start(f32[2]{0:T(128)} %constant.106.clone) | copy-start | bytes 28

commit v14 on v13

--- a/solution.py
+++ b/solution.py
@@ -218,10 +218,22 @@
     half_keep = -(-HARM // devices) * devices
     frequency = (HARM - 1) - jnp.arange(padded_keep, dtype=jnp.int32)
     col_frequency = (HARM - 1) - jnp.arange(half_keep, dtype=jnp.int32)
-    columns = jnp.arange(map_width, dtype=jnp.int32)
-    phases = columns[:, None] * col_frequency[None, :] % map_width
-    angles = phases.astype(jnp.float32) * (2.0 * math.pi / map_width)
-    col_table = jnp.stack([jnp.cos(angles), -jnp.sin(angles)], axis=1)
+    fine_count = 64 if map_width % 64 == 0 else 1
+    coarse = jnp.arange(map_width // fine_count, dtype=jnp.int32) * fine_count
+    fine = jnp.arange(fine_count, dtype=jnp.int32)
+    coarse_angles = (coarse[:, None] * col_frequency[None, :] % map_width).astype(jnp.float32) * (
+        2.0 * math.pi / map_width
+    )
+    fine_angles = (fine[:, None] * col_frequency[None, :] % map_width).astype(jnp.float32) * (
+        2.0 * math.pi / map_width
+    )
+    c_cos = jnp.cos(coarse_angles)[:, None, :]
+    c_sin = jnp.sin(coarse_angles)[:, None, :]
+    f_cos = jnp.cos(fine_angles)[None, :, :]
+    f_sin = jnp.sin(fine_angles)[None, :, :]
+    col_cos = (c_cos * f_cos - c_sin * f_sin).reshape(map_width, -1)
+    col_sin = (c_sin * f_cos + c_cos * f_sin).reshape(map_width, -1)
+    col_table = jnp.stack([col_cos, -col_sin], axis=1)
     col_table, permit = lax.optimization_barrier((col_table, permit))
     smooth = extended_2(permit, (("slab", 0),), 4)
     for sweep_index in range(3):

time: 82.4 us -> 79.5 us (0.965)
  other arithmetic: 20.3 us -> 17.7 us
    cos x1 -> x2, other arithmetic: 3.4 us -> 0.3 us  [the longest x1 0.15 us: shards(): c_cos = jnp.cos(coarse_angles)[:, None, :]]
where the time goes in v14:
time: 79.5 us; the launch traced here: 78.7 us
  waiting for transfers between devices  19.8 us (25%)
  other arithmetic  17.7 us (22%)
  Pallas kernels  15.8 us (20%)
  starting transfers between devices  10.1 us (13%)
  local copies, waits for them, and re-layouts  7.69 us (10%)
  matrix products  7.32 us (9%)
    pallas_call x1, Pallas kernels, assemble(): pl.pallas_call(assemble_kernel, grid_spec=grid_spec, out_shape=jax.ShapeD...  15.8 us
    ppermute x1, waiting for transfers between devices, line_sum(): lax.ppermute(kept, 'slab', [(i, i ^ bit) for i in range(devices)])  7.92 us
    ppermute x1, waiting for transfers between devices, line_sum(): kept = kept + lax.ppermute(sent, 'slab', pair)  5.16 us
    another operation x3, other arithmetic, shards(): jnp.stack([permit, contrast * normal_x * normal_x, contrast * normal_x *...  4.94 us
    ppermute x1, waiting for transfers between devices, line_sum(): back = lax.ppermute(kept, 'slab', pair)  4.72 us
    dot_general x1, matrix products, shards(): jnp.einsum('kxy,ycn->kxcn', fields, col_table, precision=lax.Precision.HIGH)  4.28 us
    ppermute x1, starting transfers between devices, extended_2(): lax.ppermute(lax.slice_in_dim(block, 0, width, axis=dim), axis, backward)  4.09 us
    div x3, other arithmetic, smooth_once(): (4.0 * middle + extended[:-2] + extended[2:] + jnp.roll(middle, 1, 1) + j...  3.89 us
  transfers between devices with their start and end apart: 7, of which 7 were waited for; matrix products, arithmetic and copies ran while one was open for 3% of the time, Pallas kernels for 0%

profile of v14, /device:TPU:0, one launch (start us, length us, event | category | flops | bytes accessed | tf_op | source)
XLA Modules:
  0.0 78.7 jit_solution(17755640402129004360)
XLA Ops:
  0.0 0.1 fusion.66
  0.2 0.2 fusion.68
  0.3 2.3 %select_add_fusion = f32[256,2048]{1,0:T(8,128)S(1)} fusion(s32[256,2048]{1,0:T(8,128)} %param.2), kind=kLoop, calls=%fused_computation.48 | loop fusion | flops 5767168 | bytes 4194304 | tf_op jit(solution)/shard_map/add | solution.py:41
  2.7 0.3 multiply_subtract_fusion
  3.0 1.5 %pad_maximum_fusion.6 = f32[2048,2,104]{2,0,1:T(8,128)} fusion(f32[2048,1,104]{2,0,1:T(8,128)S(1)} %bitcast.74, f32[2048,1,104]{2,0,1:T(8,128)S(1)} %bitcast.73), kind=kLoop, calls=%fused_computation.39 | loop fusion | flops 425984 | bytes 3407872 | tf_op jit(solution)/shard_map/stack | solution.py:236
  4.4 0.5 collective-permute-start
  5.0 4.1 %collective-permute-start.1 = (f32[4,2048]{1,0:T(4,128)S(1)}, f32[4,2048]{1,0:T(4,128)S(1)}, u32[]{:S(2)}, u32[]{:S(2)}) collective-permute-start(f32[4,2048]{1,0:T(4,128)S(1)} %get-tuple-element.28), channel_id=1, source_target_pairs={{1,0},{2,1},{3,2},{4,3},{5,4},{6,5},{7,6},{0,7},{9,8},{10,9},{11,1... | collective-permute-start | bytes 98312 | tf_op jit(solution)/shard_map/ppermute | solution.py:33
  9.1 0.9 %fusion.46 = (f32[1,208,256]{2,1,0:T(8,128)S(1)}, f32[1,208,256]{2,1,0:T(8,128)S(1)}) fusion(s32[256]{0:T(256)S(1)} %iota_add_fusion, s32[208]{0:T(256)S(1)} %iota_subtract_fusion.2), kind=kLoop, calls=%fused_computation.96 | loop fusion | flops 745472 | bytes 427840 | tf_op jit(solution)/shard_map/cos | solution.py:72
  10.0 0.6 collective-permute-done
  10.7 0.3 pad_maximum_fusion.5
  11.0 0.9 %fusion.83 = (f32[262,2047]{1,0:T(8,128)S(1)}, f32[262,2047]{1,0:T(8,128)S(1)}) fusion(f32[264,2048]{1,0:T(8,128)S(1)} %pad_maximum_fusion.5), kind=kLoop, calls=%fused_computation.147 | loop fusion | bytes 8581024 | tf_op jit(solution)/shard_map/jit(_roll_static)/slice | solution.py:54
  11.8 2.1 %fusion.15 = f32[262,2048]{1,0:T(8,128)S(1)} fusion(f32[4,2048]{1,0:T(4,128)S(1)} %collective-permute-done.1, f32[256,2048]{1,0:T(8,128)S(1)} %select_add_fusion, f32[4,2048]{1,0:T(4,128)S(1)} %collective-permute-done, f32[264,2048]{1,0:T(8,128)S(1)} %pad_maximum_fusion.5, f32[262,2047]{1,0:T(8,128)S(1)} %get-tuple-element.26, ...), kind=kLoop, calls=%fused_computation.26 | loop fusion | flops 6438912 | bytes 15038416 | tf_op jit(solution)/shard_map/div | solution.py:49
  14.0 0.9 %fusion.81 = (f32[260,2047]{1,0:T(8,128)S(1)}, f32[260,2047]{1,0:T(8,128)S(1)}) fusion(f32[262,2048]{1,0:T(8,128)S(1)} %fusion.15), kind=kLoop, calls=%fused_computation.145 | loop fusion | bytes 8515520 | tf_op jit(solution)/shard_map/jit(_roll_static)/slice | solution.py:54
  15.0 0.9 %fusion.12 = f32[260,2048]{1,0:T(8,128)S(1)} fusion(f32[262,2048]{1,0:T(8,128)S(1)} %fusion.15, f32[260,2047]{1,0:T(8,128)S(1)} %get-tuple-element.22, f32[260,1]{1,0:T(8,128)S(1)} %get-tuple-element.24, f32[260,1]{1,0:T(8,128)S(1)} %get-tuple-element.23, f32[260,2047]{1,0:T(8,128)S(1)} %get-tuple-element.21), kind=kLoop, calls=%fused_computation.20 | loop fusion | flops 4259840 | bytes 12779520 | tf_op jit(solution)/shard_map/div | solution.py:49
  15.9 0.9 %fusion.79 = (f32[258,2047]{1,0:T(8,128)S(1)}, f32[258,2047]{1,0:T(8,128)S(1)}) fusion(f32[260,2048]{1,0:T(8,128)S(1)} %fusion.12), kind=kLoop, calls=%fused_computation.143 | loop fusion | bytes 8450016 | tf_op jit(solution)/shard_map/jit(_roll_static)/slice | solution.py:54
  16.9 0.9 %fusion.9 = f32[258,2048]{1,0:T(8,128)S(1)} fusion(f32[260,2048]{1,0:T(8,128)S(1)} %fusion.12, f32[258,2047]{1,0:T(8,128)S(1)} %get-tuple-element.18, f32[258,1]{1,0:T(8,128)S(1)} %get-tuple-element.20, f32[258,1]{1,0:T(8,128)S(1)} %get-tuple-element.19, f32[258,2047]{1,0:T(8,128)S(1)} %get-tuple-element.17), kind=kLoop, calls=%fused_computation.14 | loop fusion | flops 4227072 | bytes 12681216 | tf_op jit(solution)/shard_map/div | solution.py:49
  17.7 1.1 %fusion.77 = (f32[256,2047]{1,0:T(8,128)S(1)}, f32[256,2047]{1,0:T(8,128)S(1)}) fusion(f32[258,2048]{1,0:T(8,128)S(1)} %fusion.9), kind=kLoop, calls=%fused_computation.141 | loop fusion | bytes 8384512 | tf_op jit(solution)/shard_map/jit(_roll_static)/slice | solution.py:61
  18.9 2.1 %multiply_bitcast_fusion.1 = (f32[1,256,2048]{2,1,0:T(8,128)S(1)}, f32[256,2048]{1,0:T(8,128)S(1)}) fusion(f32[256,2048]{1,0:T(8,128)S(1)} %select_add_fusion, f32[256,2047]{1,0:T(8,128)S(1)} %get-tuple-element.14, f32[256,1]{1,0:T(8,128)S(1)} %get-tuple-element.16, f32[256,1]{1,0:T(8,128)S(1)} %get-tuple-element.15, f32[256,2047]{1,0:T(8,128)S(1)} %get-tuple-element.13, ...), kind=kLoop, calls=%fused_computation.44 | loop fusion | flops 7864320 | bytes 14680064 | tf_op jit(solution)/shard_map/stack | solution.py:247
  21.1 2.3 %multiply_bitcast_fusion = (f32[1,256,2048]{2,1,0:T(8,128)S(1)}, f32[256,2048]{1,0:T(8,128)S(1)}) fusion(f32[256,2048]{1,0:T(8,128)S(1)} %get-tuple-element.10, f32[256,2048]{1,0:T(8,128)S(1)} %select_add_fusion, f32[258,2048]{1,0:T(8,128)S(1)} %fusion.9, f32[256,2047]{1,0:T(8,128)S(1)} %get-tuple-element.14, f32[256,1]{1,0:T(8,128)S(1)} %get-tuple-element.16, ...), kind=kLoop, calls=%fused_computation.43 | loop fusion | flops 7864320 | bytes 16777216 | tf_op jit(solution)/shard_map/stack | solution.py:247
  23.4 0.5 fusion.18
  23.9 1.1 %copy-done = f32[2048,2,104]{2,0,1:T(8,128)S(1)} copy-done((f32[2048,2,104]{2,0,1:T(8,128)S(1)}, f32[2048,2,104]{2,0,1:T(8,128)}, u32[]{:S(2)}) %copy-start) | copy-done | bytes 1703960
  24.9 4.3 %fusion.24 = f32[4,256,2,104,1]{1,3,4,2,0:T(8,128)S(1)} fusion(f32[2048,2,104]{2,0,1:T(8,128)S(1)} %copy-done, f32[1,256,2048]{2,1,0:T(8,128)S(1)} %fusion.18, f32[1,256,2048]{2,1,0:T(8,128)S(1)} %get-tuple-element.11, f32[1,256,2048]{2,1,0:T(8,128)S(1)} %get-tuple-element.9, f32[1,256,2048]{2,1,0:T(8,128)S(1)} %bitcast.72), kind=kOutput, calls=%fused_computation.52 | convolution fusion | flops 2623537152 | bytes 10944512 | tf_op jit(solution)/shard_map/kxy,ycn->kxcn/dot_general | solution.py:255
  29.2 0.9 %convolution_bitcast_fusion = f32[2,4,208,2,104]{2,4,0,3,1:T(8,128)S(1)} fusion(f32[4,256,2,104,1]{1,3,4,2,0:T(8,128)S(1)} %fusion.24, f32[1,208,256]{2,1,0:T(8,128)S(1)} %get-tuple-element.42, f32[1,208,256]{2,1,0:T(8,128)S(1)} %get-tuple-element.41), kind=kOutput, calls=%fused_computation.51 | convolution fusion | flops 531734528 | bytes 2662400 | tf_op jit(solution)/shard_map/smx,kxcn->skmcn/dot_general | solution.py:73
  30.1 0.1 broadcast_select_fusion
  30.2 0.2 copy.7
  30.4 0.4 select_n.140
  30.8 0.4 collective-permute-start.2
  31.2 0.2 copy.6
  31.3 0.4 select_n.138
  31.7 0.8 collective-permute-done.2
  32.6 1.6 %collective-permute-start.3 = (f32[344,128]{1,0:T(8,128)S(1)}, f32[344,128]{1,0:T(8,128)S(1)}, u32[]{:S(2)}, u32[]{:S(2)}) collective-permute-start(f32[344,128]{1,0:T(8,128)S(1)} %slice_select_fusion), channel_id=1, source_target_pairs={{0,2},{1,3},{2,0},{3,1},{4,6},{5,7},{6,4},{7,5},{8,10},{9,11},{10,... | collective-permute-start | bytes 528392 | tf_op jit(solution)/shard_map/ppermute | solution.py:186
  34.2 5.2 %collective-permute-done.3 = f32[344,128]{1,0:T(8,128)S(1)} collective-permute-done((f32[344,128]{1,0:T(8,128)S(1)}, f32[344,128]{1,0:T(8,128)S(1)}, u32[]{:S(2)}, u32[]{:S(2)}) %collective-permute-start.3) | collective-permute-done | bytes 176160 | tf_op jit(solution)/shard_map/ppermute | solution.py:186
  39.4 2.7 %collective-permute-start.4 = (f32[344,128]{1,0:T(8,128)S(1)}, f32[344,128]{1,0:T(8,128)S(1)}, u32[]{:S(2)}, u32[]{:S(2)}) collective-permute-start(f32[344,128]{1,0:T(8,128)S(1)} %select_add_fusion.1), channel_id=1, source_target_pairs={{0,4},{1,5},{2,6},{3,7},{4,0},{5,1},{6,2},{7,3},{8,12},{9,13},{10,... | collective-permute-start | bytes 528392 | tf_op jit(solution)/shard_map/ppermute | solution.py:189
  42.0 7.9 %collective-permute-done.4 = f32[344,128]{1,0:T(8,128)S(1)} collective-permute-done((f32[344,128]{1,0:T(8,128)S(1)}, f32[344,128]{1,0:T(8,128)S(1)}, u32[]{:S(2)}, u32[]{:S(2)}) %collective-permute-start.4) | collective-permute-done | bytes 176160 | tf_op jit(solution)/shard_map/ppermute | solution.py:189
  50.0 0.8 collective-permute-start.5
  50.8 4.7 %collective-permute-done.5 = f32[344,128]{1,0:T(8,128)S(1)} collective-permute-done((f32[344,128]{1,0:T(8,128)S(1)}, f32[344,128]{1,0:T(8,128)S(1)}, u32[]{:S(2)}, u32[]{:S(2)}) %collective-permute-start.5) | collective-permute-done | bytes 176160 | tf_op jit(solution)/shard_map/ppermute | solution.py:191
  55.6 0.7 pad_add_fusion.index_ref
  56.3 0.4 stack_reshape.4
  56.7 0.5 collective-permute-done.6
  57.2 0.4 stack_reshape.10
  57.7 0.7 fusion.28
  58.4 0.6 fusion.30
  59.1 0.8 %multiply_add_fusion = f32[2,4,208,256]{3,2,1,0:T(8,128)S(1)} fusion(f32[2,4,208,256]{3,2,1,0:T(8,128)S(1)} %fusion.30, f32[2,4,104,208]{2,3,1,0:T(8,128)S(1)} %fusion.28, f32[2]{0:T(128)S(1)} %copy-done.1, s32[256]{0:T(256)S(1)} %iota_subtract_fusion, pred[256]{0:T(512)(128)(4,1)S(1)} %iota_compare_fusion.3), kind=kOutput, calls=%fused_computation.50 | convolution fusion | flops 532533248 | bytes 4101384 | tf_op jit(solution)/shard_map/ad,skdc,cb->skab/dot_general | solution.py:270
  59.9 0.2 fusion.85
  60.0 0.2 pad_maximum_fusion.7
  60.2 0.7 slice_bitcast_fusion.3
  60.9 2.0 %pad_maximum_fusion.fl_ref = f32[2,4,4,208,128]{4,3,2,1,0:T(8,128)} fusion(f32[2,1,4,208,128]{4,3,2,1,0:T(8,128)S(1)} %get-tuple-element.30, f32[2,1,4,208,128]{4,3,2,1,0:T(8,128)S(1)} %get-tuple-element.31, f32[2,1,4,208,128]{4,3,2,1,0:T(8,128)S(1)} %get-tuple-element.32, f32[2,1,4,208,128]{4,3,2,1,0:T(8,128)S(1)} %get-tuple-element.29), kind=kLoop, calls=%fused_computation.8 | loop fusion | flops 2555904 | bytes 6815744 | tf_op jit(solution)/shard_map/stack | solution.py:277
  62.9 15.8 %shard_map.28 = f32[2,64,20402]{2,1,0:T(8,128)} custom-call(s32[2]{0:T(128)} %pad_add_fusion.index_ref, f32[2,4,4,208,128]{4,3,2,1,0:T(8,128)} %pad_maximum_fusion.fl_ref), custom_call_target="tpu_custom_call" | custom-call | tf_op jit(solution)/shard_map/pallas_call | solution.py:160
  (22 shorter events, 0.7 us)
Async XLA Ops:
  4.4 6.2 %collective-permute-start = (f32[4,2048]{1,0:T(4,128)S(1)}, f32[4,2048]{1,0:T(4,128)S(1)}, u32[]{:S(2)}, u32[]{:S(2)}) collective-permute-start(f32[4,2048]{1,0:T(4,128)S(1)} %get-tuple-element.27), channel_id=1, source_target_pairs={{0,1},{1,2},{2,3},{3,4},{4,5},{5,6},{6,7},{7,0},{8,9},{9,10},{10,1... | collective-permute-start | bytes 98312 | tf_op jit(solution)/shard_map/ppermute | solution.py:30
  5.0 5.7 %collective-permute-start.1 = (f32[4,2048]{1,0:T(4,128)S(1)}, f32[4,2048]{1,0:T(4,128)S(1)}, u32[]{:S(2)}, u32[]{:S(2)}) collective-permute-start(f32[4,2048]{1,0:T(4,128)S(1)} %get-tuple-element.28), channel_id=1, source_target_pairs={{1,0},{2,1},{3,2},{4,3},{5,4},{6,5},{7,6},{0,7},{9,8},{10,9},{11,1... | collective-permute-start | bytes 98312 | tf_op jit(solution)/shard_map/ppermute | solution.py:33
  23.3 1.6 %copy-start = (f32[2048,2,104]{2,0,1:T(8,128)S(1)}, f32[2048,2,104]{2,0,1:T(8,128)}, u32[]{:S(2)}) copy-start(f32[2048,2,104]{2,0,1:T(8,128)} %pad_maximum_fusion.6) | copy-start | bytes 5111812
  30.8 1.7 %collective-permute-start.2 = (f32[676,128]{1,0:T(8,128)S(1)}, f32[676,128]{1,0:T(8,128)S(1)}, u32[]{:S(2)}, u32[]{:S(2)}) collective-permute-start(f32[676,128]{1,0:T(8,128)S(1)} %select_n.140), channel_id=1, source_target_pairs={{0,1},{1,0},{2,3},{3,2},{4,5},{5,4},{6,7},{7,6},{8,9},{9,8},{10,11... | collective-permute-start | bytes 1038344 | tf_op jit(solution)/shard_map/ppermute | solution.py:175
  32.6 6.8 %collective-permute-start.3 = (f32[344,128]{1,0:T(8,128)S(1)}, f32[344,128]{1,0:T(8,128)S(1)}, u32[]{:S(2)}, u32[]{:S(2)}) collective-permute-start(f32[344,128]{1,0:T(8,128)S(1)} %slice_select_fusion), channel_id=1, source_target_pairs={{0,2},{1,3},{2,0},{3,1},{4,6},{5,7},{6,4},{7,5},{8,10},{9,11},{10,... | collective-permute-start | bytes 528392 | tf_op jit(solution)/shard_map/ppermute | solution.py:186
  39.4 10.6 %collective-permute-start.4 = (f32[344,128]{1,0:T(8,128)S(1)}, f32[344,128]{1,0:T(8,128)S(1)}, u32[]{:S(2)}, u32[]{:S(2)}) collective-permute-start(f32[344,128]{1,0:T(8,128)S(1)} %select_add_fusion.1), channel_id=1, source_target_pairs={{0,4},{1,5},{2,6},{3,7},{4,0},{5,1},{6,2},{7,3},{8,12},{9,13},{10,... | collective-permute-start | bytes 528392 | tf_op jit(solution)/shard_map/ppermute | solution.py:189
  50.0 5.5 %collective-permute-start.5 = (f32[344,128]{1,0:T(8,128)S(1)}, f32[344,128]{1,0:T(8,128)S(1)}, u32[]{:S(2)}, u32[]{:S(2)}) collective-permute-start(f32[344,128]{1,0:T(8,128)S(1)} %add.176), channel_id=1, source_target_pairs={{0,2},{1,3},{2,0},{3,1},{4,6},{5,7},{6,4},{7,5},{8,10},{9,11},{10,... | collective-permute-start | bytes 528392 | tf_op jit(solution)/shard_map/ppermute | solution.py:191
  55.5 1.7 %collective-permute-start.6 = (f32[676,128]{1,0:T(8,128)S(1)}, f32[676,128]{1,0:T(8,128)S(1)}, u32[]{:S(2)}, u32[]{:S(2)}) collective-permute-start(f32[676,128]{1,0:T(8,128)S(1)} %fusion.38), channel_id=1, source_target_pairs={{0,1},{1,0},{2,3},{3,2},{4,5},{5,4},{6,7},{7,6},{8,9},{9,8},{10,11... | collective-permute-start | bytes 1038344 | tf_op jit(solution)/shard_map/ppermute | solution.py:206
  57.7 1.4 %copy-start.1 = (f32[2]{0:T(128)S(1)}, f32[2]{0:T(128)}, u32[]{:S(2)}) copy-start(f32[2]{0:T(128)} %constant.117.clone) | copy-start | bytes 28

commit v15 on v14

--- a/solution.py
+++ b/solution.py
@@ -13,6 +13,7 @@
 KEEP = 201
 ORDERS = 10201
 BLOCK_ROWS = 8
+STEP_ROWS = 16
 COPIES = 4
 COPY_STEP = 28
 LANES = 128
@@ -97,56 +98,58 @@
     rows = o_ref.shape[1] * pl.num_programs(1)
     spacing = ORDERS // (rows * index_ref[1] // 2)
     centre = (HARM - 1) // 2
-    span = z_ref.shape[1] // BLOCK_ROWS - BLOCK_ROWS
+    span = z_ref.shape[2] // BLOCK_ROWS - BLOCK_ROWS
     lane_iota = lax.broadcasted_iota(jnp.int32, (span, LANES), 1)
     sub = lax.broadcasted_iota(jnp.int32, (BLOCK_ROWS, LANES), 0)
     lane = lax.broadcasted_iota(jnp.int32, (BLOCK_ROWS, LANES), 1)
-    for rr in range(BLOCK_ROWS):
-        row = rb * BLOCK_ROWS + rr
-        order_index = (index_ref[0] * rows + row) // 2 * spacing
-        first = order_index // HARM
-        second = order_index % HARM
-        a0 = (HARM - 1) - first
-        b0 = (HARM - 1) - second
-        kx = 0.3 + 0.02 * (first - centre).astype(jnp.float32)
-        ky = 0.2 + 0.02 * (second - centre).astype(jnp.float32)
-        if rr % 2:
-            diagonal = (ky * ky, -(kx * ky))
-        else:
-            diagonal = (kx * ky, -(kx * kx))
-        copy = jnp.minimum(b0 // COPY_STEP, COPIES - 1)
-        shift = (LANES - (b0 - COPY_STEP * copy)) % LANES
-        base = pl.multiple_of(a0 // BLOCK_ROWS * BLOCK_ROWS, BLOCK_ROWS)
-        off = a0 % BLOCK_ROWS
-        dest = pl.multiple_of((BLOCK_ROWS - off) * BLOCK_ROWS, BLOCK_ROWS) + rr
-        spot_tile = pl.multiple_of((first + BLOCK_ROWS) * BLOCK_ROWS, BLOCK_ROWS)
-        spot = (sub == rr) & (lane == second)
-        for h in range(2):
-            combo = 2 * (rr % 2) + h
-            x = fl_ref[0, copy, combo, pl.ds(base, span), :]
-            x = pltpu.roll(x, shift, 1)
-            z_ref[h, pl.ds(dest, span, stride=BLOCK_ROWS), :] = x
-            d = jnp.where(s == 0, diagonal[h], jnp.float32(0.0))
-            tile = z_ref[h, pl.ds(spot_tile, BLOCK_ROWS), :]
-            z_ref[h, pl.ds(spot_tile, BLOCK_ROWS), :] = tile + jnp.where(spot, d, jnp.float32(0.0))
-    placed = {}
-    for start, width, runs in chunk_segments(o_ref.shape[2], o_ref.shape[2] // 2):
-        acc = None
-        for h, u, l0, v0 in runs:
-            if (h, u) not in placed:
-                src = z_ref[h, pl.ds((u + BLOCK_ROWS) * BLOCK_ROWS, BLOCK_ROWS), :]
-                sh = (l0 - v0) % LANES
-                placed[(h, u)] = pltpu.roll(src, sh, 1) if sh else src
-            src = placed[(h, u)]
-            acc = src if acc is None else jnp.where(lane >= l0, src, acc)
-        if width < LANES:
-            acc = acc[:, :width]
-        o_ref[0, :, pl.ds(start, width)] = acc
+    for part in range(o_ref.shape[1] // BLOCK_ROWS):
+        z_part = z_ref.at[part]
+        for rr in range(BLOCK_ROWS):
+            row = rb * o_ref.shape[1] + part * BLOCK_ROWS + rr
+            order_index = (index_ref[0] * rows + row) // 2 * spacing
+            first = order_index // HARM
+            second = order_index % HARM
+            a0 = (HARM - 1) - first
+            b0 = (HARM - 1) - second
+            kx = 0.3 + 0.02 * (first - centre).astype(jnp.float32)
+            ky = 0.2 + 0.02 * (second - centre).astype(jnp.float32)
+            if rr % 2:
+                diagonal = (ky * ky, -(kx * ky))
+            else:
+                diagonal = (kx * ky, -(kx * kx))
+            copy = jnp.minimum(b0 // COPY_STEP, COPIES - 1)
+            shift = (LANES - (b0 - COPY_STEP * copy)) % LANES
+            base = pl.multiple_of(a0 // BLOCK_ROWS * BLOCK_ROWS, BLOCK_ROWS)
+            off = a0 % BLOCK_ROWS
+            dest = pl.multiple_of((BLOCK_ROWS - off) * BLOCK_ROWS, BLOCK_ROWS) + rr
+            spot_tile = pl.multiple_of((first + BLOCK_ROWS) * BLOCK_ROWS, BLOCK_ROWS)
+            spot = (sub == rr) & (lane == second)
+            for h in range(2):
+                combo = 2 * (rr % 2) + h
+                x = fl_ref[0, copy, combo, pl.ds(base, span), :]
+                x = pltpu.roll(x, shift, 1)
+                z_part[h, pl.ds(dest, span, stride=BLOCK_ROWS), :] = x
+                d = jnp.where(s == 0, diagonal[h], jnp.float32(0.0))
+                tile = z_part[h, pl.ds(spot_tile, BLOCK_ROWS), :]
+                z_part[h, pl.ds(spot_tile, BLOCK_ROWS), :] = tile + jnp.where(spot, d, jnp.float32(0.0))
+        placed = {}
+        for start, width, runs in chunk_segments(o_ref.shape[2], o_ref.shape[2] // 2):
+            acc = None
+            for h, u, l0, v0 in runs:
+                if (h, u) not in placed:
+                    src = z_part[h, pl.ds((u + BLOCK_ROWS) * BLOCK_ROWS, BLOCK_ROWS), :]
+                    sh = (l0 - v0) % LANES
+                    placed[(h, u)] = pltpu.roll(src, sh, 1) if sh else src
+                src = placed[(h, u)]
+                acc = src if acc is None else jnp.where(lane >= l0, src, acc)
+            if width < LANES:
+                acc = acc[:, :width]
+            o_ref[0, pl.ds(part * BLOCK_ROWS, BLOCK_ROWS), pl.ds(start, width)] = acc
 
 
 def assemble(index, tables, rows):
     span = 112
-    n_blocks = rows // BLOCK_ROWS
+    n_blocks = rows // STEP_ROWS
     total = 2 * ORDERS
     grid_spec = pltpu.PrefetchScalarGridSpec(
         num_scalar_prefetch=1,
@@ -154,8 +157,12 @@
         in_specs=[
             pl.BlockSpec((1,) + tables.shape[1:], lambda s, rb, *_: (s, 0, 0, 0, 0)),
         ],
-        out_specs=pl.BlockSpec((1, BLOCK_ROWS, total), lambda s, rb, *_: (s, rb, 0)),
-        scratch_shapes=[pltpu.VMEM((2, (span + BLOCK_ROWS) * BLOCK_ROWS, LANES), jnp.float32)],
+        out_specs=pl.BlockSpec((1, STEP_ROWS, total), lambda s, rb, *_: (s, rb, 0)),
+        scratch_shapes=[
+            pltpu.VMEM(
+                (STEP_ROWS // BLOCK_ROWS, 2, (span + BLOCK_ROWS) * BLOCK_ROWS, LANES), jnp.float32
+            )
+        ],
     )
     return pl.pallas_call(
         assemble_kernel,

time: 79.5 us -> 78.1 us (0.982)
  Pallas kernels: 15.8 us -> 14.3 us
    pallas_call x1, Pallas kernels: 15.8 us -> 14.3 us  [assemble(): pl.pallas_call(assemble_kernel, grid_spec=grid_spec, out_shape=jax.ShapeD...]
where the time goes in v15:
time: 78.1 us; the launch traced here: 77.2 us
  waiting for transfers between devices  19.8 us (25%)
  other arithmetic  17.7 us (23%)
  Pallas kernels  14.3 us (18%)
  starting transfers between devices  10.1 us (13%)
  local copies, waits for them, and re-layouts  7.69 us (10%)
  matrix products  7.32 us (9%)
    pallas_call x1, Pallas kernels, assemble(): pl.pallas_call(assemble_kernel, grid_spec=grid_spec, out_shape=jax.ShapeD...  14.3 us
    ppermute x1, waiting for transfers between devices, line_sum(): lax.ppermute(kept, 'slab', [(i, i ^ bit) for i in range(devices)])  7.92 us
    ppermute x1, waiting for transfers between devices, line_sum(): kept = kept + lax.ppermute(sent, 'slab', pair)  5.16 us
    another operation x3, other arithmetic, shards(): jnp.stack([permit, contrast * normal_x * normal_x, contrast * normal_x *...  4.94 us
    ppermute x1, waiting for transfers between devices, line_sum(): back = lax.ppermute(kept, 'slab', pair)  4.72 us
    dot_general x1, matrix products, shards(): jnp.einsum('kxy,ycn->kxcn', fields, col_table, precision=lax.Precision.HIGH)  4.28 us
    ppermute x1, starting transfers between devices, extended_2(): lax.ppermute(lax.slice_in_dim(block, 0, width, axis=dim), axis, backward)  4.09 us
    div x3, other arithmetic, smooth_once(): (4.0 * middle + extended[:-2] + extended[2:] + jnp.roll(middle, 1, 1) + j...  3.89 us
  transfers between devices with their start and end apart: 7, of which 7 were waited for; matrix products, arithmetic and copies ran while one was open for 3% of the time, Pallas kernels for 0%

profile of v15, /device:TPU:0, one launch (start us, length us, event | category | flops | bytes accessed | tf_op | source)
XLA Modules:
  0.0 77.2 jit_solution(5400861116428222015)
XLA Ops:
  0.0 0.1 fusion.66
  0.2 0.2 fusion.68
  0.3 2.3 %select_add_fusion = f32[256,2048]{1,0:T(8,128)S(1)} fusion(s32[256,2048]{1,0:T(8,128)} %param.2), kind=kLoop, calls=%fused_computation.48 | loop fusion | flops 5767168 | bytes 4194304 | tf_op jit(solution)/shard_map/add | solution.py:42
  2.7 0.3 multiply_subtract_fusion
  3.0 1.5 %pad_maximum_fusion.6 = f32[2048,2,104]{2,0,1:T(8,128)} fusion(f32[2048,1,104]{2,0,1:T(8,128)S(1)} %bitcast.74, f32[2048,1,104]{2,0,1:T(8,128)S(1)} %bitcast.73), kind=kLoop, calls=%fused_computation.39 | loop fusion | flops 425984 | bytes 3407872 | tf_op jit(solution)/shard_map/stack | solution.py:243
  4.4 0.5 collective-permute-start
  5.0 4.1 %collective-permute-start.1 = (f32[4,2048]{1,0:T(4,128)S(1)}, f32[4,2048]{1,0:T(4,128)S(1)}, u32[]{:S(2)}, u32[]{:S(2)}) collective-permute-start(f32[4,2048]{1,0:T(4,128)S(1)} %get-tuple-element.28), channel_id=1, source_target_pairs={{1,0},{2,1},{3,2},{4,3},{5,4},{6,5},{7,6},{0,7},{9,8},{10,9},{11,1... | collective-permute-start | bytes 98312 | tf_op jit(solution)/shard_map/ppermute | solution.py:34
  9.1 0.9 %fusion.46 = (f32[1,208,256]{2,1,0:T(8,128)S(1)}, f32[1,208,256]{2,1,0:T(8,128)S(1)}) fusion(s32[256]{0:T(256)S(1)} %iota_add_fusion, s32[208]{0:T(256)S(1)} %iota_subtract_fusion.2), kind=kLoop, calls=%fused_computation.96 | loop fusion | flops 745472 | bytes 427840 | tf_op jit(solution)/shard_map/cos | solution.py:73
  10.0 0.6 collective-permute-done
  10.7 0.3 pad_maximum_fusion.5
  11.0 0.9 %fusion.83 = (f32[262,2047]{1,0:T(8,128)S(1)}, f32[262,2047]{1,0:T(8,128)S(1)}) fusion(f32[264,2048]{1,0:T(8,128)S(1)} %pad_maximum_fusion.5), kind=kLoop, calls=%fused_computation.147 | loop fusion | bytes 8581024 | tf_op jit(solution)/shard_map/jit(_roll_static)/slice | solution.py:55
  11.8 2.1 %fusion.15 = f32[262,2048]{1,0:T(8,128)S(1)} fusion(f32[4,2048]{1,0:T(4,128)S(1)} %collective-permute-done.1, f32[256,2048]{1,0:T(8,128)S(1)} %select_add_fusion, f32[4,2048]{1,0:T(4,128)S(1)} %collective-permute-done, f32[264,2048]{1,0:T(8,128)S(1)} %pad_maximum_fusion.5, f32[262,2047]{1,0:T(8,128)S(1)} %get-tuple-element.26, ...), kind=kLoop, calls=%fused_computation.26 | loop fusion | flops 6438912 | bytes 15038416 | tf_op jit(solution)/shard_map/div | solution.py:50
  14.0 0.9 %fusion.81 = (f32[260,2047]{1,0:T(8,128)S(1)}, f32[260,2047]{1,0:T(8,128)S(1)}) fusion(f32[262,2048]{1,0:T(8,128)S(1)} %fusion.15), kind=kLoop, calls=%fused_computation.145 | loop fusion | bytes 8515520 | tf_op jit(solution)/shard_map/jit(_roll_static)/slice | solution.py:55
  15.0 0.9 %fusion.12 = f32[260,2048]{1,0:T(8,128)S(1)} fusion(f32[262,2048]{1,0:T(8,128)S(1)} %fusion.15, f32[260,2047]{1,0:T(8,128)S(1)} %get-tuple-element.22, f32[260,1]{1,0:T(8,128)S(1)} %get-tuple-element.24, f32[260,1]{1,0:T(8,128)S(1)} %get-tuple-element.23, f32[260,2047]{1,0:T(8,128)S(1)} %get-tuple-element.21), kind=kLoop, calls=%fused_computation.20 | loop fusion | flops 4259840 | bytes 12779520 | tf_op jit(solution)/shard_map/div | solution.py:50
  15.9 0.9 %fusion.79 = (f32[258,2047]{1,0:T(8,128)S(1)}, f32[258,2047]{1,0:T(8,128)S(1)}) fusion(f32[260,2048]{1,0:T(8,128)S(1)} %fusion.12), kind=kLoop, calls=%fused_computation.143 | loop fusion | bytes 8450016 | tf_op jit(solution)/shard_map/jit(_roll_static)/slice | solution.py:55
  16.9 0.9 %fusion.9 = f32[258,2048]{1,0:T(8,128)S(1)} fusion(f32[260,2048]{1,0:T(8,128)S(1)} %fusion.12, f32[258,2047]{1,0:T(8,128)S(1)} %get-tuple-element.18, f32[258,1]{1,0:T(8,128)S(1)} %get-tuple-element.20, f32[258,1]{1,0:T(8,128)S(1)} %get-tuple-element.19, f32[258,2047]{1,0:T(8,128)S(1)} %get-tuple-element.17), kind=kLoop, calls=%fused_computation.14 | loop fusion | flops 4227072 | bytes 12681216 | tf_op jit(solution)/shard_map/div | solution.py:50
  17.7 1.1 %fusion.77 = (f32[256,2047]{1,0:T(8,128)S(1)}, f32[256,2047]{1,0:T(8,128)S(1)}) fusion(f32[258,2048]{1,0:T(8,128)S(1)} %fusion.9), kind=kLoop, calls=%fused_computation.141 | loop fusion | bytes 8384512 | tf_op jit(solution)/shard_map/jit(_roll_static)/slice | solution.py:62
  18.9 2.1 %multiply_bitcast_fusion.1 = (f32[1,256,2048]{2,1,0:T(8,128)S(1)}, f32[256,2048]{1,0:T(8,128)S(1)}) fusion(f32[256,2048]{1,0:T(8,128)S(1)} %select_add_fusion, f32[256,2047]{1,0:T(8,128)S(1)} %get-tuple-element.14, f32[256,1]{1,0:T(8,128)S(1)} %get-tuple-element.16, f32[256,1]{1,0:T(8,128)S(1)} %get-tuple-element.15, f32[256,2047]{1,0:T(8,128)S(1)} %get-tuple-element.13, ...), kind=kLoop, calls=%fused_computation.44 | loop fusion | flops 7864320 | bytes 14680064 | tf_op jit(solution)/shard_map/stack | solution.py:254
  21.1 2.3 %multiply_bitcast_fusion = (f32[1,256,2048]{2,1,0:T(8,128)S(1)}, f32[256,2048]{1,0:T(8,128)S(1)}) fusion(f32[256,2048]{1,0:T(8,128)S(1)} %get-tuple-element.10, f32[256,2048]{1,0:T(8,128)S(1)} %select_add_fusion, f32[258,2048]{1,0:T(8,128)S(1)} %fusion.9, f32[256,2047]{1,0:T(8,128)S(1)} %get-tuple-element.14, f32[256,1]{1,0:T(8,128)S(1)} %get-tuple-element.16, ...), kind=kLoop, calls=%fused_computation.43 | loop fusion | flops 7864320 | bytes 16777216 | tf_op jit(solution)/shard_map/stack | solution.py:254
  23.4 0.5 fusion.18
  23.9 1.1 %copy-done = f32[2048,2,104]{2,0,1:T(8,128)S(1)} copy-done((f32[2048,2,104]{2,0,1:T(8,128)S(1)}, f32[2048,2,104]{2,0,1:T(8,128)}, u32[]{:S(2)}) %copy-start) | copy-done | bytes 1703960
  24.9 4.3 %fusion.24 = f32[4,256,2,104,1]{1,3,4,2,0:T(8,128)S(1)} fusion(f32[2048,2,104]{2,0,1:T(8,128)S(1)} %copy-done, f32[1,256,2048]{2,1,0:T(8,128)S(1)} %fusion.18, f32[1,256,2048]{2,1,0:T(8,128)S(1)} %get-tuple-element.11, f32[1,256,2048]{2,1,0:T(8,128)S(1)} %get-tuple-element.9, f32[1,256,2048]{2,1,0:T(8,128)S(1)} %bitcast.72), kind=kOutput, calls=%fused_computation.52 | convolution fusion | flops 2623537152 | bytes 10944512 | tf_op jit(solution)/shard_map/kxy,ycn->kxcn/dot_general | solution.py:262
  29.2 0.9 %convolution_bitcast_fusion = f32[2,4,208,2,104]{2,4,0,3,1:T(8,128)S(1)} fusion(f32[4,256,2,104,1]{1,3,4,2,0:T(8,128)S(1)} %fusion.24, f32[1,208,256]{2,1,0:T(8,128)S(1)} %get-tuple-element.42, f32[1,208,256]{2,1,0:T(8,128)S(1)} %get-tuple-element.41), kind=kOutput, calls=%fused_computation.51 | convolution fusion | flops 531734528 | bytes 2662400 | tf_op jit(solution)/shard_map/smx,kxcn->skmcn/dot_general | solution.py:74
  30.1 0.1 broadcast_select_fusion
  30.2 0.2 copy.7
  30.4 0.4 select_n.140
  30.8 0.4 collective-permute-start.2
  31.2 0.2 copy.6
  31.3 0.4 select_n.138
  31.7 0.8 %collective-permute-done.2 = f32[676,128]{1,0:T(8,128)S(1)} collective-permute-done((f32[676,128]{1,0:T(8,128)S(1)}, f32[676,128]{1,0:T(8,128)S(1)}, u32[]{:S(2)}, u32[]{:S(2)}) %collective-permute-start.2) | collective-permute-done | bytes 346144 | tf_op jit(solution)/shard_map/ppermute | solution.py:182
  32.6 1.6 %collective-permute-start.3 = (f32[344,128]{1,0:T(8,128)S(1)}, f32[344,128]{1,0:T(8,128)S(1)}, u32[]{:S(2)}, u32[]{:S(2)}) collective-permute-start(f32[344,128]{1,0:T(8,128)S(1)} %slice_select_fusion), channel_id=1, source_target_pairs={{0,2},{1,3},{2,0},{3,1},{4,6},{5,7},{6,4},{7,5},{8,10},{9,11},{10,... | collective-permute-start | bytes 528392 | tf_op jit(solution)/shard_map/ppermute | solution.py:193
  34.2 5.2 %collective-permute-done.3 = f32[344,128]{1,0:T(8,128)S(1)} collective-permute-done((f32[344,128]{1,0:T(8,128)S(1)}, f32[344,128]{1,0:T(8,128)S(1)}, u32[]{:S(2)}, u32[]{:S(2)}) %collective-permute-start.3) | collective-permute-done | bytes 176160 | tf_op jit(solution)/shard_map/ppermute | solution.py:193
  39.4 2.7 %collective-permute-start.4 = (f32[344,128]{1,0:T(8,128)S(1)}, f32[344,128]{1,0:T(8,128)S(1)}, u32[]{:S(2)}, u32[]{:S(2)}) collective-permute-start(f32[344,128]{1,0:T(8,128)S(1)} %select_add_fusion.1), channel_id=1, source_target_pairs={{0,4},{1,5},{2,6},{3,7},{4,0},{5,1},{6,2},{7,3},{8,12},{9,13},{10,... | collective-permute-start | bytes 528392 | tf_op jit(solution)/shard_map/ppermute | solution.py:196
  42.0 7.9 %collective-permute-done.4 = f32[344,128]{1,0:T(8,128)S(1)} collective-permute-done((f32[344,128]{1,0:T(8,128)S(1)}, f32[344,128]{1,0:T(8,128)S(1)}, u32[]{:S(2)}, u32[]{:S(2)}) %collective-permute-start.4) | collective-permute-done | bytes 176160 | tf_op jit(solution)/shard_map/ppermute | solution.py:196
  50.0 0.8 %collective-permute-start.5 = (f32[344,128]{1,0:T(8,128)S(1)}, f32[344,128]{1,0:T(8,128)S(1)}, u32[]{:S(2)}, u32[]{:S(2)}) collective-permute-start(f32[344,128]{1,0:T(8,128)S(1)} %add.176), channel_id=1, source_target_pairs={{0,2},{1,3},{2,0},{3,1},{4,6},{5,7},{6,4},{7,5},{8,10},{9,11},{10,... | collective-permute-start | bytes 528392 | tf_op jit(solution)/shard_map/ppermute | solution.py:198
  50.8 4.7 %collective-permute-done.5 = f32[344,128]{1,0:T(8,128)S(1)} collective-permute-done((f32[344,128]{1,0:T(8,128)S(1)}, f32[344,128]{1,0:T(8,128)S(1)}, u32[]{:S(2)}, u32[]{:S(2)}) %collective-permute-start.5) | collective-permute-done | bytes 176160 | tf_op jit(solution)/shard_map/ppermute | solution.py:198
  55.6 0.7 pad_add_fusion.index_ref
  56.3 0.4 stack_reshape.4
  56.7 0.5 collective-permute-done.6
  57.2 0.4 stack_reshape.10
  57.7 0.7 fusion.28
  58.4 0.6 fusion.30
  59.1 0.8 %multiply_add_fusion = f32[2,4,208,256]{3,2,1,0:T(8,128)S(1)} fusion(f32[2,4,208,256]{3,2,1,0:T(8,128)S(1)} %fusion.30, f32[2,4,104,208]{2,3,1,0:T(8,128)S(1)} %fusion.28, f32[2]{0:T(128)S(1)} %copy-done.1, s32[256]{0:T(256)S(1)} %iota_subtract_fusion, pred[256]{0:T(512)(128)(4,1)S(1)} %iota_compare_fusion.3), kind=kOutput, calls=%fused_computation.50 | convolution fusion | flops 532533248 | bytes 4101384 | tf_op jit(solution)/shard_map/ad,skdc,cb->skab/dot_general | solution.py:277
  59.9 0.2 fusion.85
  60.0 0.2 pad_maximum_fusion.7
  60.2 0.7 slice_bitcast_fusion.3
  60.9 2.0 %pad_maximum_fusion.fl_ref = f32[2,4,4,208,128]{4,3,2,1,0:T(8,128)} fusion(f32[2,1,4,208,128]{4,3,2,1,0:T(8,128)S(1)} %get-tuple-element.30, f32[2,1,4,208,128]{4,3,2,1,0:T(8,128)S(1)} %get-tuple-element.31, f32[2,1,4,208,128]{4,3,2,1,0:T(8,128)S(1)} %get-tuple-element.32, f32[2,1,4,208,128]{4,3,2,1,0:T(8,128)S(1)} %get-tuple-element.29), kind=kLoop, calls=%fused_computation.8 | loop fusion | flops 2555904 | bytes 6815744 | tf_op jit(solution)/shard_map/stack | solution.py:284
  62.9 14.3 %shard_map.28 = f32[2,64,20402]{2,1,0:T(8,128)} custom-call(s32[2]{0:T(128)} %pad_add_fusion.index_ref, f32[2,4,4,208,128]{4,3,2,1,0:T(8,128)} %pad_maximum_fusion.fl_ref), custom_call_target="tpu_custom_call" | custom-call | tf_op jit(solution)/shard_map/pallas_call | solution.py:167
  (22 shorter events, 0.7 us)
Async XLA Ops:
  4.4 6.2 %collective-permute-start = (f32[4,2048]{1,0:T(4,128)S(1)}, f32[4,2048]{1,0:T(4,128)S(1)}, u32[]{:S(2)}, u32[]{:S(2)}) collective-permute-start(f32[4,2048]{1,0:T(4,128)S(1)} %get-tuple-element.27), channel_id=1, source_target_pairs={{0,1},{1,2},{2,3},{3,4},{4,5},{5,6},{6,7},{7,0},{8,9},{9,10},{10,1... | collective-permute-start | bytes 98312 | tf_op jit(solution)/shard_map/ppermute | solution.py:31
  5.0 5.7 %collective-permute-start.1 = (f32[4,2048]{1,0:T(4,128)S(1)}, f32[4,2048]{1,0:T(4,128)S(1)}, u32[]{:S(2)}, u32[]{:S(2)}) collective-permute-start(f32[4,2048]{1,0:T(4,128)S(1)} %get-tuple-element.28), channel_id=1, source_target_pairs={{1,0},{2,1},{3,2},{4,3},{5,4},{6,5},{7,6},{0,7},{9,8},{10,9},{11,1... | collective-permute-start | bytes 98312 | tf_op jit(solution)/shard_map/ppermute | solution.py:34
  23.3 1.6 %copy-start = (f32[2048,2,104]{2,0,1:T(8,128)S(1)}, f32[2048,2,104]{2,0,1:T(8,128)}, u32[]{:S(2)}) copy-start(f32[2048,2,104]{2,0,1:T(8,128)} %pad_maximum_fusion.6) | copy-start | bytes 5111812
  30.8 1.7 %collective-permute-start.2 = (f32[676,128]{1,0:T(8,128)S(1)}, f32[676,128]{1,0:T(8,128)S(1)}, u32[]{:S(2)}, u32[]{:S(2)}) collective-permute-start(f32[676,128]{1,0:T(8,128)S(1)} %select_n.140), channel_id=1, source_target_pairs={{0,1},{1,0},{2,3},{3,2},{4,5},{5,4},{6,7},{7,6},{8,9},{9,8},{10,11... | collective-permute-start | bytes 1038344 | tf_op jit(solution)/shard_map/ppermute | solution.py:182
  32.6 6.8 %collective-permute-start.3 = (f32[344,128]{1,0:T(8,128)S(1)}, f32[344,128]{1,0:T(8,128)S(1)}, u32[]{:S(2)}, u32[]{:S(2)}) collective-permute-start(f32[344,128]{1,0:T(8,128)S(1)} %slice_select_fusion), channel_id=1, source_target_pairs={{0,2},{1,3},{2,0},{3,1},{4,6},{5,7},{6,4},{7,5},{8,10},{9,11},{10,... | collective-permute-start | bytes 528392 | tf_op jit(solution)/shard_map/ppermute | solution.py:193
  39.4 10.6 %collective-permute-start.4 = (f32[344,128]{1,0:T(8,128)S(1)}, f32[344,128]{1,0:T(8,128)S(1)}, u32[]{:S(2)}, u32[]{:S(2)}) collective-permute-start(f32[344,128]{1,0:T(8,128)S(1)} %select_add_fusion.1), channel_id=1, source_target_pairs={{0,4},{1,5},{2,6},{3,7},{4,0},{5,1},{6,2},{7,3},{8,12},{9,13},{10,... | collective-permute-start | bytes 528392 | tf_op jit(solution)/shard_map/ppermute | solution.py:196
  50.0 5.5 %collective-permute-start.5 = (f32[344,128]{1,0:T(8,128)S(1)}, f32[344,128]{1,0:T(8,128)S(1)}, u32[]{:S(2)}, u32[]{:S(2)}) collective-permute-start(f32[344,128]{1,0:T(8,128)S(1)} %add.176), channel_id=1, source_target_pairs={{0,2},{1,3},{2,0},{3,1},{4,6},{5,7},{6,4},{7,5},{8,10},{9,11},{10,... | collective-permute-start | bytes 528392 | tf_op jit(solution)/shard_map/ppermute | solution.py:198
  55.5 1.7 %collective-permute-start.6 = (f32[676,128]{1,0:T(8,128)S(1)}, f32[676,128]{1,0:T(8,128)S(1)}, u32[]{:S(2)}, u32[]{:S(2)}) collective-permute-start(f32[676,128]{1,0:T(8,128)S(1)} %fusion.38), channel_id=1, source_target_pairs={{0,1},{1,0},{2,3},{3,2},{4,5},{5,4},{6,7},{7,6},{8,9},{9,8},{10,11... | collective-permute-start | bytes 1038344 | tf_op jit(solution)/shard_map/ppermute | solution.py:213
  57.7 1.4 %copy-start.1 = (f32[2]{0:T(128)S(1)}, f32[2]{0:T(128)}, u32[]{:S(2)}) copy-start(f32[2]{0:T(128)} %constant.117.clone) | copy-start | bytes 28

commit v16 on v15

--- a/solution.py
+++ b/solution.py
@@ -13,7 +13,7 @@
 KEEP = 201
 ORDERS = 10201
 BLOCK_ROWS = 8
-STEP_ROWS = 16
+STEP_ROWS = 32
 COPIES = 4
 COPY_STEP = 28
 LANES = 128

time: 78.1 us -> 77.5 us (level)
  no operation moved by 1% of the time
where the time goes in v16:
time: 77.5 us; the launch traced here: 76.7 us
  waiting for transfers between devices  19.8 us (26%)
  other arithmetic  17.7 us (23%)
  Pallas kernels  13.8 us (18%)
  starting transfers between devices  10.1 us (13%)
  local copies, waits for them, and re-layouts  7.69 us (10%)
  matrix products  7.32 us (9%)
    pallas_call x1, Pallas kernels, assemble(): pl.pallas_call(assemble_kernel, grid_spec=grid_spec, out_shape=jax.ShapeD...  13.8 us
    ppermute x1, waiting for transfers between devices, line_sum(): lax.ppermute(kept, 'slab', [(i, i ^ bit) for i in range(devices)])  7.92 us
    ppermute x1, waiting for transfers between devices, line_sum(): kept = kept + lax.ppermute(sent, 'slab', pair)  5.16 us
    another operation x3, other arithmetic, shards(): jnp.stack([permit, contrast * normal_x * normal_x, contrast * normal_x *...  4.94 us
    ppermute x1, waiting for transfers between devices, line_sum(): back = lax.ppermute(kept, 'slab', pair)  4.72 us
    dot_general x1, matrix products, shards(): jnp.einsum('kxy,ycn->kxcn', fields, col_table, precision=lax.Precision.HIGH)  4.28 us
    ppermute x1, starting transfers between devices, extended_2(): lax.ppermute(lax.slice_in_dim(block, 0, width, axis=dim), axis, backward)  4.09 us
    div x3, other arithmetic, smooth_once(): (4.0 * middle + extended[:-2] + extended[2:] + jnp.roll(middle, 1, 1) + j...  3.89 us
  transfers between devices with their start and end apart: 7, of which 7 were waited for; matrix products, arithmetic and copies ran while one was open for 3% of the time, Pallas kernels for 0%

profile of v16, /device:TPU:0, one launch (start us, length us, event | category | flops | bytes accessed | tf_op | source)
XLA Modules:
  0.0 76.7 jit_solution(17296022906354429207)
XLA Ops:
  0.0 0.1 fusion.66
  0.2 0.2 fusion.68
  0.3 2.3 %select_add_fusion = f32[256,2048]{1,0:T(8,128)S(1)} fusion(s32[256,2048]{1,0:T(8,128)} %param.2), kind=kLoop, calls=%fused_computation.48 | loop fusion | flops 5767168 | bytes 4194304 | tf_op jit(solution)/shard_map/add | solution.py:42
  2.7 0.3 multiply_subtract_fusion
  3.0 1.5 %pad_maximum_fusion.6 = f32[2048,2,104]{2,0,1:T(8,128)} fusion(f32[2048,1,104]{2,0,1:T(8,128)S(1)} %bitcast.74, f32[2048,1,104]{2,0,1:T(8,128)S(1)} %bitcast.73), kind=kLoop, calls=%fused_computation.39 | loop fusion | flops 425984 | bytes 3407872 | tf_op jit(solution)/shard_map/stack | solution.py:243
  4.4 0.5 collective-permute-start
  5.0 4.1 %collective-permute-start.1 = (f32[4,2048]{1,0:T(4,128)S(1)}, f32[4,2048]{1,0:T(4,128)S(1)}, u32[]{:S(2)}, u32[]{:S(2)}) collective-permute-start(f32[4,2048]{1,0:T(4,128)S(1)} %get-tuple-element.28), channel_id=1, source_target_pairs={{1,0},{2,1},{3,2},{4,3},{5,4},{6,5},{7,6},{0,7},{9,8},{10,9},{11,1... | collective-permute-start | bytes 98312 | tf_op jit(solution)/shard_map/ppermute | solution.py:34
  9.1 0.9 %fusion.46 = (f32[1,208,256]{2,1,0:T(8,128)S(1)}, f32[1,208,256]{2,1,0:T(8,128)S(1)}) fusion(s32[256]{0:T(256)S(1)} %iota_add_fusion, s32[208]{0:T(256)S(1)} %iota_subtract_fusion.2), kind=kLoop, calls=%fused_computation.96 | loop fusion | flops 745472 | bytes 427840 | tf_op jit(solution)/shard_map/cos | solution.py:73
  10.0 0.6 collective-permute-done
  10.7 0.3 pad_maximum_fusion.5
  11.0 0.9 %fusion.83 = (f32[262,2047]{1,0:T(8,128)S(1)}, f32[262,2047]{1,0:T(8,128)S(1)}) fusion(f32[264,2048]{1,0:T(8,128)S(1)} %pad_maximum_fusion.5), kind=kLoop, calls=%fused_computation.147 | loop fusion | bytes 8581024 | tf_op jit(solution)/shard_map/jit(_roll_static)/slice | solution.py:55
  11.8 2.1 %fusion.15 = f32[262,2048]{1,0:T(8,128)S(1)} fusion(f32[4,2048]{1,0:T(4,128)S(1)} %collective-permute-done.1, f32[256,2048]{1,0:T(8,128)S(1)} %select_add_fusion, f32[4,2048]{1,0:T(4,128)S(1)} %collective-permute-done, f32[264,2048]{1,0:T(8,128)S(1)} %pad_maximum_fusion.5, f32[262,2047]{1,0:T(8,128)S(1)} %get-tuple-element.26, ...), kind=kLoop, calls=%fused_computation.26 | loop fusion | flops 6438912 | bytes 15038416 | tf_op jit(solution)/shard_map/div | solution.py:50
  14.0 0.9 %fusion.81 = (f32[260,2047]{1,0:T(8,128)S(1)}, f32[260,2047]{1,0:T(8,128)S(1)}) fusion(f32[262,2048]{1,0:T(8,128)S(1)} %fusion.15), kind=kLoop, calls=%fused_computation.145 | loop fusion | bytes 8515520 | tf_op jit(solution)/shard_map/jit(_roll_static)/slice | solution.py:55
  15.0 0.9 %fusion.12 = f32[260,2048]{1,0:T(8,128)S(1)} fusion(f32[262,2048]{1,0:T(8,128)S(1)} %fusion.15, f32[260,2047]{1,0:T(8,128)S(1)} %get-tuple-element.22, f32[260,1]{1,0:T(8,128)S(1)} %get-tuple-element.24, f32[260,1]{1,0:T(8,128)S(1)} %get-tuple-element.23, f32[260,2047]{1,0:T(8,128)S(1)} %get-tuple-element.21), kind=kLoop, calls=%fused_computation.20 | loop fusion | flops 4259840 | bytes 12779520 | tf_op jit(solution)/shard_map/div | solution.py:50
  15.9 0.9 %fusion.79 = (f32[258,2047]{1,0:T(8,128)S(1)}, f32[258,2047]{1,0:T(8,128)S(1)}) fusion(f32[260,2048]{1,0:T(8,128)S(1)} %fusion.12), kind=kLoop, calls=%fused_computation.143 | loop fusion | bytes 8450016 | tf_op jit(solution)/shard_map/jit(_roll_static)/slice | solution.py:55
  16.9 0.9 %fusion.9 = f32[258,2048]{1,0:T(8,128)S(1)} fusion(f32[260,2048]{1,0:T(8,128)S(1)} %fusion.12, f32[258,2047]{1,0:T(8,128)S(1)} %get-tuple-element.18, f32[258,1]{1,0:T(8,128)S(1)} %get-tuple-element.20, f32[258,1]{1,0:T(8,128)S(1)} %get-tuple-element.19, f32[258,2047]{1,0:T(8,128)S(1)} %get-tuple-element.17), kind=kLoop, calls=%fused_computation.14 | loop fusion | flops 4227072 | bytes 12681216 | tf_op jit(solution)/shard_map/div | solution.py:50
  17.7 1.1 %fusion.77 = (f32[256,2047]{1,0:T(8,128)S(1)}, f32[256,2047]{1,0:T(8,128)S(1)}) fusion(f32[258,2048]{1,0:T(8,128)S(1)} %fusion.9), kind=kLoop, calls=%fused_computation.141 | loop fusion | bytes 8384512 | tf_op jit(solution)/shard_map/jit(_roll_static)/slice | solution.py:62
  18.9 2.1 %multiply_bitcast_fusion.1 = (f32[1,256,2048]{2,1,0:T(8,128)S(1)}, f32[256,2048]{1,0:T(8,128)S(1)}) fusion(f32[256,2048]{1,0:T(8,128)S(1)} %select_add_fusion, f32[256,2047]{1,0:T(8,128)S(1)} %get-tuple-element.14, f32[256,1]{1,0:T(8,128)S(1)} %get-tuple-element.16, f32[256,1]{1,0:T(8,128)S(1)} %get-tuple-element.15, f32[256,2047]{1,0:T(8,128)S(1)} %get-tuple-element.13, ...), kind=kLoop, calls=%fused_computation.44 | loop fusion | flops 7864320 | bytes 14680064 | tf_op jit(solution)/shard_map/stack | solution.py:254
  21.1 2.3 %multiply_bitcast_fusion = (f32[1,256,2048]{2,1,0:T(8,128)S(1)}, f32[256,2048]{1,0:T(8,128)S(1)}) fusion(f32[256,2048]{1,0:T(8,128)S(1)} %get-tuple-element.10, f32[256,2048]{1,0:T(8,128)S(1)} %select_add_fusion, f32[258,2048]{1,0:T(8,128)S(1)} %fusion.9, f32[256,2047]{1,0:T(8,128)S(1)} %get-tuple-element.14, f32[256,1]{1,0:T(8,128)S(1)} %get-tuple-element.16, ...), kind=kLoop, calls=%fused_computation.43 | loop fusion | flops 7864320 | bytes 16777216 | tf_op jit(solution)/shard_map/stack | solution.py:254
  23.4 0.5 fusion.18
  23.9 1.1 %copy-done = f32[2048,2,104]{2,0,1:T(8,128)S(1)} copy-done((f32[2048,2,104]{2,0,1:T(8,128)S(1)}, f32[2048,2,104]{2,0,1:T(8,128)}, u32[]{:S(2)}) %copy-start) | copy-done | bytes 1703960
  24.9 4.3 %fusion.24 = f32[4,256,2,104,1]{1,3,4,2,0:T(8,128)S(1)} fusion(f32[2048,2,104]{2,0,1:T(8,128)S(1)} %copy-done, f32[1,256,2048]{2,1,0:T(8,128)S(1)} %fusion.18, f32[1,256,2048]{2,1,0:T(8,128)S(1)} %get-tuple-element.11, f32[1,256,2048]{2,1,0:T(8,128)S(1)} %get-tuple-element.9, f32[1,256,2048]{2,1,0:T(8,128)S(1)} %bitcast.72), kind=kOutput, calls=%fused_computation.52 | convolution fusion | flops 2623537152 | bytes 10944512 | tf_op jit(solution)/shard_map/kxy,ycn->kxcn/dot_general | solution.py:262
  29.2 0.9 %convolution_bitcast_fusion = f32[2,4,208,2,104]{2,4,0,3,1:T(8,128)S(1)} fusion(f32[4,256,2,104,1]{1,3,4,2,0:T(8,128)S(1)} %fusion.24, f32[1,208,256]{2,1,0:T(8,128)S(1)} %get-tuple-element.42, f32[1,208,256]{2,1,0:T(8,128)S(1)} %get-tuple-element.41), kind=kOutput, calls=%fused_computation.51 | convolution fusion | flops 531734528 | bytes 2662400 | tf_op jit(solution)/shard_map/smx,kxcn->skmcn/dot_general | solution.py:74
  30.1 0.1 broadcast_select_fusion
  30.2 0.2 copy.7
  30.4 0.4 select_n.140
  30.8 0.4 collective-permute-start.2
  31.2 0.2 copy.6
  31.3 0.4 select_n.138
  31.7 0.8 %collective-permute-done.2 = f32[676,128]{1,0:T(8,128)S(1)} collective-permute-done((f32[676,128]{1,0:T(8,128)S(1)}, f32[676,128]{1,0:T(8,128)S(1)}, u32[]{:S(2)}, u32[]{:S(2)}) %collective-permute-start.2) | collective-permute-done | bytes 346144 | tf_op jit(solution)/shard_map/ppermute | solution.py:182
  32.6 1.6 %collective-permute-start.3 = (f32[344,128]{1,0:T(8,128)S(1)}, f32[344,128]{1,0:T(8,128)S(1)}, u32[]{:S(2)}, u32[]{:S(2)}) collective-permute-start(f32[344,128]{1,0:T(8,128)S(1)} %slice_select_fusion), channel_id=1, source_target_pairs={{0,2},{1,3},{2,0},{3,1},{4,6},{5,7},{6,4},{7,5},{8,10},{9,11},{10,... | collective-permute-start | bytes 528392 | tf_op jit(solution)/shard_map/ppermute | solution.py:193
  34.2 5.2 %collective-permute-done.3 = f32[344,128]{1,0:T(8,128)S(1)} collective-permute-done((f32[344,128]{1,0:T(8,128)S(1)}, f32[344,128]{1,0:T(8,128)S(1)}, u32[]{:S(2)}, u32[]{:S(2)}) %collective-permute-start.3) | collective-permute-done | bytes 176160 | tf_op jit(solution)/shard_map/ppermute | solution.py:193
  39.4 2.7 %collective-permute-start.4 = (f32[344,128]{1,0:T(8,128)S(1)}, f32[344,128]{1,0:T(8,128)S(1)}, u32[]{:S(2)}, u32[]{:S(2)}) collective-permute-start(f32[344,128]{1,0:T(8,128)S(1)} %select_add_fusion.1), channel_id=1, source_target_pairs={{0,4},{1,5},{2,6},{3,7},{4,0},{5,1},{6,2},{7,3},{8,12},{9,13},{10,... | collective-permute-start | bytes 528392 | tf_op jit(solution)/shard_map/ppermute | solution.py:196
  42.0 7.9 %collective-permute-done.4 = f32[344,128]{1,0:T(8,128)S(1)} collective-permute-done((f32[344,128]{1,0:T(8,128)S(1)}, f32[344,128]{1,0:T(8,128)S(1)}, u32[]{:S(2)}, u32[]{:S(2)}) %collective-permute-start.4) | collective-permute-done | bytes 176160 | tf_op jit(solution)/shard_map/ppermute | solution.py:196
  50.0 0.8 %collective-permute-start.5 = (f32[344,128]{1,0:T(8,128)S(1)}, f32[344,128]{1,0:T(8,128)S(1)}, u32[]{:S(2)}, u32[]{:S(2)}) collective-permute-start(f32[344,128]{1,0:T(8,128)S(1)} %add.176), channel_id=1, source_target_pairs={{0,2},{1,3},{2,0},{3,1},{4,6},{5,7},{6,4},{7,5},{8,10},{9,11},{10,... | collective-permute-start | bytes 528392 | tf_op jit(solution)/shard_map/ppermute | solution.py:198
  50.8 4.7 %collective-permute-done.5 = f32[344,128]{1,0:T(8,128)S(1)} collective-permute-done((f32[344,128]{1,0:T(8,128)S(1)}, f32[344,128]{1,0:T(8,128)S(1)}, u32[]{:S(2)}, u32[]{:S(2)}) %collective-permute-start.5) | collective-permute-done | bytes 176160 | tf_op jit(solution)/shard_map/ppermute | solution.py:198
  55.6 0.7 pad_add_fusion.index_ref
  56.3 0.4 stack_reshape.4
  56.7 0.5 collective-permute-done.6
  57.2 0.4 stack_reshape.10
  57.7 0.7 fusion.28
  58.4 0.6 fusion.30
  59.1 0.8 %multiply_add_fusion = f32[2,4,208,256]{3,2,1,0:T(8,128)S(1)} fusion(f32[2,4,208,256]{3,2,1,0:T(8,128)S(1)} %fusion.30, f32[2,4,104,208]{2,3,1,0:T(8,128)S(1)} %fusion.28, f32[2]{0:T(128)S(1)} %copy-done.1, s32[256]{0:T(256)S(1)} %iota_subtract_fusion, pred[256]{0:T(512)(128)(4,1)S(1)} %iota_compare_fusion.3), kind=kOutput, calls=%fused_computation.50 | convolution fusion | flops 532533248 | bytes 4101384 | tf_op jit(solution)/shard_map/ad,skdc,cb->skab/dot_general | solution.py:277
  59.9 0.2 fusion.85
  60.0 0.2 pad_maximum_fusion.7
  60.2 0.7 slice_bitcast_fusion.3
  60.9 2.0 %pad_maximum_fusion.fl_ref = f32[2,4,4,208,128]{4,3,2,1,0:T(8,128)} fusion(f32[2,1,4,208,128]{4,3,2,1,0:T(8,128)S(1)} %get-tuple-element.30, f32[2,1,4,208,128]{4,3,2,1,0:T(8,128)S(1)} %get-tuple-element.31, f32[2,1,4,208,128]{4,3,2,1,0:T(8,128)S(1)} %get-tuple-element.32, f32[2,1,4,208,128]{4,3,2,1,0:T(8,128)S(1)} %get-tuple-element.29), kind=kLoop, calls=%fused_computation.8 | loop fusion | flops 2555904 | bytes 6815744 | tf_op jit(solution)/shard_map/stack | solution.py:284
  62.9 13.8 %shard_map.28 = f32[2,64,20402]{2,1,0:T(8,128)} custom-call(s32[2]{0:T(128)} %pad_add_fusion.index_ref, f32[2,4,4,208,128]{4,3,2,1,0:T(8,128)} %pad_maximum_fusion.fl_ref), custom_call_target="tpu_custom_call" | custom-call | tf_op jit(solution)/shard_map/pallas_call | solution.py:167
  (22 shorter events, 0.7 us)
Async XLA Ops:
  4.4 6.2 %collective-permute-start = (f32[4,2048]{1,0:T(4,128)S(1)}, f32[4,2048]{1,0:T(4,128)S(1)}, u32[]{:S(2)}, u32[]{:S(2)}) collective-permute-start(f32[4,2048]{1,0:T(4,128)S(1)} %get-tuple-element.27), channel_id=1, source_target_pairs={{0,1},{1,2},{2,3},{3,4},{4,5},{5,6},{6,7},{7,0},{8,9},{9,10},{10,1... | collective-permute-start | bytes 98312 | tf_op jit(solution)/shard_map/ppermute | solution.py:31
  5.0 5.7 %collective-permute-start.1 = (f32[4,2048]{1,0:T(4,128)S(1)}, f32[4,2048]{1,0:T(4,128)S(1)}, u32[]{:S(2)}, u32[]{:S(2)}) collective-permute-start(f32[4,2048]{1,0:T(4,128)S(1)} %get-tuple-element.28), channel_id=1, source_target_pairs={{1,0},{2,1},{3,2},{4,3},{5,4},{6,5},{7,6},{0,7},{9,8},{10,9},{11,1... | collective-permute-start | bytes 98312 | tf_op jit(solution)/shard_map/ppermute | solution.py:34
  23.3 1.6 %copy-start = (f32[2048,2,104]{2,0,1:T(8,128)S(1)}, f32[2048,2,104]{2,0,1:T(8,128)}, u32[]{:S(2)}) copy-start(f32[2048,2,104]{2,0,1:T(8,128)} %pad_maximum_fusion.6) | copy-start | bytes 5111812
  30.8 1.7 %collective-permute-start.2 = (f32[676,128]{1,0:T(8,128)S(1)}, f32[676,128]{1,0:T(8,128)S(1)}, u32[]{:S(2)}, u32[]{:S(2)}) collective-permute-start(f32[676,128]{1,0:T(8,128)S(1)} %select_n.140), channel_id=1, source_target_pairs={{0,1},{1,0},{2,3},{3,2},{4,5},{5,4},{6,7},{7,6},{8,9},{9,8},{10,11... | collective-permute-start | bytes 1038344 | tf_op jit(solution)/shard_map/ppermute | solution.py:182
  32.6 6.8 %collective-permute-start.3 = (f32[344,128]{1,0:T(8,128)S(1)}, f32[344,128]{1,0:T(8,128)S(1)}, u32[]{:S(2)}, u32[]{:S(2)}) collective-permute-start(f32[344,128]{1,0:T(8,128)S(1)} %slice_select_fusion), channel_id=1, source_target_pairs={{0,2},{1,3},{2,0},{3,1},{4,6},{5,7},{6,4},{7,5},{8,10},{9,11},{10,... | collective-permute-start | bytes 528392 | tf_op jit(solution)/shard_map/ppermute | solution.py:193
  39.4 10.6 %collective-permute-start.4 = (f32[344,128]{1,0:T(8,128)S(1)}, f32[344,128]{1,0:T(8,128)S(1)}, u32[]{:S(2)}, u32[]{:S(2)}) collective-permute-start(f32[344,128]{1,0:T(8,128)S(1)} %select_add_fusion.1), channel_id=1, source_target_pairs={{0,4},{1,5},{2,6},{3,7},{4,0},{5,1},{6,2},{7,3},{8,12},{9,13},{10,... | collective-permute-start | bytes 528392 | tf_op jit(solution)/shard_map/ppermute | solution.py:196
  50.0 5.5 %collective-permute-start.5 = (f32[344,128]{1,0:T(8,128)S(1)}, f32[344,128]{1,0:T(8,128)S(1)}, u32[]{:S(2)}, u32[]{:S(2)}) collective-permute-start(f32[344,128]{1,0:T(8,128)S(1)} %add.176), channel_id=1, source_target_pairs={{0,2},{1,3},{2,0},{3,1},{4,6},{5,7},{6,4},{7,5},{8,10},{9,11},{10,... | collective-permute-start | bytes 528392 | tf_op jit(solution)/shard_map/ppermute | solution.py:198
  55.5 1.7 %collective-permute-start.6 = (f32[676,128]{1,0:T(8,128)S(1)}, f32[676,128]{1,0:T(8,128)S(1)}, u32[]{:S(2)}, u32[]{:S(2)}) collective-permute-start(f32[676,128]{1,0:T(8,128)S(1)} %fusion.38), channel_id=1, source_target_pairs={{0,1},{1,0},{2,3},{3,2},{4,5},{5,4},{6,7},{7,6},{8,9},{9,8},{10,11... | collective-permute-start | bytes 1038344 | tf_op jit(solution)/shard_map/ppermute | solution.py:213
  57.7 1.4 %copy-start.1 = (f32[2]{0:T(128)S(1)}, f32[2]{0:T(128)}, u32[]{:S(2)}) copy-start(f32[2]{0:T(128)} %constant.117.clone) | copy-start | bytes 28

commit v17 on v15

--- a/solution.py
+++ b/solution.py
@@ -1,4 +1,5 @@
 import functools
+import itertools
 import math
 
 import jax
@@ -93,17 +94,16 @@
 
 
 def assemble_kernel(index_ref, fl_ref, o_ref, z_ref):
-    s = pl.program_id(0)
-    rb = pl.program_id(1)
-    rows = o_ref.shape[1] * pl.num_programs(1)
+    rb = pl.program_id(0)
+    rows = o_ref.shape[1] * pl.num_programs(0)
     spacing = ORDERS // (rows * index_ref[1] // 2)
     centre = (HARM - 1) // 2
-    span = z_ref.shape[2] // BLOCK_ROWS - BLOCK_ROWS
+    span = z_ref.shape[-2] // BLOCK_ROWS - BLOCK_ROWS
     lane_iota = lax.broadcasted_iota(jnp.int32, (span, LANES), 1)
     sub = lax.broadcasted_iota(jnp.int32, (BLOCK_ROWS, LANES), 0)
     lane = lax.broadcasted_iota(jnp.int32, (BLOCK_ROWS, LANES), 1)
-    for part in range(o_ref.shape[1] // BLOCK_ROWS):
-        z_part = z_ref.at[part]
+    for part, s in itertools.product(range(o_ref.shape[1] // BLOCK_ROWS), range(2)):
+        z_part = z_ref.at[part, s]
         for rr in range(BLOCK_ROWS):
             row = rb * o_ref.shape[1] + part * BLOCK_ROWS + rr
             order_index = (index_ref[0] * rows + row) // 2 * spacing
@@ -126,10 +126,12 @@
             spot = (sub == rr) & (lane == second)
             for h in range(2):
                 combo = 2 * (rr % 2) + h
-                x = fl_ref[0, copy, combo, pl.ds(base, span), :]
+                x = fl_ref[s, copy, combo, pl.ds(base, span), :]
                 x = pltpu.roll(x, shift, 1)
                 z_part[h, pl.ds(dest, span, stride=BLOCK_ROWS), :] = x
-                d = jnp.where(s == 0, diagonal[h], jnp.float32(0.0))
+                if s:
+                    continue
+                d = diagonal[h]
                 tile = z_part[h, pl.ds(spot_tile, BLOCK_ROWS), :]
                 z_part[h, pl.ds(spot_tile, BLOCK_ROWS), :] = tile + jnp.where(spot, d, jnp.float32(0.0))
         placed = {}
@@ -144,7 +146,7 @@
                 acc = src if acc is None else jnp.where(lane >= l0, src, acc)
             if width < LANES:
                 acc = acc[:, :width]
-            o_ref[0, pl.ds(part * BLOCK_ROWS, BLOCK_ROWS), pl.ds(start, width)] = acc
+            o_ref[s, pl.ds(part * BLOCK_ROWS, BLOCK_ROWS), pl.ds(start, width)] = acc
 
 
 def assemble(index, tables, rows):
@@ -153,14 +155,14 @@
     total = 2 * ORDERS
     grid_spec = pltpu.PrefetchScalarGridSpec(
         num_scalar_prefetch=1,
-        grid=(2, n_blocks),
+        grid=(n_blocks,),
         in_specs=[
-            pl.BlockSpec((1,) + tables.shape[1:], lambda s, rb, *_: (s, 0, 0, 0, 0)),
+            pl.BlockSpec(tables.shape, lambda rb, *_: (0, 0, 0, 0, 0)),
         ],
-        out_specs=pl.BlockSpec((1, STEP_ROWS, total), lambda s, rb, *_: (s, rb, 0)),
+        out_specs=pl.BlockSpec((2, STEP_ROWS, total), lambda rb, *_: (0, rb, 0)),
         scratch_shapes=[
             pltpu.VMEM(
-                (STEP_ROWS // BLOCK_ROWS, 2, (span + BLOCK_ROWS) * BLOCK_ROWS, LANES), jnp.float32
+                (STEP_ROWS // BLOCK_ROWS, 2, 2, (span + BLOCK_ROWS) * BLOCK_ROWS, LANES), jnp.float32
             )
         ],
     )
@@ -168,7 +170,7 @@
         assemble_kernel,
         grid_spec=grid_spec,
         out_shape=jax.ShapeDtypeStruct((2, rows, total), jnp.float32),
-        compiler_params=pltpu.CompilerParams(dimension_semantics=("arbitrary", "arbitrary")),
+        compiler_params=pltpu.CompilerParams(dimension_semantics=("arbitrary",)),
     )(index, tables)
 
 

time: 78.1 us -> 77.3 us (0.990)
  no operation moved by 1% of the time
where the time goes in v17:
time: 77.3 us; the launch traced here: 76.6 us
  waiting for transfers between devices  19.8 us (26%)
  other arithmetic  17.7 us (23%)
  Pallas kernels  13.7 us (18%)
  starting transfers between devices  10.1 us (13%)
  local copies, waits for them, and re-layouts  7.69 us (10%)
  matrix products  7.32 us (9%)
    pallas_call x1, Pallas kernels, assemble(): pl.pallas_call(assemble_kernel, grid_spec=grid_spec, out_shape=jax.ShapeD...  13.7 us
    ppermute x1, waiting for transfers between devices, line_sum(): lax.ppermute(kept, 'slab', [(i, i ^ bit) for i in range(devices)])  7.92 us
    ppermute x1, waiting for transfers between devices, line_sum(): kept = kept + lax.ppermute(sent, 'slab', pair)  5.16 us
    another operation x3, other arithmetic, shards(): jnp.stack([permit, contrast * normal_x * normal_x, contrast * normal_x *...  4.94 us
    ppermute x1, waiting for transfers between devices, line_sum(): back = lax.ppermute(kept, 'slab', pair)  4.72 us
    dot_general x1, matrix products, shards(): jnp.einsum('kxy,ycn->kxcn', fields, col_table, precision=lax.Precision.HIGH)  4.28 us
    ppermute x1, starting transfers between devices, extended_2(): lax.ppermute(lax.slice_in_dim(block, 0, width, axis=dim), axis, backward)  4.09 us
    div x3, other arithmetic, smooth_once(): (4.0 * middle + extended[:-2] + extended[2:] + jnp.roll(middle, 1, 1) + j...  3.89 us
  transfers between devices with their start and end apart: 7, of which 7 were waited for; matrix products, arithmetic and copies ran while one was open for 3% of the time, Pallas kernels for 0%

profile of v17, /device:TPU:0, one launch (start us, length us, event | category | flops | bytes accessed | tf_op | source)
XLA Modules:
  0.0 76.6 jit_solution(17620137392938214288)
XLA Ops:
  0.0 0.1 fusion.66
  0.2 0.2 fusion.68
  0.3 2.3 %select_add_fusion = f32[256,2048]{1,0:T(8,128)S(1)} fusion(s32[256,2048]{1,0:T(8,128)} %param.2), kind=kLoop, calls=%fused_computation.48 | loop fusion | flops 5767168 | bytes 4194304 | tf_op jit(solution)/shard_map/add | solution.py:43
  2.7 0.3 multiply_subtract_fusion
  3.0 1.5 %pad_maximum_fusion.6 = f32[2048,2,104]{2,0,1:T(8,128)} fusion(f32[2048,1,104]{2,0,1:T(8,128)S(1)} %bitcast.74, f32[2048,1,104]{2,0,1:T(8,128)S(1)} %bitcast.73), kind=kLoop, calls=%fused_computation.39 | loop fusion | flops 425984 | bytes 3407872 | tf_op jit(solution)/shard_map/stack | solution.py:245
  4.4 0.5 collective-permute-start
  5.0 4.1 %collective-permute-start.1 = (f32[4,2048]{1,0:T(4,128)S(1)}, f32[4,2048]{1,0:T(4,128)S(1)}, u32[]{:S(2)}, u32[]{:S(2)}) collective-permute-start(f32[4,2048]{1,0:T(4,128)S(1)} %get-tuple-element.28), channel_id=1, source_target_pairs={{1,0},{2,1},{3,2},{4,3},{5,4},{6,5},{7,6},{0,7},{9,8},{10,9},{11,1... | collective-permute-start | bytes 98312 | tf_op jit(solution)/shard_map/ppermute | solution.py:35
  9.1 0.9 %fusion.46 = (f32[1,208,256]{2,1,0:T(8,128)S(1)}, f32[1,208,256]{2,1,0:T(8,128)S(1)}) fusion(s32[256]{0:T(256)S(1)} %iota_add_fusion, s32[208]{0:T(256)S(1)} %iota_subtract_fusion.2), kind=kLoop, calls=%fused_computation.96 | loop fusion | flops 745472 | bytes 427840 | tf_op jit(solution)/shard_map/cos | solution.py:74
  10.0 0.6 collective-permute-done
  10.7 0.3 pad_maximum_fusion.5
  11.0 0.9 %fusion.83 = (f32[262,2047]{1,0:T(8,128)S(1)}, f32[262,2047]{1,0:T(8,128)S(1)}) fusion(f32[264,2048]{1,0:T(8,128)S(1)} %pad_maximum_fusion.5), kind=kLoop, calls=%fused_computation.147 | loop fusion | bytes 8581024 | tf_op jit(solution)/shard_map/jit(_roll_static)/slice | solution.py:56
  11.8 2.1 %fusion.15 = f32[262,2048]{1,0:T(8,128)S(1)} fusion(f32[4,2048]{1,0:T(4,128)S(1)} %collective-permute-done.1, f32[256,2048]{1,0:T(8,128)S(1)} %select_add_fusion, f32[4,2048]{1,0:T(4,128)S(1)} %collective-permute-done, f32[264,2048]{1,0:T(8,128)S(1)} %pad_maximum_fusion.5, f32[262,2047]{1,0:T(8,128)S(1)} %get-tuple-element.26, ...), kind=kLoop, calls=%fused_computation.26 | loop fusion | flops 6438912 | bytes 15038416 | tf_op jit(solution)/shard_map/div | solution.py:51
  14.0 0.9 %fusion.81 = (f32[260,2047]{1,0:T(8,128)S(1)}, f32[260,2047]{1,0:T(8,128)S(1)}) fusion(f32[262,2048]{1,0:T(8,128)S(1)} %fusion.15), kind=kLoop, calls=%fused_computation.145 | loop fusion | bytes 8515520 | tf_op jit(solution)/shard_map/jit(_roll_static)/slice | solution.py:56
  15.0 0.9 %fusion.12 = f32[260,2048]{1,0:T(8,128)S(1)} fusion(f32[262,2048]{1,0:T(8,128)S(1)} %fusion.15, f32[260,2047]{1,0:T(8,128)S(1)} %get-tuple-element.22, f32[260,1]{1,0:T(8,128)S(1)} %get-tuple-element.24, f32[260,1]{1,0:T(8,128)S(1)} %get-tuple-element.23, f32[260,2047]{1,0:T(8,128)S(1)} %get-tuple-element.21), kind=kLoop, calls=%fused_computation.20 | loop fusion | flops 4259840 | bytes 12779520 | tf_op jit(solution)/shard_map/div | solution.py:51
  15.9 0.9 %fusion.79 = (f32[258,2047]{1,0:T(8,128)S(1)}, f32[258,2047]{1,0:T(8,128)S(1)}) fusion(f32[260,2048]{1,0:T(8,128)S(1)} %fusion.12), kind=kLoop, calls=%fused_computation.143 | loop fusion | bytes 8450016 | tf_op jit(solution)/shard_map/jit(_roll_static)/slice | solution.py:56
  16.9 0.9 %fusion.9 = f32[258,2048]{1,0:T(8,128)S(1)} fusion(f32[260,2048]{1,0:T(8,128)S(1)} %fusion.12, f32[258,2047]{1,0:T(8,128)S(1)} %get-tuple-element.18, f32[258,1]{1,0:T(8,128)S(1)} %get-tuple-element.20, f32[258,1]{1,0:T(8,128)S(1)} %get-tuple-element.19, f32[258,2047]{1,0:T(8,128)S(1)} %get-tuple-element.17), kind=kLoop, calls=%fused_computation.14 | loop fusion | flops 4227072 | bytes 12681216 | tf_op jit(solution)/shard_map/div | solution.py:51
  17.7 1.1 %fusion.77 = (f32[256,2047]{1,0:T(8,128)S(1)}, f32[256,2047]{1,0:T(8,128)S(1)}) fusion(f32[258,2048]{1,0:T(8,128)S(1)} %fusion.9), kind=kLoop, calls=%fused_computation.141 | loop fusion | bytes 8384512 | tf_op jit(solution)/shard_map/jit(_roll_static)/slice | solution.py:63
  18.9 2.1 %multiply_bitcast_fusion.1 = (f32[1,256,2048]{2,1,0:T(8,128)S(1)}, f32[256,2048]{1,0:T(8,128)S(1)}) fusion(f32[256,2048]{1,0:T(8,128)S(1)} %select_add_fusion, f32[256,2047]{1,0:T(8,128)S(1)} %get-tuple-element.14, f32[256,1]{1,0:T(8,128)S(1)} %get-tuple-element.16, f32[256,1]{1,0:T(8,128)S(1)} %get-tuple-element.15, f32[256,2047]{1,0:T(8,128)S(1)} %get-tuple-element.13, ...), kind=kLoop, calls=%fused_computation.44 | loop fusion | flops 7864320 | bytes 14680064 | tf_op jit(solution)/shard_map/stack | solution.py:256
  21.1 2.3 %multiply_bitcast_fusion = (f32[1,256,2048]{2,1,0:T(8,128)S(1)}, f32[256,2048]{1,0:T(8,128)S(1)}) fusion(f32[256,2048]{1,0:T(8,128)S(1)} %get-tuple-element.10, f32[256,2048]{1,0:T(8,128)S(1)} %select_add_fusion, f32[258,2048]{1,0:T(8,128)S(1)} %fusion.9, f32[256,2047]{1,0:T(8,128)S(1)} %get-tuple-element.14, f32[256,1]{1,0:T(8,128)S(1)} %get-tuple-element.16, ...), kind=kLoop, calls=%fused_computation.43 | loop fusion | flops 7864320 | bytes 16777216 | tf_op jit(solution)/shard_map/stack | solution.py:256
  23.4 0.5 fusion.18
  23.9 1.1 %copy-done = f32[2048,2,104]{2,0,1:T(8,128)S(1)} copy-done((f32[2048,2,104]{2,0,1:T(8,128)S(1)}, f32[2048,2,104]{2,0,1:T(8,128)}, u32[]{:S(2)}) %copy-start) | copy-done | bytes 1703960
  24.9 4.3 %fusion.24 = f32[4,256,2,104,1]{1,3,4,2,0:T(8,128)S(1)} fusion(f32[2048,2,104]{2,0,1:T(8,128)S(1)} %copy-done, f32[1,256,2048]{2,1,0:T(8,128)S(1)} %fusion.18, f32[1,256,2048]{2,1,0:T(8,128)S(1)} %get-tuple-element.11, f32[1,256,2048]{2,1,0:T(8,128)S(1)} %get-tuple-element.9, f32[1,256,2048]{2,1,0:T(8,128)S(1)} %bitcast.72), kind=kOutput, calls=%fused_computation.52 | convolution fusion | flops 2623537152 | bytes 10944512 | tf_op jit(solution)/shard_map/kxy,ycn->kxcn/dot_general | solution.py:264
  29.2 0.9 %convolution_bitcast_fusion = f32[2,4,208,2,104]{2,4,0,3,1:T(8,128)S(1)} fusion(f32[4,256,2,104,1]{1,3,4,2,0:T(8,128)S(1)} %fusion.24, f32[1,208,256]{2,1,0:T(8,128)S(1)} %get-tuple-element.42, f32[1,208,256]{2,1,0:T(8,128)S(1)} %get-tuple-element.41), kind=kOutput, calls=%fused_computation.51 | convolution fusion | flops 531734528 | bytes 2662400 | tf_op jit(solution)/shard_map/smx,kxcn->skmcn/dot_general | solution.py:75
  30.1 0.1 broadcast_select_fusion
  30.2 0.2 copy.7
  30.4 0.4 select_n.140
  30.8 0.4 collective-permute-start.2
  31.2 0.2 copy.6
  31.3 0.4 select_n.138
  31.7 0.8 %collective-permute-done.2 = f32[676,128]{1,0:T(8,128)S(1)} collective-permute-done((f32[676,128]{1,0:T(8,128)S(1)}, f32[676,128]{1,0:T(8,128)S(1)}, u32[]{:S(2)}, u32[]{:S(2)}) %collective-permute-start.2) | collective-permute-done | bytes 346144 | tf_op jit(solution)/shard_map/ppermute | solution.py:184
  32.6 1.6 %collective-permute-start.3 = (f32[344,128]{1,0:T(8,128)S(1)}, f32[344,128]{1,0:T(8,128)S(1)}, u32[]{:S(2)}, u32[]{:S(2)}) collective-permute-start(f32[344,128]{1,0:T(8,128)S(1)} %slice_select_fusion), channel_id=1, source_target_pairs={{0,2},{1,3},{2,0},{3,1},{4,6},{5,7},{6,4},{7,5},{8,10},{9,11},{10,... | collective-permute-start | bytes 528392 | tf_op jit(solution)/shard_map/ppermute | solution.py:195
  34.2 5.2 %collective-permute-done.3 = f32[344,128]{1,0:T(8,128)S(1)} collective-permute-done((f32[344,128]{1,0:T(8,128)S(1)}, f32[344,128]{1,0:T(8,128)S(1)}, u32[]{:S(2)}, u32[]{:S(2)}) %collective-permute-start.3) | collective-permute-done | bytes 176160 | tf_op jit(solution)/shard_map/ppermute | solution.py:195
  39.4 2.7 %collective-permute-start.4 = (f32[344,128]{1,0:T(8,128)S(1)}, f32[344,128]{1,0:T(8,128)S(1)}, u32[]{:S(2)}, u32[]{:S(2)}) collective-permute-start(f32[344,128]{1,0:T(8,128)S(1)} %select_add_fusion.1), channel_id=1, source_target_pairs={{0,4},{1,5},{2,6},{3,7},{4,0},{5,1},{6,2},{7,3},{8,12},{9,13},{10,... | collective-permute-start | bytes 528392 | tf_op jit(solution)/shard_map/ppermute | solution.py:198
  42.0 7.9 %collective-permute-done.4 = f32[344,128]{1,0:T(8,128)S(1)} collective-permute-done((f32[344,128]{1,0:T(8,128)S(1)}, f32[344,128]{1,0:T(8,128)S(1)}, u32[]{:S(2)}, u32[]{:S(2)}) %collective-permute-start.4) | collective-permute-done | bytes 176160 | tf_op jit(solution)/shard_map/ppermute | solution.py:198
  50.0 0.8 %collective-permute-start.5 = (f32[344,128]{1,0:T(8,128)S(1)}, f32[344,128]{1,0:T(8,128)S(1)}, u32[]{:S(2)}, u32[]{:S(2)}) collective-permute-start(f32[344,128]{1,0:T(8,128)S(1)} %add.176), channel_id=1, source_target_pairs={{0,2},{1,3},{2,0},{3,1},{4,6},{5,7},{6,4},{7,5},{8,10},{9,11},{10,... | collective-permute-start | bytes 528392 | tf_op jit(solution)/shard_map/ppermute | solution.py:200
  50.8 4.7 %collective-permute-done.5 = f32[344,128]{1,0:T(8,128)S(1)} collective-permute-done((f32[344,128]{1,0:T(8,128)S(1)}, f32[344,128]{1,0:T(8,128)S(1)}, u32[]{:S(2)}, u32[]{:S(2)}) %collective-permute-start.5) | collective-permute-done | bytes 176160 | tf_op jit(solution)/shard_map/ppermute | solution.py:200
  55.6 0.7 pad_add_fusion.index_ref
  56.3 0.4 stack_reshape.4
  56.7 0.5 collective-permute-done.6
  57.2 0.4 stack_reshape.10
  57.7 0.7 fusion.28
  58.4 0.6 fusion.30
  59.1 0.8 %multiply_add_fusion = f32[2,4,208,256]{3,2,1,0:T(8,128)S(1)} fusion(f32[2,4,208,256]{3,2,1,0:T(8,128)S(1)} %fusion.30, f32[2,4,104,208]{2,3,1,0:T(8,128)S(1)} %fusion.28, f32[2]{0:T(128)S(1)} %copy-done.1, s32[256]{0:T(256)S(1)} %iota_subtract_fusion, pred[256]{0:T(512)(128)(4,1)S(1)} %iota_compare_fusion.3), kind=kOutput, calls=%fused_computation.50 | convolution fusion | flops 532533248 | bytes 4101384 | tf_op jit(solution)/shard_map/ad,skdc,cb->skab/dot_general | solution.py:279
  59.9 0.2 fusion.85
  60.0 0.2 pad_maximum_fusion.7
  60.2 0.7 slice_bitcast_fusion.3
  60.9 2.0 %pad_maximum_fusion.fl_ref = f32[2,4,4,208,128]{4,3,2,1,0:T(8,128)} fusion(f32[2,1,4,208,128]{4,3,2,1,0:T(8,128)S(1)} %get-tuple-element.30, f32[2,1,4,208,128]{4,3,2,1,0:T(8,128)S(1)} %get-tuple-element.31, f32[2,1,4,208,128]{4,3,2,1,0:T(8,128)S(1)} %get-tuple-element.32, f32[2,1,4,208,128]{4,3,2,1,0:T(8,128)S(1)} %get-tuple-element.29), kind=kLoop, calls=%fused_computation.8 | loop fusion | flops 2555904 | bytes 6815744 | tf_op jit(solution)/shard_map/stack | solution.py:286
  62.9 13.7 %shard_map.28 = f32[2,64,20402]{2,1,0:T(8,128)} custom-call(s32[2]{0:T(128)} %pad_add_fusion.index_ref, f32[2,4,4,208,128]{4,3,2,1,0:T(8,128)} %pad_maximum_fusion.fl_ref), custom_call_target="tpu_custom_call" | custom-call | tf_op jit(solution)/shard_map/pallas_call | solution.py:169
  (22 shorter events, 0.7 us)
Async XLA Ops:
  4.4 6.2 %collective-permute-start = (f32[4,2048]{1,0:T(4,128)S(1)}, f32[4,2048]{1,0:T(4,128)S(1)}, u32[]{:S(2)}, u32[]{:S(2)}) collective-permute-start(f32[4,2048]{1,0:T(4,128)S(1)} %get-tuple-element.27), channel_id=1, source_target_pairs={{0,1},{1,2},{2,3},{3,4},{4,5},{5,6},{6,7},{7,0},{8,9},{9,10},{10,1... | collective-permute-start | bytes 98312 | tf_op jit(solution)/shard_map/ppermute | solution.py:32
  5.0 5.7 %collective-permute-start.1 = (f32[4,2048]{1,0:T(4,128)S(1)}, f32[4,2048]{1,0:T(4,128)S(1)}, u32[]{:S(2)}, u32[]{:S(2)}) collective-permute-start(f32[4,2048]{1,0:T(4,128)S(1)} %get-tuple-element.28), channel_id=1, source_target_pairs={{1,0},{2,1},{3,2},{4,3},{5,4},{6,5},{7,6},{0,7},{9,8},{10,9},{11,1... | collective-permute-start | bytes 98312 | tf_op jit(solution)/shard_map/ppermute | solution.py:35
  23.3 1.6 %copy-start = (f32[2048,2,104]{2,0,1:T(8,128)S(1)}, f32[2048,2,104]{2,0,1:T(8,128)}, u32[]{:S(2)}) copy-start(f32[2048,2,104]{2,0,1:T(8,128)} %pad_maximum_fusion.6) | copy-start | bytes 5111812
  30.8 1.7 %collective-permute-start.2 = (f32[676,128]{1,0:T(8,128)S(1)}, f32[676,128]{1,0:T(8,128)S(1)}, u32[]{:S(2)}, u32[]{:S(2)}) collective-permute-start(f32[676,128]{1,0:T(8,128)S(1)} %select_n.140), channel_id=1, source_target_pairs={{0,1},{1,0},{2,3},{3,2},{4,5},{5,4},{6,7},{7,6},{8,9},{9,8},{10,11... | collective-permute-start | bytes 1038344 | tf_op jit(solution)/shard_map/ppermute | solution.py:184
  32.6 6.8 %collective-permute-start.3 = (f32[344,128]{1,0:T(8,128)S(1)}, f32[344,128]{1,0:T(8,128)S(1)}, u32[]{:S(2)}, u32[]{:S(2)}) collective-permute-start(f32[344,128]{1,0:T(8,128)S(1)} %slice_select_fusion), channel_id=1, source_target_pairs={{0,2},{1,3},{2,0},{3,1},{4,6},{5,7},{6,4},{7,5},{8,10},{9,11},{10,... | collective-permute-start | bytes 528392 | tf_op jit(solution)/shard_map/ppermute | solution.py:195
  39.4 10.6 %collective-permute-start.4 = (f32[344,128]{1,0:T(8,128)S(1)}, f32[344,128]{1,0:T(8,128)S(1)}, u32[]{:S(2)}, u32[]{:S(2)}) collective-permute-start(f32[344,128]{1,0:T(8,128)S(1)} %select_add_fusion.1), channel_id=1, source_target_pairs={{0,4},{1,5},{2,6},{3,7},{4,0},{5,1},{6,2},{7,3},{8,12},{9,13},{10,... | collective-permute-start | bytes 528392 | tf_op jit(solution)/shard_map/ppermute | solution.py:198
  50.0 5.5 %collective-permute-start.5 = (f32[344,128]{1,0:T(8,128)S(1)}, f32[344,128]{1,0:T(8,128)S(1)}, u32[]{:S(2)}, u32[]{:S(2)}) collective-permute-start(f32[344,128]{1,0:T(8,128)S(1)} %add.176), channel_id=1, source_target_pairs={{0,2},{1,3},{2,0},{3,1},{4,6},{5,7},{6,4},{7,5},{8,10},{9,11},{10,... | collective-permute-start | bytes 528392 | tf_op jit(solution)/shard_map/ppermute | solution.py:200
  55.5 1.7 %collective-permute-start.6 = (f32[676,128]{1,0:T(8,128)S(1)}, f32[676,128]{1,0:T(8,128)S(1)}, u32[]{:S(2)}, u32[]{:S(2)}) collective-permute-start(f32[676,128]{1,0:T(8,128)S(1)} %fusion.38), channel_id=1, source_target_pairs={{0,1},{1,0},{2,3},{3,2},{4,5},{5,4},{6,7},{7,6},{8,9},{9,8},{10,11... | collective-permute-start | bytes 1038344 | tf_op jit(solution)/shard_map/ppermute | solution.py:215
  57.7 1.4 %copy-start.1 = (f32[2]{0:T(128)S(1)}, f32[2]{0:T(128)}, u32[]{:S(2)}) copy-start(f32[2]{0:T(128)} %constant.117.clone) | copy-start | bytes 28

commit v18 on v17

--- a/solution.py
+++ b/solution.py
@@ -68,10 +68,20 @@
     return extended_2(field_in, (("slab", 0),), 1)
 
 
-def row_transform(spectra_in, positions, frequency, map_width):
-    phases = frequency[:, None] * positions[None, :] % map_width
-    angles = phases.astype(jnp.float32) * (2.0 * math.pi / map_width)
-    table = jnp.stack([jnp.cos(angles), jnp.sin(angles)])
+def row_transform(spectra_in, start, count, frequency, map_width):
+    fine_count = 16 if count % 16 == 0 else 1
+    coarse = start + jnp.arange(count // fine_count, dtype=jnp.int32) * fine_count
+    fine = jnp.arange(fine_count, dtype=jnp.int32)
+    scale = 2.0 * math.pi / map_width
+    c_angles = (frequency[:, None] * coarse[None, :] % map_width).astype(jnp.float32) * scale
+    f_angles = (frequency[:, None] * fine[None, :] % map_width).astype(jnp.float32) * scale
+    c_cos = jnp.cos(c_angles)[:, :, None]
+    c_sin = jnp.sin(c_angles)[:, :, None]
+    f_cos = jnp.cos(f_angles)[:, None, :]
+    f_sin = jnp.sin(f_angles)[:, None, :]
+    table_cos = (c_cos * f_cos - c_sin * f_sin).reshape(frequency.shape[0], count)
+    table_sin = (c_sin * f_cos + c_cos * f_sin).reshape(frequency.shape[0], count)
+    table = jnp.stack([table_cos, table_sin])
     products = jnp.einsum("smx,kxcn->skmcn", table, spectra_in, precision=lax.Precision.HIGH)
     real_part = products[0, :, :, 0] + products[1, :, :, 1]
     imag_part = products[0, :, :, 1] - products[1, :, :, 0]
@@ -262,8 +272,7 @@
         ]
     )
     half_spectra = jnp.einsum("kxy,ycn->kxcn", fields, col_table, precision=lax.Precision.HIGH)
-    my_positions = my_index * slab_rows + jnp.arange(slab_rows, dtype=jnp.int32)
-    partial_value = row_transform(half_spectra, my_positions, frequency, map_width)
+    partial_value = row_transform(half_spectra, my_index * slab_rows, slab_rows, frequency, map_width)
     summed = line_sum(partial_value, my_index, devices)
     coef = summed / float(map_width * map_width)
     a_in = jnp.arange(padded_keep, dtype=jnp.int32)

time: 77.3 us -> 77.3 us (level)
  other arithmetic: 17.7 us -> 16.9 us
where the time goes in v18:
time: 77.3 us; the launch traced here: 76.7 us
  waiting for transfers between devices  20.3 us (26%)
  other arithmetic  16.9 us (22%)
  Pallas kernels  13.7 us (18%)
  starting transfers between devices  10.1 us (13%)
  local copies, waits for them, and re-layouts  7.92 us (10%)
  matrix products  7.32 us (9%)
    pallas_call x1, Pallas kernels, assemble(): pl.pallas_call(assemble_kernel, grid_spec=grid_spec, out_shape=jax.ShapeD...  13.7 us
    ppermute x1, waiting for transfers between devices, line_sum(): lax.ppermute(kept, 'slab', [(i, i ^ bit) for i in range(devices)])  7.93 us
    ppermute x1, waiting for transfers between devices, line_sum(): kept = kept + lax.ppermute(sent, 'slab', pair)  5.16 us
    another operation x3, other arithmetic, shards(): jnp.stack([permit, contrast * normal_x * normal_x, contrast * normal_x *...  4.94 us
    ppermute x1, waiting for transfers between devices, line_sum(): back = lax.ppermute(kept, 'slab', pair)  4.74 us
    dot_general x1, matrix products, shards(): jnp.einsum('kxy,ycn->kxcn', fields, col_table, precision=lax.Precision.HIGH)  4.28 us
    ppermute x1, starting transfers between devices, extended_2(): lax.ppermute(lax.slice_in_dim(block, 0, width, axis=dim), axis, backward)  4.09 us
    div x3, other arithmetic, smooth_once(): (4.0 * middle + extended[:-2] + extended[2:] + jnp.roll(middle, 1, 1) + j...  3.89 us
  transfers between devices with their start and end apart: 7, of which 7 were waited for; matrix products, arithmetic and copies ran while one was open for 3% of the time, Pallas kernels for 0%

profile of v18, /device:TPU:0, one launch (start us, length us, event | category | flops | bytes accessed | tf_op | source)
XLA Modules:
  0.0 76.7 jit_solution(3518690724564156171)
XLA Ops:
  0.0 0.1 fusion.69
  0.2 0.2 fusion.76
  0.3 2.3 %select_add_fusion = f32[256,2048]{1,0:T(8,128)S(1)} fusion(s32[256,2048]{1,0:T(8,128)} %param.2), kind=kLoop, calls=%fused_computation.48 | loop fusion | flops 5767168 | bytes 4194304 | tf_op jit(solution)/shard_map/add | solution.py:43
  2.7 0.3 multiply_subtract_fusion
  3.0 1.5 %pad_maximum_fusion.6 = f32[2048,2,104]{2,0,1:T(8,128)} fusion(f32[2048,1,104]{2,0,1:T(8,128)S(1)} %bitcast.76, f32[2048,1,104]{2,0,1:T(8,128)S(1)} %bitcast.75), kind=kLoop, calls=%fused_computation.39 | loop fusion | flops 425984 | bytes 3407872 | tf_op jit(solution)/shard_map/stack | solution.py:255
  4.4 0.5 collective-permute-start
  5.0 4.1 %collective-permute-start.1 = (f32[4,2048]{1,0:T(4,128)S(1)}, f32[4,2048]{1,0:T(4,128)S(1)}, u32[]{:S(2)}, u32[]{:S(2)}) collective-permute-start(f32[4,2048]{1,0:T(4,128)S(1)} %get-tuple-element.28), channel_id=1, source_target_pairs={{1,0},{2,1},{3,2},{4,3},{5,4},{6,5},{7,6},{0,7},{9,8},{10,9},{11,1... | collective-permute-start | bytes 98312 | tf_op jit(solution)/shard_map/ppermute | solution.py:35
  9.1 0.2 fusion.74
  9.5 0.1 copy.7
  9.6 1.0 %collective-permute-done = f32[4,2048]{1,0:T(4,128)S(1)} collective-permute-done((f32[4,2048]{1,0:T(4,128)S(1)}, f32[4,2048]{1,0:T(4,128)S(1)}, u32[]{:S(2)}, u32[]{:S(2)}) %collective-permute-start) | collective-permute-done | bytes 32800 | tf_op jit(solution)/shard_map/ppermute | solution.py:32
  10.7 0.3 pad_maximum_fusion.5
  11.0 0.9 %fusion.91 = (f32[262,2047]{1,0:T(8,128)S(1)}, f32[262,2047]{1,0:T(8,128)S(1)}) fusion(f32[264,2048]{1,0:T(8,128)S(1)} %pad_maximum_fusion.5), kind=kLoop, calls=%fused_computation.160 | loop fusion | bytes 8581024 | tf_op jit(solution)/shard_map/jit(_roll_static)/slice | solution.py:56
  11.8 2.1 %fusion.15 = f32[262,2048]{1,0:T(8,128)S(1)} fusion(f32[4,2048]{1,0:T(4,128)S(1)} %collective-permute-done.1, f32[256,2048]{1,0:T(8,128)S(1)} %select_add_fusion, f32[4,2048]{1,0:T(4,128)S(1)} %collective-permute-done, f32[264,2048]{1,0:T(8,128)S(1)} %pad_maximum_fusion.5, f32[262,2047]{1,0:T(8,128)S(1)} %get-tuple-element.26, ...), kind=kLoop, calls=%fused_computation.26 | loop fusion | flops 6438912 | bytes 15038416 | tf_op jit(solution)/shard_map/div | solution.py:51
  14.0 0.9 %fusion.89 = (f32[260,2047]{1,0:T(8,128)S(1)}, f32[260,2047]{1,0:T(8,128)S(1)}) fusion(f32[262,2048]{1,0:T(8,128)S(1)} %fusion.15), kind=kLoop, calls=%fused_computation.158 | loop fusion | bytes 8515520 | tf_op jit(solution)/shard_map/jit(_roll_static)/slice | solution.py:56
  15.0 0.9 %fusion.12 = f32[260,2048]{1,0:T(8,128)S(1)} fusion(f32[262,2048]{1,0:T(8,128)S(1)} %fusion.15, f32[260,2047]{1,0:T(8,128)S(1)} %get-tuple-element.22, f32[260,1]{1,0:T(8,128)S(1)} %get-tuple-element.24, f32[260,1]{1,0:T(8,128)S(1)} %get-tuple-element.23, f32[260,2047]{1,0:T(8,128)S(1)} %get-tuple-element.21), kind=kLoop, calls=%fused_computation.20 | loop fusion | flops 4259840 | bytes 12779520 | tf_op jit(solution)/shard_map/div | solution.py:51
  15.9 0.9 %fusion.87 = (f32[258,2047]{1,0:T(8,128)S(1)}, f32[258,2047]{1,0:T(8,128)S(1)}) fusion(f32[260,2048]{1,0:T(8,128)S(1)} %fusion.12), kind=kLoop, calls=%fused_computation.156 | loop fusion | bytes 8450016 | tf_op jit(solution)/shard_map/jit(_roll_static)/slice | solution.py:56
  16.9 0.9 %fusion.9 = f32[258,2048]{1,0:T(8,128)S(1)} fusion(f32[260,2048]{1,0:T(8,128)S(1)} %fusion.12, f32[258,2047]{1,0:T(8,128)S(1)} %get-tuple-element.18, f32[258,1]{1,0:T(8,128)S(1)} %get-tuple-element.20, f32[258,1]{1,0:T(8,128)S(1)} %get-tuple-element.19, f32[258,2047]{1,0:T(8,128)S(1)} %get-tuple-element.17), kind=kLoop, calls=%fused_computation.14 | loop fusion | flops 4227072 | bytes 12681216 | tf_op jit(solution)/shard_map/div | solution.py:51
  17.7 1.1 %fusion.85 = (f32[256,2047]{1,0:T(8,128)S(1)}, f32[256,2047]{1,0:T(8,128)S(1)}) fusion(f32[258,2048]{1,0:T(8,128)S(1)} %fusion.9), kind=kLoop, calls=%fused_computation.154 | loop fusion | bytes 8384512 | tf_op jit(solution)/shard_map/jit(_roll_static)/slice | solution.py:63
  18.9 2.1 %multiply_bitcast_fusion.1 = (f32[1,256,2048]{2,1,0:T(8,128)S(1)}, f32[256,2048]{1,0:T(8,128)S(1)}) fusion(f32[256,2048]{1,0:T(8,128)S(1)} %select_add_fusion, f32[256,2047]{1,0:T(8,128)S(1)} %get-tuple-element.14, f32[256,1]{1,0:T(8,128)S(1)} %get-tuple-element.16, f32[256,1]{1,0:T(8,128)S(1)} %get-tuple-element.15, f32[256,2047]{1,0:T(8,128)S(1)} %get-tuple-element.13, ...), kind=kLoop, calls=%fused_computation.44 | loop fusion | flops 7864320 | bytes 14680064 | tf_op jit(solution)/shard_map/stack | solution.py:266
  21.1 2.3 %multiply_bitcast_fusion = (f32[1,256,2048]{2,1,0:T(8,128)S(1)}, f32[256,2048]{1,0:T(8,128)S(1)}) fusion(f32[256,2048]{1,0:T(8,128)S(1)} %get-tuple-element.10, f32[256,2048]{1,0:T(8,128)S(1)} %select_add_fusion, f32[258,2048]{1,0:T(8,128)S(1)} %fusion.9, f32[256,2047]{1,0:T(8,128)S(1)} %get-tuple-element.14, f32[256,1]{1,0:T(8,128)S(1)} %get-tuple-element.16, ...), kind=kLoop, calls=%fused_computation.43 | loop fusion | flops 7864320 | bytes 16777216 | tf_op jit(solution)/shard_map/stack | solution.py:266
  23.4 0.5 fusion.18
  23.9 1.1 %copy-done = f32[2048,2,104]{2,0,1:T(8,128)S(1)} copy-done((f32[2048,2,104]{2,0,1:T(8,128)S(1)}, f32[2048,2,104]{2,0,1:T(8,128)}, u32[]{:S(2)}) %copy-start) | copy-done | bytes 1703960
  24.9 4.3 %fusion.24 = f32[4,256,2,104,1]{1,3,4,2,0:T(8,128)S(1)} fusion(f32[2048,2,104]{2,0,1:T(8,128)S(1)} %copy-done, f32[1,256,2048]{2,1,0:T(8,128)S(1)} %fusion.18, f32[1,256,2048]{2,1,0:T(8,128)S(1)} %get-tuple-element.11, f32[1,256,2048]{2,1,0:T(8,128)S(1)} %get-tuple-element.9, f32[1,256,2048]{2,1,0:T(8,128)S(1)} %bitcast.74), kind=kOutput, calls=%fused_computation.52 | convolution fusion | flops 2623537152 | bytes 10944512 | tf_op jit(solution)/shard_map/kxy,ycn->kxcn/dot_general | solution.py:274
  29.2 0.9 %convolution_bitcast_fusion = f32[2,4,208,2,104]{2,4,0,3,1:T(8,128)S(1)} fusion(f32[4,256,2,104,1]{1,3,4,2,0:T(8,128)S(1)} %fusion.24, f32[1,208,256]{2,1,0:T(8,128)S(1)} %copy.7, f32[1,208,256]{2,1,0:T(8,128)S(1)} %copy.6), kind=kOutput, calls=%fused_computation.51 | convolution fusion | flops 531734528 | bytes 2662400 | tf_op jit(solution)/shard_map/smx,kxcn->skmcn/dot_general | solution.py:85
  30.2 0.2 copy.9
  30.4 0.4 select_n.154
  30.8 0.4 collective-permute-start.2
  31.2 0.2 copy.8
  31.3 0.4 select_n.152
  31.7 0.8 %collective-permute-done.2 = f32[676,128]{1,0:T(8,128)S(1)} collective-permute-done((f32[676,128]{1,0:T(8,128)S(1)}, f32[676,128]{1,0:T(8,128)S(1)}, u32[]{:S(2)}, u32[]{:S(2)}) %collective-permute-start.2) | collective-permute-done | bytes 346144 | tf_op jit(solution)/shard_map/ppermute | solution.py:194
  32.6 1.6 %collective-permute-start.3 = (f32[344,128]{1,0:T(8,128)S(1)}, f32[344,128]{1,0:T(8,128)S(1)}, u32[]{:S(2)}, u32[]{:S(2)}) collective-permute-start(f32[344,128]{1,0:T(8,128)S(1)} %slice_select_fusion), channel_id=1, source_target_pairs={{0,2},{1,3},{2,0},{3,1},{4,6},{5,7},{6,4},{7,5},{8,10},{9,11},{10,... | collective-permute-start | bytes 528392 | tf_op jit(solution)/shard_map/ppermute | solution.py:205
  34.2 5.2 %collective-permute-done.3 = f32[344,128]{1,0:T(8,128)S(1)} collective-permute-done((f32[344,128]{1,0:T(8,128)S(1)}, f32[344,128]{1,0:T(8,128)S(1)}, u32[]{:S(2)}, u32[]{:S(2)}) %collective-permute-start.3) | collective-permute-done | bytes 176160 | tf_op jit(solution)/shard_map/ppermute | solution.py:205
  39.4 2.6 %collective-permute-start.4 = (f32[344,128]{1,0:T(8,128)S(1)}, f32[344,128]{1,0:T(8,128)S(1)}, u32[]{:S(2)}, u32[]{:S(2)}) collective-permute-start(f32[344,128]{1,0:T(8,128)S(1)} %select_add_fusion.1), channel_id=1, source_target_pairs={{0,4},{1,5},{2,6},{3,7},{4,0},{5,1},{6,2},{7,3},{8,12},{9,13},{10,... | collective-permute-start | bytes 528392 | tf_op jit(solution)/shard_map/ppermute | solution.py:208
  42.0 7.9 %collective-permute-done.4 = f32[344,128]{1,0:T(8,128)S(1)} collective-permute-done((f32[344,128]{1,0:T(8,128)S(1)}, f32[344,128]{1,0:T(8,128)S(1)}, u32[]{:S(2)}, u32[]{:S(2)}) %collective-permute-start.4) | collective-permute-done | bytes 176160 | tf_op jit(solution)/shard_map/ppermute | solution.py:208
  50.0 0.8 %collective-permute-start.5 = (f32[344,128]{1,0:T(8,128)S(1)}, f32[344,128]{1,0:T(8,128)S(1)}, u32[]{:S(2)}, u32[]{:S(2)}) collective-permute-start(f32[344,128]{1,0:T(8,128)S(1)} %add.205), channel_id=1, source_target_pairs={{0,2},{1,3},{2,0},{3,1},{4,6},{5,7},{6,4},{7,5},{8,10},{9,11},{10,... | collective-permute-start | bytes 528392 | tf_op jit(solution)/shard_map/ppermute | solution.py:210
  50.7 4.7 %collective-permute-done.5 = f32[344,128]{1,0:T(8,128)S(1)} collective-permute-done((f32[344,128]{1,0:T(8,128)S(1)}, f32[344,128]{1,0:T(8,128)S(1)}, u32[]{:S(2)}, u32[]{:S(2)}) %collective-permute-start.5) | collective-permute-done | bytes 176160 | tf_op jit(solution)/shard_map/ppermute | solution.py:210
  55.6 0.6 pad_add_fusion.index_ref
  56.2 0.4 stack_reshape.4
  56.6 0.6 collective-permute-done.6
  57.2 0.4 stack_reshape.5
  57.7 0.7 fusion.28
  58.4 0.7 fusion.30
  59.1 0.8 %multiply_add_fusion = f32[2,4,208,256]{3,2,1,0:T(8,128)S(1)} fusion(f32[2,4,208,256]{3,2,1,0:T(8,128)S(1)} %fusion.30, f32[2,4,104,208]{2,3,1,0:T(8,128)S(1)} %fusion.28, f32[2]{0:T(128)S(1)} %copy-done.1, s32[256]{0:T(256)S(1)} %iota_subtract_fusion, pred[256]{0:T(512)(128)(4,1)S(1)} %iota_compare_fusion.3), kind=kOutput, calls=%fused_computation.50 | convolution fusion | flops 532533248 | bytes 4101384 | tf_op jit(solution)/shard_map/ad,skdc,cb->skab/dot_general | solution.py:288
  59.9 0.2 fusion.93
  60.1 0.2 pad_maximum_fusion.7
  60.2 0.7 slice_bitcast_fusion.3
  60.9 2.0 %pad_maximum_fusion.fl_ref = f32[2,4,4,208,128]{4,3,2,1,0:T(8,128)} fusion(f32[2,1,4,208,128]{4,3,2,1,0:T(8,128)S(1)} %get-tuple-element.30, f32[2,1,4,208,128]{4,3,2,1,0:T(8,128)S(1)} %get-tuple-element.31, f32[2,1,4,208,128]{4,3,2,1,0:T(8,128)S(1)} %get-tuple-element.32, f32[2,1,4,208,128]{4,3,2,1,0:T(8,128)S(1)} %get-tuple-element.29), kind=kLoop, calls=%fused_computation.8 | loop fusion | flops 2555904 | bytes 6815744 | tf_op jit(solution)/shard_map/stack | solution.py:295
  62.9 13.7 %shard_map.28 = f32[2,64,20402]{2,1,0:T(8,128)} custom-call(s32[2]{0:T(128)} %pad_add_fusion.index_ref, f32[2,4,4,208,128]{4,3,2,1,0:T(8,128)} %pad_maximum_fusion.fl_ref), custom_call_target="tpu_custom_call" | custom-call | tf_op jit(solution)/shard_map/pallas_call | solution.py:179
  (25 shorter events, 1.0 us)
Async XLA Ops:
  4.4 6.2 %collective-permute-start = (f32[4,2048]{1,0:T(4,128)S(1)}, f32[4,2048]{1,0:T(4,128)S(1)}, u32[]{:S(2)}, u32[]{:S(2)}) collective-permute-start(f32[4,2048]{1,0:T(4,128)S(1)} %get-tuple-element.27), channel_id=1, source_target_pairs={{0,1},{1,2},{2,3},{3,4},{4,5},{5,6},{6,7},{7,0},{8,9},{9,10},{10,1... | collective-permute-start | bytes 98312 | tf_op jit(solution)/shard_map/ppermute | solution.py:32
  5.0 5.7 %collective-permute-start.1 = (f32[4,2048]{1,0:T(4,128)S(1)}, f32[4,2048]{1,0:T(4,128)S(1)}, u32[]{:S(2)}, u32[]{:S(2)}) collective-permute-start(f32[4,2048]{1,0:T(4,128)S(1)} %get-tuple-element.28), channel_id=1, source_target_pairs={{1,0},{2,1},{3,2},{4,3},{5,4},{6,5},{7,6},{0,7},{9,8},{10,9},{11,1... | collective-permute-start | bytes 98312 | tf_op jit(solution)/shard_map/ppermute | solution.py:35
  23.3 1.6 %copy-start = (f32[2048,2,104]{2,0,1:T(8,128)S(1)}, f32[2048,2,104]{2,0,1:T(8,128)}, u32[]{:S(2)}) copy-start(f32[2048,2,104]{2,0,1:T(8,128)} %pad_maximum_fusion.6) | copy-start | bytes 5111812
  30.8 1.7 %collective-permute-start.2 = (f32[676,128]{1,0:T(8,128)S(1)}, f32[676,128]{1,0:T(8,128)S(1)}, u32[]{:S(2)}, u32[]{:S(2)}) collective-permute-start(f32[676,128]{1,0:T(8,128)S(1)} %select_n.154), channel_id=1, source_target_pairs={{0,1},{1,0},{2,3},{3,2},{4,5},{5,4},{6,7},{7,6},{8,9},{9,8},{10,11... | collective-permute-start | bytes 1038344 | tf_op jit(solution)/shard_map/ppermute | solution.py:194
  32.6 6.8 %collective-permute-start.3 = (f32[344,128]{1,0:T(8,128)S(1)}, f32[344,128]{1,0:T(8,128)S(1)}, u32[]{:S(2)}, u32[]{:S(2)}) collective-permute-start(f32[344,128]{1,0:T(8,128)S(1)} %slice_select_fusion), channel_id=1, source_target_pairs={{0,2},{1,3},{2,0},{3,1},{4,6},{5,7},{6,4},{7,5},{8,10},{9,11},{10,... | collective-permute-start | bytes 528392 | tf_op jit(solution)/shard_map/ppermute | solution.py:205
  39.4 10.6 %collective-permute-start.4 = (f32[344,128]{1,0:T(8,128)S(1)}, f32[344,128]{1,0:T(8,128)S(1)}, u32[]{:S(2)}, u32[]{:S(2)}) collective-permute-start(f32[344,128]{1,0:T(8,128)S(1)} %select_add_fusion.1), channel_id=1, source_target_pairs={{0,4},{1,5},{2,6},{3,7},{4,0},{5,1},{6,2},{7,3},{8,12},{9,13},{10,... | collective-permute-start | bytes 528392 | tf_op jit(solution)/shard_map/ppermute | solution.py:208
  50.0 5.5 %collective-permute-start.5 = (f32[344,128]{1,0:T(8,128)S(1)}, f32[344,128]{1,0:T(8,128)S(1)}, u32[]{:S(2)}, u32[]{:S(2)}) collective-permute-start(f32[344,128]{1,0:T(8,128)S(1)} %add.205), channel_id=1, source_target_pairs={{0,2},{1,3},{2,0},{3,1},{4,6},{5,7},{6,4},{7,5},{8,10},{9,11},{10,... | collective-permute-start | bytes 528392 | tf_op jit(solution)/shard_map/ppermute | solution.py:210
  55.5 1.7 %collective-permute-start.6 = (f32[676,128]{1,0:T(8,128)S(1)}, f32[676,128]{1,0:T(8,128)S(1)}, u32[]{:S(2)}, u32[]{:S(2)}) collective-permute-start(f32[676,128]{1,0:T(8,128)S(1)} %fusion.38), channel_id=1, source_target_pairs={{0,1},{1,0},{2,3},{3,2},{4,5},{5,4},{6,7},{7,6},{8,9},{9,8},{10,11... | collective-permute-start | bytes 1038344 | tf_op jit(solution)/shard_map/ppermute | solution.py:225
  57.7 1.4 %copy-start.1 = (f32[2]{0:T(128)S(1)}, f32[2]{0:T(128)}, u32[]{:S(2)}) copy-start(f32[2]{0:T(128)} %constant.124.clone) | copy-start | bytes 28

commit v19 on v18

--- a/solution.py
+++ b/solution.py
@@ -284,14 +284,14 @@
         (c_in[:, None] == (KEEP - 1) - b_out[None, :]) & (b_out[None, :] >= HARM)
     ).astype(jnp.float32)
     sign = jnp.array([1.0, -1.0], jnp.float32)[:, None, None, None]
-    direct = jnp.einsum("skac,cb->skab", coef, keep_cols, precision=lax.Precision.HIGHEST)
+    blocks = jnp.stack(
+        [coef[:, 2], coef[:, 0] - coef[:, 3], coef[:, 1] - coef[:, 0], -coef[:, 2]], axis=1
+    )
+    direct = jnp.einsum("skac,cb->skab", blocks, keep_cols, precision=lax.Precision.HIGHEST)
     mirrored = jnp.einsum(
-        "ad,skdc,cb->skab", flip_rows, coef, mirror_cols, precision=lax.Precision.HIGHEST
-    )
-    full = direct + sign * mirrored
-    tables = jnp.stack(
-        [full[:, 2], full[:, 0] - full[:, 3], full[:, 1] - full[:, 0], -full[:, 2]], axis=1
-    )
+        "ad,skdc,cb->skab", flip_rows, blocks, mirror_cols, precision=lax.Precision.HIGHEST
+    )
+    tables = direct + sign * mirrored
     tables = jnp.stack(
         [tables[..., COPY_STEP * c : COPY_STEP * c + LANES] for c in range(COPIES)], axis=1
     )

time: 77.3 us -> 77.1 us (level)
  no operation moved by 1% of the time
where the time goes in v19:
time: 77.1 us; the launch traced here: 76.4 us
  waiting for transfers between devices  20.3 us (26%)
  other arithmetic  16.8 us (22%)
  Pallas kernels  13.7 us (18%)
  starting transfers between devices  10.1 us (13%)
  local copies, waits for them, and re-layouts  7.92 us (10%)
  matrix products  7.21 us (9%)
    pallas_call x1, Pallas kernels, assemble(): pl.pallas_call(assemble_kernel, grid_spec=grid_spec, out_shape=jax.ShapeD...  13.7 us
    ppermute x1, waiting for transfers between devices, line_sum(): lax.ppermute(kept, 'slab', [(i, i ^ bit) for i in range(devices)])  7.93 us
    ppermute x1, waiting for transfers between devices, line_sum(): kept = kept + lax.ppermute(sent, 'slab', pair)  5.16 us
    another operation x3, other arithmetic, shards(): jnp.stack([permit, contrast * normal_x * normal_x, contrast * normal_x *...  4.94 us
    ppermute x1, waiting for transfers between devices, line_sum(): back = lax.ppermute(kept, 'slab', pair)  4.74 us
    dot_general x1, matrix products, shards(): jnp.einsum('kxy,ycn->kxcn', fields, col_table, precision=lax.Precision.HIGH)  4.28 us
    ppermute x1, starting transfers between devices, extended_2(): lax.ppermute(lax.slice_in_dim(block, 0, width, axis=dim), axis, backward)  4.09 us
    div x3, other arithmetic, smooth_once(): (4.0 * middle + extended[:-2] + extended[2:] + jnp.roll(middle, 1, 1) + j...  3.89 us
  transfers between devices with their start and end apart: 7, of which 7 were waited for; matrix products, arithmetic and copies ran while one was open for 3% of the time, Pallas kernels for 0%

profile of v19, /device:TPU:0, one launch (start us, length us, event | category | flops | bytes accessed | tf_op | source)
XLA Modules:
  0.0 76.4 jit_solution(9493278592623535283)
XLA Ops:
  0.0 0.1 fusion.63
  0.2 0.2 fusion.70
  0.3 2.3 %select_add_fusion = f32[256,2048]{1,0:T(8,128)S(1)} fusion(s32[256,2048]{1,0:T(8,128)} %param.2), kind=kLoop, calls=%fused_computation.48 | loop fusion | flops 5767168 | bytes 4194304 | tf_op jit(solution)/shard_map/add | solution.py:43
  2.7 0.3 multiply_subtract_fusion
  3.0 1.5 %pad_maximum_fusion.6 = f32[2048,2,104]{2,0,1:T(8,128)} fusion(f32[2048,1,104]{2,0,1:T(8,128)S(1)} %bitcast.76, f32[2048,1,104]{2,0,1:T(8,128)S(1)} %bitcast.75), kind=kLoop, calls=%fused_computation.39 | loop fusion | flops 425984 | bytes 3407872 | tf_op jit(solution)/shard_map/stack | solution.py:255
  4.4 0.5 collective-permute-start
  5.0 4.1 %collective-permute-start.1 = (f32[4,2048]{1,0:T(4,128)S(1)}, f32[4,2048]{1,0:T(4,128)S(1)}, u32[]{:S(2)}, u32[]{:S(2)}) collective-permute-start(f32[4,2048]{1,0:T(4,128)S(1)} %get-tuple-element.28), channel_id=1, source_target_pairs={{1,0},{2,1},{3,2},{4,3},{5,4},{6,5},{7,6},{0,7},{9,8},{10,9},{11,1... | collective-permute-start | bytes 98312 | tf_op jit(solution)/shard_map/ppermute | solution.py:35
  9.1 0.2 fusion.68
  9.3 0.1 copy.6
  9.5 0.1 copy.7
  9.6 1.0 %collective-permute-done = f32[4,2048]{1,0:T(4,128)S(1)} collective-permute-done((f32[4,2048]{1,0:T(4,128)S(1)}, f32[4,2048]{1,0:T(4,128)S(1)}, u32[]{:S(2)}, u32[]{:S(2)}) %collective-permute-start) | collective-permute-done | bytes 32800 | tf_op jit(solution)/shard_map/ppermute | solution.py:32
  10.7 0.3 pad_maximum_fusion.5
  11.0 0.9 %fusion.83 = (f32[262,2047]{1,0:T(8,128)S(1)}, f32[262,2047]{1,0:T(8,128)S(1)}) fusion(f32[264,2048]{1,0:T(8,128)S(1)} %pad_maximum_fusion.5), kind=kLoop, calls=%fused_computation.154 | loop fusion | bytes 8581024 | tf_op jit(solution)/shard_map/jit(_roll_static)/slice | solution.py:56
  11.8 2.1 %fusion.15 = f32[262,2048]{1,0:T(8,128)S(1)} fusion(f32[4,2048]{1,0:T(4,128)S(1)} %collective-permute-done.1, f32[256,2048]{1,0:T(8,128)S(1)} %select_add_fusion, f32[4,2048]{1,0:T(4,128)S(1)} %collective-permute-done, f32[264,2048]{1,0:T(8,128)S(1)} %pad_maximum_fusion.5, f32[262,2047]{1,0:T(8,128)S(1)} %get-tuple-element.26, ...), kind=kLoop, calls=%fused_computation.26 | loop fusion | flops 6438912 | bytes 15038416 | tf_op jit(solution)/shard_map/div | solution.py:51
  14.0 0.9 %fusion.81 = (f32[260,2047]{1,0:T(8,128)S(1)}, f32[260,2047]{1,0:T(8,128)S(1)}) fusion(f32[262,2048]{1,0:T(8,128)S(1)} %fusion.15), kind=kLoop, calls=%fused_computation.152 | loop fusion | bytes 8515520 | tf_op jit(solution)/shard_map/jit(_roll_static)/slice | solution.py:56
  15.0 0.9 %fusion.12 = f32[260,2048]{1,0:T(8,128)S(1)} fusion(f32[262,2048]{1,0:T(8,128)S(1)} %fusion.15, f32[260,2047]{1,0:T(8,128)S(1)} %get-tuple-element.22, f32[260,1]{1,0:T(8,128)S(1)} %get-tuple-element.24, f32[260,1]{1,0:T(8,128)S(1)} %get-tuple-element.23, f32[260,2047]{1,0:T(8,128)S(1)} %get-tuple-element.21), kind=kLoop, calls=%fused_computation.20 | loop fusion | flops 4259840 | bytes 12779520 | tf_op jit(solution)/shard_map/div | solution.py:51
  15.9 0.9 %fusion.79 = (f32[258,2047]{1,0:T(8,128)S(1)}, f32[258,2047]{1,0:T(8,128)S(1)}) fusion(f32[260,2048]{1,0:T(8,128)S(1)} %fusion.12), kind=kLoop, calls=%fused_computation.150 | loop fusion | bytes 8450016 | tf_op jit(solution)/shard_map/jit(_roll_static)/slice | solution.py:56
  16.9 0.9 %fusion.9 = f32[258,2048]{1,0:T(8,128)S(1)} fusion(f32[260,2048]{1,0:T(8,128)S(1)} %fusion.12, f32[258,2047]{1,0:T(8,128)S(1)} %get-tuple-element.18, f32[258,1]{1,0:T(8,128)S(1)} %get-tuple-element.20, f32[258,1]{1,0:T(8,128)S(1)} %get-tuple-element.19, f32[258,2047]{1,0:T(8,128)S(1)} %get-tuple-element.17), kind=kLoop, calls=%fused_computation.14 | loop fusion | flops 4227072 | bytes 12681216 | tf_op jit(solution)/shard_map/div | solution.py:51
  17.7 1.1 %fusion.77 = (f32[256,2047]{1,0:T(8,128)S(1)}, f32[256,2047]{1,0:T(8,128)S(1)}) fusion(f32[258,2048]{1,0:T(8,128)S(1)} %fusion.9), kind=kLoop, calls=%fused_computation.148 | loop fusion | bytes 8384512 | tf_op jit(solution)/shard_map/jit(_roll_static)/slice | solution.py:63
  18.9 2.1 %multiply_bitcast_fusion.1 = (f32[1,256,2048]{2,1,0:T(8,128)S(1)}, f32[256,2048]{1,0:T(8,128)S(1)}) fusion(f32[256,2048]{1,0:T(8,128)S(1)} %select_add_fusion, f32[256,2047]{1,0:T(8,128)S(1)} %get-tuple-element.14, f32[256,1]{1,0:T(8,128)S(1)} %get-tuple-element.16, f32[256,1]{1,0:T(8,128)S(1)} %get-tuple-element.15, f32[256,2047]{1,0:T(8,128)S(1)} %get-tuple-element.13, ...), kind=kLoop, calls=%fused_computation.44 | loop fusion | flops 7864320 | bytes 14680064 | tf_op jit(solution)/shard_map/stack | solution.py:266
  21.1 2.3 %multiply_bitcast_fusion = (f32[1,256,2048]{2,1,0:T(8,128)S(1)}, f32[256,2048]{1,0:T(8,128)S(1)}) fusion(f32[256,2048]{1,0:T(8,128)S(1)} %get-tuple-element.10, f32[256,2048]{1,0:T(8,128)S(1)} %select_add_fusion, f32[258,2048]{1,0:T(8,128)S(1)} %fusion.9, f32[256,2047]{1,0:T(8,128)S(1)} %get-tuple-element.14, f32[256,1]{1,0:T(8,128)S(1)} %get-tuple-element.16, ...), kind=kLoop, calls=%fused_computation.43 | loop fusion | flops 7864320 | bytes 16777216 | tf_op jit(solution)/shard_map/stack | solution.py:266
  23.4 0.5 fusion.18
  23.9 1.1 %copy-done = f32[2048,2,104]{2,0,1:T(8,128)S(1)} copy-done((f32[2048,2,104]{2,0,1:T(8,128)S(1)}, f32[2048,2,104]{2,0,1:T(8,128)}, u32[]{:S(2)}) %copy-start) | copy-done | bytes 1703960
  24.9 4.3 %fusion.24 = f32[4,256,2,104,1]{1,3,4,2,0:T(8,128)S(1)} fusion(f32[2048,2,104]{2,0,1:T(8,128)S(1)} %copy-done, f32[1,256,2048]{2,1,0:T(8,128)S(1)} %fusion.18, f32[1,256,2048]{2,1,0:T(8,128)S(1)} %get-tuple-element.11, f32[1,256,2048]{2,1,0:T(8,128)S(1)} %get-tuple-element.9, f32[1,256,2048]{2,1,0:T(8,128)S(1)} %bitcast.74), kind=kOutput, calls=%fused_computation.51 | convolution fusion | flops 2623537152 | bytes 10944512 | tf_op jit(solution)/shard_map/kxy,ycn->kxcn/dot_general | solution.py:274
  29.2 0.9 %convolution_bitcast_fusion = f32[2,4,208,2,104]{2,4,0,3,1:T(8,128)S(1)} fusion(f32[4,256,2,104,1]{1,3,4,2,0:T(8,128)S(1)} %fusion.24, f32[1,208,256]{2,1,0:T(8,128)S(1)} %copy.7, f32[1,208,256]{2,1,0:T(8,128)S(1)} %copy.6), kind=kOutput, calls=%fused_computation.50 | convolution fusion | flops 531734528 | bytes 2662400 | tf_op jit(solution)/shard_map/smx,kxcn->skmcn/dot_general | solution.py:85
  30.1 0.1 broadcast_select_fusion
  30.2 0.2 copy.9
  30.4 0.4 select_n.154
  30.8 0.4 collective-permute-start.2
  31.2 0.2 copy.8
  31.3 0.4 select_n.152
  31.7 0.8 %collective-permute-done.2 = f32[676,128]{1,0:T(8,128)S(1)} collective-permute-done((f32[676,128]{1,0:T(8,128)S(1)}, f32[676,128]{1,0:T(8,128)S(1)}, u32[]{:S(2)}, u32[]{:S(2)}) %collective-permute-start.2) | collective-permute-done | bytes 346144 | tf_op jit(solution)/shard_map/ppermute | solution.py:194
  32.6 1.6 %collective-permute-start.3 = (f32[344,128]{1,0:T(8,128)S(1)}, f32[344,128]{1,0:T(8,128)S(1)}, u32[]{:S(2)}, u32[]{:S(2)}) collective-permute-start(f32[344,128]{1,0:T(8,128)S(1)} %slice_select_fusion), channel_id=1, source_target_pairs={{0,2},{1,3},{2,0},{3,1},{4,6},{5,7},{6,4},{7,5},{8,10},{9,11},{10,... | collective-permute-start | bytes 528392 | tf_op jit(solution)/shard_map/ppermute | solution.py:205
  34.2 5.2 %collective-permute-done.3 = f32[344,128]{1,0:T(8,128)S(1)} collective-permute-done((f32[344,128]{1,0:T(8,128)S(1)}, f32[344,128]{1,0:T(8,128)S(1)}, u32[]{:S(2)}, u32[]{:S(2)}) %collective-permute-start.3) | collective-permute-done | bytes 176160 | tf_op jit(solution)/shard_map/ppermute | solution.py:205
  39.4 2.6 %collective-permute-start.4 = (f32[344,128]{1,0:T(8,128)S(1)}, f32[344,128]{1,0:T(8,128)S(1)}, u32[]{:S(2)}, u32[]{:S(2)}) collective-permute-start(f32[344,128]{1,0:T(8,128)S(1)} %select_add_fusion.1), channel_id=1, source_target_pairs={{0,4},{1,5},{2,6},{3,7},{4,0},{5,1},{6,2},{7,3},{8,12},{9,13},{10,... | collective-permute-start | bytes 528392 | tf_op jit(solution)/shard_map/ppermute | solution.py:208
  42.0 7.9 %collective-permute-done.4 = f32[344,128]{1,0:T(8,128)S(1)} collective-permute-done((f32[344,128]{1,0:T(8,128)S(1)}, f32[344,128]{1,0:T(8,128)S(1)}, u32[]{:S(2)}, u32[]{:S(2)}) %collective-permute-start.4) | collective-permute-done | bytes 176160 | tf_op jit(solution)/shard_map/ppermute | solution.py:208
  50.0 0.8 %collective-permute-start.5 = (f32[344,128]{1,0:T(8,128)S(1)}, f32[344,128]{1,0:T(8,128)S(1)}, u32[]{:S(2)}, u32[]{:S(2)}) collective-permute-start(f32[344,128]{1,0:T(8,128)S(1)} %add.205), channel_id=1, source_target_pairs={{0,2},{1,3},{2,0},{3,1},{4,6},{5,7},{6,4},{7,5},{8,10},{9,11},{10,... | collective-permute-start | bytes 528392 | tf_op jit(solution)/shard_map/ppermute | solution.py:210
  50.7 4.7 %collective-permute-done.5 = f32[344,128]{1,0:T(8,128)S(1)} collective-permute-done((f32[344,128]{1,0:T(8,128)S(1)}, f32[344,128]{1,0:T(8,128)S(1)}, u32[]{:S(2)}, u32[]{:S(2)}) %collective-permute-start.5) | collective-permute-done | bytes 176160 | tf_op jit(solution)/shard_map/ppermute | solution.py:210
  55.6 0.6 pad_add_fusion.index_ref
  56.2 0.4 stack_reshape.4
  56.6 0.6 collective-permute-done.6
  57.2 0.4 stack_reshape.5
  57.8 0.6 fusion.28
  58.5 0.6 fusion.29
  59.1 0.8 %multiply_add_fusion = f32[2,4,208,256]{3,2,1,0:T(8,128)S(1)} fusion(f32[2,4,208,256]{3,2,1,0:T(8,128)S(1)} %fusion.29, f32[2,4,104,208]{2,3,1,0:T(8,128)S(1)} %fusion.28, f32[2]{0:T(128)S(1)} %copy-done.1, s32[256]{0:T(256)S(1)} %iota_subtract_fusion, pred[256]{0:T(512)(128)(4,1)S(1)} %iota_compare_fusion.3), kind=kOutput, calls=%fused_computation.49 | convolution fusion | flops 532533248 | bytes 4101384 | tf_op jit(solution)/shard_map/ad,skdc,cb->skab/dot_general | solution.py:291
  59.9 0.7 slice_bitcast_fusion.3
  60.7 2.0 %pad_maximum_fusion.fl_ref = f32[2,4,4,208,128]{4,3,2,1,0:T(8,128)} fusion(f32[2,1,4,208,128]{4,3,2,1,0:T(8,128)S(1)} %get-tuple-element.30, f32[2,1,4,208,128]{4,3,2,1,0:T(8,128)S(1)} %get-tuple-element.31, f32[2,1,4,208,128]{4,3,2,1,0:T(8,128)S(1)} %get-tuple-element.32, f32[2,1,4,208,128]{4,3,2,1,0:T(8,128)S(1)} %get-tuple-element.29), kind=kLoop, calls=%fused_computation.8 | loop fusion | flops 2555904 | bytes 6815744 | tf_op jit(solution)/shard_map/stack | solution.py:295
  62.6 13.7 %shard_map.28 = f32[2,64,20402]{2,1,0:T(8,128)} custom-call(s32[2]{0:T(128)} %pad_add_fusion.index_ref, f32[2,4,4,208,128]{4,3,2,1,0:T(8,128)} %pad_maximum_fusion.fl_ref), custom_call_target="tpu_custom_call" | custom-call | tf_op jit(solution)/shard_map/pallas_call | solution.py:179
  (25 shorter events, 0.9 us)
Async XLA Ops:
  4.4 6.2 %collective-permute-start = (f32[4,2048]{1,0:T(4,128)S(1)}, f32[4,2048]{1,0:T(4,128)S(1)}, u32[]{:S(2)}, u32[]{:S(2)}) collective-permute-start(f32[4,2048]{1,0:T(4,128)S(1)} %get-tuple-element.27), channel_id=1, source_target_pairs={{0,1},{1,2},{2,3},{3,4},{4,5},{5,6},{6,7},{7,0},{8,9},{9,10},{10,1... | collective-permute-start | bytes 98312 | tf_op jit(solution)/shard_map/ppermute | solution.py:32
  5.0 5.7 %collective-permute-start.1 = (f32[4,2048]{1,0:T(4,128)S(1)}, f32[4,2048]{1,0:T(4,128)S(1)}, u32[]{:S(2)}, u32[]{:S(2)}) collective-permute-start(f32[4,2048]{1,0:T(4,128)S(1)} %get-tuple-element.28), channel_id=1, source_target_pairs={{1,0},{2,1},{3,2},{4,3},{5,4},{6,5},{7,6},{0,7},{9,8},{10,9},{11,1... | collective-permute-start | bytes 98312 | tf_op jit(solution)/shard_map/ppermute | solution.py:35
  23.3 1.6 %copy-start = (f32[2048,2,104]{2,0,1:T(8,128)S(1)}, f32[2048,2,104]{2,0,1:T(8,128)}, u32[]{:S(2)}) copy-start(f32[2048,2,104]{2,0,1:T(8,128)} %pad_maximum_fusion.6) | copy-start | bytes 5111812
  30.8 1.7 %collective-permute-start.2 = (f32[676,128]{1,0:T(8,128)S(1)}, f32[676,128]{1,0:T(8,128)S(1)}, u32[]{:S(2)}, u32[]{:S(2)}) collective-permute-start(f32[676,128]{1,0:T(8,128)S(1)} %select_n.154), channel_id=1, source_target_pairs={{0,1},{1,0},{2,3},{3,2},{4,5},{5,4},{6,7},{7,6},{8,9},{9,8},{10,11... | collective-permute-start | bytes 1038344 | tf_op jit(solution)/shard_map/ppermute | solution.py:194
  32.6 6.8 %collective-permute-start.3 = (f32[344,128]{1,0:T(8,128)S(1)}, f32[344,128]{1,0:T(8,128)S(1)}, u32[]{:S(2)}, u32[]{:S(2)}) collective-permute-start(f32[344,128]{1,0:T(8,128)S(1)} %slice_select_fusion), channel_id=1, source_target_pairs={{0,2},{1,3},{2,0},{3,1},{4,6},{5,7},{6,4},{7,5},{8,10},{9,11},{10,... | collective-permute-start | bytes 528392 | tf_op jit(solution)/shard_map/ppermute | solution.py:205
  39.4 10.6 %collective-permute-start.4 = (f32[344,128]{1,0:T(8,128)S(1)}, f32[344,128]{1,0:T(8,128)S(1)}, u32[]{:S(2)}, u32[]{:S(2)}) collective-permute-start(f32[344,128]{1,0:T(8,128)S(1)} %select_add_fusion.1), channel_id=1, source_target_pairs={{0,4},{1,5},{2,6},{3,7},{4,0},{5,1},{6,2},{7,3},{8,12},{9,13},{10,... | collective-permute-start | bytes 528392 | tf_op jit(solution)/shard_map/ppermute | solution.py:208
  50.0 5.5 %collective-permute-start.5 = (f32[344,128]{1,0:T(8,128)S(1)}, f32[344,128]{1,0:T(8,128)S(1)}, u32[]{:S(2)}, u32[]{:S(2)}) collective-permute-start(f32[344,128]{1,0:T(8,128)S(1)} %add.205), channel_id=1, source_target_pairs={{0,2},{1,3},{2,0},{3,1},{4,6},{5,7},{6,4},{7,5},{8,10},{9,11},{10,... | collective-permute-start | bytes 528392 | tf_op jit(solution)/shard_map/ppermute | solution.py:210
  55.5 1.7 %collective-permute-start.6 = (f32[676,128]{1,0:T(8,128)S(1)}, f32[676,128]{1,0:T(8,128)S(1)}, u32[]{:S(2)}, u32[]{:S(2)}) collective-permute-start(f32[676,128]{1,0:T(8,128)S(1)} %fusion.32), channel_id=1, source_target_pairs={{0,1},{1,0},{2,3},{3,2},{4,5},{5,4},{6,7},{7,6},{8,9},{9,8},{10,11... | collective-permute-start | bytes 1038344 | tf_op jit(solution)/shard_map/ppermute | solution.py:225
  57.8 1.3 %copy-start.1 = (f32[2]{0:T(128)S(1)}, f32[2]{0:T(128)}, u32[]{:S(2)}) copy-start(f32[2]{0:T(128)} %constant.124.clone) | copy-start | bytes 28

commit v20 on v19

--- a/solution.py
+++ b/solution.py
@@ -103,10 +103,11 @@
     return chunks
 
 
-def assemble_kernel(index_ref, fl_ref, o_ref, z_ref):
+def assemble_kernel(devices, fl_ref, o_ref, z_ref):
     rb = pl.program_id(0)
     rows = o_ref.shape[1] * pl.num_programs(0)
-    spacing = ORDERS // (rows * index_ref[1] // 2)
+    spacing = ORDERS // (rows * devices // 2)
+    my_index = lax.axis_index("slab")
     centre = (HARM - 1) // 2
     span = z_ref.shape[-2] // BLOCK_ROWS - BLOCK_ROWS
     lane_iota = lax.broadcasted_iota(jnp.int32, (span, LANES), 1)
@@ -116,7 +117,7 @@
         z_part = z_ref.at[part, s]
         for rr in range(BLOCK_ROWS):
             row = rb * o_ref.shape[1] + part * BLOCK_ROWS + rr
-            order_index = (index_ref[0] * rows + row) // 2 * spacing
+            order_index = (my_index * rows + row) // 2 * spacing
             first = order_index // HARM
             second = order_index % HARM
             a0 = (HARM - 1) - first
@@ -159,17 +160,16 @@
             o_ref[s, pl.ds(part * BLOCK_ROWS, BLOCK_ROWS), pl.ds(start, width)] = acc
 
 
-def assemble(index, tables, rows):
+def assemble(devices, tables, rows):
     span = 112
     n_blocks = rows // STEP_ROWS
     total = 2 * ORDERS
-    grid_spec = pltpu.PrefetchScalarGridSpec(
-        num_scalar_prefetch=1,
+    grid_spec = pl.GridSpec(
         grid=(n_blocks,),
         in_specs=[
-            pl.BlockSpec(tables.shape, lambda rb, *_: (0, 0, 0, 0, 0)),
+            pl.BlockSpec(tables.shape, lambda rb: (0, 0, 0, 0, 0)),
         ],
-        out_specs=pl.BlockSpec((2, STEP_ROWS, total), lambda rb, *_: (0, rb, 0)),
+        out_specs=pl.BlockSpec((2, STEP_ROWS, total), lambda rb: (0, rb, 0)),
         scratch_shapes=[
             pltpu.VMEM(
                 (STEP_ROWS // BLOCK_ROWS, 2, 2, (span + BLOCK_ROWS) * BLOCK_ROWS, LANES), jnp.float32
@@ -177,11 +177,11 @@
         ],
     )
     return pl.pallas_call(
-        assemble_kernel,
+        functools.partial(assemble_kernel, devices),
         grid_spec=grid_spec,
         out_shape=jax.ShapeDtypeStruct((2, rows, total), jnp.float32),
         compiler_params=pltpu.CompilerParams(dimension_semantics=("arbitrary",)),
-    )(index, tables)
+    )(tables)
 
 
 def line_sum(partial_value, my_index, devices):
@@ -295,8 +295,7 @@
     tables = jnp.stack(
         [tables[..., COPY_STEP * c : COPY_STEP * c + LANES] for c in range(COPIES)], axis=1
     )
-    index = jnp.stack([my_index, devices]).astype(jnp.int32)
-    return assemble(index, tables, ROWS_DEV)
+    return assemble(devices, tables, ROWS_DEV)
 
 
 def solution(mesh):

time: 77.1 us -> 76.3 us (0.990)
  transfers between devices with their start and end apart: 7 -> 7, of which waited for: 7 -> 7; matrix products, arithmetic and copies ran while one was open for 3% -> 2% of each run, Pallas kernels for 0% -> 0%
where the time goes in v20:
time: 76.3 us; the launch traced here: 75.6 us
  waiting for transfers between devices  20.9 us (27%)
  other arithmetic  16.2 us (21%)
  Pallas kernels  13 us (17%)
  starting transfers between devices  10.1 us (13%)
  local copies, waits for them, and re-layouts  7.92 us (10%)
  matrix products  7.21 us (9%)
    pallas_call x1, Pallas kernels, assemble(): pl.pallas_call(functools.partial(assemble_kernel, devices), grid_spec=gri...  13 us
    ppermute x1, waiting for transfers between devices, line_sum(): lax.ppermute(kept, 'slab', [(i, i ^ bit) for i in range(devices)])  7.93 us
    ppermute x1, waiting for transfers between devices, line_sum(): kept = kept + lax.ppermute(sent, 'slab', pair)  5.16 us
    another operation x3, other arithmetic, shards(): jnp.stack([permit, contrast * normal_x * normal_x, contrast * normal_x *...  4.94 us
    ppermute x1, waiting for transfers between devices, line_sum(): back = lax.ppermute(kept, 'slab', pair)  4.74 us
    dot_general x1, matrix products, shards(): jnp.einsum('kxy,ycn->kxcn', fields, col_table, precision=lax.Precision.HIGH)  4.28 us
    ppermute x1, starting transfers between devices, extended_2(): lax.ppermute(lax.slice_in_dim(block, 0, width, axis=dim), axis, backward)  4.09 us
    div x3, other arithmetic, smooth_once(): (4.0 * middle + extended[:-2] + extended[2:] + jnp.roll(middle, 1, 1) + j...  3.89 us
  transfers between devices with their start and end apart: 7, of which 7 were waited for; matrix products, arithmetic and copies ran while one was open for 2% of the time, Pallas kernels for 0%

profile of v20, /device:TPU:0, one launch (start us, length us, event | category | flops | bytes accessed | tf_op | source)
XLA Modules:
  0.0 75.6 jit_solution(5600413276618499717)
XLA Ops:
  0.0 0.1 fusion.63
  0.2 0.2 fusion.70
  0.3 2.3 %select_add_fusion = f32[256,2048]{1,0:T(8,128)S(1)} fusion(s32[256,2048]{1,0:T(8,128)} %param.2), kind=kLoop, calls=%fused_computation.48 | loop fusion | flops 5767168 | bytes 4194304 | tf_op jit(solution)/shard_map/add | solution.py:43
  2.7 0.3 multiply_subtract_fusion
  3.0 1.5 %pad_maximum_fusion.6 = f32[2048,2,104]{2,0,1:T(8,128)} fusion(f32[2048,1,104]{2,0,1:T(8,128)S(1)} %bitcast.75, f32[2048,1,104]{2,0,1:T(8,128)S(1)} %bitcast.74), kind=kLoop, calls=%fused_computation.39 | loop fusion | flops 425984 | bytes 3407872 | tf_op jit(solution)/shard_map/stack | solution.py:255
  4.4 0.5 collective-permute-start
  5.0 4.1 %collective-permute-start.1 = (f32[4,2048]{1,0:T(4,128)S(1)}, f32[4,2048]{1,0:T(4,128)S(1)}, u32[]{:S(2)}, u32[]{:S(2)}) collective-permute-start(f32[4,2048]{1,0:T(4,128)S(1)} %get-tuple-element.28), channel_id=1, source_target_pairs={{1,0},{2,1},{3,2},{4,3},{5,4},{6,5},{7,6},{0,7},{9,8},{10,9},{11,1... | collective-permute-start | bytes 98312 | tf_op jit(solution)/shard_map/ppermute | solution.py:35
  9.1 0.2 fusion.68
  9.3 0.1 copy.6
  9.5 0.1 copy.7
  9.6 1.0 %collective-permute-done = f32[4,2048]{1,0:T(4,128)S(1)} collective-permute-done((f32[4,2048]{1,0:T(4,128)S(1)}, f32[4,2048]{1,0:T(4,128)S(1)}, u32[]{:S(2)}, u32[]{:S(2)}) %collective-permute-start) | collective-permute-done | bytes 32800 | tf_op jit(solution)/shard_map/ppermute | solution.py:32
  10.7 0.3 pad_maximum_fusion.5
  11.0 0.9 %fusion.83 = (f32[262,2047]{1,0:T(8,128)S(1)}, f32[262,2047]{1,0:T(8,128)S(1)}) fusion(f32[264,2048]{1,0:T(8,128)S(1)} %pad_maximum_fusion.5), kind=kLoop, calls=%fused_computation.153 | loop fusion | bytes 8581024 | tf_op jit(solution)/shard_map/jit(_roll_static)/slice | solution.py:56
  11.8 2.1 %fusion.15 = f32[262,2048]{1,0:T(8,128)S(1)} fusion(f32[4,2048]{1,0:T(4,128)S(1)} %collective-permute-done.1, f32[256,2048]{1,0:T(8,128)S(1)} %select_add_fusion, f32[4,2048]{1,0:T(4,128)S(1)} %collective-permute-done, f32[264,2048]{1,0:T(8,128)S(1)} %pad_maximum_fusion.5, f32[262,2047]{1,0:T(8,128)S(1)} %get-tuple-element.26, ...), kind=kLoop, calls=%fused_computation.26 | loop fusion | flops 6438912 | bytes 15038416 | tf_op jit(solution)/shard_map/div | solution.py:51
  14.0 0.9 %fusion.81 = (f32[260,2047]{1,0:T(8,128)S(1)}, f32[260,2047]{1,0:T(8,128)S(1)}) fusion(f32[262,2048]{1,0:T(8,128)S(1)} %fusion.15), kind=kLoop, calls=%fused_computation.151 | loop fusion | bytes 8515520 | tf_op jit(solution)/shard_map/jit(_roll_static)/slice | solution.py:56
  14.9 0.1 fusion.82
  15.0 0.9 %fusion.12 = f32[260,2048]{1,0:T(8,128)S(1)} fusion(f32[262,2048]{1,0:T(8,128)S(1)} %fusion.15, f32[260,2047]{1,0:T(8,128)S(1)} %get-tuple-element.22, f32[260,1]{1,0:T(8,128)S(1)} %get-tuple-element.24, f32[260,1]{1,0:T(8,128)S(1)} %get-tuple-element.23, f32[260,2047]{1,0:T(8,128)S(1)} %get-tuple-element.21), kind=kLoop, calls=%fused_computation.20 | loop fusion | flops 4259840 | bytes 12779520 | tf_op jit(solution)/shard_map/div | solution.py:51
  15.9 0.9 %fusion.79 = (f32[258,2047]{1,0:T(8,128)S(1)}, f32[258,2047]{1,0:T(8,128)S(1)}) fusion(f32[260,2048]{1,0:T(8,128)S(1)} %fusion.12), kind=kLoop, calls=%fused_computation.149 | loop fusion | bytes 8450016 | tf_op jit(solution)/shard_map/jit(_roll_static)/slice | solution.py:56
  16.9 0.9 %fusion.9 = f32[258,2048]{1,0:T(8,128)S(1)} fusion(f32[260,2048]{1,0:T(8,128)S(1)} %fusion.12, f32[258,2047]{1,0:T(8,128)S(1)} %get-tuple-element.18, f32[258,1]{1,0:T(8,128)S(1)} %get-tuple-element.20, f32[258,1]{1,0:T(8,128)S(1)} %get-tuple-element.19, f32[258,2047]{1,0:T(8,128)S(1)} %get-tuple-element.17), kind=kLoop, calls=%fused_computation.14 | loop fusion | flops 4227072 | bytes 12681216 | tf_op jit(solution)/shard_map/div | solution.py:51
  17.7 1.1 %fusion.77 = (f32[256,2047]{1,0:T(8,128)S(1)}, f32[256,2047]{1,0:T(8,128)S(1)}) fusion(f32[258,2048]{1,0:T(8,128)S(1)} %fusion.9), kind=kLoop, calls=%fused_computation.147 | loop fusion | bytes 8384512 | tf_op jit(solution)/shard_map/jit(_roll_static)/slice | solution.py:63
  18.9 2.1 %multiply_bitcast_fusion.1 = (f32[1,256,2048]{2,1,0:T(8,128)S(1)}, f32[256,2048]{1,0:T(8,128)S(1)}) fusion(f32[256,2048]{1,0:T(8,128)S(1)} %select_add_fusion, f32[256,2047]{1,0:T(8,128)S(1)} %get-tuple-element.14, f32[256,1]{1,0:T(8,128)S(1)} %get-tuple-element.16, f32[256,1]{1,0:T(8,128)S(1)} %get-tuple-element.15, f32[256,2047]{1,0:T(8,128)S(1)} %get-tuple-element.13, ...), kind=kLoop, calls=%fused_computation.44 | loop fusion | flops 7864320 | bytes 14680064 | tf_op jit(solution)/shard_map/stack | solution.py:266
  21.1 2.3 %multiply_bitcast_fusion = (f32[1,256,2048]{2,1,0:T(8,128)S(1)}, f32[256,2048]{1,0:T(8,128)S(1)}) fusion(f32[256,2048]{1,0:T(8,128)S(1)} %get-tuple-element.10, f32[256,2048]{1,0:T(8,128)S(1)} %select_add_fusion, f32[258,2048]{1,0:T(8,128)S(1)} %fusion.9, f32[256,2047]{1,0:T(8,128)S(1)} %get-tuple-element.14, f32[256,1]{1,0:T(8,128)S(1)} %get-tuple-element.16, ...), kind=kLoop, calls=%fused_computation.43 | loop fusion | flops 7864320 | bytes 16777216 | tf_op jit(solution)/shard_map/stack | solution.py:266
  23.4 0.5 fusion.18
  23.9 1.1 %copy-done = f32[2048,2,104]{2,0,1:T(8,128)S(1)} copy-done((f32[2048,2,104]{2,0,1:T(8,128)S(1)}, f32[2048,2,104]{2,0,1:T(8,128)}, u32[]{:S(2)}) %copy-start) | copy-done | bytes 1703960
  24.9 4.3 %fusion.24 = f32[4,256,2,104,1]{1,3,4,2,0:T(8,128)S(1)} fusion(f32[2048,2,104]{2,0,1:T(8,128)S(1)} %copy-done, f32[1,256,2048]{2,1,0:T(8,128)S(1)} %fusion.18, f32[1,256,2048]{2,1,0:T(8,128)S(1)} %get-tuple-element.11, f32[1,256,2048]{2,1,0:T(8,128)S(1)} %get-tuple-element.9, f32[1,256,2048]{2,1,0:T(8,128)S(1)} %bitcast.73), kind=kOutput, calls=%fused_computation.51 | convolution fusion | flops 2623537152 | bytes 10944512 | tf_op jit(solution)/shard_map/kxy,ycn->kxcn/dot_general | solution.py:274
  29.2 0.9 %convolution_bitcast_fusion = f32[2,4,208,2,104]{2,4,0,3,1:T(8,128)S(1)} fusion(f32[4,256,2,104,1]{1,3,4,2,0:T(8,128)S(1)} %fusion.24, f32[1,208,256]{2,1,0:T(8,128)S(1)} %copy.7, f32[1,208,256]{2,1,0:T(8,128)S(1)} %copy.6), kind=kOutput, calls=%fused_computation.50 | convolution fusion | flops 531734528 | bytes 2662400 | tf_op jit(solution)/shard_map/smx,kxcn->skmcn/dot_general | solution.py:85
  30.1 0.1 broadcast_select_fusion
  30.2 0.2 copy.9
  30.4 0.4 select_n.154
  30.8 0.4 collective-permute-start.2
  31.2 0.2 copy.8
  31.3 0.4 select_n.152
  31.7 0.8 %collective-permute-done.2 = f32[676,128]{1,0:T(8,128)S(1)} collective-permute-done((f32[676,128]{1,0:T(8,128)S(1)}, f32[676,128]{1,0:T(8,128)S(1)}, u32[]{:S(2)}, u32[]{:S(2)}) %collective-permute-start.2) | collective-permute-done | bytes 346144 | tf_op jit(solution)/shard_map/ppermute | solution.py:194
  32.6 1.6 %collective-permute-start.3 = (f32[344,128]{1,0:T(8,128)S(1)}, f32[344,128]{1,0:T(8,128)S(1)}, u32[]{:S(2)}, u32[]{:S(2)}) collective-permute-start(f32[344,128]{1,0:T(8,128)S(1)} %slice_select_fusion), channel_id=1, source_target_pairs={{0,2},{1,3},{2,0},{3,1},{4,6},{5,7},{6,4},{7,5},{8,10},{9,11},{10,... | collective-permute-start | bytes 528392 | tf_op jit(solution)/shard_map/ppermute | solution.py:205
  34.2 5.2 %collective-permute-done.3 = f32[344,128]{1,0:T(8,128)S(1)} collective-permute-done((f32[344,128]{1,0:T(8,128)S(1)}, f32[344,128]{1,0:T(8,128)S(1)}, u32[]{:S(2)}, u32[]{:S(2)}) %collective-permute-start.3) | collective-permute-done | bytes 176160 | tf_op jit(solution)/shard_map/ppermute | solution.py:205
  39.4 2.6 %collective-permute-start.4 = (f32[344,128]{1,0:T(8,128)S(1)}, f32[344,128]{1,0:T(8,128)S(1)}, u32[]{:S(2)}, u32[]{:S(2)}) collective-permute-start(f32[344,128]{1,0:T(8,128)S(1)} %select_add_fusion.1), channel_id=1, source_target_pairs={{0,4},{1,5},{2,6},{3,7},{4,0},{5,1},{6,2},{7,3},{8,12},{9,13},{10,... | collective-permute-start | bytes 528392 | tf_op jit(solution)/shard_map/ppermute | solution.py:208
  42.0 7.9 %collective-permute-done.4 = f32[344,128]{1,0:T(8,128)S(1)} collective-permute-done((f32[344,128]{1,0:T(8,128)S(1)}, f32[344,128]{1,0:T(8,128)S(1)}, u32[]{:S(2)}, u32[]{:S(2)}) %collective-permute-start.4) | collective-permute-done | bytes 176160 | tf_op jit(solution)/shard_map/ppermute | solution.py:208
  50.0 0.8 %collective-permute-start.5 = (f32[344,128]{1,0:T(8,128)S(1)}, f32[344,128]{1,0:T(8,128)S(1)}, u32[]{:S(2)}, u32[]{:S(2)}) collective-permute-start(f32[344,128]{1,0:T(8,128)S(1)} %add.205), channel_id=1, source_target_pairs={{0,2},{1,3},{2,0},{3,1},{4,6},{5,7},{6,4},{7,5},{8,10},{9,11},{10,... | collective-permute-start | bytes 528392 | tf_op jit(solution)/shard_map/ppermute | solution.py:210
  50.7 4.7 %collective-permute-done.5 = f32[344,128]{1,0:T(8,128)S(1)} collective-permute-done((f32[344,128]{1,0:T(8,128)S(1)}, f32[344,128]{1,0:T(8,128)S(1)}, u32[]{:S(2)}, u32[]{:S(2)}) %collective-permute-start.5) | collective-permute-done | bytes 176160 | tf_op jit(solution)/shard_map/ppermute | solution.py:210
  55.6 0.4 stack_reshape.4
  56.1 1.2 %collective-permute-done.6 = f32[676,128]{1,0:T(8,128)S(1)} collective-permute-done((f32[676,128]{1,0:T(8,128)S(1)}, f32[676,128]{1,0:T(8,128)S(1)}, u32[]{:S(2)}, u32[]{:S(2)}) %collective-permute-start.6) | collective-permute-done | bytes 346144 | tf_op jit(solution)/shard_map/ppermute | solution.py:225
  57.2 0.4 stack_reshape.5
  57.8 0.6 fusion.28
  58.5 0.6 fusion.29
  59.1 0.8 %multiply_add_fusion = f32[2,4,208,256]{3,2,1,0:T(8,128)S(1)} fusion(f32[2,4,208,256]{3,2,1,0:T(8,128)S(1)} %fusion.29, f32[2,4,104,208]{2,3,1,0:T(8,128)S(1)} %fusion.28, f32[2]{0:T(128)S(1)} %copy-done.1, s32[256]{0:T(256)S(1)} %iota_subtract_fusion, pred[256]{0:T(512)(128)(4,1)S(1)} %iota_compare_fusion.3), kind=kOutput, calls=%fused_computation.49 | convolution fusion | flops 532533248 | bytes 4101384 | tf_op jit(solution)/shard_map/ad,skdc,cb->skab/dot_general | solution.py:291
  59.9 0.7 slice_bitcast_fusion.3
  60.7 2.0 %pad_maximum_fusion.fl_ref = f32[2,4,4,208,128]{4,3,2,1,0:T(8,128)} fusion(f32[2,1,4,208,128]{4,3,2,1,0:T(8,128)S(1)} %get-tuple-element.30, f32[2,1,4,208,128]{4,3,2,1,0:T(8,128)S(1)} %get-tuple-element.31, f32[2,1,4,208,128]{4,3,2,1,0:T(8,128)S(1)} %get-tuple-element.32, f32[2,1,4,208,128]{4,3,2,1,0:T(8,128)S(1)} %get-tuple-element.29), kind=kLoop, calls=%fused_computation.8 | loop fusion | flops 2555904 | bytes 6815744 | tf_op jit(solution)/shard_map/stack | solution.py:295
  62.6 13.0 %shard_map.28 = f32[2,64,20402]{2,1,0:T(8,128)} custom-call(f32[2,4,4,208,128]{4,3,2,1,0:T(8,128)} %pad_maximum_fusion.fl_ref), custom_call_target="tpu_custom_call" | custom-call | tf_op jit(solution)/shard_map/pallas_call | solution.py:179
  (24 shorter events, 0.8 us)
Async XLA Ops:
  4.4 6.2 %collective-permute-start = (f32[4,2048]{1,0:T(4,128)S(1)}, f32[4,2048]{1,0:T(4,128)S(1)}, u32[]{:S(2)}, u32[]{:S(2)}) collective-permute-start(f32[4,2048]{1,0:T(4,128)S(1)} %get-tuple-element.27), channel_id=1, source_target_pairs={{0,1},{1,2},{2,3},{3,4},{4,5},{5,6},{6,7},{7,0},{8,9},{9,10},{10,1... | collective-permute-start | bytes 98312 | tf_op jit(solution)/shard_map/ppermute | solution.py:32
  5.0 5.7 %collective-permute-start.1 = (f32[4,2048]{1,0:T(4,128)S(1)}, f32[4,2048]{1,0:T(4,128)S(1)}, u32[]{:S(2)}, u32[]{:S(2)}) collective-permute-start(f32[4,2048]{1,0:T(4,128)S(1)} %get-tuple-element.28), channel_id=1, source_target_pairs={{1,0},{2,1},{3,2},{4,3},{5,4},{6,5},{7,6},{0,7},{9,8},{10,9},{11,1... | collective-permute-start | bytes 98312 | tf_op jit(solution)/shard_map/ppermute | solution.py:35
  23.3 1.6 %copy-start = (f32[2048,2,104]{2,0,1:T(8,128)S(1)}, f32[2048,2,104]{2,0,1:T(8,128)}, u32[]{:S(2)}) copy-start(f32[2048,2,104]{2,0,1:T(8,128)} %pad_maximum_fusion.6) | copy-start | bytes 5111812
  30.8 1.7 %collective-permute-start.2 = (f32[676,128]{1,0:T(8,128)S(1)}, f32[676,128]{1,0:T(8,128)S(1)}, u32[]{:S(2)}, u32[]{:S(2)}) collective-permute-start(f32[676,128]{1,0:T(8,128)S(1)} %select_n.154), channel_id=1, source_target_pairs={{0,1},{1,0},{2,3},{3,2},{4,5},{5,4},{6,7},{7,6},{8,9},{9,8},{10,11... | collective-permute-start | bytes 1038344 | tf_op jit(solution)/shard_map/ppermute | solution.py:194
  32.6 6.8 %collective-permute-start.3 = (f32[344,128]{1,0:T(8,128)S(1)}, f32[344,128]{1,0:T(8,128)S(1)}, u32[]{:S(2)}, u32[]{:S(2)}) collective-permute-start(f32[344,128]{1,0:T(8,128)S(1)} %slice_select_fusion), channel_id=1, source_target_pairs={{0,2},{1,3},{2,0},{3,1},{4,6},{5,7},{6,4},{7,5},{8,10},{9,11},{10,... | collective-permute-start | bytes 528392 | tf_op jit(solution)/shard_map/ppermute | solution.py:205
  39.4 10.6 %collective-permute-start.4 = (f32[344,128]{1,0:T(8,128)S(1)}, f32[344,128]{1,0:T(8,128)S(1)}, u32[]{:S(2)}, u32[]{:S(2)}) collective-permute-start(f32[344,128]{1,0:T(8,128)S(1)} %select_add_fusion.1), channel_id=1, source_target_pairs={{0,4},{1,5},{2,6},{3,7},{4,0},{5,1},{6,2},{7,3},{8,12},{9,13},{10,... | collective-permute-start | bytes 528392 | tf_op jit(solution)/shard_map/ppermute | solution.py:208
  50.0 5.5 %collective-permute-start.5 = (f32[344,128]{1,0:T(8,128)S(1)}, f32[344,128]{1,0:T(8,128)S(1)}, u32[]{:S(2)}, u32[]{:S(2)}) collective-permute-start(f32[344,128]{1,0:T(8,128)S(1)} %add.205), channel_id=1, source_target_pairs={{0,2},{1,3},{2,0},{3,1},{4,6},{5,7},{6,4},{7,5},{8,10},{9,11},{10,... | collective-permute-start | bytes 528392 | tf_op jit(solution)/shard_map/ppermute | solution.py:210
  55.5 1.7 %collective-permute-start.6 = (f32[676,128]{1,0:T(8,128)S(1)}, f32[676,128]{1,0:T(8,128)S(1)}, u32[]{:S(2)}, u32[]{:S(2)}) collective-permute-start(f32[676,128]{1,0:T(8,128)S(1)} %fusion.32), channel_id=1, source_target_pairs={{0,1},{1,0},{2,3},{3,2},{4,5},{5,4},{6,7},{7,6},{8,9},{9,8},{10,11... | collective-permute-start | bytes 1038344 | tf_op jit(solution)/shard_map/ppermute | solution.py:225
  57.8 1.3 %copy-start.1 = (f32[2]{0:T(128)S(1)}, f32[2]{0:T(128)}, u32[]{:S(2)}) copy-start(f32[2]{0:T(128)} %constant.122.clone) | copy-start | bytes 28
